TPU v7x, 128 devices: a whole 4x4x4 slice. The times are simulated.
128 devices in a mesh: row: 16 (over z, y), col: 8 (over x, core).
Axes of the slice: x: 4, y: 4, z: 4, core: 2. Of those that a mesh axis runs over, the one named last changes fastest.
Arguments:
- holograms: float32 [2, 8192, 8192], P(None, 'row', 'col'), may hold values from -6 to 6
- sideband_centre: int32 [2, 2], replicated, may hold values from 1024 to 4095
- strip_owner: int32 [128], replicated, may hold values from 0 to 127, as said below
Outputs:
- slm_pattern: float32 [2, 2, 12288, 4096], P(None, None, ('row', 'col'))
Inputs may be any that keep to these rules, and one draw needn't show every extreme that they name: `strip_owner`: every device drives at most 3 strips, and in every draw some device drives exactly 3; some drive none.
All inputs are finite; a program needn't handle non-finite values.
Results may differ from a plain program's by a relative error of at most 0.0003.
Values sent between devices are 32-bit elements; how exact they have to be, the bound alone decides.
No kernel may reach another device: no remote copies, remote signals or barrier semaphores. Data moves between devices by JAX's collectives and lax.ppermute only.
A program may use at most 128 MiB of HBM per device.

v0:
```python
import math

import jax
import jax.numpy as jnp
from jax import lax
from jax.sharding import PartitionSpec as P

H = 8192
S = 2048
P_SIZE = 4096
MOST = 3


two_pi = 2.0 * math.pi
radix = 128
headroom = 1.25
softness = 0.01
epsilon = 1e-06


def contract(form, left, right):
    return jnp.einsum(
        form, left, right, precision=lax.Precision.HIGHEST, preferred_element_type=jnp.float32
    )


def make_tables(frequency, in_len, length, offset, sign):
    accum = length // radix
    blocks = in_len // radix
    first = frequency[:, :accum] % accum
    inner_index = first[:, :, None] * jnp.arange(blocks, dtype=jnp.int32)[None, None, :] % accum
    inner_angle = sign * two_pi / accum * inner_index.astype(jnp.float32)
    column = (jnp.arange(radix, dtype=jnp.int32) + offset) % length
    outer_index = frequency[:, :, None] * column[None, None, :] % length
    outer_angle = sign * two_pi / length * outer_index.astype(jnp.float32)
    shape_four = (frequency.shape[0], frequency.shape[1] // accum, accum, radix)
    return (
        jnp.cos(inner_angle),
        jnp.sin(inner_angle),
        jnp.cos(outer_angle).reshape(shape_four),
        jnp.sin(outer_angle).reshape(shape_four),
    )


def transform(real_part, imag_part, tables):
    inner_cos, inner_sin, outer_cos, outer_sin = tables
    batch, rows, width = real_part.shape
    blocks = width // radix
    real_four = real_part.reshape(batch, rows, blocks, radix)
    mid_real = contract("kpa,krab->krpb", inner_cos, real_four)
    mid_imag = contract("kpa,krab->krpb", inner_sin, real_four)
    if imag_part is not None:
        imag_four = imag_part.reshape(batch, rows, blocks, radix)
        mid_real = mid_real - contract("kpa,krab->krpb", inner_sin, imag_four)
        mid_imag = mid_imag + contract("kpa,krab->krpb", inner_cos, imag_four)
    out_real = contract("kqpb,krpb->krqp", outer_cos, mid_real) - contract(
        "kqpb,krpb->krqp", outer_sin, mid_imag
    )
    out_imag = contract("kqpb,krpb->krqp", outer_cos, mid_imag) + contract(
        "kqpb,krpb->krqp", outer_sin, mid_real
    )
    count = outer_cos.shape[1] * outer_cos.shape[2]
    return (out_real.reshape(batch, rows, count), out_imag.reshape(batch, rows, count))


def encode(field_real, field_imag, peak):
    scale = headroom * peak + epsilon
    unit_real = field_real / scale
    unit_imag = field_imag / scale
    square = unit_real * unit_real + unit_imag * unit_imag
    height = jnp.sqrt(1.0 - square)
    spread = jnp.sqrt(square + softness)
    phase_real = unit_real / spread
    phase_imag = unit_imag / spread
    plus_real = unit_real - phase_imag * height
    plus_imag = unit_imag + phase_real * height
    minus_real = unit_real + phase_imag * height
    minus_imag = unit_imag - phase_real * height
    return (plus_real, plus_imag, minus_real, minus_imag)


def body(holograms, sideband_centre, strip_owner):
    holo_count = holograms.shape[0]
    row_devices = lax.axis_size("row")
    col_devices = lax.axis_size("col")
    devices = row_devices * col_devices
    half = S // 2
    offsets = jnp.arange(S, dtype=jnp.int32) - half
    along_u = (sideband_centre[:, 0:1] + offsets[None, :]) % H
    along_v = (sideband_centre[:, 1:2] + offsets[None, :]) % H
    table_v = make_tables(along_v, H, H, 0, -1.0)
    table_u = make_tables(along_u, H, H, 0, -1.0)
    pixels = jnp.broadcast_to(jnp.arange(P_SIZE, dtype=jnp.int32)[None, :], (holo_count, P_SIZE))
    table_p = make_tables(pixels, S, P_SIZE, P_SIZE - half, 1.0)
    local_rows = holograms.shape[1]
    local_cols = holograms.shape[2]
    blocks = holograms.reshape(holo_count, col_devices, local_rows // col_devices, local_cols)
    piece = lax.all_to_all(blocks, "col", split_axis=1, concat_axis=3, tiled=True)
    lead, single, count, width = piece.shape
    out_real, out_imag = transform(piece.reshape(lead, count, width), None, table_v)
    spec_real = out_real.reshape(lead, single, count, S)
    spec_imag = out_imag.reshape(lead, single, count, S)
    pencil = spec_real.shape[2]
    share = S // devices
    col_real = jnp.swapaxes(spec_real.reshape(holo_count, pencil, S), 1, 2)
    col_imag = jnp.swapaxes(spec_imag.reshape(holo_count, pencil, S), 1, 2)
    piece_real = lax.all_to_all(
        col_real.reshape(holo_count, devices, share, pencil),
        ("row", "col"),
        split_axis=1,
        concat_axis=3,
        tiled=True,
    )
    piece_imag = lax.all_to_all(
        col_imag.reshape(holo_count, devices, share, pencil),
        ("row", "col"),
        split_axis=1,
        concat_axis=3,
        tiled=True,
    )
    lead, single, count, width = piece_real.shape
    out_real, out_imag = transform(
        piece_real.reshape(lead, count, width), piece_imag.reshape(lead, count, width), table_u
    )
    side_real = out_real.reshape(lead, single, count, S)
    side_imag = out_imag.reshape(lead, single, count, S)
    lift_real, lift_imag = transform(
        side_real.reshape(holo_count, share, S), side_imag.reshape(holo_count, share, S), table_p
    )
    strips = strip_owner.shape[0]
    strip_rows = P_SIZE // strips
    slot_rows = MOST * strip_rows
    strip_ids = jnp.arange(strips, dtype=jnp.int32)
    same = strip_owner[:, None] == strip_owner[None, :]
    before = strip_ids[None, :] < strip_ids[:, None]
    rank = jnp.sum((same & before).astype(jnp.int32), axis=1)
    slot_of = strip_owner * MOST + rank
    slot_ids = jnp.arange(strips * MOST, dtype=jnp.int32)
    match = slot_of[None, :] == slot_ids[:, None]
    source = jnp.sum(jnp.where(match, strip_ids[None, :], 0), axis=1)
    filled = jnp.any(match, axis=1).astype(jnp.float32)

    def pack(part):
        grouped = part.reshape(holo_count, share, strips, strip_rows)
        picked = jnp.take(grouped, source, axis=2) * filled[None, None, :, None]
        return jnp.transpose(picked.reshape(holo_count, share, strips, slot_rows), (2, 0, 1, 3))

    send_real = pack(lift_real)
    send_imag = pack(lift_imag)
    piece_real = lax.all_to_all(send_real, ("row", "col"), split_axis=0, concat_axis=2, tiled=True)
    piece_imag = lax.all_to_all(send_imag, ("row", "col"), split_axis=0, concat_axis=2, tiled=True)
    single, lead, width, count = piece_real.shape
    rows_real = jnp.swapaxes(piece_real.reshape(lead, width, count), 1, 2)
    rows_imag = jnp.swapaxes(piece_imag.reshape(lead, width, count), 1, 2)
    out_real, out_imag = transform(rows_real, rows_imag, table_p)
    field_real = out_real.reshape(single, lead, count, P_SIZE)
    field_imag = out_imag.reshape(single, lead, count, P_SIZE)
    field_real = field_real.reshape(holo_count, slot_rows, P_SIZE)
    field_imag = field_imag.reshape(holo_count, slot_rows, P_SIZE)
    magnitude = jnp.sqrt(field_real * field_real + field_imag * field_imag)
    local_peak = jnp.max(magnitude, axis=(1, 2))
    peak = lax.pmax(local_peak, ("row", "col"))
    plus_real, plus_imag, minus_real, minus_imag = encode(
        field_real, field_imag, peak[:, None, None]
    )
    device_index = lax.axis_index("row") * col_devices + lax.axis_index("col")
    my_source = lax.dynamic_slice_in_dim(source, device_index * MOST, MOST)
    row_number = (
        my_source[:, None] * strip_rows + jnp.arange(strip_rows, dtype=jnp.int32)[None, :]
    ).reshape(slot_rows)
    even = (row_number[:, None] + jnp.arange(P_SIZE, dtype=jnp.int32)[None, :]) % 2 == 0
    out_real = jnp.where(even[None, :, :], plus_real, minus_real)
    out_imag = jnp.where(even[None, :, :], plus_imag, minus_imag)
    return jnp.stack([out_real, out_imag], axis=1)


def solution(mesh):
    placed = (P(None, "row", "col"), P(), P())
    return jax.shard_map(
        body,
        mesh=mesh,
        in_specs=placed,
        out_specs=P(None, None, ("row", "col"), None),
        check_vma=False,
    )
```

profile of v0, /device:TPU:0, one launch (start us, length us, event | category | flops | bytes accessed | tf_op | source)
XLA Modules:
  0.0 617.8 jit_solution(9792790491537633555)
XLA Ops:
  10.6 48.5 %all-to-all-done = f32[2,8,64,1024]{3,2,0,1:T(8,128)} async-done(((f32[2,8,64,1024]{3,2,0,1:T(8,128)}), f32[2,8,64,1024]{3,2,0,1:T(8,128)}, u32[]{:S(2)}, u32[]{:S(2)}) %all-to-all-start) | async-done | bytes 4194336 | tf_op jit(solution)/shard_map/all_to_all | solution.py:98
  59.1 6.6 %copy.180 = f32[2,1,64,8,1024]{4,3,2,0,1:T(8,128)} copy(f32[2,1,64,8,1024]{4,2,0,3,1:T(8,128)} %bitcast.4) | data formatting | bytes 8388608 | tf_op jit(solution)/shard_map/all_to_all | solution.py:98
  70.6 6.2 %convolution_bitcast_fusion = f32[2,64,64,128]{3,2,1,0:T(8,128)S(1)} fusion(f32[2,64,64,128]{3,2,1,0:T(8,128)} %reshape_reshape.9, s32[2,64]{1,0:T(2,128)S(1)} %get-tuple-element.21), kind=kOutput, calls=%fused_computation.56 | convolution fusion | flops 805421056 | bytes 8389120 | tf_op jit(solution)/shard_map/kpa,krab->krpb/dot_general | solution.py:22
  81.2 15.5 %fusion.7 = f32[2,64,64,32]{2,3,1,0:T(8,128)S(1)} fusion(f32[2,64,64,128]{3,2,1,0:T(8,128)S(1)} %convolution_bitcast_fusion, s32[128]{0:T(128)S(1)} %and_select_fusion.3, s32[2,32,64]{1,2,0:T(8,128)S(1)} %get-tuple-element.10), kind=kOutput, calls=%fused_computation.24 | convolution fusion | flops 409993216 | bytes 5259776 | tf_op jit(solution)/shard_map/kqpb,krpb->krqp/dot_general | solution.py:22
  96.7 17.6 %subtract_bitcast_fusion.2 = f32[2,64,32,64]{1,2,3,0:T(8,128)} fusion(f32[2,64,64,32]{2,3,1,0:T(8,128)S(1)} %fusion.7, f32[2,64,64,128]{3,2,1,0:T(8,128)S(1)} %convolution_bitcast_fusion.1, s32[128]{0:T(128)S(1)} %and_select_fusion.3, s32[2,32,64]{1,2,0:T(8,128)S(1)} %get-tuple-element.10), kind=kOutput, calls=%fused_computation.73 | convolution fusion | flops 410255360 | bytes 6308352 | tf_op jit(solution)/shard_map/kqpb,krpb->krqp/dot_general | solution.py:22
  124.0 9.9 %all-to-all-start.1 = ((f32[128,1,2048]{2,1,0:T(1,128)}), f32[128,1,2048]{2,1,0:T(1,128)}, u32[]{:S(2)}, u32[]{:S(2)}) async-start(f32[128,1,2048]{2,1,0:T(1,128)} %reshape.373), calls=%async_computation.1 | async-start | bytes 2097152 | tf_op jit(solution)/shard_map/all_to_all | solution.py:107
  133.8 17.1 %fusion.5 = f32[2,64,64,32]{2,3,1,0:T(8,128)S(1)} fusion(f32[2,64,64,128]{3,2,1,0:T(8,128)} %copy-done.5, s32[128]{0:T(128)S(1)} %and_select_fusion.3, s32[2,32,64]{1,2,0:T(8,128)S(1)} %get-tuple-element.10), kind=kOutput, calls=%fused_computation.22 | convolution fusion | flops 409993216 | bytes 5259776 | tf_op jit(solution)/shard_map/kqpb,krpb->krqp/dot_general | solution.py:22
  150.9 17.7 %add_bitcast_fusion.2 = f32[2,64,32,64]{1,2,3,0:T(8,128)} fusion(f32[2,64,64,32]{2,3,1,0:T(8,128)S(1)} %fusion.5, f32[2,64,64,128]{3,2,1,0:T(8,128)S(1)} %copy-done.4, s32[128]{0:T(128)S(1)} %and_select_fusion.3, s32[2,32,64]{1,2,0:T(8,128)S(1)} %get-tuple-element.10), kind=kOutput, calls=%fused_computation.72 | convolution fusion | flops 410255360 | bytes 6308352 | tf_op jit(solution)/shard_map/kqpb,krpb->krqp/dot_general | solution.py:22
  178.3 10.4 %all-to-all-start.2 = ((f32[128,1,2048]{2,1,0:T(1,128)}), f32[128,1,2048]{2,1,0:T(1,128)}, u32[]{:S(2)}, u32[]{:S(2)}) async-start(f32[128,1,2048]{2,1,0:T(1,128)} %reshape.375), calls=%async_computation.2 | async-start | bytes 2097152 | tf_op jit(solution)/shard_map/all_to_all | solution.py:114
  201.1 6.1 all-to-all-done.2
  218.8 11.5 %fusion.80 = f32[2,64,16,32]{3,2,1,0:T(8,128)S(1)} fusion(s32[128]{0:T(128)S(1)} %and_select_fusion.3, s32[2,32,64]{1,2,0:T(8,128)S(1)} %get-tuple-element.11, f32[2,16,64,128]{3,2,1,0:T(8,128)S(1)} %fusion.61), kind=kOutput, calls=%fused_computation.98 | convolution fusion | flops 108003328 | bytes 1327616 | tf_op jit(solution)/shard_map/kqpb,krpb->krqp/dot_general | solution.py:22
  230.3 13.6 %fusion.78 = f32[2,64,16,32]{3,2,1,0:T(8,128)} fusion(s32[128]{0:T(128)S(1)} %and_select_fusion.3, s32[2,32,64]{1,2,0:T(8,128)S(1)} %get-tuple-element.11, f32[2,16,64,128]{3,2,1,0:T(8,128)S(1)} %fusion.60), kind=kOutput, calls=%fused_computation.97 | convolution fusion | flops 108003328 | bytes 1327616 | tf_op jit(solution)/shard_map/kqpb,krpb->krqp/dot_general | solution.py:22
  243.9 11.4 %fusion.59 = f32[2,16,32,64]{2,1,3,0:T(8,128)S(1)} fusion(f32[2,64,16,32]{3,2,1,0:T(8,128)S(1)} %fusion.80, s32[128]{0:T(128)S(1)} %and_select_fusion.3, s32[2,32,64]{1,2,0:T(8,128)S(1)} %get-tuple-element.11, f32[2,16,64,128]{3,2,1,0:T(8,128)S(1)} %fusion.60), kind=kOutput, calls=%fused_computation.82 | convolution fusion | flops 108068864 | bytes 1589760 | tf_op jit(solution)/shard_map/kqpb,krpb->krqp/dot_general | solution.py:22
  257.6 13.1 %fusion.58 = f32[2,16,32,64]{2,1,3,0:T(8,128)S(1)} fusion(f32[2,64,16,32]{3,2,1,0:T(8,128)} %fusion.78, s32[128]{0:T(128)S(1)} %and_select_fusion.3, s32[2,32,64]{1,2,0:T(8,128)S(1)} %get-tuple-element.11, f32[2,16,64,128]{3,2,1,0:T(8,128)} %copy-done.9), kind=kOutput, calls=%fused_computation.80 | convolution fusion | flops 108068864 | bytes 1589760 | tf_op jit(solution)/shard_map/kqpb,krpb->krqp/dot_general | solution.py:22
  272.6 14.0 %fusion.35 = f32[2,32,16,128]{3,2,1,0:T(8,128)S(1)} fusion(s32[128]{0:T(128)S(1)} %and_select_fusion, s32[128,32]{0,1:T(8,128)S(1)} %multiply_add_fusion.1, f32[2,16,32,128]{3,2,1,0:T(8,128)S(1)} %fusion.63), kind=kOutput, calls=%fused_computation.69 | convolution fusion | flops 216006656 | bytes 1065472 | tf_op jit(solution)/shard_map/kqpb,krpb->krqp/dot_general | solution.py:22
  286.7 14.1 %fusion.33 = f32[2,32,16,128]{3,2,1,0:T(8,128)S(1)} fusion(s32[128]{0:T(128)S(1)} %and_select_fusion, s32[128,32]{0,1:T(8,128)S(1)} %multiply_add_fusion.1, f32[2,16,32,128]{3,2,1,0:T(8,128)S(1)} %fusion.62), kind=kOutput, calls=%fused_computation.68 | convolution fusion | flops 216006656 | bytes 1065472 | tf_op jit(solution)/shard_map/kqpb,krpb->krqp/dot_general | solution.py:22
  300.8 14.4 %fusion.67 = f32[2,16,128,32]{2,1,3,0:T(8,128)S(1)} fusion(f32[2,32,16,128]{3,2,1,0:T(8,128)S(1)} %fusion.35, s32[128]{0:T(128)S(1)} %and_select_fusion, s32[128,32]{0,1:T(8,128)S(1)} %multiply_add_fusion.1, f32[2,16,32,128]{3,2,1,0:T(8,128)S(1)} %fusion.62), kind=kOutput, calls=%fused_computation.92 | convolution fusion | flops 216137728 | bytes 1589760 | tf_op jit(solution)/shard_map/kqpb,krpb->krqp/dot_general | solution.py:22
  315.2 14.1 %fusion.73 = f32[2,16,128,32]{2,1,3,0:T(8,128)S(1)} fusion(f32[2,32,16,128]{3,2,1,0:T(8,128)S(1)} %fusion.33, s32[128]{0:T(128)S(1)} %and_select_fusion, s32[128,32]{0,1:T(8,128)S(1)} %multiply_add_fusion.1, f32[2,16,32,128]{3,2,1,0:T(8,128)S(1)} %fusion.63), kind=kOutput, calls=%fused_computation.94 | convolution fusion | flops 216137728 | bytes 1589760 | tf_op jit(solution)/shard_map/kqpb,krpb->krqp/dot_general | solution.py:22
  332.5 5.3 gather_fusion
  337.8 6.3 %copy.202 = f32[384,2,16,32]{0,3,2,1:T(8,128)} copy(f32[384,2,16,32]{3,2,1,0:T(8,128)} %gather_fusion) | data formatting | bytes 3145728 | tf_op jit(solution)/shard_map/jit(_take)/gather | solution.py:145
  348.5 5.4 copy.210
  377.5 5.2 reshape.340
  387.0 15.7 %all-to-all-done.3 = f32[128,2,16,96]{3,2,1,0:T(8,128)S(1)} async-done(((f32[128,2,16,96]{3,2,1,0:T(8,128)}), f32[128,2,16,96]{3,2,1,0:T(8,128)S(1)}, u32[]{:S(2)}, u32[]{:S(2)}) %all-to-all-start.3) | async-done | bytes 1572896 | tf_op jit(solution)/shard_map/all_to_all | solution.py:150
  402.7 6.0 all-to-all-start.4
  423.0 15.6 %all-to-all-done.4 = f32[128,2,16,96]{3,2,1,0:T(8,128)} async-done(((f32[128,2,16,96]{3,2,1,0:T(8,128)}), f32[128,2,16,96]{3,2,1,0:T(8,128)}, u32[]{:S(2)}, u32[]{:S(2)}) %all-to-all-start.4) | async-done | bytes 1572896 | tf_op jit(solution)/shard_map/all_to_all | solution.py:151
  448.7 21.4 %fusion.13 = f32[2,32,96,128]{3,2,1,0:T(8,128)} fusion(f32[2,96,32,128]{3,2,1,0:T(8,128)S(1)} %add_bitcast_fusion.1, s32[128]{0:T(128)S(1)} %and_select_fusion, s32[128,32]{0,1:T(8,128)S(1)} %multiply_add_fusion.1), kind=kOutput, calls=%fused_computation.48 | convolution fusion | flops 1222639616 | bytes 6308352 | tf_op jit(solution)/shard_map/kqpb,krpb->krqp/dot_general | solution.py:22
  470.1 17.2 %fusion.15 = f32[2,32,96,128]{3,2,1,0:T(8,128)S(1)} fusion(f32[2,96,32,128]{3,2,1,0:T(8,128)S(1)} %add_bitcast_fusion.1, s32[128]{0:T(128)S(1)} %and_select_fusion, s32[128,32]{0,1:T(8,128)S(1)} %multiply_add_fusion.1), kind=kOutput, calls=%fused_computation.50 | convolution fusion | flops 1222639616 | bytes 6308352 | tf_op jit(solution)/shard_map/kqpb,krpb->krqp/dot_general | solution.py:22
  491.8 17.2 %subtract_bitcast_fusion = f32[2,96,128,32]{2,1,3,0:T(8,128)S(1)} fusion(f32[2,32,96,128]{3,2,1,0:T(8,128)S(1)} %fusion.15, s32[128]{0:T(128)S(1)} %and_select_fusion, s32[128,32]{0,1:T(8,128)S(1)} %multiply_add_fusion.1, f32[2,96,32,128]{3,2,1,0:T(8,128)S(1)} %subtract_bitcast_fusion.1), kind=kOutput, calls=%fused_computation.38 | convolution fusion | flops 1223426048 | bytes 9454080 | tf_op jit(solution)/shard_map/kqpb,krpb->krqp/dot_general | solution.py:22
  514.1 18.7 %sqrt_reduce_fusion = (f32[2]{0:T(128)S(1)}, f32[2,96,128,32]{2,1,3,0:T(8,128)S(1)}) fusion(f32[2,96,128,32]{2,1,3,0:T(8,128)} %copy-done.7, f32[2,32,96,128]{3,2,1,0:T(8,128)} %fusion.13, s32[128]{0:T(128)S(1)} %and_select_fusion, s32[128,32]{0,1:T(8,128)S(1)} %multiply_add_fusion.1, f32[2,96,32,128]{3,2,1,0:T(8,128)} %copy-done.8), kind=kOutput, calls=%fused_computation.36 | convolution fusion | flops 1226571776 | bytes 12599816 | tf_op jit(solution)/shard_map/kqpb,krpb->krqp/dot_general | solution.py:22
  532.8 62.3 %pmax.7 = f32[2]{0:T(128)S(1)} all-reduce(f32[2]{0:T(128)S(1)} %get-tuple-element.18), channel_id=1, replica_groups=mesh['row'=16,'col'=8] {'row','col'}, use_global_device_ids=true, to_apply=%region_4.6 | all-reduce | flops 2 | bytes 16 | tf_op jit(solution)/shard_map/pmax | solution.py:162
  598.5 7.0 %add_select_fusion.1 = (f32[2,1,96,4096]{2,3,0,1:T(8,128)S(1)}, f32[2,1,96,4096]{2,3,0,1:T(8,128)S(1)}) fusion(f32[2,96,128,32]{1,3,2,0:T(8,128)} %copy.220, f32[2]{0:T(128)S(1)} %multiply_add_fusion.2, f32[2,96,128,32]{1,3,2,0:T(8,128)} %copy.217, pred[96,4096]{0,1:T(8,128)(4,1)} %fusion.22), kind=kLoop, calls=%fused_computation.18 | loop fusion | flops 14155776 | bytes 12976136 | tf_op jit(solution)/shard_map/jit(_where)/select_n | solution.py:172
  609.3 8.3 %copy.221 = f32[2,2,96,4096]{3,2,1,0:T(8,128)} copy(f32[2,2,96,4096]{2,3,0,1:T(8,128)} %pad_maximum_fusion) | data formatting | bytes 12582912 | tf_op jit(solution)/shard_map/stack | solution.py:174
  (109 shorter events, 143.5 us)
Async XLA Ops:
  4.8 4.7 copy-start.11
  4.8 5.1 copy-start.10
  4.8 54.3 %all-to-all-start = ((f32[2,8,64,1024]{3,2,0,1:T(8,128)}), f32[2,8,64,1024]{3,2,0,1:T(8,128)}, u32[]{:S(2)}, u32[]{:S(2)}) async-start(f32[2,8,64,1024]{3,2,0,1:T(8,128)} %copy.179), calls=%async_computation | async-start | bytes 8388608 | tf_op jit(solution)/shard_map/all_to_all | solution.py:98
  70.6 6.2 %copy-start = (f32[2,64,64,128]{3,2,1,0:T(8,128)S(1)}, f32[2,64,64,128]{3,2,1,0:T(8,128)}, u32[]{:S(2)}) copy-start(f32[2,64,64,128]{3,2,1,0:T(8,128)} %reshape_reshape.9) | copy-start | bytes 12582916
  76.9 4.3 copy-start.5
  81.2 15.5 %copy-start.3 = (f32[2,64,64,128]{3,2,1,0:T(8,128)}, f32[2,64,64,128]{3,2,1,0:T(8,128)S(1)}, u32[]{:S(2)}) copy-start(f32[2,64,64,128]{3,2,1,0:T(8,128)S(1)} %convolution_bitcast_fusion.1) | copy-start | bytes 12582916
  124.0 54.3 %all-to-all-start.1 = ((f32[128,1,2048]{2,1,0:T(1,128)}), f32[128,1,2048]{2,1,0:T(1,128)}, u32[]{:S(2)}, u32[]{:S(2)}) async-start(f32[128,1,2048]{2,1,0:T(1,128)} %reshape.373), calls=%async_computation.1 | async-start | bytes 2097152 | tf_op jit(solution)/shard_map/all_to_all | solution.py:107
  133.8 17.1 %copy-start.4 = (f32[2,64,64,128]{3,2,1,0:T(8,128)S(1)}, f32[2,64,64,128]{3,2,1,0:T(8,128)}, u32[]{:S(2)}) copy-start(f32[2,64,64,128]{3,2,1,0:T(8,128)} %copy-done.3) | copy-start | bytes 12582916
  178.3 28.9 %all-to-all-start.2 = ((f32[128,1,2048]{2,1,0:T(1,128)}), f32[128,1,2048]{2,1,0:T(1,128)}, u32[]{:S(2)}, u32[]{:S(2)}) async-start(f32[128,1,2048]{2,1,0:T(1,128)} %reshape.375), calls=%async_computation.2 | async-start | bytes 2097152 | tf_op jit(solution)/shard_map/all_to_all | solution.py:114
  214.6 2.7 copy-start.6
  218.8 11.5 %copy-start.9 = (f32[2,16,64,128]{3,2,1,0:T(8,128)}, f32[2,16,64,128]{3,2,1,0:T(8,128)S(1)}, u32[]{:S(2)}) copy-start(f32[2,16,64,128]{3,2,1,0:T(8,128)S(1)} %fusion.61) | copy-start | bytes 3145732
  348.5 5.4 copy-start.2
  367.6 35.0 %all-to-all-start.3 = ((f32[128,2,16,96]{3,2,1,0:T(8,128)}), f32[128,2,16,96]{3,2,1,0:T(8,128)S(1)}, u32[]{:S(2)}, u32[]{:S(2)}) async-start(f32[128,2,16,96]{3,2,1,0:T(8,128)} %copy.204), calls=%async_computation.3 | async-start | bytes 4194304 | tf_op jit(solution)/shard_map/all_to_all | solution.py:150
  402.7 35.9 %all-to-all-start.4 = ((f32[128,2,16,96]{3,2,1,0:T(8,128)}), f32[128,2,16,96]{3,2,1,0:T(8,128)}, u32[]{:S(2)}, u32[]{:S(2)}) async-start(f32[128,2,16,96]{3,2,1,0:T(8,128)} %copy.212), calls=%async_computation.4 | async-start | bytes 4194304 | tf_op jit(solution)/shard_map/all_to_all | solution.py:151
  470.1 17.2 %copy-start.1 = (f32[2,96,128,32]{2,3,1,0:T(8,128)S(1)}, f32[2,96,128,32]{2,3,1,0:T(8,128)}, u32[]{:S(2)}) copy-start(f32[2,96,128,32]{2,3,1,0:T(8,128)} %fusion.136) | copy-start | bytes 9437188
  490.1 1.7 copy-start.8
  509.0 1.7 copy-start.7
where the time goes:
time: 624 us; the launch traced here: 618 us
  matrix products  287 us (46%)
  local copies, waits for them, and re-layouts  121 us (19%)
  waiting for transfers between devices  86 us (14%)
  blocking collectives  62.3 us (10%)
  starting transfers between devices  35.6 us (6%)
  other arithmetic  24.6 us (4%)
    dot_general x30, matrix products, contract(): jnp.einsum(form, left, right, precision=lax.Precision.HIGHEST, preferred_...  287 us
    pmax x1, blocking collectives, body(): peak = lax.pmax(local_peak, ('row', 'col'))  62.3 us
    all_to_all x1, waiting for transfers between devices, body(): lax.all_to_all(blocks, 'col', split_axis=1, concat_axis=3, tiled=True)  48.5 us
    gather x4, local copies, waits for them, and re-layouts, pack(): picked = jnp.take(grouped, source, axis=2) * filled[None, None, :, None]  21.4 us
    all_to_all x1, waiting for transfers between devices, body(): lax.all_to_all(send_real, ('row', 'col'), split_axis=0, concat_axis=2, ti...  15.7 us
    all_to_all x1, waiting for transfers between devices, body(): lax.all_to_all(send_imag, ('row', 'col'), split_axis=0, concat_axis=2, ti...  15.6 us
  transfers between devices with their start and end apart: 5, of which 4 were waited for; matrix products, arithmetic and copies ran while one was open for 14% of the time, Pallas kernels for 0%

commit v1 on v0

--- a/solution.py
+++ b/solution.py
@@ -90,7 +90,9 @@
     along_v = (sideband_centre[:, 1:2] + offsets[None, :]) % H
     table_v = make_tables(along_v, H, H, 0, -1.0)
     table_u = make_tables(along_u, H, H, 0, -1.0)
-    pixels = jnp.broadcast_to(jnp.arange(P_SIZE, dtype=jnp.int32)[None, :], (holo_count, P_SIZE))
+    pixels = lax.optimization_barrier(
+        jnp.broadcast_to(jnp.arange(P_SIZE, dtype=jnp.int32)[None, :], (holo_count, P_SIZE))
+    )
     table_p = make_tables(pixels, S, P_SIZE, P_SIZE - half, 1.0)
     local_rows = holograms.shape[1]
     local_cols = holograms.shape[2]
@@ -104,20 +106,10 @@
     share = S // devices
     col_real = jnp.swapaxes(spec_real.reshape(holo_count, pencil, S), 1, 2)
     col_imag = jnp.swapaxes(spec_imag.reshape(holo_count, pencil, S), 1, 2)
-    piece_real = lax.all_to_all(
-        col_real.reshape(holo_count, devices, share, pencil),
-        ("row", "col"),
-        split_axis=1,
-        concat_axis=3,
-        tiled=True,
-    )
-    piece_imag = lax.all_to_all(
-        col_imag.reshape(holo_count, devices, share, pencil),
-        ("row", "col"),
-        split_axis=1,
-        concat_axis=3,
-        tiled=True,
-    )
+    col_both = jnp.stack([col_real, col_imag]).reshape(2, holo_count, devices, share, pencil)
+    piece_both = lax.all_to_all(col_both, ("row", "col"), split_axis=2, concat_axis=4, tiled=True)
+    piece_real = piece_both[0]
+    piece_imag = piece_both[1]
     lead, single, count, width = piece_real.shape
     out_real, out_imag = transform(
         piece_real.reshape(lead, count, width), piece_imag.reshape(lead, count, width), table_u
@@ -145,10 +137,10 @@
         picked = jnp.take(grouped, source, axis=2) * filled[None, None, :, None]
         return jnp.transpose(picked.reshape(holo_count, share, strips, slot_rows), (2, 0, 1, 3))
 
-    send_real = pack(lift_real)
-    send_imag = pack(lift_imag)
-    piece_real = lax.all_to_all(send_real, ("row", "col"), split_axis=0, concat_axis=2, tiled=True)
-    piece_imag = lax.all_to_all(send_imag, ("row", "col"), split_axis=0, concat_axis=2, tiled=True)
+    send_both = jnp.stack([pack(lift_real), pack(lift_imag)], axis=1)
+    piece_both = lax.all_to_all(send_both, ("row", "col"), split_axis=0, concat_axis=3, tiled=True)
+    piece_real = piece_both[:, 0]
+    piece_imag = piece_both[:, 1]
     single, lead, width, count = piece_real.shape
     rows_real = jnp.swapaxes(piece_real.reshape(lead, width, count), 1, 2)
     rows_imag = jnp.swapaxes(piece_imag.reshape(lead, width, count), 1, 2)
@@ -159,7 +151,7 @@
     field_imag = field_imag.reshape(holo_count, slot_rows, P_SIZE)
     magnitude = jnp.sqrt(field_real * field_real + field_imag * field_imag)
     local_peak = jnp.max(magnitude, axis=(1, 2))
-    peak = lax.pmax(local_peak, ("row", "col"))
+    peak = lax.pmax(lax.pmax(local_peak, "col"), "row")
     plus_real, plus_imag, minus_real, minus_imag = encode(
         field_real, field_imag, peak[:, None, None]
     )

time: 624 us -> 703 us (1.13)
  matrix products: 287 us -> 345 us
  waiting for transfers between devices: 86 us -> 129 us
  starting transfers between devices: 35.6 us -> 20 us
  blocking collectives: 62.3 us -> 49.3 us
    dot_general x30, matrix products: 287 us -> 345 us  [contract(): jnp.einsum(form, left, right, precision=lax.Precision.HIGHEST, preferred_...]
    all_to_all x4 -> x2, waiting for transfers between devices: 37.5 us -> 79.8 us  [the longest x1 50.2 us: body(): lax.all_to_all(send_both, ('row', 'col'), split_axis=0, concat_axis=3, ti...]
    all_to_all x4 -> x2, starting transfers between devices: 30.9 us -> 15.3 us  [the longest x1 9.28 us: body(): lax.all_to_all(col_both, ('row', 'col'), split_axis=2, concat_axis=4, til...]
    pmax x1 -> x2, blocking collectives: 62.3 us -> 49.3 us  [body(): peak = lax.pmax(lax.pmax(local_peak, 'col'), 'row')]
  transfers between devices with their start and end apart: 5 -> 3, of which waited for: 4 -> 3; matrix products, arithmetic and copies ran while one was open for 14% -> 0% of each run, Pallas kernels for 0% -> 0%
where the time goes in v1:
time: 703 us; the launch traced here: 697 us
  matrix products  345 us (49%)
  waiting for transfers between devices  129 us (18%)
  local copies, waits for them, and re-layouts  123 us (17%)
  blocking collectives  49.3 us (7%)
  other arithmetic  29.5 us (4%)
  starting transfers between devices  20 us (3%)
    dot_general x30, matrix products, contract(): jnp.einsum(form, left, right, precision=lax.Precision.HIGHEST, preferred_...  345 us
    all_to_all x1, waiting for transfers between devices, body(): lax.all_to_all(send_both, ('row', 'col'), split_axis=0, concat_axis=3, ti...  50.2 us
    pmax x2, blocking collectives, body(): peak = lax.pmax(lax.pmax(local_peak, 'col'), 'row')  49.3 us
    all_to_all x1, waiting for transfers between devices, body(): lax.all_to_all(blocks, 'col', split_axis=1, concat_axis=3, tiled=True)  49.1 us
    all_to_all x1, waiting for transfers between devices, body(): lax.all_to_all(col_both, ('row', 'col'), split_axis=2, concat_axis=4, til...  29.6 us
    gather x4, local copies, waits for them, and re-layouts, pack(): picked = jnp.take(grouped, source, axis=2) * filled[None, None, :, None]  21.5 us
  transfers between devices with their start and end apart: 3, of which 3 were waited for; matrix products, arithmetic and copies ran while one was open for 0% of the time, Pallas kernels for 0%

profile of v1, /device:TPU:0, one launch (start us, length us, event | category | flops | bytes accessed | tf_op | source)
XLA Modules:
  0.0 696.7 jit_solution(14287282095920259123)
XLA Ops:
  10.0 49.1 %all-to-all-done = f32[2,8,64,1024]{3,2,0,1:T(8,128)} async-done(((f32[2,8,64,1024]{3,2,0,1:T(8,128)}), f32[2,8,64,1024]{3,2,0,1:T(8,128)}, u32[]{:S(2)}, u32[]{:S(2)}) %all-to-all-start) | async-done | bytes 4194336 | tf_op jit(solution)/shard_map/all_to_all | solution.py:100
  59.1 6.6 copy.174
  70.6 6.3 convolution_bitcast_fusion
  81.3 15.6 %fusion.5 = f32[2,64,64,32]{2,3,1,0:T(8,128)S(1)} fusion(f32[2,64,64,128]{3,2,1,0:T(8,128)S(1)} %convolution_bitcast_fusion, s32[128]{0:T(128)S(1)} %and_select_fusion.4, s32[2,32,64]{1,2,0:T(8,128)S(1)} %get-tuple-element.14), kind=kOutput, calls=%fused_computation.24 | convolution fusion | flops 409993216 | bytes 5259776 | tf_op jit(solution)/shard_map/kqpb,krpb->krqp/dot_general | solution.py:22
  96.9 15.4 %fusion.7 = f32[2,64,64,32]{2,3,1,0:T(8,128)S(1)} fusion(f32[2,64,64,128]{3,2,1,0:T(8,128)S(1)} %convolution_bitcast_fusion, s32[128]{0:T(128)S(1)} %and_select_fusion.4, s32[2,32,64]{1,2,0:T(8,128)S(1)} %get-tuple-element.14), kind=kOutput, calls=%fused_computation.26 | convolution fusion | flops 409993216 | bytes 5259776 | tf_op jit(solution)/shard_map/kqpb,krpb->krqp/dot_general | solution.py:22
  112.3 17.6 %subtract_bitcast_fusion.2 = f32[2,64,32,64]{1,2,3,0:T(8,128)} fusion(f32[2,64,64,32]{2,3,1,0:T(8,128)S(1)} %fusion.7, f32[2,64,64,128]{3,2,1,0:T(8,128)S(1)} %convolution_bitcast_fusion.1, s32[128]{0:T(128)S(1)} %and_select_fusion.4, s32[2,32,64]{1,2,0:T(8,128)S(1)} %get-tuple-element.14), kind=kOutput, calls=%fused_computation.75 | convolution fusion | flops 410255360 | bytes 6308352 | tf_op jit(solution)/shard_map/kqpb,krpb->krqp/dot_general | solution.py:22
  129.9 18.1 %add_bitcast_fusion.2 = f32[2,64,32,64]{1,2,3,0:T(8,128)} fusion(f32[2,64,64,32]{2,3,1,0:T(8,128)S(1)} %fusion.5, f32[2,64,64,128]{3,2,1,0:T(8,128)S(1)} %convolution_bitcast_fusion.1, s32[128]{0:T(128)S(1)} %and_select_fusion.4, s32[2,32,64]{1,2,0:T(8,128)S(1)} %get-tuple-element.14), kind=kOutput, calls=%fused_computation.74 | convolution fusion | flops 410255360 | bytes 6308352 | tf_op jit(solution)/shard_map/kqpb,krpb->krqp/dot_general | solution.py:22
  165.0 5.6 reshape.345
  170.5 9.3 %all-to-all-start.1 = ((f32[128,1,4096]{2,1,0:T(1,128)}), f32[128,1,4096]{2,1,0:T(1,128)S(1)}, u32[]{:S(2)}, u32[]{:S(2)}) async-start(f32[128,1,4096]{2,1,0:T(1,128)} %reshape.345), calls=%async_computation.1 | async-start | bytes 4194304 | tf_op jit(solution)/shard_map/all_to_all | solution.py:110
  180.6 29.6 %all-to-all-done.1 = f32[128,1,4096]{2,1,0:T(1,128)S(1)} async-done(((f32[128,1,4096]{2,1,0:T(1,128)}), f32[128,1,4096]{2,1,0:T(1,128)S(1)}, u32[]{:S(2)}, u32[]{:S(2)}) %all-to-all-start.1) | async-done | bytes 2097184 | tf_op jit(solution)/shard_map/all_to_all | solution.py:110
  212.1 7.4 %reduce.5 = f32[128,4096]{1,0:T(8,128)S(1)} reduce(f32[128,1,4096]{2,1,0:T(1,128)} %copy-done.2, f32[]{:T(128)} %broadcast.578), dimensions={1}, to_apply=%all_to_all.38.reduce_sub_computation | reduce | bytes 4194308 | tf_op jit(solution)/shard_map/all_to_all | solution.py:110
  239.3 11.5 %fusion.80 = f32[2,64,16,32]{3,2,1,0:T(8,128)S(1)} fusion(s32[128]{0:T(128)S(1)} %and_select_fusion.4, s32[2,32,64]{1,2,0:T(8,128)S(1)} %get-tuple-element.15, f32[2,16,64,128]{3,2,1,0:T(8,128)S(1)} %fusion.61), kind=kOutput, calls=%fused_computation.100 | convolution fusion | flops 108003328 | bytes 1327616 | tf_op jit(solution)/shard_map/kqpb,krpb->krqp/dot_general | solution.py:22
  250.9 14.0 %fusion.78 = f32[2,64,16,32]{3,2,1,0:T(8,128)} fusion(s32[128]{0:T(128)S(1)} %and_select_fusion.4, s32[2,32,64]{1,2,0:T(8,128)S(1)} %get-tuple-element.15, f32[2,16,64,128]{3,2,1,0:T(8,128)S(1)} %fusion.60), kind=kOutput, calls=%fused_computation.99 | convolution fusion | flops 108003328 | bytes 1327616 | tf_op jit(solution)/shard_map/kqpb,krpb->krqp/dot_general | solution.py:22
  264.9 11.4 %fusion.59 = f32[2,16,32,64]{2,1,3,0:T(8,128)S(1)} fusion(f32[2,64,16,32]{3,2,1,0:T(8,128)S(1)} %fusion.80, s32[128]{0:T(128)S(1)} %and_select_fusion.4, s32[2,32,64]{1,2,0:T(8,128)S(1)} %get-tuple-element.15, f32[2,16,64,128]{3,2,1,0:T(8,128)S(1)} %fusion.60), kind=kOutput, calls=%fused_computation.84 | convolution fusion | flops 108068864 | bytes 1589760 | tf_op jit(solution)/shard_map/kqpb,krpb->krqp/dot_general | solution.py:22
  278.4 13.1 %fusion.58 = f32[2,16,32,64]{2,1,3,0:T(8,128)S(1)} fusion(f32[2,64,16,32]{3,2,1,0:T(8,128)} %fusion.78, s32[128]{0:T(128)S(1)} %and_select_fusion.4, s32[2,32,64]{1,2,0:T(8,128)S(1)} %get-tuple-element.15, f32[2,16,64,128]{3,2,1,0:T(8,128)} %copy-done.7), kind=kOutput, calls=%fused_computation.82 | convolution fusion | flops 108068864 | bytes 1589760 | tf_op jit(solution)/shard_map/kqpb,krpb->krqp/dot_general | solution.py:22
  293.4 22.0 %fusion.35 = f32[2,32,16,128]{3,2,1,0:T(8,128)S(1)} fusion(s32[128]{0:T(128)S(1)} %and_select_fusion, s32[2,128,32]{1,2,0:T(8,128)S(1)} %copy.192, f32[2,16,32,128]{3,2,1,0:T(8,128)S(1)} %fusion.63), kind=kOutput, calls=%fused_computation.71 | convolution fusion | flops 216006656 | bytes 1081856 | tf_op jit(solution)/shard_map/kqpb,krpb->krqp/dot_general | solution.py:22
  315.4 22.4 %fusion.33 = f32[2,32,16,128]{3,2,1,0:T(8,128)S(1)} fusion(s32[128]{0:T(128)S(1)} %and_select_fusion, s32[2,128,32]{1,2,0:T(8,128)S(1)} %copy.192, f32[2,16,32,128]{3,2,1,0:T(8,128)S(1)} %fusion.62), kind=kOutput, calls=%fused_computation.70 | convolution fusion | flops 216006656 | bytes 1081856 | tf_op jit(solution)/shard_map/kqpb,krpb->krqp/dot_general | solution.py:22
  337.8 22.3 %fusion.67 = f32[2,16,128,32]{2,1,3,0:T(8,128)S(1)} fusion(f32[2,32,16,128]{3,2,1,0:T(8,128)S(1)} %fusion.35, s32[128]{0:T(128)S(1)} %and_select_fusion, s32[2,128,32]{1,2,0:T(8,128)S(1)} %copy.192, f32[2,16,32,128]{3,2,1,0:T(8,128)S(1)} %fusion.62), kind=kOutput, calls=%fused_computation.94 | convolution fusion | flops 216137728 | bytes 1606144 | tf_op jit(solution)/shard_map/kqpb,krpb->krqp/dot_general | solution.py:22
  360.1 22.7 %fusion.73 = f32[2,16,128,32]{2,1,3,0:T(8,128)S(1)} fusion(f32[2,32,16,128]{3,2,1,0:T(8,128)S(1)} %fusion.33, s32[128]{0:T(128)S(1)} %and_select_fusion, s32[2,128,32]{1,2,0:T(8,128)S(1)} %copy.192, f32[2,16,32,128]{3,2,1,0:T(8,128)S(1)} %fusion.63), kind=kOutput, calls=%fused_computation.96 | convolution fusion | flops 216137728 | bytes 1606144 | tf_op jit(solution)/shard_map/kqpb,krpb->krqp/dot_general | solution.py:22
  386.0 5.3 gather_fusion
  391.3 6.4 copy.196
  402.0 5.4 copy.201
  435.4 6.0 all-to-all-start.2
  443.6 50.2 %all-to-all-done.2 = f32[128,2,2,16,96]{4,3,2,1,0:T(8,128)} async-done(((f32[128,2,2,16,96]{4,3,2,1,0:T(8,128)}), f32[128,2,2,16,96]{4,3,2,1,0:T(8,128)}, u32[]{:S(2)}, u32[]{:S(2)}) %all-to-all-start.2) | async-done | bytes 3145760 | tf_op jit(solution)/shard_map/all_to_all | solution.py:141
  516.6 25.0 %fusion.13 = f32[2,32,96,128]{3,2,1,0:T(8,128)S(1)} fusion(f32[2,96,32,128]{3,2,1,0:T(8,128)S(1)} %add_bitcast_fusion.1, s32[128]{0:T(128)S(1)} %and_select_fusion, s32[2,128,32]{1,2,0:T(8,128)S(1)} %copy.192), kind=kOutput, calls=%fused_computation.50 | convolution fusion | flops 1222639616 | bytes 6324736 | tf_op jit(solution)/shard_map/kqpb,krpb->krqp/dot_general | solution.py:22
  541.6 25.5 %fusion.15 = f32[2,32,96,128]{3,2,1,0:T(8,128)S(1)} fusion(f32[2,96,32,128]{3,2,1,0:T(8,128)S(1)} %add_bitcast_fusion.1, s32[128]{0:T(128)S(1)} %and_select_fusion, s32[2,128,32]{1,2,0:T(8,128)S(1)} %copy.192), kind=kOutput, calls=%fused_computation.52 | convolution fusion | flops 1222639616 | bytes 6324736 | tf_op jit(solution)/shard_map/kqpb,krpb->krqp/dot_general | solution.py:22
  570.0 24.8 %subtract_bitcast_fusion = f32[2,96,128,32]{2,1,3,0:T(8,128)S(1)} fusion(f32[2,32,96,128]{3,2,1,0:T(8,128)S(1)} %fusion.15, s32[128]{0:T(128)S(1)} %and_select_fusion, s32[2,128,32]{1,2,0:T(8,128)S(1)} %copy.192, f32[2,96,32,128]{3,2,1,0:T(8,128)S(1)} %subtract_bitcast_fusion.1), kind=kOutput, calls=%fused_computation.40 | convolution fusion | flops 1223426048 | bytes 9470464 | tf_op jit(solution)/shard_map/kqpb,krpb->krqp/dot_general | solution.py:22
  594.8 24.5 %sqrt_reduce_fusion = (f32[2]{0:T(128)S(1)}, f32[2,96,128,32]{2,1,3,0:T(8,128)S(1)}) fusion(f32[2,96,128,32]{2,1,3,0:T(8,128)S(1)} %subtract_bitcast_fusion, f32[2,32,96,128]{3,2,1,0:T(8,128)S(1)} %fusion.13, s32[128]{0:T(128)S(1)} %and_select_fusion, s32[2,128,32]{1,2,0:T(8,128)S(1)} %copy.192, f32[2,96,32,128]{3,2,1,0:T(8,128)S(1)} %subtract_bitcast_fusion.1), kind=kOutput, calls=%fused_computation.38 | convolution fusion | flops 1226571776 | bytes 12616200 | tf_op jit(solution)/shard_map/kqpb,krpb->krqp/dot_general | solution.py:22
  619.3 12.4 %pmax.14 = f32[2]{0:T(128)S(1)} all-reduce(f32[2]{0:T(128)S(1)} %get-tuple-element.22), channel_id=1, replica_groups=mesh['row'=16,'col'=8] {'col'}, use_global_device_ids=true, to_apply=%region_4.6 | all-reduce | flops 2 | bytes 16 | tf_op jit(solution)/shard_map/pmax | solution.py:154
  637.0 36.8 %pmax.15 = f32[2]{0:T(128)S(1)} all-reduce(f32[2]{0:T(128)S(1)} %pmax.14), channel_id=1, replica_groups=mesh['row'=16,'col'=8] {'row'}, use_global_device_ids=true, to_apply=%region_5.7 | all-reduce | flops 2 | bytes 16 | tf_op jit(solution)/shard_map/pmax | solution.py:154
  677.1 7.0 %add_select_fusion.1 = (f32[2,1,96,4096]{2,3,0,1:T(8,128)S(1)}, f32[2,1,96,4096]{2,3,0,1:T(8,128)S(1)}) fusion(f32[2,96,128,32]{1,3,2,0:T(8,128)} %copy.212, f32[2]{0:T(128)S(1)} %multiply_add_fusion.1, f32[2,96,128,32]{1,3,2,0:T(8,128)} %copy.209, pred[96,4096]{0,1:T(8,128)(4,1)} %fusion.22), kind=kLoop, calls=%fused_computation.20 | loop fusion | flops 14155776 | bytes 12976136 | tf_op jit(solution)/shard_map/jit(_where)/select_n | solution.py:164
  688.0 8.3 %copy.213 = f32[2,2,96,4096]{3,2,1,0:T(8,128)} copy(f32[2,2,96,4096]{2,3,0,1:T(8,128)} %pad_maximum_fusion) | data formatting | bytes 12582912 | tf_op jit(solution)/shard_map/stack | solution.py:166
  (98 shorter events, 138.1 us)
Async XLA Ops:
  4.8 4.7 copy-start.8
  4.8 54.3 %all-to-all-start = ((f32[2,8,64,1024]{3,2,0,1:T(8,128)}), f32[2,8,64,1024]{3,2,0,1:T(8,128)}, u32[]{:S(2)}, u32[]{:S(2)}) async-start(f32[2,8,64,1024]{3,2,0,1:T(8,128)} %copy.173), calls=%async_computation | async-start | bytes 8388608 | tf_op jit(solution)/shard_map/all_to_all | solution.py:100
  70.6 6.3 copy-start
  170.5 9.3 %copy-start.9 = (s32[128]{0:T(128)S(1)}, s32[128]{0:T(128)}, u32[]{:S(2)}) copy-start(s32[128]{0:T(128)} %param.7) | copy-start | bytes 1540
  170.5 39.7 %all-to-all-start.1 = ((f32[128,1,4096]{2,1,0:T(1,128)}), f32[128,1,4096]{2,1,0:T(1,128)S(1)}, u32[]{:S(2)}, u32[]{:S(2)}) async-start(f32[128,1,4096]{2,1,0:T(1,128)} %reshape.345), calls=%async_computation.1 | async-start | bytes 4194304 | tf_op jit(solution)/shard_map/all_to_all | solution.py:110
  210.2 1.3 copy-start.2
  228.7 4.9 copy-start.3
  235.2 2.7 copy-start.5
  239.3 11.5 %copy-start.7 = (f32[2,16,64,128]{3,2,1,0:T(8,128)}, f32[2,16,64,128]{3,2,1,0:T(8,128)S(1)}, u32[]{:S(2)}) copy-start(f32[2,16,64,128]{3,2,1,0:T(8,128)S(1)} %fusion.61) | copy-start | bytes 3145732
  402.0 5.4 copy-start.4
  435.4 58.4 %all-to-all-start.2 = ((f32[128,2,2,16,96]{4,3,2,1,0:T(8,128)}), f32[128,2,2,16,96]{4,3,2,1,0:T(8,128)}, u32[]{:S(2)}, u32[]{:S(2)}) async-start(f32[128,2,2,16,96]{4,3,2,1,0:T(8,128)} %copy.203), calls=%async_computation.2 | async-start | bytes 8388608 | tf_op jit(solution)/shard_map/all_to_all | solution.py:141
  541.6 25.6 %copy-start.1 = (f32[2,96,128,32]{2,3,1,0:T(8,128)S(1)}, f32[2,96,128,32]{2,3,1,0:T(8,128)}, u32[]{:S(2)}) copy-start(f32[2,96,128,32]{2,3,1,0:T(8,128)} %fusion.136) | copy-start | bytes 9437188
  594.8 24.5 %copy-start.6 = (f32[2,96,128,32]{2,1,3,0:T(8,128)}, f32[2,96,128,32]{2,1,3,0:T(8,128)S(1)}, u32[]{:S(2)}) copy-start(f32[2,96,128,32]{2,1,3,0:T(8,128)S(1)} %subtract_bitcast_fusion) | copy-start | bytes 9437188

commit v2 on v0

--- a/solution.py
+++ b/solution.py
@@ -34,11 +34,13 @@
     outer_index = frequency[:, :, None] * column[None, None, :] % length
     outer_angle = sign * two_pi / length * outer_index.astype(jnp.float32)
     shape_four = (frequency.shape[0], frequency.shape[1] // accum, accum, radix)
-    return (
-        jnp.cos(inner_angle),
-        jnp.sin(inner_angle),
-        jnp.cos(outer_angle).reshape(shape_four),
-        jnp.sin(outer_angle).reshape(shape_four),
+    return lax.optimization_barrier(
+        (
+            jnp.cos(inner_angle),
+            jnp.sin(inner_angle),
+            jnp.cos(outer_angle).reshape(shape_four),
+            jnp.sin(outer_angle).reshape(shape_four),
+        )
     )
 
 
@@ -159,7 +161,7 @@
     field_imag = field_imag.reshape(holo_count, slot_rows, P_SIZE)
     magnitude = jnp.sqrt(field_real * field_real + field_imag * field_imag)
     local_peak = jnp.max(magnitude, axis=(1, 2))
-    peak = lax.pmax(local_peak, ("row", "col"))
+    peak = lax.pmax(lax.pmax(local_peak, "col"), "row")
     plus_real, plus_imag, minus_real, minus_imag = encode(
         field_real, field_imag, peak[:, None, None]
     )

time: 624 us -> 511 us (0.82)
  matrix products: 287 us -> 162 us
  other arithmetic: 24.6 us -> 55.4 us
  waiting for transfers between devices: 86 us -> 55.3 us
  local copies, waits for them, and re-layouts: 121 us -> 145 us
  blocking collectives: 62.3 us -> 49.1 us
    dot_general x30, matrix products: 287 us -> 162 us  [contract(): jnp.einsum(form, left, right, precision=lax.Precision.HIGHEST, preferred_...]
    sin x0 -> x5, other arithmetic: none -> 30.1 us  [the longest x2 29.3 us: make_tables(): jnp.sin(outer_angle).reshape(shape_four)]
    all_to_all x1, waiting for transfers between devices: 48.5 us -> 18.7 us  [body(): lax.all_to_all(blocks, 'col', split_axis=1, concat_axis=3, tiled=True)]
    pmax x1 -> x2, blocking collectives: 62.3 us -> 49.1 us  [body(): peak = lax.pmax(lax.pmax(local_peak, 'col'), 'row')]
  transfers between devices with their start and end apart: 5 -> 5, of which waited for: 4 -> 4; matrix products, arithmetic and copies ran while one was open for 14% -> 22% of each run, Pallas kernels for 0% -> 0%
where the time goes in v2:
time: 511 us; the launch traced here: 503 us
  matrix products  162 us (32%)
  local copies, waits for them, and re-layouts  145 us (28%)
  other arithmetic  55.4 us (11%)
  waiting for transfers between devices  55.3 us (11%)
  blocking collectives  49.1 us (10%)
  starting transfers between devices  35.6 us (7%)
    dot_general x30, matrix products, contract(): jnp.einsum(form, left, right, precision=lax.Precision.HIGHEST, preferred_...  162 us
    pmax x2, blocking collectives, body(): peak = lax.pmax(lax.pmax(local_peak, 'col'), 'row')  49.1 us
    sin x2, other arithmetic, make_tables(): jnp.sin(outer_angle).reshape(shape_four)  29.3 us
    gather x4, local copies, waits for them, and re-layouts, pack(): picked = jnp.take(grouped, source, axis=2) * filled[None, None, :, None]  21.5 us
    all_to_all x1, waiting for transfers between devices, body(): lax.all_to_all(blocks, 'col', split_axis=1, concat_axis=3, tiled=True)  18.7 us
    all_to_all x1, waiting for transfers between devices, body(): lax.all_to_all(send_imag, ('row', 'col'), split_axis=0, concat_axis=2, ti...  15.6 us
    all_to_all x1, waiting for transfers between devices, body(): lax.all_to_all(send_real, ('row', 'col'), split_axis=0, concat_axis=2, ti...  15.6 us
    add x4, local copies, waits for them, and re-layouts, transform(): contract('kqpb,krpb->krqp', outer_cos, mid_imag)  13.1 us
  transfers between devices with their start and end apart: 5, of which 4 were waited for; matrix products, arithmetic and copies ran while one was open for 22% of the time, Pallas kernels for 0%

profile of v2, /device:TPU:0, one launch (start us, length us, event | category | flops | bytes accessed | tf_op | source)
XLA Modules:
  0.0 502.8 jit_solution(13136670033226159593)
XLA Ops:
  10.4 18.6 %fusion.52 = (f32[2,32,64,128]{3,1,2,0:T(8,128)}, f32[2,32,64,128]{3,1,2,0:T(8,128)}, f32[2,32,64,128]{3,1,2,0:T(8,128)}, f32[2,32,64,128]{3,1,2,0:T(8,128)S(1)}) fusion(s32[128]{0:T(128)S(1)} %and_select_fusion.3, s32[2,32,64]{1,2,0:T(8,128)S(1)} %get-tuple-element.38, s32[2,32,64]{1,2,0:T(8,128)S(1)} %get-tuple-element.39), kind=kLoop, calls=%fused_computation.93 | loop fusion | flops 14680064 | bytes 8421888 | tf_op jit(solution)/shard_map/sin | solution.py:42
  29.7 10.7 %fusion.29 = (f32[2,128,32,128]{3,1,2,0:T(8,128)}, f32[2,128,32,128]{3,1,2,0:T(8,128)}) fusion(s32[128]{0:T(128)S(1)} %and_select_fusion, s32[128,32]{0,1:T(8,128)S(1)} %multiply_add_fusion.1), kind=kLoop, calls=%fused_computation.66 | loop fusion | flops 14680064 | bytes 8405504 | tf_op jit(solution)/shard_map/sin | solution.py:42
  40.4 18.7 %all-to-all-done = f32[2,8,64,1024]{3,2,0,1:T(8,128)} async-done(((f32[2,8,64,1024]{3,2,0,1:T(8,128)}), f32[2,8,64,1024]{3,2,0,1:T(8,128)}, u32[]{:S(2)}, u32[]{:S(2)}) %all-to-all-start) | async-done | bytes 4194336 | tf_op jit(solution)/shard_map/all_to_all | solution.py:100
  59.1 6.6 %copy.180 = f32[2,1,64,8,1024]{4,3,2,0,1:T(8,128)} copy(f32[2,1,64,8,1024]{4,2,0,3,1:T(8,128)} %bitcast.4) | data formatting | bytes 8388608 | tf_op jit(solution)/shard_map/all_to_all | solution.py:100
  70.7 5.9 %convolution_bitcast_fusion.1 = f32[2,64,64,128]{3,2,1,0:T(8,128)S(1)} fusion(f32[2,64,64,128]{3,2,1,0:T(8,128)} %reshape_reshape.9, f32[2,64,64]{2,1,0:T(8,128)S(1)} %get-tuple-element.18), kind=kOutput, calls=%fused_computation.57 | convolution fusion | flops 805306368 | bytes 8421376 | tf_op jit(solution)/shard_map/kpa,krab->krpb/dot_general | solution.py:22
  80.8 8.7 %fusion.5 = f32[2,64,64,32]{2,3,1,0:T(8,128)S(1)} fusion(f32[2,32,64,128]{3,1,2,0:T(8,128)S(1)} %copy-done.9, f32[2,64,64,128]{3,2,1,0:T(8,128)S(1)} %convolution_bitcast_fusion), kind=kOutput, calls=%fused_computation.22 | convolution fusion | flops 402653184 | bytes 7340032 | tf_op jit(solution)/shard_map/kqpb,krpb->krqp/dot_general | solution.py:22
  89.6 10.4 %add_bitcast_fusion.2 = f32[2,64,32,64]{1,2,3,0:T(8,128)} fusion(f32[2,64,64,32]{2,3,1,0:T(8,128)S(1)} %fusion.5, f32[2,32,64,128]{3,1,2,0:T(8,128)S(1)} %copy-done.11, f32[2,64,64,128]{3,2,1,0:T(8,128)S(1)} %convolution_bitcast_fusion.1), kind=kOutput, calls=%fused_computation.68 | convolution fusion | flops 402915328 | bytes 8388608 | tf_op jit(solution)/shard_map/kqpb,krpb->krqp/dot_general | solution.py:22
  114.8 9.8 %all-to-all-start.2 = ((f32[128,1,2048]{2,1,0:T(1,128)}), f32[128,1,2048]{2,1,0:T(1,128)}, u32[]{:S(2)}, u32[]{:S(2)}) async-start(f32[128,1,2048]{2,1,0:T(1,128)} %reshape.375), calls=%async_computation.2 | async-start | bytes 2097152 | tf_op jit(solution)/shard_map/all_to_all | solution.py:116
  124.7 11.4 %fusion.7 = f32[2,64,64,32]{2,3,1,0:T(8,128)S(1)} fusion(f32[2,32,64,128]{3,1,2,0:T(8,128)} %get-tuple-element.21, f32[2,64,64,128]{3,2,1,0:T(8,128)} %copy-done.6), kind=kOutput, calls=%fused_computation.24 | convolution fusion | flops 402653184 | bytes 7340032 | tf_op jit(solution)/shard_map/kqpb,krpb->krqp/dot_general | solution.py:22
  136.1 10.0 %subtract_bitcast_fusion.2 = f32[2,64,32,64]{1,2,3,0:T(8,128)} fusion(f32[2,64,64,32]{2,3,1,0:T(8,128)S(1)} %fusion.7, f32[2,32,64,128]{3,1,2,0:T(8,128)S(1)} %copy-done.10, f32[2,64,64,128]{3,2,1,0:T(8,128)S(1)} %copy-done.5), kind=kOutput, calls=%fused_computation.69 | convolution fusion | flops 402915328 | bytes 8388608 | tf_op jit(solution)/shard_map/kqpb,krpb->krqp/dot_general | solution.py:22
  160.9 10.4 %all-to-all-start.1 = ((f32[128,1,2048]{2,1,0:T(1,128)}), f32[128,1,2048]{2,1,0:T(1,128)}, u32[]{:S(2)}, u32[]{:S(2)}) async-start(f32[128,1,2048]{2,1,0:T(1,128)} %reshape.373), calls=%async_computation.1 | async-start | bytes 2097152 | tf_op jit(solution)/shard_map/all_to_all | solution.py:109
  184.7 5.4 %all-to-all-done.1 = f32[128,1,2048]{2,1,0:T(1,128)} async-done(((f32[128,1,2048]{2,1,0:T(1,128)}), f32[128,1,2048]{2,1,0:T(1,128)}, u32[]{:S(2)}, u32[]{:S(2)}) %all-to-all-start.1) | async-done | bytes 1048608 | tf_op jit(solution)/shard_map/all_to_all | solution.py:109
  190.1 5.2 %reduce.5 = f32[128,2048]{1,0:T(8,128)} reduce(f32[128,1,2048]{2,1,0:T(1,128)} %all-to-all-done.1, f32[]{:T(128)} %broadcast.531), dimensions={1}, to_apply=%all_to_all.58.reduce_sub_computation | reduce | bytes 2097156 | tf_op jit(solution)/shard_map/all_to_all | solution.py:109
  233.4 6.8 %fusion.60 = f32[2,32,16,128]{3,2,1,0:T(8,128)S(1)} fusion(f32[2,128,32,128]{3,1,2,0:T(8,128)S(1)} %copy-done.2, f32[2,16,32,128]{3,2,1,0:T(8,128)S(1)} %fusion.46), kind=kOutput, calls=%fused_computation.101 | convolution fusion | flops 201326592 | bytes 5242880 | tf_op jit(solution)/shard_map/kqpb,krpb->krqp/dot_general | solution.py:22
  240.2 6.7 %fusion.64 = f32[2,32,16,128]{3,2,1,0:T(8,128)S(1)} fusion(f32[2,128,32,128]{3,1,2,0:T(8,128)S(1)} %copy-done.2, f32[2,16,32,128]{3,2,1,0:T(8,128)S(1)} %fusion.47), kind=kOutput, calls=%fused_computation.105 | convolution fusion | flops 201326592 | bytes 5242880 | tf_op jit(solution)/shard_map/kqpb,krpb->krqp/dot_general | solution.py:22
  246.9 6.6 %fusion.49 = f32[2,16,128,32]{2,1,3,0:T(8,128)S(1)} fusion(f32[2,32,16,128]{3,2,1,0:T(8,128)S(1)} %fusion.60, f32[2,128,32,128]{3,1,2,0:T(8,128)S(1)} %copy-done, f32[2,16,32,128]{3,2,1,0:T(8,128)S(1)} %fusion.47), kind=kOutput, calls=%fused_computation.90 | convolution fusion | flops 201457664 | bytes 5767168 | tf_op jit(solution)/shard_map/kqpb,krpb->krqp/dot_general | solution.py:22
  253.5 7.0 %fusion.48 = f32[2,16,128,32]{2,1,3,0:T(8,128)S(1)} fusion(f32[2,32,16,128]{3,2,1,0:T(8,128)S(1)} %fusion.64, f32[2,128,32,128]{3,1,2,0:T(8,128)S(1)} %copy-done, f32[2,16,32,128]{3,2,1,0:T(8,128)S(1)} %fusion.46), kind=kOutput, calls=%fused_computation.89 | convolution fusion | flops 201457664 | bytes 5767168 | tf_op jit(solution)/shard_map/kqpb,krpb->krqp/dot_general | solution.py:22
  263.8 5.3 %gather_fusion.1 = f32[384,2,16,32]{3,2,1,0:T(8,128)} fusion(f32[2,16,128,32]{3,1,2,0:T(8,128)} %copy.209, s32[1024]{0:T(1024)S(1)} %pad_clamp_fusion), kind=kCustom, calls=%fused_computation.1.clone | custom fusion | bytes 3147264 | tf_op jit(solution)/shard_map/jit(_take)/gather | solution.py:147
  269.1 6.4 %copy.210 = f32[384,2,16,32]{0,3,2,1:T(8,128)} copy(f32[384,2,16,32]{3,2,1,0:T(8,128)} %gather_fusion.1) | data formatting | bytes 3145728 | tf_op jit(solution)/shard_map/jit(_take)/gather | solution.py:147
  279.9 5.4 %copy.202 = f32[384,2,16,32]{0,3,2,1:T(8,128)S(1)} copy(f32[384,2,16,32]{3,2,1,0:T(8,128)} %gather_fusion) | data formatting | bytes 3145728 | tf_op jit(solution)/shard_map/jit(_take)/gather | solution.py:147
  309.1 5.2 %reshape.340 = f32[2,16,128,96]{3,2,1,0:T(8,128)} reshape(f32[2,16,384,32]{3,2,1,0:T(8,128)} %copy.211) | data formatting | bytes 3145728 | tf_op jit(solution)/shard_map/reshape | solution.py:148
  318.6 15.6 %all-to-all-done.3 = f32[128,2,16,96]{3,2,1,0:T(8,128)S(1)} async-done(((f32[128,2,16,96]{3,2,1,0:T(8,128)}), f32[128,2,16,96]{3,2,1,0:T(8,128)S(1)}, u32[]{:S(2)}, u32[]{:S(2)}) %all-to-all-start.3) | async-done | bytes 1572896 | tf_op jit(solution)/shard_map/all_to_all | solution.py:152
  334.2 5.8 %all-to-all-start.4 = ((f32[128,2,16,96]{3,2,1,0:T(8,128)}), f32[128,2,16,96]{3,2,1,0:T(8,128)}, u32[]{:S(2)}, u32[]{:S(2)}) async-start(f32[128,2,16,96]{3,2,1,0:T(8,128)} %copy.212), calls=%async_computation.4 | async-start | bytes 4194304 | tf_op jit(solution)/shard_map/all_to_all | solution.py:153
  354.3 15.6 %all-to-all-done.4 = f32[128,2,16,96]{3,2,1,0:T(8,128)} async-done(((f32[128,2,16,96]{3,2,1,0:T(8,128)}), f32[128,2,16,96]{3,2,1,0:T(8,128)}, u32[]{:S(2)}, u32[]{:S(2)}) %all-to-all-start.4) | async-done | bytes 1572896 | tf_op jit(solution)/shard_map/all_to_all | solution.py:153
  380.4 10.0 %fusion.13 = f32[2,32,96,128]{3,2,1,0:T(8,128)S(1)} fusion(f32[2,128,32,128]{3,1,2,0:T(8,128)S(1)} %copy-done.3, f32[2,96,32,128]{3,2,1,0:T(8,128)S(1)} %add_bitcast_fusion.1), kind=kOutput, calls=%fused_computation.48 | convolution fusion | flops 1207959552 | bytes 10485760 | tf_op jit(solution)/shard_map/kqpb,krpb->krqp/dot_general | solution.py:22
  390.4 10.4 %fusion.15 = f32[2,32,96,128]{3,2,1,0:T(8,128)S(1)} fusion(f32[2,128,32,128]{3,1,2,0:T(8,128)S(1)} %copy-done.1, f32[2,96,32,128]{3,2,1,0:T(8,128)S(1)} %add_bitcast_fusion.1), kind=kOutput, calls=%fused_computation.50 | convolution fusion | flops 1207959552 | bytes 10485760 | tf_op jit(solution)/shard_map/kqpb,krpb->krqp/dot_general | solution.py:22
  403.7 10.0 %subtract_bitcast_fusion = f32[2,96,128,32]{2,1,3,0:T(8,128)S(1)} fusion(f32[2,32,96,128]{3,2,1,0:T(8,128)S(1)} %fusion.15, f32[2,128,32,128]{3,1,2,0:T(8,128)S(1)} %copy-done.3, f32[2,96,32,128]{3,2,1,0:T(8,128)S(1)} %subtract_bitcast_fusion.1), kind=kOutput, calls=%fused_computation.38 | convolution fusion | flops 1208745984 | bytes 13631488 | tf_op jit(solution)/shard_map/kqpb,krpb->krqp/dot_general | solution.py:22
  413.7 12.1 %sqrt_reduce_fusion = (f32[2]{0:T(128)S(1)}, f32[2,96,128,32]{2,1,3,0:T(8,128)}) fusion(f32[2,96,128,32]{2,1,3,0:T(8,128)S(1)} %subtract_bitcast_fusion, f32[2,32,96,128]{3,2,1,0:T(8,128)S(1)} %fusion.13, f32[2,128,32,128]{3,1,2,0:T(8,128)S(1)} %copy-done.1, f32[2,96,32,128]{3,2,1,0:T(8,128)S(1)} %subtract_bitcast_fusion.1), kind=kOutput, calls=%fused_computation.36 | convolution fusion | flops 1211891712 | bytes 16777224 | tf_op jit(solution)/shard_map/kqpb,krpb->krqp/dot_general | solution.py:22
  425.8 12.4 %pmax.14 = f32[2]{0:T(128)S(1)} all-reduce(f32[2]{0:T(128)S(1)} %get-tuple-element.56), channel_id=1, replica_groups=mesh['row'=16,'col'=8] {'col'}, use_global_device_ids=true, to_apply=%region_4.6 | all-reduce | flops 2 | bytes 16 | tf_op jit(solution)/shard_map/pmax | solution.py:164
  441.7 36.7 %pmax.15 = f32[2]{0:T(128)S(1)} all-reduce(f32[2]{0:T(128)S(1)} %pmax.14), channel_id=1, replica_groups=mesh['row'=16,'col'=8] {'row'}, use_global_device_ids=true, to_apply=%region_5.7 | all-reduce | flops 2 | bytes 16 | tf_op jit(solution)/shard_map/pmax | solution.py:164
  483.5 7.0 %add_select_fusion.1 = (f32[2,1,96,4096]{2,3,0,1:T(8,128)S(1)}, f32[2,1,96,4096]{2,3,0,1:T(8,128)S(1)}) fusion(f32[2,96,128,32]{1,3,2,0:T(8,128)} %copy.220, f32[2]{0:T(128)S(1)} %multiply_add_fusion.2, f32[2,96,128,32]{1,3,2,0:T(8,128)} %copy.217, pred[96,4096]{0,1:T(8,128)(4,1)S(1)} %copy-done.14), kind=kLoop, calls=%fused_computation.18 | loop fusion | flops 14155776 | bytes 12976136 | tf_op jit(solution)/shard_map/jit(_where)/select_n | solution.py:174
  494.3 8.3 %copy.221 = f32[2,2,96,4096]{3,2,1,0:T(8,128)} copy(f32[2,2,96,4096]{2,3,0,1:T(8,128)} %pad_maximum_fusion) | data formatting | bytes 12582912 | tf_op jit(solution)/shard_map/stack | solution.py:176
  (125 shorter events, 176.5 us)
Async XLA Ops:
  4.8 4.7 copy-start.15
  4.8 54.4 %all-to-all-start = ((f32[2,8,64,1024]{3,2,0,1:T(8,128)}), f32[2,8,64,1024]{3,2,0,1:T(8,128)}, u32[]{:S(2)}, u32[]{:S(2)}) async-start(f32[2,8,64,1024]{3,2,0,1:T(8,128)} %copy.179), calls=%async_computation | async-start | bytes 8388608 | tf_op jit(solution)/shard_map/all_to_all | solution.py:100
  10.4 18.7 %copy-start.16 = (s32[128]{0:T(128)S(1)}, s32[128]{0:T(128)}, u32[]{:S(2)}) copy-start(s32[128]{0:T(128)} %param.7) | copy-start | bytes 1540
  70.7 5.9 %copy-start.7 = (f32[2,64,64,128]{3,2,1,0:T(8,128)S(1)}, f32[2,64,64,128]{3,2,1,0:T(8,128)}, u32[]{:S(2)}) copy-start(f32[2,64,64,128]{3,2,1,0:T(8,128)} %reshape_reshape.9) | copy-start | bytes 12582916
  76.6 12.9 %copy-start.4 = (f32[2,64,64,128]{3,2,1,0:T(8,128)}, f32[2,64,64,128]{3,2,1,0:T(8,128)S(1)}, u32[]{:S(2)}) copy-start(f32[2,64,64,128]{3,2,1,0:T(8,128)S(1)} %convolution_bitcast_fusion.1) | copy-start | bytes 12582916
  76.6 4.1 copy-start.9
  80.8 8.8 %copy-start.6 = (f32[2,64,64,128]{3,2,1,0:T(8,128)}, f32[2,64,64,128]{3,2,1,0:T(8,128)S(1)}, u32[]{:S(2)}) copy-start(f32[2,64,64,128]{3,2,1,0:T(8,128)S(1)} %convolution_bitcast_fusion) | copy-start | bytes 12582916
  80.8 8.8 %copy-start.11 = (f32[2,32,64,128]{3,1,2,0:T(8,128)S(1)}, f32[2,32,64,128]{3,1,2,0:T(8,128)}, u32[]{:S(2)}) copy-start(f32[2,32,64,128]{3,1,2,0:T(8,128)} %get-tuple-element.21) | copy-start | bytes 6291460
  114.8 46.1 %all-to-all-start.2 = ((f32[128,1,2048]{2,1,0:T(1,128)}), f32[128,1,2048]{2,1,0:T(1,128)}, u32[]{:S(2)}, u32[]{:S(2)}) async-start(f32[128,1,2048]{2,1,0:T(1,128)} %reshape.375), calls=%async_computation.2 | async-start | bytes 2097152 | tf_op jit(solution)/shard_map/all_to_all | solution.py:116
  124.7 11.4 %copy-start.5 = (f32[2,64,64,128]{3,2,1,0:T(8,128)S(1)}, f32[2,64,64,128]{3,2,1,0:T(8,128)}, u32[]{:S(2)}) copy-start(f32[2,64,64,128]{3,2,1,0:T(8,128)} %copy-done.4) | copy-start | bytes 12582916
  124.7 11.4 %copy-start.10 = (f32[2,32,64,128]{3,1,2,0:T(8,128)S(1)}, f32[2,32,64,128]{3,1,2,0:T(8,128)}, u32[]{:S(2)}) copy-start(f32[2,32,64,128]{3,1,2,0:T(8,128)} %get-tuple-element.19) | copy-start | bytes 6291460
  160.9 29.1 %all-to-all-start.1 = ((f32[128,1,2048]{2,1,0:T(1,128)}), f32[128,1,2048]{2,1,0:T(1,128)}, u32[]{:S(2)}, u32[]{:S(2)}) async-start(f32[128,1,2048]{2,1,0:T(1,128)} %reshape.373), calls=%async_computation.1 | async-start | bytes 2097152 | tf_op jit(solution)/shard_map/all_to_all | solution.py:109
  210.2 2.2 copy-start.8
  230.9 2.5 copy-start.2
  240.2 6.7 %copy-start = (f32[2,128,32,128]{3,1,2,0:T(8,128)S(1)}, f32[2,128,32,128]{3,1,2,0:T(8,128)}, u32[]{:S(2)}) copy-start(f32[2,128,32,128]{3,1,2,0:T(8,128)} %get-tuple-element.29) | copy-start | bytes 12582916
  279.9 5.4 %copy-start.13 = (f32[384,2,16,32]{0,3,2,1:T(8,128)S(1)}, f32[384,2,16,32]{0,3,2,1:T(8,128)}, u32[]{:S(2)}) copy-start(f32[384,2,16,32]{0,3,2,1:T(8,128)} %copy.210) | copy-start | bytes 4718596
  299.1 35.2 %all-to-all-start.3 = ((f32[128,2,16,96]{3,2,1,0:T(8,128)}), f32[128,2,16,96]{3,2,1,0:T(8,128)S(1)}, u32[]{:S(2)}, u32[]{:S(2)}) async-start(f32[128,2,16,96]{3,2,1,0:T(8,128)} %copy.204), calls=%async_computation.3 | async-start | bytes 4194304 | tf_op jit(solution)/shard_map/all_to_all | solution.py:152
  334.2 35.7 %all-to-all-start.4 = ((f32[128,2,16,96]{3,2,1,0:T(8,128)}), f32[128,2,16,96]{3,2,1,0:T(8,128)}, u32[]{:S(2)}, u32[]{:S(2)}) async-start(f32[128,2,16,96]{3,2,1,0:T(8,128)} %copy.212), calls=%async_computation.4 | async-start | bytes 4194304 | tf_op jit(solution)/shard_map/all_to_all | solution.py:153
  375.5 4.9 copy-start.3
  380.4 10.0 %copy-start.1 = (f32[2,128,32,128]{3,1,2,0:T(8,128)S(1)}, f32[2,128,32,128]{3,1,2,0:T(8,128)}, u32[]{:S(2)}) copy-start(f32[2,128,32,128]{3,1,2,0:T(8,128)} %get-tuple-element.29) | copy-start | bytes 12582916
  390.4 10.4 %copy-start.12 = (f32[2,96,128,32]{2,3,1,0:T(8,128)S(1)}, f32[2,96,128,32]{2,3,1,0:T(8,128)}, u32[]{:S(2)}) copy-start(f32[2,96,128,32]{2,3,1,0:T(8,128)} %fusion.98) | copy-start | bytes 9437188
  478.4 5.1 %copy-start.14 = (pred[96,4096]{0,1:T(8,128)(4,1)S(1)}, pred[96,4096]{0,1:T(8,128)(4,1)}, u32[]{:S(2)}) copy-start(pred[96,4096]{0,1:T(8,128)(4,1)} %fusion.22) | copy-start | bytes 1179652

commit v3 on v2

--- a/solution.py
+++ b/solution.py
@@ -20,7 +20,7 @@
 
 def contract(form, left, right):
     return jnp.einsum(
-        form, left, right, precision=lax.Precision.HIGHEST, preferred_element_type=jnp.float32
+        form, left, right, precision=lax.Precision.HIGH, preferred_element_type=jnp.float32
     )
 
 

time: 511 us -> 450 us (0.88)
  matrix products: 162 us -> 97.5 us
    dot_general x30, matrix products: 162 us -> 97.5 us  [contract(): jnp.einsum(form, left, right, precision=lax.Precision.HIGH, preferred_ele...]
  transfers between devices with their start and end apart: 5 -> 5, of which waited for: 4 -> 4; matrix products, arithmetic and copies ran while one was open for 22% -> 23% of each run, Pallas kernels for 0% -> 0%
where the time goes in v3:
time: 450 us; the launch traced here: 443 us
  local copies, waits for them, and re-layouts  147 us (33%)
  matrix products  97.5 us (22%)
  waiting for transfers between devices  57.8 us (13%)
  other arithmetic  55.4 us (12%)
  blocking collectives  49.3 us (11%)
  starting transfers between devices  35.2 us (8%)
    dot_general x30, matrix products, contract(): jnp.einsum(form, left, right, precision=lax.Precision.HIGH, preferred_ele...  97.5 us
    pmax x2, blocking collectives, body(): peak = lax.pmax(lax.pmax(local_peak, 'col'), 'row')  49.3 us
    sin x2, other arithmetic, make_tables(): jnp.sin(outer_angle).reshape(shape_four)  29.3 us
    gather x4, local copies, waits for them, and re-layouts, pack(): picked = jnp.take(grouped, source, axis=2) * filled[None, None, :, None]  21.5 us
    all_to_all x1, waiting for transfers between devices, body(): lax.all_to_all(blocks, 'col', split_axis=1, concat_axis=3, tiled=True)  18.7 us
    all_to_all x1, waiting for transfers between devices, body(): lax.all_to_all(send_imag, ('row', 'col'), split_axis=0, concat_axis=2, ti...  18.1 us
    all_to_all x1, waiting for transfers between devices, body(): lax.all_to_all(send_real, ('row', 'col'), split_axis=0, concat_axis=2, ti...  15.6 us
    unnamed x38, local copies, waits for them, and re-layouts  14 us
  transfers between devices with their start and end apart: 5, of which 4 were waited for; matrix products, arithmetic and copies ran while one was open for 23% of the time, Pallas kernels for 0%

profile of v3, /device:TPU:0, one launch (start us, length us, event | category | flops | bytes accessed | tf_op | source)
XLA Modules:
  0.0 443.1 jit_solution(8519288267998963508)
XLA Ops:
  0.0 4.8 %copy.179 = f32[2,8,64,1024]{3,2,0,1:T(8,128)} copy(f32[2,8,64,1024]{3,2,1,0:T(8,128)} %bitcast.213) | data formatting | bytes 8388608 | tf_op jit(solution)/shard_map/reshape | solution.py:99
  10.4 18.6 %fusion.52 = (f32[2,32,64,128]{3,1,2,0:T(8,128)}, f32[2,32,64,128]{3,1,2,0:T(8,128)}, f32[2,32,64,128]{3,1,2,0:T(8,128)}, f32[2,32,64,128]{3,1,2,0:T(8,128)S(1)}) fusion(s32[128]{0:T(128)S(1)} %and_select_fusion.3, s32[2,32,64]{1,2,0:T(8,128)S(1)} %get-tuple-element.38, s32[2,32,64]{1,2,0:T(8,128)S(1)} %get-tuple-element.39), kind=kLoop, calls=%fused_computation.93 | loop fusion | flops 14680064 | bytes 8421888 | tf_op jit(solution)/shard_map/sin | solution.py:42
  29.7 10.7 %fusion.29 = (f32[2,128,32,128]{3,1,2,0:T(8,128)}, f32[2,128,32,128]{3,1,2,0:T(8,128)}) fusion(s32[128]{0:T(128)S(1)} %and_select_fusion, s32[128,32]{0,1:T(8,128)S(1)} %multiply_add_fusion.1), kind=kLoop, calls=%fused_computation.66 | loop fusion | flops 14680064 | bytes 8405504 | tf_op jit(solution)/shard_map/sin | solution.py:42
  40.4 18.7 %all-to-all-done = f32[2,8,64,1024]{3,2,0,1:T(8,128)} async-done(((f32[2,8,64,1024]{3,2,0,1:T(8,128)}), f32[2,8,64,1024]{3,2,0,1:T(8,128)}, u32[]{:S(2)}, u32[]{:S(2)}) %all-to-all-start) | async-done | bytes 4194336 | tf_op jit(solution)/shard_map/all_to_all | solution.py:100
  59.1 6.6 %copy.180 = f32[2,1,64,8,1024]{4,3,2,0,1:T(8,128)} copy(f32[2,1,64,8,1024]{4,2,0,3,1:T(8,128)} %bitcast.4) | data formatting | bytes 8388608 | tf_op jit(solution)/shard_map/all_to_all | solution.py:100
  65.8 5.1 %reshape_reshape.9 = f32[2,64,64,128]{3,2,1,0:T(8,128)} reshape(f32[2,1,64,8,1024]{4,3,2,0,1:T(8,128)} %copy.180) | data formatting | bytes 8388608 | tf_op jit(solution)/shard_map/reshape;reshape | solution.py:51
  78.4 5.1 %fusion.5 = f32[2,64,64,32]{2,3,1,0:T(8,128)S(1)} fusion(f32[2,32,64,128]{3,1,2,0:T(8,128)S(1)} %copy-done.9, f32[2,64,64,128]{3,2,1,0:T(8,128)S(1)} %convolution_bitcast_fusion), kind=kOutput, calls=%fused_computation.22 | convolution fusion | flops 201326592 | bytes 7340032 | tf_op jit(solution)/shard_map/kqpb,krpb->krqp/dot_general | solution.py:22
  83.5 6.8 %add_bitcast_fusion.2 = f32[2,64,32,64]{1,2,3,0:T(8,128)} fusion(f32[2,64,64,32]{2,3,1,0:T(8,128)S(1)} %fusion.5, f32[2,32,64,128]{3,1,2,0:T(8,128)S(1)} %copy-done.11, f32[2,64,64,128]{3,2,1,0:T(8,128)S(1)} %convolution_bitcast_fusion.1), kind=kOutput, calls=%fused_computation.68 | convolution fusion | flops 201588736 | bytes 8388608 | tf_op jit(solution)/shard_map/kqpb,krpb->krqp/dot_general | solution.py:22
  105.1 9.8 %all-to-all-start.2 = ((f32[128,1,2048]{2,1,0:T(1,128)}), f32[128,1,2048]{2,1,0:T(1,128)}, u32[]{:S(2)}, u32[]{:S(2)}) async-start(f32[128,1,2048]{2,1,0:T(1,128)} %reshape.375), calls=%async_computation.2 | async-start | bytes 2097152 | tf_op jit(solution)/shard_map/all_to_all | solution.py:116
  115.0 7.9 %fusion.7 = f32[2,64,64,32]{2,3,1,0:T(8,128)S(1)} fusion(f32[2,32,64,128]{3,1,2,0:T(8,128)} %get-tuple-element.21, f32[2,64,64,128]{3,2,1,0:T(8,128)} %copy-done.6), kind=kOutput, calls=%fused_computation.24 | convolution fusion | flops 201326592 | bytes 7340032 | tf_op jit(solution)/shard_map/kqpb,krpb->krqp/dot_general | solution.py:22
  122.9 6.4 %subtract_bitcast_fusion.2 = f32[2,64,32,64]{1,2,3,0:T(8,128)} fusion(f32[2,64,64,32]{2,3,1,0:T(8,128)S(1)} %fusion.7, f32[2,32,64,128]{3,1,2,0:T(8,128)S(1)} %copy-done.10, f32[2,64,64,128]{3,2,1,0:T(8,128)S(1)} %copy-done.5), kind=kOutput, calls=%fused_computation.69 | convolution fusion | flops 201588736 | bytes 8388608 | tf_op jit(solution)/shard_map/kqpb,krpb->krqp/dot_general | solution.py:22
  144.3 10.2 %all-to-all-start.1 = ((f32[128,1,2048]{2,1,0:T(1,128)}), f32[128,1,2048]{2,1,0:T(1,128)}, u32[]{:S(2)}, u32[]{:S(2)}) async-start(f32[128,1,2048]{2,1,0:T(1,128)} %reshape.373), calls=%async_computation.1 | async-start | bytes 2097152 | tf_op jit(solution)/shard_map/all_to_all | solution.py:109
  167.9 5.3 %all-to-all-done.1 = f32[128,1,2048]{2,1,0:T(1,128)} async-done(((f32[128,1,2048]{2,1,0:T(1,128)}), f32[128,1,2048]{2,1,0:T(1,128)}, u32[]{:S(2)}, u32[]{:S(2)}) %all-to-all-start.1) | async-done | bytes 1048608 | tf_op jit(solution)/shard_map/all_to_all | solution.py:109
  173.2 5.2 %reduce.5 = f32[128,2048]{1,0:T(8,128)} reduce(f32[128,1,2048]{2,1,0:T(1,128)} %all-to-all-done.1, f32[]{:T(128)} %broadcast.531), dimensions={1}, to_apply=%all_to_all.58.reduce_sub_computation | reduce | bytes 2097156 | tf_op jit(solution)/shard_map/all_to_all | solution.py:109
  225.1 5.3 %gather_fusion.1 = f32[384,2,16,32]{3,2,1,0:T(8,128)} fusion(f32[2,16,128,32]{3,1,2,0:T(8,128)} %copy.209, s32[1024]{0:T(1024)S(1)} %pad_clamp_fusion), kind=kCustom, calls=%fused_computation.1.clone | custom fusion | bytes 3147264 | tf_op jit(solution)/shard_map/jit(_take)/gather | solution.py:147
  230.4 6.4 %copy.210 = f32[384,2,16,32]{0,3,2,1:T(8,128)} copy(f32[384,2,16,32]{3,2,1,0:T(8,128)} %gather_fusion.1) | data formatting | bytes 3145728 | tf_op jit(solution)/shard_map/jit(_take)/gather | solution.py:147
  241.1 5.4 %copy.202 = f32[384,2,16,32]{0,3,2,1:T(8,128)S(1)} copy(f32[384,2,16,32]{3,2,1,0:T(8,128)} %gather_fusion) | data formatting | bytes 3145728 | tf_op jit(solution)/shard_map/jit(_take)/gather | solution.py:147
  248.7 5.0 %copy.203 = f32[2,16,384,32]{3,2,1,0:T(8,128)} copy(f32[2,16,384,32]{2,3,1,0:T(8,128)} %get-tuple-element.47) | data formatting | bytes 3145728 | tf_op jit(solution)/shard_map/mul | solution.py:147
  265.2 5.0 %copy.211 = f32[2,16,384,32]{3,2,1,0:T(8,128)} copy(f32[2,16,384,32]{2,3,1,0:T(8,128)} %get-tuple-element.46) | data formatting | bytes 3145728 | tf_op jit(solution)/shard_map/mul | solution.py:147
  270.2 5.2 %reshape.340 = f32[2,16,128,96]{3,2,1,0:T(8,128)} reshape(f32[2,16,384,32]{3,2,1,0:T(8,128)} %copy.211) | data formatting | bytes 3145728 | tf_op jit(solution)/shard_map/reshape | solution.py:148
  279.7 15.6 %all-to-all-done.3 = f32[128,2,16,96]{3,2,1,0:T(8,128)S(1)} async-done(((f32[128,2,16,96]{3,2,1,0:T(8,128)}), f32[128,2,16,96]{3,2,1,0:T(8,128)S(1)}, u32[]{:S(2)}, u32[]{:S(2)}) %all-to-all-start.3) | async-done | bytes 1572896 | tf_op jit(solution)/shard_map/all_to_all | solution.py:152
  295.4 5.8 %all-to-all-start.4 = ((f32[128,2,16,96]{3,2,1,0:T(8,128)}), f32[128,2,16,96]{3,2,1,0:T(8,128)}, u32[]{:S(2)}, u32[]{:S(2)}) async-start(f32[128,2,16,96]{3,2,1,0:T(8,128)} %copy.212), calls=%async_computation.4 | async-start | bytes 4194304 | tf_op jit(solution)/shard_map/all_to_all | solution.py:153
  313.0 18.1 %all-to-all-done.4 = f32[128,2,16,96]{3,2,1,0:T(8,128)} async-done(((f32[128,2,16,96]{3,2,1,0:T(8,128)}), f32[128,2,16,96]{3,2,1,0:T(8,128)}, u32[]{:S(2)}, u32[]{:S(2)}) %all-to-all-start.4) | async-done | bytes 1572896 | tf_op jit(solution)/shard_map/all_to_all | solution.py:153
  340.2 5.4 %fusion.13 = f32[2,32,96,128]{3,2,1,0:T(8,128)S(1)} fusion(f32[2,128,32,128]{3,1,2,0:T(8,128)S(1)} %copy-done.3, f32[2,96,32,128]{3,2,1,0:T(8,128)S(1)} %add_bitcast_fusion.1), kind=kOutput, calls=%fused_computation.48 | convolution fusion | flops 603979776 | bytes 10485760 | tf_op jit(solution)/shard_map/kqpb,krpb->krqp/dot_general | solution.py:22
  345.6 5.4 %fusion.15 = f32[2,32,96,128]{3,2,1,0:T(8,128)S(1)} fusion(f32[2,128,32,128]{3,1,2,0:T(8,128)S(1)} %copy-done.1, f32[2,96,32,128]{3,2,1,0:T(8,128)S(1)} %add_bitcast_fusion.1), kind=kOutput, calls=%fused_computation.50 | convolution fusion | flops 603979776 | bytes 10485760 | tf_op jit(solution)/shard_map/kqpb,krpb->krqp/dot_general | solution.py:22
  352.8 5.6 %subtract_bitcast_fusion = f32[2,96,128,32]{2,1,3,0:T(8,128)S(1)} fusion(f32[2,32,96,128]{3,2,1,0:T(8,128)S(1)} %fusion.15, f32[2,128,32,128]{3,1,2,0:T(8,128)S(1)} %copy-done.3, f32[2,96,32,128]{3,2,1,0:T(8,128)S(1)} %subtract_bitcast_fusion.1), kind=kOutput, calls=%fused_computation.38 | convolution fusion | flops 604766208 | bytes 13631488 | tf_op jit(solution)/shard_map/kqpb,krpb->krqp/dot_general | solution.py:22
  358.4 7.4 %sqrt_reduce_fusion = (f32[2]{0:T(128)S(1)}, f32[2,96,128,32]{2,1,3,0:T(8,128)}) fusion(f32[2,96,128,32]{2,1,3,0:T(8,128)S(1)} %subtract_bitcast_fusion, f32[2,32,96,128]{3,2,1,0:T(8,128)S(1)} %fusion.13, f32[2,128,32,128]{3,1,2,0:T(8,128)S(1)} %copy-done.1, f32[2,96,32,128]{3,2,1,0:T(8,128)S(1)} %subtract_bitcast_fusion.1), kind=kOutput, calls=%fused_computation.36 | convolution fusion | flops 607911936 | bytes 16777224 | tf_op jit(solution)/shard_map/kqpb,krpb->krqp/dot_general | solution.py:22
  365.8 12.4 %pmax.14 = f32[2]{0:T(128)S(1)} all-reduce(f32[2]{0:T(128)S(1)} %get-tuple-element.56), channel_id=1, replica_groups=mesh['row'=16,'col'=8] {'col'}, use_global_device_ids=true, to_apply=%region_4.6 | all-reduce | flops 2 | bytes 16 | tf_op jit(solution)/shard_map/pmax | solution.py:164
  381.7 36.9 %pmax.15 = f32[2]{0:T(128)S(1)} all-reduce(f32[2]{0:T(128)S(1)} %pmax.14), channel_id=1, replica_groups=mesh['row'=16,'col'=8] {'row'}, use_global_device_ids=true, to_apply=%region_5.7 | all-reduce | flops 2 | bytes 16 | tf_op jit(solution)/shard_map/pmax | solution.py:164
  418.6 5.1 %copy.220 = f32[2,96,128,32]{1,3,2,0:T(8,128)} copy(f32[2,96,128,32]{2,1,3,0:T(8,128)} %get-tuple-element.57) | data formatting | bytes 6291456 | tf_op jit(solution)/shard_map/add | solution.py:61
  423.7 7.0 %add_select_fusion.1 = (f32[2,1,96,4096]{2,3,0,1:T(8,128)S(1)}, f32[2,1,96,4096]{2,3,0,1:T(8,128)S(1)}) fusion(f32[2,96,128,32]{1,3,2,0:T(8,128)} %copy.220, f32[2]{0:T(128)S(1)} %multiply_add_fusion.2, f32[2,96,128,32]{1,3,2,0:T(8,128)} %copy.217, pred[96,4096]{0,1:T(8,128)(4,1)S(1)} %copy-done.14), kind=kLoop, calls=%fused_computation.18 | loop fusion | flops 14155776 | bytes 12976136 | tf_op jit(solution)/shard_map/jit(_where)/select_n | solution.py:174
  434.5 8.3 %copy.221 = f32[2,2,96,4096]{3,2,1,0:T(8,128)} copy(f32[2,2,96,4096]{2,3,0,1:T(8,128)} %pad_maximum_fusion) | data formatting | bytes 12582912 | tf_op jit(solution)/shard_map/stack | solution.py:176
  (125 shorter events, 155.4 us)
Async XLA Ops:
  4.8 4.7 %copy-start.15 = (s32[2,2]{1,0:T(2,128)S(1)}, s32[2,2]{1,0:T(2,128)}, u32[]{:S(2)}) copy-start(s32[2,2]{1,0:T(2,128)} %param.6) | copy-start | bytes 52
  4.8 54.4 %all-to-all-start = ((f32[2,8,64,1024]{3,2,0,1:T(8,128)}), f32[2,8,64,1024]{3,2,0,1:T(8,128)}, u32[]{:S(2)}, u32[]{:S(2)}) async-start(f32[2,8,64,1024]{3,2,0,1:T(8,128)} %copy.179), calls=%async_computation | async-start | bytes 8388608 | tf_op jit(solution)/shard_map/all_to_all | solution.py:100
  10.4 18.7 %copy-start.16 = (s32[128]{0:T(128)S(1)}, s32[128]{0:T(128)}, u32[]{:S(2)}) copy-start(s32[128]{0:T(128)} %param.7) | copy-start | bytes 1540
  70.8 4.4 copy-start.7
  75.2 8.3 %copy-start.4 = (f32[2,64,64,128]{3,2,1,0:T(8,128)}, f32[2,64,64,128]{3,2,1,0:T(8,128)S(1)}, u32[]{:S(2)}) copy-start(f32[2,64,64,128]{3,2,1,0:T(8,128)S(1)} %convolution_bitcast_fusion.1) | copy-start | bytes 12582916
  75.2 3.1 copy-start.9
  78.3 5.2 %copy-start.6 = (f32[2,64,64,128]{3,2,1,0:T(8,128)}, f32[2,64,64,128]{3,2,1,0:T(8,128)S(1)}, u32[]{:S(2)}) copy-start(f32[2,64,64,128]{3,2,1,0:T(8,128)S(1)} %convolution_bitcast_fusion) | copy-start | bytes 12582916
  78.3 5.2 %copy-start.11 = (f32[2,32,64,128]{3,1,2,0:T(8,128)S(1)}, f32[2,32,64,128]{3,1,2,0:T(8,128)}, u32[]{:S(2)}) copy-start(f32[2,32,64,128]{3,1,2,0:T(8,128)} %get-tuple-element.21) | copy-start | bytes 6291460
  105.1 39.2 %all-to-all-start.2 = ((f32[128,1,2048]{2,1,0:T(1,128)}), f32[128,1,2048]{2,1,0:T(1,128)}, u32[]{:S(2)}, u32[]{:S(2)}) async-start(f32[128,1,2048]{2,1,0:T(1,128)} %reshape.375), calls=%async_computation.2 | async-start | bytes 2097152 | tf_op jit(solution)/shard_map/all_to_all | solution.py:116
  115.0 7.9 %copy-start.5 = (f32[2,64,64,128]{3,2,1,0:T(8,128)S(1)}, f32[2,64,64,128]{3,2,1,0:T(8,128)}, u32[]{:S(2)}) copy-start(f32[2,64,64,128]{3,2,1,0:T(8,128)} %copy-done.4) | copy-start | bytes 12582916
  115.0 7.9 %copy-start.10 = (f32[2,32,64,128]{3,1,2,0:T(8,128)S(1)}, f32[2,32,64,128]{3,1,2,0:T(8,128)}, u32[]{:S(2)}) copy-start(f32[2,32,64,128]{3,1,2,0:T(8,128)} %get-tuple-element.19) | copy-start | bytes 6291460
  144.3 28.9 %all-to-all-start.1 = ((f32[128,1,2048]{2,1,0:T(1,128)}), f32[128,1,2048]{2,1,0:T(1,128)}, u32[]{:S(2)}, u32[]{:S(2)}) async-start(f32[128,1,2048]{2,1,0:T(1,128)} %reshape.373), calls=%async_computation.1 | async-start | bytes 2097152 | tf_op jit(solution)/shard_map/all_to_all | solution.py:109
  192.4 1.6 copy-start.8
  205.5 2.2 copy-start.2
  211.1 3.5 copy-start
  241.1 5.4 %copy-start.13 = (f32[384,2,16,32]{0,3,2,1:T(8,128)S(1)}, f32[384,2,16,32]{0,3,2,1:T(8,128)}, u32[]{:S(2)}) copy-start(f32[384,2,16,32]{0,3,2,1:T(8,128)} %copy.210) | copy-start | bytes 4718596
  260.3 35.0 %all-to-all-start.3 = ((f32[128,2,16,96]{3,2,1,0:T(8,128)}), f32[128,2,16,96]{3,2,1,0:T(8,128)S(1)}, u32[]{:S(2)}, u32[]{:S(2)}) async-start(f32[128,2,16,96]{3,2,1,0:T(8,128)} %copy.204), calls=%async_computation.3 | async-start | bytes 4194304 | tf_op jit(solution)/shard_map/all_to_all | solution.py:152
  295.4 35.7 %all-to-all-start.4 = ((f32[128,2,16,96]{3,2,1,0:T(8,128)}), f32[128,2,16,96]{3,2,1,0:T(8,128)}, u32[]{:S(2)}, u32[]{:S(2)}) async-start(f32[128,2,16,96]{3,2,1,0:T(8,128)} %copy.212), calls=%async_computation.4 | async-start | bytes 4194304 | tf_op jit(solution)/shard_map/all_to_all | solution.py:153
  336.6 3.6 copy-start.3
  340.2 5.4 %copy-start.1 = (f32[2,128,32,128]{3,1,2,0:T(8,128)S(1)}, f32[2,128,32,128]{3,1,2,0:T(8,128)}, u32[]{:S(2)}) copy-start(f32[2,128,32,128]{3,1,2,0:T(8,128)} %get-tuple-element.29) | copy-start | bytes 12582916
  345.6 5.4 %copy-start.12 = (f32[2,96,128,32]{2,3,1,0:T(8,128)S(1)}, f32[2,96,128,32]{2,3,1,0:T(8,128)}, u32[]{:S(2)}) copy-start(f32[2,96,128,32]{2,3,1,0:T(8,128)} %fusion.98) | copy-start | bytes 9437188
  418.6 5.1 %copy-start.14 = (pred[96,4096]{0,1:T(8,128)(4,1)S(1)}, pred[96,4096]{0,1:T(8,128)(4,1)}, u32[]{:S(2)}) copy-start(pred[96,4096]{0,1:T(8,128)(4,1)} %fusion.22) | copy-start | bytes 1179652

commit v4 on v3

--- a/solution.py
+++ b/solution.py
@@ -161,7 +161,8 @@
     field_imag = field_imag.reshape(holo_count, slot_rows, P_SIZE)
     magnitude = jnp.sqrt(field_real * field_real + field_imag * field_imag)
     local_peak = jnp.max(magnitude, axis=(1, 2))
-    peak = lax.pmax(lax.pmax(local_peak, "col"), "row")
+    every = jnp.broadcast_to(local_peak[None, :], (devices, holo_count))
+    peak = jnp.max(lax.all_to_all(every, ("row", "col"), 0, 0, tiled=True), axis=0)
     plus_real, plus_imag, minus_real, minus_imag = encode(
         field_real, field_imag, peak[:, None, None]
     )

time: 450 us -> 409 us (0.909)
  blocking collectives: 49.3 us -> 0 us
  starting transfers between devices: 35.2 us -> 40 us
    pmax x2 -> x0, blocking collectives: 49.3 us -> none  [body(): peak = lax.pmax(lax.pmax(local_peak, 'col'), 'row')]
    all_to_all x0 -> x1, starting transfers between devices: none -> 4.78 us  [body(): lax.all_to_all(every, ('row', 'col'), 0, 0, tiled=True)]
  transfers between devices with their start and end apart: 5 -> 6, of which waited for: 4 -> 4; matrix products, arithmetic and copies ran while one was open for 23% -> 27% of each run, Pallas kernels for 0% -> 0%
where the time goes in v4:
time: 409 us; the launch traced here: 402 us
  local copies, waits for them, and re-layouts  148 us (36%)
  matrix products  97.6 us (24%)
  waiting for transfers between devices  59.5 us (15%)
  other arithmetic  55.9 us (14%)
  starting transfers between devices  40 us (10%)
    dot_general x30, matrix products, contract(): jnp.einsum(form, left, right, precision=lax.Precision.HIGH, preferred_ele...  97.6 us
    sin x2, other arithmetic, make_tables(): jnp.sin(outer_angle).reshape(shape_four)  29.3 us
    gather x4, local copies, waits for them, and re-layouts, pack(): picked = jnp.take(grouped, source, axis=2) * filled[None, None, :, None]  21.5 us
    all_to_all x1, waiting for transfers between devices, body(): lax.all_to_all(send_imag, ('row', 'col'), split_axis=0, concat_axis=2, ti...  19.8 us
    all_to_all x1, waiting for transfers between devices, body(): lax.all_to_all(blocks, 'col', split_axis=1, concat_axis=3, tiled=True)  18.7 us
    all_to_all x1, waiting for transfers between devices, body(): lax.all_to_all(send_real, ('row', 'col'), split_axis=0, concat_axis=2, ti...  15.8 us
    unnamed x38, local copies, waits for them, and re-layouts  14 us
    add x4, local copies, waits for them, and re-layouts, transform(): contract('kqpb,krpb->krqp', outer_cos, mid_imag)  13.5 us
  transfers between devices with their start and end apart: 6, of which 4 were waited for; matrix products, arithmetic and copies ran while one was open for 27% of the time, Pallas kernels for 0%

profile of v4, /device:TPU:0, one launch (start us, length us, event | category | flops | bytes accessed | tf_op | source)
XLA Modules:
  0.0 401.7 jit_solution(17833581154242366548)
XLA Ops:
  0.0 4.8 %copy.221 = f32[2,8,64,1024]{3,2,0,1:T(8,128)} copy(f32[2,8,64,1024]{3,2,1,0:T(8,128)} %bitcast.213) | data formatting | bytes 8388608 | tf_op jit(solution)/shard_map/reshape | solution.py:99
  4.8 4.7 %all-to-all-start = ((f32[2,8,64,1024]{3,2,0,1:T(8,128)}), f32[2,8,64,1024]{3,2,0,1:T(8,128)}, u32[]{:S(2)}, u32[]{:S(2)}) async-start(f32[2,8,64,1024]{3,2,0,1:T(8,128)} %copy.221), calls=%async_computation | async-start | bytes 8388608 | tf_op jit(solution)/shard_map/all_to_all | solution.py:100
  10.4 18.6 %fusion.52 = (f32[2,32,64,128]{3,1,2,0:T(8,128)}, f32[2,32,64,128]{3,1,2,0:T(8,128)}, f32[2,32,64,128]{3,1,2,0:T(8,128)}, f32[2,32,64,128]{3,1,2,0:T(8,128)S(1)}) fusion(s32[128]{0:T(128)S(1)} %and_select_fusion.3, s32[2,32,64]{1,2,0:T(8,128)S(1)} %get-tuple-element.38, s32[2,32,64]{1,2,0:T(8,128)S(1)} %get-tuple-element.39), kind=kLoop, calls=%fused_computation.93 | loop fusion | flops 14680064 | bytes 8421888 | tf_op jit(solution)/shard_map/sin | solution.py:42
  29.7 10.7 %fusion.29 = (f32[2,128,32,128]{3,1,2,0:T(8,128)}, f32[2,128,32,128]{3,1,2,0:T(8,128)}) fusion(s32[128]{0:T(128)S(1)} %and_select_fusion, s32[128,32]{0,1:T(8,128)S(1)} %multiply_add_fusion.1), kind=kLoop, calls=%fused_computation.66 | loop fusion | flops 14680064 | bytes 8405504 | tf_op jit(solution)/shard_map/sin | solution.py:42
  40.4 18.7 %all-to-all-done = f32[2,8,64,1024]{3,2,0,1:T(8,128)} async-done(((f32[2,8,64,1024]{3,2,0,1:T(8,128)}), f32[2,8,64,1024]{3,2,0,1:T(8,128)}, u32[]{:S(2)}, u32[]{:S(2)}) %all-to-all-start) | async-done | bytes 4194336 | tf_op jit(solution)/shard_map/all_to_all | solution.py:100
  59.2 6.6 %copy.222 = f32[2,1,64,8,1024]{4,3,2,0,1:T(8,128)} copy(f32[2,1,64,8,1024]{4,2,0,3,1:T(8,128)} %bitcast.4) | data formatting | bytes 8388608 | tf_op jit(solution)/shard_map/all_to_all | solution.py:100
  65.8 5.1 %reshape_reshape.9 = f32[2,64,64,128]{3,2,1,0:T(8,128)} reshape(f32[2,1,64,8,1024]{4,3,2,0,1:T(8,128)} %copy.222) | data formatting | bytes 8388608 | tf_op jit(solution)/shard_map/reshape;reshape | solution.py:51
  78.4 5.1 %fusion.5 = f32[2,64,64,32]{2,3,1,0:T(8,128)S(1)} fusion(f32[2,32,64,128]{3,1,2,0:T(8,128)S(1)} %copy-done.9, f32[2,64,64,128]{3,2,1,0:T(8,128)S(1)} %convolution_bitcast_fusion), kind=kOutput, calls=%fused_computation.22 | convolution fusion | flops 201326592 | bytes 7340032 | tf_op jit(solution)/shard_map/kqpb,krpb->krqp/dot_general | solution.py:22
  83.5 6.8 %add_bitcast_fusion.2 = f32[2,64,32,64]{1,2,3,0:T(8,128)} fusion(f32[2,64,64,32]{2,3,1,0:T(8,128)S(1)} %fusion.5, f32[2,32,64,128]{3,1,2,0:T(8,128)S(1)} %copy-done.11, f32[2,64,64,128]{3,2,1,0:T(8,128)S(1)} %convolution_bitcast_fusion.1), kind=kOutput, calls=%fused_computation.68 | convolution fusion | flops 201588736 | bytes 8388608 | tf_op jit(solution)/shard_map/kqpb,krpb->krqp/dot_general | solution.py:22
  105.2 9.8 %all-to-all-start.2 = ((f32[128,1,2048]{2,1,0:T(1,128)}), f32[128,1,2048]{2,1,0:T(1,128)}, u32[]{:S(2)}, u32[]{:S(2)}) async-start(f32[128,1,2048]{2,1,0:T(1,128)} %reshape.384), calls=%async_computation.2 | async-start | bytes 2097152 | tf_op jit(solution)/shard_map/all_to_all | solution.py:116
  115.1 7.9 %fusion.7 = f32[2,64,64,32]{2,3,1,0:T(8,128)S(1)} fusion(f32[2,32,64,128]{3,1,2,0:T(8,128)} %get-tuple-element.21, f32[2,64,64,128]{3,2,1,0:T(8,128)} %copy-done.6), kind=kOutput, calls=%fused_computation.24 | convolution fusion | flops 201326592 | bytes 7340032 | tf_op jit(solution)/shard_map/kqpb,krpb->krqp/dot_general | solution.py:22
  123.0 6.4 %subtract_bitcast_fusion.2 = f32[2,64,32,64]{1,2,3,0:T(8,128)} fusion(f32[2,64,64,32]{2,3,1,0:T(8,128)S(1)} %fusion.7, f32[2,32,64,128]{3,1,2,0:T(8,128)S(1)} %copy-done.10, f32[2,64,64,128]{3,2,1,0:T(8,128)S(1)} %copy-done.5), kind=kOutput, calls=%fused_computation.69 | convolution fusion | flops 201588736 | bytes 8388608 | tf_op jit(solution)/shard_map/kqpb,krpb->krqp/dot_general | solution.py:22
  144.4 10.2 %all-to-all-start.1 = ((f32[128,1,2048]{2,1,0:T(1,128)}), f32[128,1,2048]{2,1,0:T(1,128)}, u32[]{:S(2)}, u32[]{:S(2)}) async-start(f32[128,1,2048]{2,1,0:T(1,128)} %reshape.382), calls=%async_computation.1 | async-start | bytes 2097152 | tf_op jit(solution)/shard_map/all_to_all | solution.py:109
  168.3 5.1 %all-to-all-done.1 = f32[128,1,2048]{2,1,0:T(1,128)} async-done(((f32[128,1,2048]{2,1,0:T(1,128)}), f32[128,1,2048]{2,1,0:T(1,128)}, u32[]{:S(2)}, u32[]{:S(2)}) %all-to-all-start.1) | async-done | bytes 1048608 | tf_op jit(solution)/shard_map/all_to_all | solution.py:109
  173.4 5.4 %reduce.6 = f32[128,2048]{1,0:T(8,128)} reduce(f32[128,1,2048]{2,1,0:T(1,128)} %all-to-all-done.1, f32[]{:T(128)} %broadcast.541), dimensions={1}, to_apply=%all_to_all.62.reduce_sub_computation | reduce | bytes 2097156 | tf_op jit(solution)/shard_map/all_to_all | solution.py:109
  225.4 5.3 %gather_fusion.1 = f32[384,2,16,32]{3,2,1,0:T(8,128)} fusion(f32[2,16,128,32]{3,1,2,0:T(8,128)} %copy.251, s32[1024]{0:T(1024)S(1)} %pad_clamp_fusion), kind=kCustom, calls=%fused_computation.1.clone | custom fusion | bytes 3147264 | tf_op jit(solution)/shard_map/jit(_take)/gather | solution.py:147
  230.7 6.4 %copy.252 = f32[384,2,16,32]{0,3,2,1:T(8,128)} copy(f32[384,2,16,32]{3,2,1,0:T(8,128)} %gather_fusion.1) | data formatting | bytes 3145728 | tf_op jit(solution)/shard_map/jit(_take)/gather | solution.py:147
  241.5 5.4 %copy.244 = f32[384,2,16,32]{0,3,2,1:T(8,128)S(1)} copy(f32[384,2,16,32]{3,2,1,0:T(8,128)} %gather_fusion) | data formatting | bytes 3145728 | tf_op jit(solution)/shard_map/jit(_take)/gather | solution.py:147
  249.0 5.0 %copy.245 = f32[2,16,384,32]{3,2,1,0:T(8,128)} copy(f32[2,16,384,32]{2,3,1,0:T(8,128)} %get-tuple-element.47) | data formatting | bytes 3145728 | tf_op jit(solution)/shard_map/mul | solution.py:147
  265.3 5.0 %copy.253 = f32[2,16,384,32]{3,2,1,0:T(8,128)} copy(f32[2,16,384,32]{2,3,1,0:T(8,128)} %get-tuple-element.46) | data formatting | bytes 3145728 | tf_op jit(solution)/shard_map/mul | solution.py:147
  270.4 5.3 %reshape.349 = f32[2,16,128,96]{3,2,1,0:T(8,128)} reshape(f32[2,16,384,32]{3,2,1,0:T(8,128)} %copy.253) | data formatting | bytes 3145728 | tf_op jit(solution)/shard_map/reshape | solution.py:148
  279.9 15.8 %all-to-all-done.3 = f32[128,2,16,96]{3,2,1,0:T(8,128)S(1)} async-done(((f32[128,2,16,96]{3,2,1,0:T(8,128)}), f32[128,2,16,96]{3,2,1,0:T(8,128)S(1)}, u32[]{:S(2)}, u32[]{:S(2)}) %all-to-all-start.3) | async-done | bytes 1572896 | tf_op jit(solution)/shard_map/all_to_all | solution.py:152
  295.7 5.8 %all-to-all-start.4 = ((f32[128,2,16,96]{3,2,1,0:T(8,128)}), f32[128,2,16,96]{3,2,1,0:T(8,128)}, u32[]{:S(2)}, u32[]{:S(2)}) async-start(f32[128,2,16,96]{3,2,1,0:T(8,128)} %copy.254), calls=%async_computation.4 | async-start | bytes 4194304 | tf_op jit(solution)/shard_map/all_to_all | solution.py:153
  311.6 19.8 %all-to-all-done.4 = f32[128,2,16,96]{3,2,1,0:T(8,128)} async-done(((f32[128,2,16,96]{3,2,1,0:T(8,128)}), f32[128,2,16,96]{3,2,1,0:T(8,128)}, u32[]{:S(2)}, u32[]{:S(2)}) %all-to-all-start.4) | async-done | bytes 1572896 | tf_op jit(solution)/shard_map/all_to_all | solution.py:153
  340.5 5.4 %fusion.13 = f32[2,32,96,128]{3,2,1,0:T(8,128)S(1)} fusion(f32[2,128,32,128]{3,1,2,0:T(8,128)S(1)} %copy-done.3, f32[2,96,32,128]{3,2,1,0:T(8,128)S(1)} %add_bitcast_fusion.1), kind=kOutput, calls=%fused_computation.48 | convolution fusion | flops 603979776 | bytes 10485760 | tf_op jit(solution)/shard_map/kqpb,krpb->krqp/dot_general | solution.py:22
  346.0 5.4 %fusion.15 = f32[2,32,96,128]{3,2,1,0:T(8,128)S(1)} fusion(f32[2,128,32,128]{3,1,2,0:T(8,128)S(1)} %copy-done.1, f32[2,96,32,128]{3,2,1,0:T(8,128)S(1)} %add_bitcast_fusion.1), kind=kOutput, calls=%fused_computation.50 | convolution fusion | flops 603979776 | bytes 10485760 | tf_op jit(solution)/shard_map/kqpb,krpb->krqp/dot_general | solution.py:22
  353.2 5.6 %subtract_bitcast_fusion = f32[2,96,128,32]{2,1,3,0:T(8,128)S(1)} fusion(f32[2,32,96,128]{3,2,1,0:T(8,128)S(1)} %fusion.15, f32[2,128,32,128]{3,1,2,0:T(8,128)S(1)} %copy-done.3, f32[2,96,32,128]{3,2,1,0:T(8,128)S(1)} %subtract_bitcast_fusion.1), kind=kOutput, calls=%fused_computation.38 | convolution fusion | flops 604766208 | bytes 13631488 | tf_op jit(solution)/shard_map/kqpb,krpb->krqp/dot_general | solution.py:22
  358.7 7.5 %sqrt_reduce_fusion = (f32[2]{0:T(128)S(1)}, f32[2,96,128,32]{2,1,3,0:T(8,128)}) fusion(f32[2,96,128,32]{2,1,3,0:T(8,128)S(1)} %subtract_bitcast_fusion, f32[2,32,96,128]{3,2,1,0:T(8,128)S(1)} %fusion.13, f32[2,128,32,128]{3,1,2,0:T(8,128)S(1)} %copy-done.1, f32[2,96,32,128]{3,2,1,0:T(8,128)S(1)} %subtract_bitcast_fusion.1), kind=kOutput, calls=%fused_computation.36 | convolution fusion | flops 607911936 | bytes 16777224 | tf_op jit(solution)/shard_map/kqpb,krpb->krqp/dot_general | solution.py:22
  366.8 4.8 %all-to-all-start.5 = ((f32[128,1,2]{2,1,0:T(1,128)}), f32[128,1,2]{2,1,0:T(1,128)S(1)}, u32[]{:S(2)}, u32[]{:S(2)}) async-start(f32[128,1,2]{2,1,0:T(1,128)} %broadcast_in_dim.49), calls=%async_computation.5 | async-start | bytes 131072 | tf_op jit(solution)/shard_map/all_to_all | solution.py:165
  377.1 5.1 %copy.263 = f32[2,96,128,32]{1,3,2,0:T(8,128)} copy(f32[2,96,128,32]{2,1,3,0:T(8,128)} %get-tuple-element.57) | data formatting | bytes 6291456 | tf_op jit(solution)/shard_map/add | solution.py:61
  382.4 7.0 %add_select_fusion.1 = (f32[2,1,96,4096]{2,3,0,1:T(8,128)S(1)}, f32[2,1,96,4096]{2,3,0,1:T(8,128)S(1)}) fusion(f32[2,96,128,32]{1,3,2,0:T(8,128)} %copy.263, f32[2]{0:T(128)S(1)} %multiply_add_fusion.2, f32[2,96,128,32]{1,3,2,0:T(8,128)} %copy.259, pred[96,4096]{0,1:T(8,128)(4,1)S(1)} %copy-done.14), kind=kLoop, calls=%fused_computation.18 | loop fusion | flops 14155776 | bytes 12976136 | tf_op jit(solution)/shard_map/jit(_where)/select_n | solution.py:175
  393.2 8.3 %copy.264 = f32[2,2,96,4096]{3,2,1,0:T(8,128)} copy(f32[2,2,96,4096]{2,3,0,1:T(8,128)} %pad_maximum_fusion) | data formatting | bytes 12582912 | tf_op jit(solution)/shard_map/stack | solution.py:177
  (127 shorter events, 151.9 us)
Async XLA Ops:
  4.8 4.7 %copy-start.15 = (s32[2,2]{1,0:T(2,128)S(1)}, s32[2,2]{1,0:T(2,128)}, u32[]{:S(2)}) copy-start(s32[2,2]{1,0:T(2,128)} %param.6) | copy-start | bytes 52
  4.8 54.4 %all-to-all-start = ((f32[2,8,64,1024]{3,2,0,1:T(8,128)}), f32[2,8,64,1024]{3,2,0,1:T(8,128)}, u32[]{:S(2)}, u32[]{:S(2)}) async-start(f32[2,8,64,1024]{3,2,0,1:T(8,128)} %copy.221), calls=%async_computation | async-start | bytes 8388608 | tf_op jit(solution)/shard_map/all_to_all | solution.py:100
  10.4 18.7 %copy-start.16 = (s32[128]{0:T(128)S(1)}, s32[128]{0:T(128)}, u32[]{:S(2)}) copy-start(s32[128]{0:T(128)} %param.7) | copy-start | bytes 1540
  70.9 4.4 %copy-start.7 = (f32[2,64,64,128]{3,2,1,0:T(8,128)S(1)}, f32[2,64,64,128]{3,2,1,0:T(8,128)}, u32[]{:S(2)}) copy-start(f32[2,64,64,128]{3,2,1,0:T(8,128)} %reshape_reshape.9) | copy-start | bytes 12582916
  75.2 8.3 %copy-start.4 = (f32[2,64,64,128]{3,2,1,0:T(8,128)}, f32[2,64,64,128]{3,2,1,0:T(8,128)S(1)}, u32[]{:S(2)}) copy-start(f32[2,64,64,128]{3,2,1,0:T(8,128)S(1)} %convolution_bitcast_fusion.1) | copy-start | bytes 12582916
  75.3 3.1 copy-start.9
  78.4 5.2 %copy-start.6 = (f32[2,64,64,128]{3,2,1,0:T(8,128)}, f32[2,64,64,128]{3,2,1,0:T(8,128)S(1)}, u32[]{:S(2)}) copy-start(f32[2,64,64,128]{3,2,1,0:T(8,128)S(1)} %convolution_bitcast_fusion) | copy-start | bytes 12582916
  78.4 5.2 %copy-start.11 = (f32[2,32,64,128]{3,1,2,0:T(8,128)S(1)}, f32[2,32,64,128]{3,1,2,0:T(8,128)}, u32[]{:S(2)}) copy-start(f32[2,32,64,128]{3,1,2,0:T(8,128)} %get-tuple-element.21) | copy-start | bytes 6291460
  105.2 39.2 %all-to-all-start.2 = ((f32[128,1,2048]{2,1,0:T(1,128)}), f32[128,1,2048]{2,1,0:T(1,128)}, u32[]{:S(2)}, u32[]{:S(2)}) async-start(f32[128,1,2048]{2,1,0:T(1,128)} %reshape.384), calls=%async_computation.2 | async-start | bytes 2097152 | tf_op jit(solution)/shard_map/all_to_all | solution.py:116
  115.1 7.9 %copy-start.5 = (f32[2,64,64,128]{3,2,1,0:T(8,128)S(1)}, f32[2,64,64,128]{3,2,1,0:T(8,128)}, u32[]{:S(2)}) copy-start(f32[2,64,64,128]{3,2,1,0:T(8,128)} %copy-done.4) | copy-start | bytes 12582916
  115.1 7.9 %copy-start.10 = (f32[2,32,64,128]{3,1,2,0:T(8,128)S(1)}, f32[2,32,64,128]{3,1,2,0:T(8,128)}, u32[]{:S(2)}) copy-start(f32[2,32,64,128]{3,1,2,0:T(8,128)} %get-tuple-element.19) | copy-start | bytes 6291460
  144.4 28.9 %all-to-all-start.1 = ((f32[128,1,2048]{2,1,0:T(1,128)}), f32[128,1,2048]{2,1,0:T(1,128)}, u32[]{:S(2)}, u32[]{:S(2)}) async-start(f32[128,1,2048]{2,1,0:T(1,128)} %reshape.382), calls=%async_computation.1 | async-start | bytes 2097152 | tf_op jit(solution)/shard_map/all_to_all | solution.py:109
  192.7 1.6 copy-start.8
  205.8 2.2 copy-start.2
  211.4 3.5 copy-start
  241.5 5.4 %copy-start.13 = (f32[384,2,16,32]{0,3,2,1:T(8,128)S(1)}, f32[384,2,16,32]{0,3,2,1:T(8,128)}, u32[]{:S(2)}) copy-start(f32[384,2,16,32]{0,3,2,1:T(8,128)} %copy.252) | copy-start | bytes 4718596
  260.7 35.0 %all-to-all-start.3 = ((f32[128,2,16,96]{3,2,1,0:T(8,128)}), f32[128,2,16,96]{3,2,1,0:T(8,128)S(1)}, u32[]{:S(2)}, u32[]{:S(2)}) async-start(f32[128,2,16,96]{3,2,1,0:T(8,128)} %copy.246), calls=%async_computation.3 | async-start | bytes 4194304 | tf_op jit(solution)/shard_map/all_to_all | solution.py:152
  295.7 35.7 %all-to-all-start.4 = ((f32[128,2,16,96]{3,2,1,0:T(8,128)}), f32[128,2,16,96]{3,2,1,0:T(8,128)}, u32[]{:S(2)}, u32[]{:S(2)}) async-start(f32[128,2,16,96]{3,2,1,0:T(8,128)} %copy.254), calls=%async_computation.4 | async-start | bytes 4194304 | tf_op jit(solution)/shard_map/all_to_all | solution.py:153
  336.9 3.6 copy-start.3
  340.5 5.5 %copy-start.1 = (f32[2,128,32,128]{3,1,2,0:T(8,128)S(1)}, f32[2,128,32,128]{3,1,2,0:T(8,128)}, u32[]{:S(2)}) copy-start(f32[2,128,32,128]{3,1,2,0:T(8,128)} %get-tuple-element.29) | copy-start | bytes 12582916
  346.0 5.4 %copy-start.12 = (f32[2,96,128,32]{2,3,1,0:T(8,128)S(1)}, f32[2,96,128,32]{2,3,1,0:T(8,128)}, u32[]{:S(2)}) copy-start(f32[2,96,128,32]{2,3,1,0:T(8,128)} %fusion.98) | copy-start | bytes 9437188
  366.8 15.4 %all-to-all-start.5 = ((f32[128,1,2]{2,1,0:T(1,128)}), f32[128,1,2]{2,1,0:T(1,128)S(1)}, u32[]{:S(2)}, u32[]{:S(2)}) async-start(f32[128,1,2]{2,1,0:T(1,128)} %broadcast_in_dim.49), calls=%async_computation.5 | async-start | bytes 131072 | tf_op jit(solution)/shard_map/all_to_all | solution.py:165
  377.1 5.3 %copy-start.14 = (pred[96,4096]{0,1:T(8,128)(4,1)S(1)}, pred[96,4096]{0,1:T(8,128)(4,1)}, u32[]{:S(2)}) copy-start(pred[96,4096]{0,1:T(8,128)(4,1)} %fusion.22) | copy-start | bytes 1179652

commit v5 on v4

--- a/solution.py
+++ b/solution.py
@@ -81,7 +81,21 @@
     return (plus_real, plus_imag, minus_real, minus_imag)
 
 
-def body(holograms, sideband_centre, strip_owner):
+def slot_plan(strip_owner):
+    strips = strip_owner.shape[0]
+    strip_ids = jnp.arange(strips, dtype=jnp.int32)
+    same = strip_owner[:, None] == strip_owner[None, :]
+    before = strip_ids[None, :] < strip_ids[:, None]
+    rank = jnp.sum((same & before).astype(jnp.int32), axis=1)
+    slot_of = strip_owner * MOST + rank
+    slot_ids = jnp.arange(strips * MOST, dtype=jnp.int32)
+    match = slot_of[None, :] == slot_ids[:, None]
+    source = jnp.sum(jnp.where(match, strip_ids[None, :], 0), axis=1)
+    filled = jnp.any(match, axis=1).astype(jnp.float32)
+    return source, filled
+
+
+def field_rows(holograms, sideband_centre, source, filled, strips):
     holo_count = holograms.shape[0]
     row_devices = lax.axis_size("row")
     col_devices = lax.axis_size("col")
@@ -129,18 +143,8 @@
     lift_real, lift_imag = transform(
         side_real.reshape(holo_count, share, S), side_imag.reshape(holo_count, share, S), table_p
     )
-    strips = strip_owner.shape[0]
     strip_rows = P_SIZE // strips
     slot_rows = MOST * strip_rows
-    strip_ids = jnp.arange(strips, dtype=jnp.int32)
-    same = strip_owner[:, None] == strip_owner[None, :]
-    before = strip_ids[None, :] < strip_ids[:, None]
-    rank = jnp.sum((same & before).astype(jnp.int32), axis=1)
-    slot_of = strip_owner * MOST + rank
-    slot_ids = jnp.arange(strips * MOST, dtype=jnp.int32)
-    match = slot_of[None, :] == slot_ids[:, None]
-    source = jnp.sum(jnp.where(match, strip_ids[None, :], 0), axis=1)
-    filled = jnp.any(match, axis=1).astype(jnp.float32)
 
     def pack(part):
         grouped = part.reshape(holo_count, share, strips, strip_rows)
@@ -155,12 +159,28 @@
     rows_real = jnp.swapaxes(piece_real.reshape(lead, width, count), 1, 2)
     rows_imag = jnp.swapaxes(piece_imag.reshape(lead, width, count), 1, 2)
     out_real, out_imag = transform(rows_real, rows_imag, table_p)
-    field_real = out_real.reshape(single, lead, count, P_SIZE)
-    field_imag = out_imag.reshape(single, lead, count, P_SIZE)
-    field_real = field_real.reshape(holo_count, slot_rows, P_SIZE)
-    field_imag = field_imag.reshape(holo_count, slot_rows, P_SIZE)
+    field_real = out_real.reshape(holo_count, slot_rows, P_SIZE)
+    field_imag = out_imag.reshape(holo_count, slot_rows, P_SIZE)
     magnitude = jnp.sqrt(field_real * field_real + field_imag * field_imag)
     local_peak = jnp.max(magnitude, axis=(1, 2))
+    return field_real, field_imag, local_peak
+
+
+def body(holograms, sideband_centre, strip_owner):
+    holo_count = holograms.shape[0]
+    col_devices = lax.axis_size("col")
+    devices = lax.axis_size("row") * col_devices
+    strips = strip_owner.shape[0]
+    strip_rows = P_SIZE // strips
+    slot_rows = MOST * strip_rows
+    source, filled = slot_plan(strip_owner)
+    parts = [
+        field_rows(holograms[k : k + 1], sideband_centre[k : k + 1], source, filled, strips)
+        for k in range(holo_count)
+    ]
+    field_real = jnp.concatenate([part[0] for part in parts])
+    field_imag = jnp.concatenate([part[1] for part in parts])
+    local_peak = jnp.concatenate([part[2] for part in parts])
     every = jnp.broadcast_to(local_peak[None, :], (devices, holo_count))
     peak = jnp.max(lax.all_to_all(every, ("row", "col"), 0, 0, tiled=True), axis=0)
     plus_real, plus_imag, minus_real, minus_imag = encode(

time: 409 us -> 520 us (1.27)
  starting transfers between devices: 40 us -> 90.9 us
  matrix products: 97.6 us -> 139 us
  local copies, waits for them, and re-layouts: 148 us -> 189 us
  waiting for transfers between devices: 59.5 us -> 19.3 us
  other arithmetic: 55.9 us -> 72.4 us
    all_to_all x5 -> x10, starting transfers between devices: 35.2 us -> 84.7 us  [the longest x2 22.3 us: field_rows(): lax.all_to_all(col_real.reshape(holo_count, devices, share, pencil), ('ro...]
    dot_general x30 -> x60, matrix products: 97.6 us -> 139 us  [contract(): jnp.einsum(form, left, right, precision=lax.Precision.HIGH, preferred_ele...]
    all_to_all x5 -> x10, waiting for transfers between devices: 59.5 us -> 19.3 us  [the longest x2 15.6 us: field_rows(): lax.all_to_all(send_real, ('row', 'col'), split_axis=0, concat_axis=2, ti...]
    another operation x7 -> x22, local copies, waits for them, and re-layouts: 14.4 us -> 37.9 us  [the longest x3 8.25 us: transform(): real_four = real_part.reshape(batch, rows, blocks, radix)]
    reshape x5 -> x0, local copies, waits for them, and re-layouts: 15.7 us -> none  [the longest x1 4.79 us: body(): holograms.reshape(holo_count, col_devices, local_rows // col_devices, loc...]
    unnamed x38 -> x114, local copies, waits for them, and re-layouts: 14 us -> 24.6 us
    transpose x2 -> x4, local copies, waits for them, and re-layouts: 3.89 us -> 9.49 us  [the longest x2 4.79 us: field_rows(): col_real = jnp.swapaxes(spec_real.reshape(holo_count, pencil, S), 1, 2)]
    all_to_all x2 -> x4, other arithmetic: 9.77 us -> 15.2 us  [the longest x2 7.63 us: field_rows(): lax.all_to_all(col_real.reshape(holo_count, devices, share, pencil), ('ro...]
  transfers between devices with their start and end apart: 6 -> 11, of which waited for: 4 -> 3; matrix products, arithmetic and copies ran while one was open for 27% -> 49% of each run, Pallas kernels for 0% -> 0%
where the time goes in v5:
time: 520 us; the launch traced here: 512 us
  local copies, waits for them, and re-layouts  189 us (36%)
  matrix products  139 us (27%)
  starting transfers between devices  90.9 us (17%)
  other arithmetic  72.4 us (14%)
  waiting for transfers between devices  19.3 us (4%)
    dot_general x60, matrix products, contract(): jnp.einsum(form, left, right, precision=lax.Precision.HIGH, preferred_ele...  139 us
    sin x2, other arithmetic, make_tables(): jnp.sin(outer_angle).reshape(shape_four)  28.3 us
    unnamed x114, local copies, waits for them, and re-layouts  24.6 us
    gather x8, local copies, waits for them, and re-layouts, pack(): picked = jnp.take(grouped, source, axis=2) * filled[None, None, :, None]  24 us
    another operation x14, local copies, waits for them, and re-layouts  22.6 us
    all_to_all x2, starting transfers between devices, field_rows(): lax.all_to_all(col_real.reshape(holo_count, devices, share, pencil), ('ro...  22.3 us
    all_to_all x2, starting transfers between devices, field_rows(): lax.all_to_all(col_imag.reshape(holo_count, devices, share, pencil), ('ro...  20.8 us
    all_to_all x2, starting transfers between devices, field_rows(): lax.all_to_all(send_real, ('row', 'col'), split_axis=0, concat_axis=2, ti...  20.1 us
  transfers between devices with their start and end apart: 11, of which 3 were waited for; matrix products, arithmetic and copies ran while one was open for 49% of the time, Pallas kernels for 0%

profile of v5, /device:TPU:0, one launch (start us, length us, event | category | flops | bytes accessed | tf_op | source)
XLA Modules:
  0.0 511.5 jit_solution(17573166836947147483)
XLA Ops:
  0.0 4.9 fusion.300
  4.9 4.5 all-to-all-start
  17.2 9.6 %fusion.165 = (f32[1,128,32,128]{3,1,2,0:T(8,128)S(1)}, f32[1,128,32,128]{3,1,2,0:T(8,128)}) fusion(s32[128]{0:T(128)S(1)} %and_select_fusion.4, s32[128,32]{0,1:T(8,128)S(1)} %multiply_add_fusion.1), kind=kLoop, calls=%fused_computation.191 | loop fusion | flops 7340032 | bytes 4211200 | tf_op jit(solution)/shard_map/sin | solution.py:42
  26.8 18.7 %fusion.177 = (f32[1,32,64,128]{3,1,2,0:T(8,128)}, f32[1,32,64,128]{3,1,2,0:T(8,128)}, f32[1,32,64,128]{3,1,2,0:T(8,128)}, f32[1,32,64,128]{3,1,2,0:T(8,128)}, f...) fusion(s32[128]{0:T(128)S(1)} %and_select_fusion.8, ...), kind=kLoop, calls=%fused_computation.207 | loop fusion | flops 14680064 | bytes 8421888 | tf_op jit(solution)/shard_map/sin | solution.py:42
  50.1 4.8 all-to-all-start.5
  54.9 4.1 copy.335
  83.8 4.5 fusion.49
  88.4 4.0 fusion.82
  103.0 12.1 %all-to-all-start.1 = ((f32[128,1,1024]{2,1,0:T(1,128)}), f32[128,1,1024]{2,1,0:T(1,128)}, u32[]{:S(2)}, u32[]{:S(2)}) async-start(f32[128,1,1024]{2,1,0:T(1,128)} %reshape.2230), calls=%async_computation.1 | async-start | bytes 1048576 | tf_op jit(solution)/shard_map/all_to_all | solution.py:123
  115.1 4.1 copy.371
  143.6 5.4 %fusion.41 = f32[64,64,32]{1,2,0:T(8,128)} fusion(f32[64,64,128]{2,1,0:T(8,128)} %copy-done.8, f32[1,32,64,128]{3,1,2,0:T(8,128)} %get-tuple-element.39), kind=kOutput, calls=%fused_computation.61 | convolution fusion | flops 100663296 | bytes 3670016 | tf_op jit(solution)/shard_map/kqpb,krpb->krqp/dot_general | solution.py:22
  149.0 10.2 %all-to-all-start.2 = ((f32[128,1,1024]{2,1,0:T(1,128)}), f32[128,1,1024]{2,1,0:T(1,128)}, u32[]{:S(2)}, u32[]{:S(2)}) async-start(f32[128,1,1024]{2,1,0:T(1,128)} %reshape.2232), calls=%async_computation.2 | async-start | bytes 1048576 | tf_op jit(solution)/shard_map/all_to_all | solution.py:130
  159.2 5.7 %fusion.94 = f32[1,64,32,64]{1,2,3,0:T(8,128)} fusion(f32[64,64,32]{1,2,0:T(8,128)} %fusion.41, f32[64,64,128]{2,1,0:T(8,128)} %copy-done.4, f32[1,32,64,128]{3,1,2,0:T(8,128)} %get-tuple-element.41), kind=kOutput, calls=%fused_computation.126 | convolution fusion | flops 100794368 | bytes 4194304 | tf_op jit(solution)/shard_map/kqpb,krpb->krqp/dot_general | solution.py:22
  187.0 10.2 %all-to-all-start.6 = ((f32[128,1,1024]{2,1,0:T(1,128)}), f32[128,1,1024]{2,1,0:T(1,128)}, u32[]{:S(2)}, u32[]{:S(2)}) async-start(f32[128,1,1024]{2,1,0:T(1,128)} %reshape.2226), calls=%async_computation.6 | async-start | bytes 1048576 | tf_op jit(solution)/shard_map/all_to_all | solution.py:123
  216.4 10.6 %all-to-all-start.7 = ((f32[128,1,1024]{2,1,0:T(1,128)}), f32[128,1,1024]{2,1,0:T(1,128)}, u32[]{:S(2)}, u32[]{:S(2)}) async-start(f32[128,1,1024]{2,1,0:T(1,128)} %reshape.2228), calls=%async_computation.7 | async-start | bytes 1048576 | tf_op jit(solution)/shard_map/all_to_all | solution.py:130
  308.5 4.0 fusion.120
  319.9 4.0 fusion.114
  341.6 9.7 %all-to-all-start.3 = ((f32[128,1,16,96]{3,2,1,0:T(8,128)}), f32[128,1,16,96]{3,2,1,0:T(8,128)S(1)}, u32[]{:S(2)}, u32[]{:S(2)}) async-start(f32[128,1,16,96]{3,2,1,0:T(8,128)} %copy.359), calls=%async_computation.3 | async-start | bytes 2097152 | tf_op jit(solution)/shard_map/all_to_all | solution.py:156
  360.3 10.1 %all-to-all-done.3 = f32[128,1,16,96]{3,2,1,0:T(8,128)S(1)} async-done(((f32[128,1,16,96]{3,2,1,0:T(8,128)}), f32[128,1,16,96]{3,2,1,0:T(8,128)S(1)}, u32[]{:S(2)}, u32[]{:S(2)}) %all-to-all-start.3) | async-done | bytes 786464 | tf_op jit(solution)/shard_map/all_to_all | solution.py:156
  370.5 6.2 %all-to-all-start.4 = ((f32[128,1,16,96]{3,2,1,0:T(8,128)}), f32[128,1,16,96]{3,2,1,0:T(8,128)}, u32[]{:S(2)}, u32[]{:S(2)}) async-start(f32[128,1,16,96]{3,2,1,0:T(8,128)} %copy.366), calls=%async_computation.4 | async-start | bytes 2097152 | tf_op jit(solution)/shard_map/all_to_all | solution.py:157
  396.3 10.4 %all-to-all-start.8 = ((f32[128,1,16,96]{3,2,1,0:T(8,128)}), f32[128,1,16,96]{3,2,1,0:T(8,128)}, u32[]{:S(2)}, u32[]{:S(2)}) async-start(f32[128,1,16,96]{3,2,1,0:T(8,128)} %copy.395), calls=%async_computation.8 | async-start | bytes 2097152 | tf_op jit(solution)/shard_map/all_to_all | solution.py:156
  416.1 3.9 fusion.16
  420.0 5.4 %all-to-all-done.8 = f32[128,1,16,96]{3,2,1,0:T(8,128)} async-done(((f32[128,1,16,96]{3,2,1,0:T(8,128)}), f32[128,1,16,96]{3,2,1,0:T(8,128)}, u32[]{:S(2)}, u32[]{:S(2)}) %all-to-all-start.8) | async-done | bytes 786464 | tf_op jit(solution)/shard_map/all_to_all | solution.py:156
  425.4 5.9 %all-to-all-start.9 = ((f32[128,1,16,96]{3,2,1,0:T(8,128)}), f32[128,1,16,96]{3,2,1,0:T(8,128)}, u32[]{:S(2)}, u32[]{:S(2)}) async-start(f32[128,1,16,96]{3,2,1,0:T(8,128)} %copy.402), calls=%async_computation.9 | async-start | bytes 2097152 | tf_op jit(solution)/shard_map/all_to_all | solution.py:157
  437.0 5.3 %subtract_bitcast_fusion.2 = f32[1,96,128,32]{2,1,3,0:T(8,128)} fusion(f32[32,96,128]{2,1,0:T(8,128)} %fusion.16, f32[1,128,32,128]{3,1,2,0:T(8,128)S(1)} %copy-done.2, f32[96,32,128]{2,1,0:T(8,128)S(1)} %copy-done.15), kind=kOutput, calls=%fused_computation.104 | convolution fusion | flops 302383104 | bytes 6815744 | tf_op jit(solution)/shard_map/kqpb,krpb->krqp/dot_general | solution.py:22
  442.2 3.9 fusion.8
  463.2 4.7 sqrt_reduce_fusion.1
  467.8 4.8 sqrt_reduce_fusion
  474.7 6.2 %all-to-all-start.10 = ((f32[128,1,2]{2,1,0:T(1,128)}), f32[128,1,2]{2,1,0:T(1,128)S(1)}, u32[]{:S(2)}, u32[]{:S(2)}) async-start(f32[128,1,2]{2,1,0:T(1,128)} %broadcast_in_dim.31), calls=%async_computation.10 | async-start | bytes 131072 | tf_op jit(solution)/shard_map/all_to_all | solution.py:185
  492.4 6.7 %add_select_fusion = (f32[2,1,96,4096]{2,3,1,0:T(8,128)S(1)}, f32[2,1,96,4096]{2,3,1,0:T(8,128)S(1)}) fusion(f32[1,1,96,4096]{2,3,1,0:T(8,128)} %bitcast.541, f32[1,1,96,4096]{2,3,1,0:T(8,128)} %bitcast.540, f32[1,1,96,4096]{2,3,1,0:T(8,128)} %bitcast.539, f32[1,1,96,4096]{2,3,1,0:T(8,128)S(1)} %bitcast.538, f32[2]{0:T(128)S(1)} %multiply_add_fusion.2, ...), kind=kLoop, calls=%fused_computation.8 | loop fusion | flops 15728640 | bytes 12976136 | tf_op jit(solution)/shard_map/jit(_where)/select_n | solution.py:195
  499.1 3.9 pad_maximum_fusion
  503.0 8.3 %copy.414 = f32[2,2,96,4096]{3,2,1,0:T(8,128)} copy(f32[2,2,96,4096]{2,3,1,0:T(8,128)} %pad_maximum_fusion) | data formatting | bytes 12582912 | tf_op jit(solution)/shard_map/stack | solution.py:197
  (284 shorter events, 293.3 us)
Async XLA Ops:
  4.9 4.6 copy-start.50
  4.9 45.2 %all-to-all-start = ((f32[1,8,64,1024]{3,2,0,1:T(8,128)}), f32[1,8,64,1024]{3,2,0,1:T(8,128)}, u32[]{:S(2)}, u32[]{:S(2)}) async-start(f32[1,8,64,1024]{3,2,0,1:T(8,128)} %bitcast.4), calls=%async_computation | async-start | bytes 4194304 | tf_op jit(solution)/shard_map/all_to_all | solution.py:114
  26.8 21.0 %copy-start.52 = (s32[128]{0:T(128)S(1)}, s32[128]{0:T(128)}, u32[]{:S(2)}) copy-start(s32[128]{0:T(128)} %param.7) | copy-start | bytes 1540
  45.5 215.4 %copy-start.16 = (f32[1,32,64,128]{3,1,2,0:T(8,128)}, f32[1,32,64,128]{3,1,2,0:T(8,128)S(1)}, u32[]{:S(2)}) copy-start(f32[1,32,64,128]{3,1,2,0:T(8,128)S(1)} %get-tuple-element.45) | copy-start | bytes 3145732
  50.1 52.9 %all-to-all-start.5 = ((f32[1,8,64,1024]{3,2,0,1:T(8,128)}), f32[1,8,64,1024]{3,2,0,1:T(8,128)}, u32[]{:S(2)}, u32[]{:S(2)}) async-start(f32[1,8,64,1024]{3,2,0,1:T(8,128)} %bitcast.542), calls=%async_computation.5 | async-start | bytes 4194304 | tf_op jit(solution)/shard_map/all_to_all | solution.py:114
  83.8 4.5 copy-start.7
  83.8 4.6 copy-start.25
  103.0 46.0 %all-to-all-start.1 = ((f32[128,1,1024]{2,1,0:T(1,128)}), f32[128,1,1024]{2,1,0:T(1,128)}, u32[]{:S(2)}, u32[]{:S(2)}) async-start(f32[128,1,1024]{2,1,0:T(1,128)} %reshape.2230), calls=%async_computation.1 | async-start | bytes 1048576 | tf_op jit(solution)/shard_map/all_to_all | solution.py:123
  149.0 38.0 %all-to-all-start.2 = ((f32[128,1,1024]{2,1,0:T(1,128)}), f32[128,1,1024]{2,1,0:T(1,128)}, u32[]{:S(2)}, u32[]{:S(2)}) async-start(f32[128,1,1024]{2,1,0:T(1,128)} %reshape.2232), calls=%async_computation.2 | async-start | bytes 1048576 | tf_op jit(solution)/shard_map/all_to_all | solution.py:130
  187.0 29.4 %all-to-all-start.6 = ((f32[128,1,1024]{2,1,0:T(1,128)}), f32[128,1,1024]{2,1,0:T(1,128)}, u32[]{:S(2)}, u32[]{:S(2)}) async-start(f32[128,1,1024]{2,1,0:T(1,128)} %reshape.2226), calls=%async_computation.6 | async-start | bytes 1048576 | tf_op jit(solution)/shard_map/all_to_all | solution.py:123
  216.4 26.9 %all-to-all-start.7 = ((f32[128,1,1024]{2,1,0:T(1,128)}), f32[128,1,1024]{2,1,0:T(1,128)}, u32[]{:S(2)}, u32[]{:S(2)}) async-start(f32[128,1,1024]{2,1,0:T(1,128)} %reshape.2228), calls=%async_computation.7 | async-start | bytes 1048576 | tf_op jit(solution)/shard_map/all_to_all | solution.py:130
  250.7 3.5 copy-start.45
  250.7 5.0 copy-start.46
  262.8 3.5 copy-start.19
  273.4 4.2 copy-start
  277.6 3.9 copy-start.47
  284.3 3.2 copy-start.17
  290.5 5.1 copy-start.42
  305.3 3.2 copy-start.44
  328.2 3.2 copy-start.39
  328.2 3.2 copy-start.49
  328.2 3.2 copy-start.51
  341.6 28.8 %all-to-all-start.3 = ((f32[128,1,16,96]{3,2,1,0:T(8,128)}), f32[128,1,16,96]{3,2,1,0:T(8,128)S(1)}, u32[]{:S(2)}, u32[]{:S(2)}) async-start(f32[128,1,16,96]{3,2,1,0:T(8,128)} %copy.359), calls=%async_computation.3 | async-start | bytes 2097152 | tf_op jit(solution)/shard_map/all_to_all | solution.py:156
  370.5 10.2 %copy-start.37 = (f32[128,1,16,96]{3,2,1,0:T(8,128)}, f32[128,1,16,96]{3,2,1,0:T(8,128)S(1)}, u32[]{:S(2)}) copy-start(f32[128,1,16,96]{3,2,1,0:T(8,128)S(1)} %all-to-all-done.3) | copy-start | bytes 2359300
  370.5 25.8 %all-to-all-start.4 = ((f32[128,1,16,96]{3,2,1,0:T(8,128)}), f32[128,1,16,96]{3,2,1,0:T(8,128)}, u32[]{:S(2)}, u32[]{:S(2)}) async-start(f32[128,1,16,96]{3,2,1,0:T(8,128)} %copy.366), calls=%async_computation.4 | async-start | bytes 2097152 | tf_op jit(solution)/shard_map/all_to_all | solution.py:157
  396.3 29.1 %all-to-all-start.8 = ((f32[128,1,16,96]{3,2,1,0:T(8,128)}), f32[128,1,16,96]{3,2,1,0:T(8,128)}, u32[]{:S(2)}, u32[]{:S(2)}) async-start(f32[128,1,16,96]{3,2,1,0:T(8,128)} %copy.395), calls=%async_computation.8 | async-start | bytes 2097152 | tf_op jit(solution)/shard_map/all_to_all | solution.py:156
  425.4 24.5 %all-to-all-start.9 = ((f32[128,1,16,96]{3,2,1,0:T(8,128)}), f32[128,1,16,96]{3,2,1,0:T(8,128)}, u32[]{:S(2)}, u32[]{:S(2)}) async-start(f32[128,1,16,96]{3,2,1,0:T(8,128)} %copy.402), calls=%async_computation.9 | async-start | bytes 2097152 | tf_op jit(solution)/shard_map/all_to_all | solution.py:157
  433.0 4.0 copy-start.2
  433.0 4.0 copy-start.15
  463.2 4.7 copy-start.14
  474.7 17.5 %all-to-all-start.10 = ((f32[128,1,2]{2,1,0:T(1,128)}), f32[128,1,2]{2,1,0:T(1,128)S(1)}, u32[]{:S(2)}, u32[]{:S(2)}) async-start(f32[128,1,2]{2,1,0:T(1,128)} %broadcast_in_dim.31), calls=%async_computation.10 | async-start | bytes 131072 | tf_op jit(solution)/shard_map/all_to_all | solution.py:185
  489.2 3.2 copy-start.27
  (32 other events, 73.9 us)

commit v6 on v4

--- a/solution.py
+++ b/solution.py
@@ -55,6 +55,12 @@
         imag_four = imag_part.reshape(batch, rows, blocks, radix)
         mid_real = mid_real - contract("kpa,krab->krpb", inner_sin, imag_four)
         mid_imag = mid_imag + contract("kpa,krab->krpb", inner_cos, imag_four)
+    return finish(mid_real, mid_imag, tables)
+
+
+def finish(mid_real, mid_imag, tables):
+    inner_cos, inner_sin, outer_cos, outer_sin = tables
+    batch, rows = mid_real.shape[:2]
     out_real = contract("kqpb,krpb->krqp", outer_cos, mid_real) - contract(
         "kqpb,krpb->krqp", outer_sin, mid_imag
     )
@@ -97,9 +103,16 @@
     local_rows = holograms.shape[1]
     local_cols = holograms.shape[2]
     blocks = holograms.reshape(holo_count, col_devices, local_rows // col_devices, local_cols)
-    piece = lax.all_to_all(blocks, "col", split_axis=1, concat_axis=3, tiled=True)
-    lead, single, count, width = piece.shape
-    out_real, out_imag = transform(piece.reshape(lead, count, width), None, table_v)
+    piece = lax.all_to_all(blocks, "col", split_axis=1, concat_axis=1, tiled=True)
+    lead, senders, count, width = piece.shape
+    single = 1
+    sender_blocks = width // radix
+    piece_five = piece.reshape(lead, senders, count, sender_blocks, radix)
+    inner_cos, inner_sin = table_v[0], table_v[1]
+    per_sender = inner_cos.shape[:2] + (senders, sender_blocks)
+    mid_real = contract("kpjc,kjrcb->krpb", inner_cos.reshape(per_sender), piece_five)
+    mid_imag = contract("kpjc,kjrcb->krpb", inner_sin.reshape(per_sender), piece_five)
+    out_real, out_imag = finish(mid_real, mid_imag, table_v)
     spec_real = out_real.reshape(lead, single, count, S)
     spec_imag = out_imag.reshape(lead, single, count, S)
     pencil = spec_real.shape[2]

time: 409 us -> 396 us (0.968)
  local copies, waits for them, and re-layouts: 148 us -> 139 us
    all_to_all x1 -> x0, local copies, waits for them, and re-layouts: 6.63 us -> none  [body(): lax.all_to_all(blocks, 'col', split_axis=1, concat_axis=3, tiled=True)]
    another operation x3 -> x2, local copies, waits for them, and re-layouts: 8.25 us -> 3.18 us  [transform(): real_four = real_part.reshape(batch, rows, blocks, radix)]
    unnamed x38 -> x37, local copies, waits for them, and re-layouts: 14 us -> 17.1 us
  transfers between devices with their start and end apart: 6 -> 6, of which waited for: 4 -> 4; matrix products, arithmetic and copies ran while one was open for 27% -> 28% of each run, Pallas kernels for 0% -> 0%
where the time goes in v6:
time: 396 us; the launch traced here: 391 us
  local copies, waits for them, and re-layouts  139 us (35%)
  matrix products  95.4 us (24%)
  waiting for transfers between devices  59.5 us (15%)
  other arithmetic  55.8 us (14%)
  starting transfers between devices  40.1 us (10%)
    dot_general x30, matrix products, contract(): jnp.einsum(form, left, right, precision=lax.Precision.HIGH, preferred_ele...  95.4 us
    sin x2, other arithmetic, make_tables(): jnp.sin(outer_angle).reshape(shape_four)  29.5 us
    gather x4, local copies, waits for them, and re-layouts, pack(): picked = jnp.take(grouped, source, axis=2) * filled[None, None, :, None]  21.4 us
    all_to_all x1, waiting for transfers between devices, body(): lax.all_to_all(send_imag, ('row', 'col'), split_axis=0, concat_axis=2, ti...  19.8 us
    all_to_all x1, waiting for transfers between devices, body(): lax.all_to_all(blocks, 'col', split_axis=1, concat_axis=1, tiled=True)  18.7 us
    unnamed x37, local copies, waits for them, and re-layouts  17.1 us
    all_to_all x1, waiting for transfers between devices, body(): lax.all_to_all(send_real, ('row', 'col'), split_axis=0, concat_axis=2, ti...  15.8 us
    add x4, local copies, waits for them, and re-layouts, finish(): contract('kqpb,krpb->krqp', outer_cos, mid_imag)  13.5 us
  transfers between devices with their start and end apart: 6, of which 4 were waited for; matrix products, arithmetic and copies ran while one was open for 28% of the time, Pallas kernels for 0%

profile of v6, /device:TPU:0, one launch (start us, length us, event | category | flops | bytes accessed | tf_op | source)
XLA Modules:
  0.0 390.9 jit_solution(14541427480826295331)
XLA Ops:
  0.0 4.8 %copy.253 = f32[2,8,64,1024]{3,2,0,1:T(8,128)} copy(f32[2,8,64,1024]{3,2,1,0:T(8,128)} %bitcast.225) | data formatting | bytes 8388608 | tf_op jit(solution)/shard_map/reshape | solution.py:105
  4.8 4.7 %all-to-all-start = ((f32[2,8,64,1024]{3,2,0,1:T(8,128)}), f32[2,8,64,1024]{3,2,0,1:T(8,128)}, u32[]{:S(2)}, u32[]{:S(2)}) async-start(f32[2,8,64,1024]{3,2,0,1:T(8,128)} %copy.253), calls=%async_computation | async-start | bytes 8388608 | tf_op jit(solution)/shard_map/all_to_all | solution.py:106
  10.4 18.6 %fusion.62 = (f32[2,32,64,128]{3,1,2,0:T(8,128)}, f32[2,32,64,128]{3,1,2,0:T(8,128)}, f32[2,32,64,128]{3,1,2,0:T(8,128)}, f32[2,32,64,128]{3,1,2,0:T(8,128)S(1)}) fusion(s32[128]{0:T(128)S(1)} %and_select_fusion.3, s32[2,32,64]{1,2,0:T(8,128)S(1)} %get-tuple-element.38, s32[2,32,64]{1,2,0:T(8,128)S(1)} %get-tuple-element.39), kind=kLoop, calls=%fused_computation.97 | loop fusion | flops 14680064 | bytes 8421888 | tf_op jit(solution)/shard_map/sin | solution.py:42
  29.6 10.9 %fusion.39 = (f32[2,128,32,128]{3,1,2,0:T(8,128)}, f32[2,128,32,128]{3,1,2,0:T(8,128)}) fusion(s32[128]{0:T(128)S(1)} %and_select_fusion, s32[128,32]{0,1:T(8,128)S(1)} %multiply_add_fusion.1), kind=kLoop, calls=%fused_computation.70 | loop fusion | flops 14680064 | bytes 8405504 | tf_op jit(solution)/shard_map/sin | solution.py:42
  40.5 18.7 %all-to-all-done = f32[2,8,64,1024]{3,2,0,1:T(8,128)} async-done(((f32[2,8,64,1024]{3,2,0,1:T(8,128)}), f32[2,8,64,1024]{3,2,0,1:T(8,128)}, u32[]{:S(2)}, u32[]{:S(2)}) %all-to-all-start) | async-done | bytes 4194336 | tf_op jit(solution)/shard_map/all_to_all | solution.py:106
  67.6 5.1 %fusion.9 = f32[2,64,64,32]{2,3,1,0:T(8,128)S(1)} fusion(f32[2,32,64,128]{3,1,2,0:T(8,128)S(1)} %copy-done.8, f32[2,64,64,128]{3,2,1,0:T(8,128)S(1)} %fusion.28), kind=kOutput, calls=%fused_computation.26 | convolution fusion | flops 201326592 | bytes 7340032 | tf_op jit(solution)/shard_map/kqpb,krpb->krqp/dot_general | solution.py:22
  72.7 6.8 %add_bitcast_fusion.2 = f32[2,64,32,64]{1,2,3,0:T(8,128)} fusion(f32[2,64,64,32]{2,3,1,0:T(8,128)S(1)} %fusion.9, f32[2,32,64,128]{3,1,2,0:T(8,128)S(1)} %copy-done.10, f32[2,64,64,128]{3,2,1,0:T(8,128)S(1)} %fusion.25), kind=kOutput, calls=%fused_computation.72 | convolution fusion | flops 201588736 | bytes 8388608 | tf_op jit(solution)/shard_map/kqpb,krpb->krqp/dot_general | solution.py:22
  94.3 9.8 %all-to-all-start.2 = ((f32[128,1,2048]{2,1,0:T(1,128)}), f32[128,1,2048]{2,1,0:T(1,128)}, u32[]{:S(2)}, u32[]{:S(2)}) async-start(f32[128,1,2048]{2,1,0:T(1,128)} %reshape.400), calls=%async_computation.2 | async-start | bytes 2097152 | tf_op jit(solution)/shard_map/all_to_all | solution.py:129
  104.2 7.9 %fusion.11 = f32[2,64,64,32]{2,3,1,0:T(8,128)S(1)} fusion(f32[2,32,64,128]{3,1,2,0:T(8,128)} %get-tuple-element.21, f32[2,64,64,128]{3,2,1,0:T(8,128)} %copy-done.6), kind=kOutput, calls=%fused_computation.28 | convolution fusion | flops 201326592 | bytes 7340032 | tf_op jit(solution)/shard_map/kqpb,krpb->krqp/dot_general | solution.py:22
  112.1 6.4 %subtract_bitcast_fusion.2 = f32[2,64,32,64]{1,2,3,0:T(8,128)} fusion(f32[2,64,64,32]{2,3,1,0:T(8,128)S(1)} %fusion.11, f32[2,32,64,128]{3,1,2,0:T(8,128)S(1)} %copy-done.9, f32[2,64,64,128]{3,2,1,0:T(8,128)S(1)} %copy-done.5), kind=kOutput, calls=%fused_computation.73 | convolution fusion | flops 201588736 | bytes 8388608 | tf_op jit(solution)/shard_map/kqpb,krpb->krqp/dot_general | solution.py:22
  133.5 10.2 %all-to-all-start.1 = ((f32[128,1,2048]{2,1,0:T(1,128)}), f32[128,1,2048]{2,1,0:T(1,128)}, u32[]{:S(2)}, u32[]{:S(2)}) async-start(f32[128,1,2048]{2,1,0:T(1,128)} %reshape.398), calls=%async_computation.1 | async-start | bytes 2097152 | tf_op jit(solution)/shard_map/all_to_all | solution.py:122
  144.6 4.3 %reduce.7 = f32[128,2048]{1,0:T(8,128)S(1)} reduce(f32[128,1,2048]{2,1,0:T(1,128)} %all-to-all-done.2, f32[]{:T(128)} %broadcast.541), dimensions={1}, to_apply=%all_to_all.55.reduce_sub_computation | reduce | bytes 2097156 | tf_op jit(solution)/shard_map/all_to_all | solution.py:129
  157.2 5.2 %all-to-all-done.1 = f32[128,1,2048]{2,1,0:T(1,128)} async-done(((f32[128,1,2048]{2,1,0:T(1,128)}), f32[128,1,2048]{2,1,0:T(1,128)}, u32[]{:S(2)}, u32[]{:S(2)}) %all-to-all-start.1) | async-done | bytes 1048608 | tf_op jit(solution)/shard_map/all_to_all | solution.py:122
  162.4 5.3 %reduce.6 = f32[128,2048]{1,0:T(8,128)} reduce(f32[128,1,2048]{2,1,0:T(1,128)} %all-to-all-done.1, f32[]{:T(128)} %broadcast.541), dimensions={1}, to_apply=%all_to_all.52.reduce_sub_computation | reduce | bytes 2097156 | tf_op jit(solution)/shard_map/all_to_all | solution.py:122
  214.6 5.3 %gather_fusion.1 = f32[384,2,16,32]{3,2,1,0:T(8,128)} fusion(f32[2,16,128,32]{3,1,2,0:T(8,128)} %copy.289, s32[1024]{0:T(1024)S(1)} %pad_clamp_fusion), kind=kCustom, calls=%fused_computation.1.clone | custom fusion | bytes 3147264 | tf_op jit(solution)/shard_map/jit(_take)/gather | solution.py:160
  219.9 6.3 %copy.290 = f32[384,2,16,32]{0,3,2,1:T(8,128)} copy(f32[384,2,16,32]{3,2,1,0:T(8,128)} %gather_fusion.1) | data formatting | bytes 3145728 | tf_op jit(solution)/shard_map/jit(_take)/gather | solution.py:160
  230.5 5.4 %copy.282 = f32[384,2,16,32]{0,3,2,1:T(8,128)S(1)} copy(f32[384,2,16,32]{3,2,1,0:T(8,128)} %gather_fusion) | data formatting | bytes 3145728 | tf_op jit(solution)/shard_map/jit(_take)/gather | solution.py:160
  238.1 5.0 %copy.283 = f32[2,16,384,32]{3,2,1,0:T(8,128)} copy(f32[2,16,384,32]{2,3,1,0:T(8,128)} %get-tuple-element.47) | data formatting | bytes 3145728 | tf_op jit(solution)/shard_map/mul | solution.py:160
  249.8 4.6 %all-to-all-start.3 = ((f32[128,2,16,96]{3,2,1,0:T(8,128)}), f32[128,2,16,96]{3,2,1,0:T(8,128)S(1)}, u32[]{:S(2)}, u32[]{:S(2)}) async-start(f32[128,2,16,96]{3,2,1,0:T(8,128)} %copy.284), calls=%async_computation.3 | async-start | bytes 4194304 | tf_op jit(solution)/shard_map/all_to_all | solution.py:165
  254.4 5.0 %copy.291 = f32[2,16,384,32]{3,2,1,0:T(8,128)} copy(f32[2,16,384,32]{2,3,1,0:T(8,128)} %get-tuple-element.46) | data formatting | bytes 3145728 | tf_op jit(solution)/shard_map/mul | solution.py:160
  259.4 5.3 %reshape.360 = f32[2,16,128,96]{3,2,1,0:T(8,128)} reshape(f32[2,16,384,32]{3,2,1,0:T(8,128)} %copy.291) | data formatting | bytes 3145728 | tf_op jit(solution)/shard_map/reshape | solution.py:161
  269.0 15.8 %all-to-all-done.3 = f32[128,2,16,96]{3,2,1,0:T(8,128)S(1)} async-done(((f32[128,2,16,96]{3,2,1,0:T(8,128)}), f32[128,2,16,96]{3,2,1,0:T(8,128)S(1)}, u32[]{:S(2)}, u32[]{:S(2)}) %all-to-all-start.3) | async-done | bytes 1572896 | tf_op jit(solution)/shard_map/all_to_all | solution.py:165
  284.8 5.8 %all-to-all-start.4 = ((f32[128,2,16,96]{3,2,1,0:T(8,128)}), f32[128,2,16,96]{3,2,1,0:T(8,128)}, u32[]{:S(2)}, u32[]{:S(2)}) async-start(f32[128,2,16,96]{3,2,1,0:T(8,128)} %copy.292), calls=%async_computation.4 | async-start | bytes 4194304 | tf_op jit(solution)/shard_map/all_to_all | solution.py:166
  300.7 19.8 %all-to-all-done.4 = f32[128,2,16,96]{3,2,1,0:T(8,128)} async-done(((f32[128,2,16,96]{3,2,1,0:T(8,128)}), f32[128,2,16,96]{3,2,1,0:T(8,128)}, u32[]{:S(2)}, u32[]{:S(2)}) %all-to-all-start.4) | async-done | bytes 1572896 | tf_op jit(solution)/shard_map/all_to_all | solution.py:166
  329.6 5.4 %fusion.17 = f32[2,32,96,128]{3,2,1,0:T(8,128)S(1)} fusion(f32[2,128,32,128]{3,1,2,0:T(8,128)S(1)} %copy-done.3, f32[2,96,32,128]{3,2,1,0:T(8,128)S(1)} %add_bitcast_fusion.1), kind=kOutput, calls=%fused_computation.52 | convolution fusion | flops 603979776 | bytes 10485760 | tf_op jit(solution)/shard_map/kqpb,krpb->krqp/dot_general | solution.py:22
  335.1 5.4 %fusion.19 = f32[2,32,96,128]{3,2,1,0:T(8,128)S(1)} fusion(f32[2,128,32,128]{3,1,2,0:T(8,128)S(1)} %copy-done.1, f32[2,96,32,128]{3,2,1,0:T(8,128)S(1)} %add_bitcast_fusion.1), kind=kOutput, calls=%fused_computation.54 | convolution fusion | flops 603979776 | bytes 10485760 | tf_op jit(solution)/shard_map/kqpb,krpb->krqp/dot_general | solution.py:22
  342.2 5.6 %subtract_bitcast_fusion = f32[2,96,128,32]{2,1,3,0:T(8,128)S(1)} fusion(f32[2,32,96,128]{3,2,1,0:T(8,128)S(1)} %fusion.19, f32[2,128,32,128]{3,1,2,0:T(8,128)S(1)} %copy-done.3, f32[2,96,32,128]{3,2,1,0:T(8,128)S(1)} %subtract_bitcast_fusion.1), kind=kOutput, calls=%fused_computation.42 | convolution fusion | flops 604766208 | bytes 13631488 | tf_op jit(solution)/shard_map/kqpb,krpb->krqp/dot_general | solution.py:22
  347.8 7.5 %sqrt_reduce_fusion = (f32[2]{0:T(128)S(1)}, f32[2,96,128,32]{2,1,3,0:T(8,128)}) fusion(f32[2,96,128,32]{2,1,3,0:T(8,128)S(1)} %subtract_bitcast_fusion, f32[2,32,96,128]{3,2,1,0:T(8,128)S(1)} %fusion.17, f32[2,128,32,128]{3,1,2,0:T(8,128)S(1)} %copy-done.1, f32[2,96,32,128]{3,2,1,0:T(8,128)S(1)} %subtract_bitcast_fusion.1), kind=kOutput, calls=%fused_computation.40 | convolution fusion | flops 607911936 | bytes 16777224 | tf_op jit(solution)/shard_map/kqpb,krpb->krqp/dot_general | solution.py:22
  355.9 4.8 %all-to-all-start.5 = ((f32[128,1,2]{2,1,0:T(1,128)}), f32[128,1,2]{2,1,0:T(1,128)S(1)}, u32[]{:S(2)}, u32[]{:S(2)}) async-start(f32[128,1,2]{2,1,0:T(1,128)} %broadcast_in_dim.49), calls=%async_computation.5 | async-start | bytes 131072 | tf_op jit(solution)/shard_map/all_to_all | solution.py:178
  366.2 5.1 %copy.301 = f32[2,96,128,32]{1,3,2,0:T(8,128)} copy(f32[2,96,128,32]{2,1,3,0:T(8,128)} %get-tuple-element.57) | data formatting | bytes 6291456 | tf_op jit(solution)/shard_map/add | solution.py:67
  371.5 7.0 %add_select_fusion.1 = (f32[2,1,96,4096]{2,3,0,1:T(8,128)S(1)}, f32[2,1,96,4096]{2,3,0,1:T(8,128)S(1)}) fusion(f32[2,96,128,32]{1,3,2,0:T(8,128)} %copy.301, f32[2]{0:T(128)S(1)} %multiply_add_fusion.2, f32[2,96,128,32]{1,3,2,0:T(8,128)} %copy.297, pred[96,4096]{0,1:T(8,128)(4,1)S(1)} %copy-done.13), kind=kLoop, calls=%fused_computation.18 | loop fusion | flops 14155776 | bytes 12976136 | tf_op jit(solution)/shard_map/jit(_where)/select_n | solution.py:188
  382.3 8.3 %copy.302 = f32[2,2,96,4096]{3,2,1,0:T(8,128)} copy(f32[2,2,96,4096]{2,3,0,1:T(8,128)} %pad_maximum_fusion) | data formatting | bytes 12582912 | tf_op jit(solution)/shard_map/stack | solution.py:190
  (124 shorter events, 143.6 us)
Async XLA Ops:
  4.8 4.7 %copy-start.14 = (s32[2,2]{1,0:T(2,128)S(1)}, s32[2,2]{1,0:T(2,128)}, u32[]{:S(2)}) copy-start(s32[2,2]{1,0:T(2,128)} %param.6) | copy-start | bytes 52
  4.8 54.4 %all-to-all-start = ((f32[2,8,64,1024]{3,2,0,1:T(8,128)}), f32[2,8,64,1024]{3,2,0,1:T(8,128)}, u32[]{:S(2)}, u32[]{:S(2)}) async-start(f32[2,8,64,1024]{3,2,0,1:T(8,128)} %copy.253), calls=%async_computation | async-start | bytes 8388608 | tf_op jit(solution)/shard_map/all_to_all | solution.py:106
  10.4 18.7 %copy-start.15 = (s32[128]{0:T(128)S(1)}, s32[128]{0:T(128)}, u32[]{:S(2)}) copy-start(s32[128]{0:T(128)} %param.7) | copy-start | bytes 1540
  64.4 8.2 %copy-start.4 = (f32[2,64,64,128]{3,2,1,0:T(8,128)}, f32[2,64,64,128]{3,2,1,0:T(8,128)S(1)}, u32[]{:S(2)}) copy-start(f32[2,64,64,128]{3,2,1,0:T(8,128)S(1)} %fusion.25) | copy-start | bytes 12582916
  64.4 3.1 copy-start.8
  67.5 5.1 %copy-start.6 = (f32[2,64,64,128]{3,2,1,0:T(8,128)}, f32[2,64,64,128]{3,2,1,0:T(8,128)S(1)}, u32[]{:S(2)}) copy-start(f32[2,64,64,128]{3,2,1,0:T(8,128)S(1)} %fusion.28) | copy-start | bytes 12582916
  67.5 5.1 %copy-start.10 = (f32[2,32,64,128]{3,1,2,0:T(8,128)S(1)}, f32[2,32,64,128]{3,1,2,0:T(8,128)}, u32[]{:S(2)}) copy-start(f32[2,32,64,128]{3,1,2,0:T(8,128)} %get-tuple-element.21) | copy-start | bytes 6291460
  94.3 39.2 %all-to-all-start.2 = ((f32[128,1,2048]{2,1,0:T(1,128)}), f32[128,1,2048]{2,1,0:T(1,128)}, u32[]{:S(2)}, u32[]{:S(2)}) async-start(f32[128,1,2048]{2,1,0:T(1,128)} %reshape.400), calls=%async_computation.2 | async-start | bytes 2097152 | tf_op jit(solution)/shard_map/all_to_all | solution.py:129
  104.2 7.9 %copy-start.5 = (f32[2,64,64,128]{3,2,1,0:T(8,128)S(1)}, f32[2,64,64,128]{3,2,1,0:T(8,128)}, u32[]{:S(2)}) copy-start(f32[2,64,64,128]{3,2,1,0:T(8,128)} %copy-done.4) | copy-start | bytes 12582916
  104.2 7.9 %copy-start.9 = (f32[2,32,64,128]{3,1,2,0:T(8,128)S(1)}, f32[2,32,64,128]{3,1,2,0:T(8,128)}, u32[]{:S(2)}) copy-start(f32[2,32,64,128]{3,1,2,0:T(8,128)} %get-tuple-element.19) | copy-start | bytes 6291460
  133.5 28.9 %all-to-all-start.1 = ((f32[128,1,2048]{2,1,0:T(1,128)}), f32[128,1,2048]{2,1,0:T(1,128)}, u32[]{:S(2)}, u32[]{:S(2)}) async-start(f32[128,1,2048]{2,1,0:T(1,128)} %reshape.398), calls=%async_computation.1 | async-start | bytes 2097152 | tf_op jit(solution)/shard_map/all_to_all | solution.py:122
  181.8 1.6 copy-start.7
  194.9 2.2 copy-start.2
  200.6 3.5 copy-start
  230.5 5.4 %copy-start.12 = (f32[384,2,16,32]{0,3,2,1:T(8,128)S(1)}, f32[384,2,16,32]{0,3,2,1:T(8,128)}, u32[]{:S(2)}) copy-start(f32[384,2,16,32]{0,3,2,1:T(8,128)} %copy.290) | copy-start | bytes 4718596
  249.8 35.0 %all-to-all-start.3 = ((f32[128,2,16,96]{3,2,1,0:T(8,128)}), f32[128,2,16,96]{3,2,1,0:T(8,128)S(1)}, u32[]{:S(2)}, u32[]{:S(2)}) async-start(f32[128,2,16,96]{3,2,1,0:T(8,128)} %copy.284), calls=%async_computation.3 | async-start | bytes 4194304 | tf_op jit(solution)/shard_map/all_to_all | solution.py:165
  284.8 35.7 %all-to-all-start.4 = ((f32[128,2,16,96]{3,2,1,0:T(8,128)}), f32[128,2,16,96]{3,2,1,0:T(8,128)}, u32[]{:S(2)}, u32[]{:S(2)}) async-start(f32[128,2,16,96]{3,2,1,0:T(8,128)} %copy.292), calls=%async_computation.4 | async-start | bytes 4194304 | tf_op jit(solution)/shard_map/all_to_all | solution.py:166
  326.0 3.6 copy-start.3
  329.6 5.5 %copy-start.1 = (f32[2,128,32,128]{3,1,2,0:T(8,128)S(1)}, f32[2,128,32,128]{3,1,2,0:T(8,128)}, u32[]{:S(2)}) copy-start(f32[2,128,32,128]{3,1,2,0:T(8,128)} %get-tuple-element.29) | copy-start | bytes 12582916
  335.1 5.4 %copy-start.11 = (f32[2,96,128,32]{2,3,1,0:T(8,128)S(1)}, f32[2,96,128,32]{2,3,1,0:T(8,128)}, u32[]{:S(2)}) copy-start(f32[2,96,128,32]{2,3,1,0:T(8,128)} %fusion.108) | copy-start | bytes 9437188
  355.9 15.4 %all-to-all-start.5 = ((f32[128,1,2]{2,1,0:T(1,128)}), f32[128,1,2]{2,1,0:T(1,128)S(1)}, u32[]{:S(2)}, u32[]{:S(2)}) async-start(f32[128,1,2]{2,1,0:T(1,128)} %broadcast_in_dim.49), calls=%async_computation.5 | async-start | bytes 131072 | tf_op jit(solution)/shard_map/all_to_all | solution.py:178
  366.2 5.3 %copy-start.13 = (pred[96,4096]{0,1:T(8,128)(4,1)S(1)}, pred[96,4096]{0,1:T(8,128)(4,1)}, u32[]{:S(2)}) copy-start(pred[96,4096]{0,1:T(8,128)(4,1)} %fusion.32) | copy-start | bytes 1179652

commit v7 on v6

--- a/solution.py
+++ b/solution.py
@@ -112,33 +112,25 @@
     per_sender = inner_cos.shape[:2] + (senders, sender_blocks)
     mid_real = contract("kpjc,kjrcb->krpb", inner_cos.reshape(per_sender), piece_five)
     mid_imag = contract("kpjc,kjrcb->krpb", inner_sin.reshape(per_sender), piece_five)
-    out_real, out_imag = finish(mid_real, mid_imag, table_v)
-    spec_real = out_real.reshape(lead, single, count, S)
-    spec_imag = out_imag.reshape(lead, single, count, S)
-    pencil = spec_real.shape[2]
     share = S // devices
-    col_real = jnp.swapaxes(spec_real.reshape(holo_count, pencil, S), 1, 2)
-    col_imag = jnp.swapaxes(spec_imag.reshape(holo_count, pencil, S), 1, 2)
-    piece_real = lax.all_to_all(
-        col_real.reshape(holo_count, devices, share, pencil),
-        ("row", "col"),
-        split_axis=1,
-        concat_axis=3,
-        tiled=True,
-    )
-    piece_imag = lax.all_to_all(
-        col_imag.reshape(holo_count, devices, share, pencil),
-        ("row", "col"),
-        split_axis=1,
-        concat_axis=3,
-        tiled=True,
-    )
-    lead, single, count, width = piece_real.shape
-    out_real, out_imag = transform(
-        piece_real.reshape(lead, count, width), piece_imag.reshape(lead, count, width), table_u
-    )
-    side_real = out_real.reshape(lead, single, count, S)
-    side_imag = out_imag.reshape(lead, single, count, S)
+    outer_cos, outer_sin = table_v[2], table_v[3]
+    form = "kqpb,krpb->qpkr"
+    spec_real = contract(form, outer_cos, mid_real) - contract(form, outer_sin, mid_imag)
+    spec_imag = contract(form, outer_cos, mid_imag) + contract(form, outer_sin, mid_real)
+    send_shape = (devices, share, holo_count, count)
+    piece_real = lax.all_to_all(spec_real.reshape(send_shape), ("row", "col"), 0, 0, tiled=True)
+    piece_imag = lax.all_to_all(spec_imag.reshape(send_shape), ("row", "col"), 0, 0, tiled=True)
+    pair = radix // count
+    col_blocks = devices // pair
+    recv_shape = (col_blocks, pair, share, holo_count, count)
+    recv_real = piece_real.reshape(recv_shape)
+    recv_imag = piece_imag.reshape(recv_shape)
+    inner_cos, inner_sin = table_u[0], table_u[1]
+    step = "kpa,alskr->ksplr"
+    mid_real = contract(step, inner_cos, recv_real) - contract(step, inner_sin, recv_imag)
+    mid_imag = contract(step, inner_sin, recv_real) + contract(step, inner_cos, recv_imag)
+    mid_shape = (holo_count, share, inner_cos.shape[1], radix)
+    side_real, side_imag = finish(mid_real.reshape(mid_shape), mid_imag.reshape(mid_shape), table_u)
     lift_real, lift_imag = transform(
         side_real.reshape(holo_count, share, S), side_imag.reshape(holo_count, share, S), table_p
     )

time: 396 us -> 385 us (0.972)
  local copies, waits for them, and re-layouts: 139 us -> 119 us
  matrix products: 95.4 us -> 101 us
  waiting for transfers between devices: 59.5 us -> 64.4 us
    reshape x2 -> x8, local copies, waits for them, and re-layouts: 6.51 us -> 19.4 us  [the longest x2 7.88 us: body(): mid_imag.reshape(mid_shape)]
    all_to_all x5 -> x1, local copies, waits for them, and re-layouts: 9.14 us -> 0.54 us  [body(): lax.all_to_all(spec_real.reshape(send_shape), ('row', 'col'), 0, 0, tiled...]
    dot_general x30, matrix products: 95.4 us -> 101 us  [contract(): jnp.einsum(form, left, right, precision=lax.Precision.HIGH, preferred_ele...]
    add x4 -> x3, local copies, waits for them, and re-layouts: 13.5 us -> 7.78 us  [finish(): contract('kqpb,krpb->krqp', outer_cos, mid_imag)]
    all_to_all x2, waiting for transfers between devices: 5.19 us -> 10.4 us  [the longest x1 10.4 us: body(): lax.all_to_all(spec_imag.reshape(send_shape), ('row', 'col'), 0, 0, tiled...]
    unnamed x37 -> x41, local copies, waits for them, and re-layouts: 17.1 us -> 12.6 us
    another operation x2 -> x0, local copies, waits for them, and re-layouts: 4.17 us -> none  [the longest x1 2.08 us: body(): col_imag = jnp.swapaxes(spec_imag.reshape(holo_count, pencil, S), 1, 2)]
    sub x4 -> x3, local copies, waits for them, and re-layouts: 9.04 us -> 4.96 us  [finish(): contract('kqpb,krpb->krqp', outer_cos, mid_real)]
  transfers between devices with their start and end apart: 6 -> 6, of which waited for: 4 -> 4; matrix products, arithmetic and copies ran while one was open for 28% -> 25% of each run, Pallas kernels for 0% -> 0%
where the time goes in v7:
time: 385 us; the launch traced here: 380 us
  local copies, waits for them, and re-layouts  119 us (31%)
  matrix products  101 us (26%)
  waiting for transfers between devices  64.4 us (17%)
  other arithmetic  55.2 us (14%)
  starting transfers between devices  39.7 us (10%)
    dot_general x30, matrix products, contract(): jnp.einsum(form, left, right, precision=lax.Precision.HIGH, preferred_ele...  101 us
    sin x2, other arithmetic, make_tables(): jnp.sin(outer_angle).reshape(shape_four)  29.8 us
    gather x4, local copies, waits for them, and re-layouts, pack(): picked = jnp.take(grouped, source, axis=2) * filled[None, None, :, None]  21.6 us
    all_to_all x1, waiting for transfers between devices, body(): lax.all_to_all(send_imag, ('row', 'col'), split_axis=0, concat_axis=2, ti...  19.8 us
    all_to_all x1, waiting for transfers between devices, body(): lax.all_to_all(blocks, 'col', split_axis=1, concat_axis=1, tiled=True)  18.3 us
    all_to_all x1, waiting for transfers between devices, body(): lax.all_to_all(send_real, ('row', 'col'), split_axis=0, concat_axis=2, ti...  15.8 us
    unnamed x41, local copies, waits for them, and re-layouts  12.6 us
    all_to_all x1, waiting for transfers between devices, body(): lax.all_to_all(spec_imag.reshape(send_shape), ('row', 'col'), 0, 0, tiled...  10.4 us
  transfers between devices with their start and end apart: 6, of which 4 were waited for; matrix products, arithmetic and copies ran while one was open for 25% of the time, Pallas kernels for 0%

profile of v7, /device:TPU:0, one launch (start us, length us, event | category | flops | bytes accessed | tf_op | source)
XLA Modules:
  0.0 380.4 jit_solution(1314083219950186347)
XLA Ops:
  0.0 4.8 %copy.285 = f32[2,8,64,1024]{3,2,0,1:T(8,128)} copy(f32[2,8,64,1024]{3,2,1,0:T(8,128)} %bitcast.207) | data formatting | bytes 8388608 | tf_op jit(solution)/shard_map/reshape | solution.py:105
  4.8 4.7 %all-to-all-start = ((f32[2,8,64,1024]{3,2,0,1:T(8,128)}), f32[2,8,64,1024]{3,2,0,1:T(8,128)}, u32[]{:S(2)}, u32[]{:S(2)}) async-start(f32[2,8,64,1024]{3,2,0,1:T(8,128)} %copy.285), calls=%async_computation | async-start | bytes 8388608 | tf_op jit(solution)/shard_map/all_to_all | solution.py:106
  10.4 18.6 %fusion.66 = (f32[2,32,64,128]{3,1,2,0:T(8,128)}, f32[2,32,64,128]{3,1,2,0:T(8,128)}, f32[2,32,64,128]{3,1,2,0:T(8,128)}, f32[2,32,64,128]{3,1,2,0:T(8,128)S(1)}) fusion(s32[128]{0:T(128)S(1)} %and_select_fusion.3, s32[2,32,64]{1,2,0:T(8,128)S(1)} %get-tuple-element.38, s32[2,32,64]{1,2,0:T(8,128)S(1)} %get-tuple-element.39), kind=kLoop, calls=%fused_computation.97 | loop fusion | flops 14680064 | bytes 8421888 | tf_op jit(solution)/shard_map/sin | solution.py:42
  29.6 11.2 %fusion.39 = (f32[2,128,32,128]{3,1,2,0:T(8,128)}, f32[2,128,32,128]{3,1,2,0:T(8,128)}) fusion(s32[128]{0:T(128)S(1)} %and_select_fusion, s32[128,32]{0,1:T(8,128)S(1)} %multiply_add_fusion.1), kind=kLoop, calls=%fused_computation.70 | loop fusion | flops 14680064 | bytes 8405504 | tf_op jit(solution)/shard_map/sin | solution.py:42
  40.9 18.3 %all-to-all-done = f32[2,8,64,1024]{3,2,0,1:T(8,128)} async-done(((f32[2,8,64,1024]{3,2,0,1:T(8,128)}), f32[2,8,64,1024]{3,2,0,1:T(8,128)}, u32[]{:S(2)}, u32[]{:S(2)}) %all-to-all-start) | async-done | bytes 4194336 | tf_op jit(solution)/shard_map/all_to_all | solution.py:106
  66.5 6.5 %fusion.11 = f32[64,2,64,32]{2,3,1,0:T(8,128)S(1)} fusion(f32[2,64,64,128]{3,2,1,0:T(8,128)S(1)} %fusion.28, f32[2,32,64,128]{3,1,2,0:T(8,128)S(1)} %get-tuple-element.21), kind=kOutput, calls=%fused_computation.28 | convolution fusion | flops 201326592 | bytes 7340032 | tf_op jit(solution)/shard_map/kqpb,krpb->qpkr/dot_general | solution.py:22
  73.0 6.5 %subtract_bitcast_fusion.3 = f32[32,64,2,64]{3,0,2,1:T(8,128)S(1)} fusion(f32[64,2,64,32]{2,3,1,0:T(8,128)S(1)} %fusion.11, f32[2,32,64,128]{3,1,2,0:T(8,128)S(1)} %copy-done.10, f32[2,64,64,128]{3,2,1,0:T(8,128)S(1)} %fusion.25), kind=kOutput, calls=%fused_computation.75 | convolution fusion | flops 201588736 | bytes 8388608 | tf_op jit(solution)/shard_map/kqpb,krpb->qpkr/dot_general | solution.py:22
  85.8 9.5 %all-to-all-start.1 = ((f32[128,1,2048]{2,1,0:T(1,128)}), f32[128,1,2048]{2,1,0:T(1,128)S(1)}, u32[]{:S(2)}, u32[]{:S(2)}) async-start(f32[128,1,2048]{2,1,0:T(1,128)} %reshape.414), calls=%async_computation.1 | async-start | bytes 2097152 | tf_op jit(solution)/shard_map/all_to_all | solution.py:121
  95.4 9.3 %fusion.9 = f32[64,2,64,32]{2,3,1,0:T(8,128)S(1)} fusion(f32[2,64,64,128]{3,2,1,0:T(8,128)} %copy-done.6, f32[2,32,64,128]{3,1,2,0:T(8,128)} %get-tuple-element.19), kind=kOutput, calls=%fused_computation.26 | convolution fusion | flops 201326592 | bytes 7340032 | tf_op jit(solution)/shard_map/kqpb,krpb->qpkr/dot_general | solution.py:22
  104.7 6.8 %add_bitcast_fusion.3 = f32[32,64,2,64]{3,0,2,1:T(8,128)S(1)} fusion(f32[64,2,64,32]{2,3,1,0:T(8,128)S(1)} %fusion.9, f32[2,32,64,128]{3,1,2,0:T(8,128)S(1)} %get-tuple-element.21, f32[2,64,64,128]{3,2,1,0:T(8,128)S(1)} %copy-done.5), kind=kOutput, calls=%fused_computation.74 | convolution fusion | flops 201588736 | bytes 8388608 | tf_op jit(solution)/shard_map/kqpb,krpb->qpkr/dot_general | solution.py:22
  115.3 10.3 %all-to-all-start.2 = ((f32[128,1,2048]{2,1,0:T(1,128)}), f32[128,1,2048]{2,1,0:T(1,128)}, u32[]{:S(2)}, u32[]{:S(2)}) async-start(f32[128,1,2048]{2,1,0:T(1,128)} %reshape.416), calls=%async_computation.2 | async-start | bytes 2097152 | tf_op jit(solution)/shard_map/all_to_all | solution.py:122
  133.9 10.4 %all-to-all-done.2 = f32[128,1,2048]{2,1,0:T(1,128)} async-done(((f32[128,1,2048]{2,1,0:T(1,128)}), f32[128,1,2048]{2,1,0:T(1,128)}, u32[]{:S(2)}, u32[]{:S(2)}) %all-to-all-start.2) | async-done | bytes 1048608 | tf_op jit(solution)/shard_map/all_to_all | solution.py:122
  144.3 4.3 %reduce.7 = f32[128,2048]{1,0:T(8,128)S(1)} reduce(f32[128,1,2048]{2,1,0:T(1,128)} %all-to-all-done.2, f32[]{:T(128)} %broadcast.541), dimensions={1}, to_apply=%all_to_all.37.reduce_sub_computation | reduce | bytes 2097156 | tf_op jit(solution)/shard_map/all_to_all | solution.py:122
  166.8 4.4 %copy.365 = f32[2,16,64,2,64]{4,3,1,2,0:T(2,128)} copy(f32[2,16,64,2,64]{2,4,1,3,0:T(8,128)} %add_bitcast_fusion.2) | data formatting | bytes 2097152 | tf_op jit(solution)/shard_map/reshape | solution.py:133
  203.8 5.3 %gather_fusion.1 = f32[384,2,16,32]{3,2,1,0:T(8,128)} fusion(f32[2,16,128,32]{3,1,2,0:T(8,128)} %copy.327, s32[1024]{0:T(1024)S(1)} %pad_clamp_fusion), kind=kCustom, calls=%fused_computation.1.clone | custom fusion | bytes 3147264 | tf_op jit(solution)/shard_map/jit(_take)/gather | solution.py:152
  209.1 6.4 %copy.328 = f32[384,2,16,32]{0,3,2,1:T(8,128)} copy(f32[384,2,16,32]{3,2,1,0:T(8,128)} %gather_fusion.1) | data formatting | bytes 3145728 | tf_op jit(solution)/shard_map/jit(_take)/gather | solution.py:152
  219.8 5.6 %copy.320 = f32[384,2,16,32]{0,3,2,1:T(8,128)S(1)} copy(f32[384,2,16,32]{3,2,1,0:T(8,128)} %gather_fusion) | data formatting | bytes 3145728 | tf_op jit(solution)/shard_map/jit(_take)/gather | solution.py:152
  227.5 5.0 %copy.321 = f32[2,16,384,32]{3,2,1,0:T(8,128)} copy(f32[2,16,384,32]{2,3,1,0:T(8,128)} %get-tuple-element.47) | data formatting | bytes 3145728 | tf_op jit(solution)/shard_map/mul | solution.py:152
  239.2 4.6 %all-to-all-start.3 = ((f32[128,2,16,96]{3,2,1,0:T(8,128)}), f32[128,2,16,96]{3,2,1,0:T(8,128)S(1)}, u32[]{:S(2)}, u32[]{:S(2)}) async-start(f32[128,2,16,96]{3,2,1,0:T(8,128)} %copy.322), calls=%async_computation.3 | async-start | bytes 4194304 | tf_op jit(solution)/shard_map/all_to_all | solution.py:157
  243.9 5.0 %copy.329 = f32[2,16,384,32]{3,2,1,0:T(8,128)} copy(f32[2,16,384,32]{2,3,1,0:T(8,128)} %get-tuple-element.46) | data formatting | bytes 3145728 | tf_op jit(solution)/shard_map/mul | solution.py:152
  248.9 5.3 %reshape.374 = f32[2,16,128,96]{3,2,1,0:T(8,128)} reshape(f32[2,16,384,32]{3,2,1,0:T(8,128)} %copy.329) | data formatting | bytes 3145728 | tf_op jit(solution)/shard_map/reshape | solution.py:153
  258.4 15.8 %all-to-all-done.3 = f32[128,2,16,96]{3,2,1,0:T(8,128)S(1)} async-done(((f32[128,2,16,96]{3,2,1,0:T(8,128)}), f32[128,2,16,96]{3,2,1,0:T(8,128)S(1)}, u32[]{:S(2)}, u32[]{:S(2)}) %all-to-all-start.3) | async-done | bytes 1572896 | tf_op jit(solution)/shard_map/all_to_all | solution.py:157
  274.2 5.8 %all-to-all-start.4 = ((f32[128,2,16,96]{3,2,1,0:T(8,128)}), f32[128,2,16,96]{3,2,1,0:T(8,128)}, u32[]{:S(2)}, u32[]{:S(2)}) async-start(f32[128,2,16,96]{3,2,1,0:T(8,128)} %copy.330), calls=%async_computation.4 | async-start | bytes 4194304 | tf_op jit(solution)/shard_map/all_to_all | solution.py:158
  290.2 19.8 %all-to-all-done.4 = f32[128,2,16,96]{3,2,1,0:T(8,128)} async-done(((f32[128,2,16,96]{3,2,1,0:T(8,128)}), f32[128,2,16,96]{3,2,1,0:T(8,128)}, u32[]{:S(2)}, u32[]{:S(2)}) %all-to-all-start.4) | async-done | bytes 1572896 | tf_op jit(solution)/shard_map/all_to_all | solution.py:158
  319.1 5.4 %fusion.17 = f32[2,32,96,128]{3,2,1,0:T(8,128)S(1)} fusion(f32[2,128,32,128]{3,1,2,0:T(8,128)S(1)} %copy-done.3, f32[2,96,32,128]{3,2,1,0:T(8,128)S(1)} %add_bitcast_fusion.1), kind=kOutput, calls=%fused_computation.52 | convolution fusion | flops 603979776 | bytes 10485760 | tf_op jit(solution)/shard_map/kqpb,krpb->krqp/dot_general | solution.py:22
  324.6 5.4 %fusion.19 = f32[2,32,96,128]{3,2,1,0:T(8,128)S(1)} fusion(f32[2,128,32,128]{3,1,2,0:T(8,128)S(1)} %copy-done.1, f32[2,96,32,128]{3,2,1,0:T(8,128)S(1)} %add_bitcast_fusion.1), kind=kOutput, calls=%fused_computation.54 | convolution fusion | flops 603979776 | bytes 10485760 | tf_op jit(solution)/shard_map/kqpb,krpb->krqp/dot_general | solution.py:22
  331.7 5.8 %subtract_bitcast_fusion = f32[2,96,128,32]{2,1,3,0:T(8,128)S(1)} fusion(f32[2,32,96,128]{3,2,1,0:T(8,128)S(1)} %fusion.19, f32[2,128,32,128]{3,1,2,0:T(8,128)S(1)} %copy-done.3, f32[2,96,32,128]{3,2,1,0:T(8,128)S(1)} %subtract_bitcast_fusion.1), kind=kOutput, calls=%fused_computation.42 | convolution fusion | flops 604766208 | bytes 13631488 | tf_op jit(solution)/shard_map/kqpb,krpb->krqp/dot_general | solution.py:22
  337.5 7.5 %sqrt_reduce_fusion = (f32[2]{0:T(128)S(1)}, f32[2,96,128,32]{2,1,3,0:T(8,128)}) fusion(f32[2,96,128,32]{2,1,3,0:T(8,128)S(1)} %subtract_bitcast_fusion, f32[2,32,96,128]{3,2,1,0:T(8,128)S(1)} %fusion.17, f32[2,128,32,128]{3,1,2,0:T(8,128)S(1)} %copy-done.1, f32[2,96,32,128]{3,2,1,0:T(8,128)S(1)} %subtract_bitcast_fusion.1), kind=kOutput, calls=%fused_computation.40 | convolution fusion | flops 607911936 | bytes 16777224 | tf_op jit(solution)/shard_map/kqpb,krpb->krqp/dot_general | solution.py:22
  345.6 4.8 %all-to-all-start.5 = ((f32[128,1,2]{2,1,0:T(1,128)}), f32[128,1,2]{2,1,0:T(1,128)S(1)}, u32[]{:S(2)}, u32[]{:S(2)}) async-start(f32[128,1,2]{2,1,0:T(1,128)} %broadcast_in_dim.49), calls=%async_computation.5 | async-start | bytes 131072 | tf_op jit(solution)/shard_map/all_to_all | solution.py:170
  355.8 5.1 %copy.339 = f32[2,96,128,32]{1,3,2,0:T(8,128)} copy(f32[2,96,128,32]{2,1,3,0:T(8,128)} %get-tuple-element.57) | data formatting | bytes 6291456 | tf_op jit(solution)/shard_map/add | solution.py:67
  361.1 7.0 %add_select_fusion.1 = (f32[2,1,96,4096]{2,3,0,1:T(8,128)S(1)}, f32[2,1,96,4096]{2,3,0,1:T(8,128)S(1)}) fusion(f32[2,96,128,32]{1,3,2,0:T(8,128)} %copy.339, f32[2]{0:T(128)S(1)} %multiply_add_fusion.2, f32[2,96,128,32]{1,3,2,0:T(8,128)} %copy.335, pred[96,4096]{0,1:T(8,128)(4,1)S(1)} %copy-done.15), kind=kLoop, calls=%fused_computation.18 | loop fusion | flops 14155776 | bytes 12976136 | tf_op jit(solution)/shard_map/jit(_where)/select_n | solution.py:180
  371.9 8.3 %copy.340 = f32[2,2,96,4096]{3,2,1,0:T(8,128)} copy(f32[2,2,96,4096]{2,3,0,1:T(8,128)} %pad_maximum_fusion) | data formatting | bytes 12582912 | tf_op jit(solution)/shard_map/stack | solution.py:182
  (124 shorter events, 125.9 us)
Async XLA Ops:
  4.8 4.8 %copy-start.16 = (s32[2,2]{1,0:T(2,128)S(1)}, s32[2,2]{1,0:T(2,128)}, u32[]{:S(2)}) copy-start(s32[2,2]{1,0:T(2,128)} %param.6) | copy-start | bytes 52
  4.8 54.4 %all-to-all-start = ((f32[2,8,64,1024]{3,2,0,1:T(8,128)}), f32[2,8,64,1024]{3,2,0,1:T(8,128)}, u32[]{:S(2)}, u32[]{:S(2)}) async-start(f32[2,8,64,1024]{3,2,0,1:T(8,128)} %copy.285), calls=%async_computation | async-start | bytes 8388608 | tf_op jit(solution)/shard_map/all_to_all | solution.py:106
  10.4 18.6 %copy-start.17 = (s32[128]{0:T(128)S(1)}, s32[128]{0:T(128)}, u32[]{:S(2)}) copy-start(s32[128]{0:T(128)} %param.7) | copy-start | bytes 1540
  64.4 8.6 %copy-start.4 = (f32[2,64,64,128]{3,2,1,0:T(8,128)}, f32[2,64,64,128]{3,2,1,0:T(8,128)S(1)}, u32[]{:S(2)}) copy-start(f32[2,64,64,128]{3,2,1,0:T(8,128)S(1)} %fusion.25) | copy-start | bytes 12582916
  66.5 6.5 %copy-start.6 = (f32[2,64,64,128]{3,2,1,0:T(8,128)}, f32[2,64,64,128]{3,2,1,0:T(8,128)S(1)}, u32[]{:S(2)}) copy-start(f32[2,64,64,128]{3,2,1,0:T(8,128)S(1)} %fusion.28) | copy-start | bytes 12582916
  66.5 6.5 %copy-start.10 = (f32[2,32,64,128]{3,1,2,0:T(8,128)S(1)}, f32[2,32,64,128]{3,1,2,0:T(8,128)}, u32[]{:S(2)}) copy-start(f32[2,32,64,128]{3,1,2,0:T(8,128)} %get-tuple-element.19) | copy-start | bytes 6291460
  85.8 29.5 %all-to-all-start.1 = ((f32[128,1,2048]{2,1,0:T(1,128)}), f32[128,1,2048]{2,1,0:T(1,128)S(1)}, u32[]{:S(2)}, u32[]{:S(2)}) async-start(f32[128,1,2048]{2,1,0:T(1,128)} %reshape.414), calls=%async_computation.1 | async-start | bytes 2097152 | tf_op jit(solution)/shard_map/all_to_all | solution.py:121
  95.4 9.3 %copy-start.5 = (f32[2,64,64,128]{3,2,1,0:T(8,128)S(1)}, f32[2,64,64,128]{3,2,1,0:T(8,128)}, u32[]{:S(2)}) copy-start(f32[2,64,64,128]{3,2,1,0:T(8,128)} %copy-done.4) | copy-start | bytes 12582916
  115.3 10.6 %copy-start.14 = (f32[128,1,2048]{2,1,0:T(1,128)}, f32[128,1,2048]{2,1,0:T(1,128)S(1)}, u32[]{:S(2)}) copy-start(f32[128,1,2048]{2,1,0:T(1,128)S(1)} %all-to-all-done.1) | copy-start | bytes 3145732
  115.3 29.0 %all-to-all-start.2 = ((f32[128,1,2048]{2,1,0:T(1,128)}), f32[128,1,2048]{2,1,0:T(1,128)}, u32[]{:S(2)}, u32[]{:S(2)}) async-start(f32[128,1,2048]{2,1,0:T(1,128)} %reshape.416), calls=%async_computation.2 | async-start | bytes 2097152 | tf_op jit(solution)/shard_map/all_to_all | solution.py:122
  153.4 2.7 copy-start.7
  166.8 7.9 %copy-start.9 = (f32[2,32,64,128]{3,1,2,0:T(8,128)S(1)}, f32[2,32,64,128]{3,1,2,0:T(8,128)}, u32[]{:S(2)}) copy-start(f32[2,32,64,128]{3,1,2,0:T(8,128)} %get-tuple-element.24) | copy-start | bytes 6291460
  177.7 1.8 copy-start.8
  179.5 1.8 copy-start.12
  184.2 2.2 copy-start.2
  189.8 3.8 %copy-start = (f32[2,128,32,128]{3,1,2,0:T(8,128)S(1)}, f32[2,128,32,128]{3,1,2,0:T(8,128)}, u32[]{:S(2)}) copy-start(f32[2,128,32,128]{3,1,2,0:T(8,128)} %get-tuple-element.29) | copy-start | bytes 12582916
  219.8 5.6 %copy-start.13 = (f32[384,2,16,32]{0,3,2,1:T(8,128)S(1)}, f32[384,2,16,32]{0,3,2,1:T(8,128)}, u32[]{:S(2)}) copy-start(f32[384,2,16,32]{0,3,2,1:T(8,128)} %copy.328) | copy-start | bytes 4718596
  239.2 35.0 %all-to-all-start.3 = ((f32[128,2,16,96]{3,2,1,0:T(8,128)}), f32[128,2,16,96]{3,2,1,0:T(8,128)S(1)}, u32[]{:S(2)}, u32[]{:S(2)}) async-start(f32[128,2,16,96]{3,2,1,0:T(8,128)} %copy.322), calls=%async_computation.3 | async-start | bytes 4194304 | tf_op jit(solution)/shard_map/all_to_all | solution.py:157
  274.2 35.7 %all-to-all-start.4 = ((f32[128,2,16,96]{3,2,1,0:T(8,128)}), f32[128,2,16,96]{3,2,1,0:T(8,128)}, u32[]{:S(2)}, u32[]{:S(2)}) async-start(f32[128,2,16,96]{3,2,1,0:T(8,128)} %copy.330), calls=%async_computation.4 | async-start | bytes 4194304 | tf_op jit(solution)/shard_map/all_to_all | solution.py:158
  315.5 3.6 copy-start.3
  319.1 5.4 %copy-start.1 = (f32[2,128,32,128]{3,1,2,0:T(8,128)S(1)}, f32[2,128,32,128]{3,1,2,0:T(8,128)}, u32[]{:S(2)}) copy-start(f32[2,128,32,128]{3,1,2,0:T(8,128)} %get-tuple-element.29) | copy-start | bytes 12582916
  324.6 5.4 %copy-start.11 = (f32[2,96,128,32]{2,3,1,0:T(8,128)S(1)}, f32[2,96,128,32]{2,3,1,0:T(8,128)}, u32[]{:S(2)}) copy-start(f32[2,96,128,32]{2,3,1,0:T(8,128)} %fusion.108) | copy-start | bytes 9437188
  345.6 15.4 %all-to-all-start.5 = ((f32[128,1,2]{2,1,0:T(1,128)}), f32[128,1,2]{2,1,0:T(1,128)S(1)}, u32[]{:S(2)}, u32[]{:S(2)}) async-start(f32[128,1,2]{2,1,0:T(1,128)} %broadcast_in_dim.49), calls=%async_computation.5 | async-start | bytes 131072 | tf_op jit(solution)/shard_map/all_to_all | solution.py:170
  355.8 5.3 %copy-start.15 = (pred[96,4096]{0,1:T(8,128)(4,1)S(1)}, pred[96,4096]{0,1:T(8,128)(4,1)}, u32[]{:S(2)}) copy-start(pred[96,4096]{0,1:T(8,128)(4,1)} %fusion.32) | copy-start | bytes 1179652

commit v8 on v7

--- a/solution.py
+++ b/solution.py
@@ -131,9 +131,6 @@
     mid_imag = contract(step, inner_sin, recv_real) + contract(step, inner_cos, recv_imag)
     mid_shape = (holo_count, share, inner_cos.shape[1], radix)
     side_real, side_imag = finish(mid_real.reshape(mid_shape), mid_imag.reshape(mid_shape), table_u)
-    lift_real, lift_imag = transform(
-        side_real.reshape(holo_count, share, S), side_imag.reshape(holo_count, share, S), table_p
-    )
     strips = strip_owner.shape[0]
     strip_rows = P_SIZE // strips
     slot_rows = MOST * strip_rows
@@ -147,23 +144,33 @@
     source = jnp.sum(jnp.where(match, strip_ids[None, :], 0), axis=1)
     filled = jnp.any(match, axis=1).astype(jnp.float32)
 
+    inner_cos, inner_sin, outer_cos, outer_sin = table_p
+    side_shape = (holo_count, share, S // radix, radix)
+    side_real = side_real.reshape(side_shape)
+    side_imag = side_imag.reshape(side_shape)
+    step = "kpa,krab->krpb"
+    mid_real = contract(step, inner_cos, side_real) - contract(step, inner_sin, side_imag)
+    mid_imag = contract(step, inner_sin, side_real) + contract(step, inner_cos, side_imag)
+    form = "kqpb,krpb->qpkr"
+    lift_real = contract(form, outer_cos, mid_real) - contract(form, outer_sin, mid_imag)
+    lift_imag = contract(form, outer_cos, mid_imag) + contract(form, outer_sin, mid_real)
+
     def pack(part):
-        grouped = part.reshape(holo_count, share, strips, strip_rows)
-        picked = jnp.take(grouped, source, axis=2) * filled[None, None, :, None]
-        return jnp.transpose(picked.reshape(holo_count, share, strips, slot_rows), (2, 0, 1, 3))
-
-    send_real = pack(lift_real)
-    send_imag = pack(lift_imag)
-    piece_real = lax.all_to_all(send_real, ("row", "col"), split_axis=0, concat_axis=2, tiled=True)
-    piece_imag = lax.all_to_all(send_imag, ("row", "col"), split_axis=0, concat_axis=2, tiled=True)
-    single, lead, width, count = piece_real.shape
-    rows_real = jnp.swapaxes(piece_real.reshape(lead, width, count), 1, 2)
-    rows_imag = jnp.swapaxes(piece_imag.reshape(lead, width, count), 1, 2)
-    out_real, out_imag = transform(rows_real, rows_imag, table_p)
-    field_real = out_real.reshape(single, lead, count, P_SIZE)
-    field_imag = out_imag.reshape(single, lead, count, P_SIZE)
-    field_real = field_real.reshape(holo_count, slot_rows, P_SIZE)
-    field_imag = field_imag.reshape(holo_count, slot_rows, P_SIZE)
+        grouped = part.reshape(strips, strip_rows, holo_count, share)
+        picked = jnp.take(grouped, source, axis=0) * filled[:, None, None, None]
+        return picked.reshape(devices, MOST, strip_rows, holo_count, share)
+
+    piece_real = lax.all_to_all(pack(lift_real), ("row", "col"), 0, 0, tiled=True)
+    piece_imag = lax.all_to_all(pack(lift_imag), ("row", "col"), 0, 0, tiled=True)
+    pair = radix // share
+    recv_shape = (devices // pair, pair, MOST, strip_rows, holo_count, share)
+    recv_real = piece_real.reshape(recv_shape)
+    recv_imag = piece_imag.reshape(recv_shape)
+    step = "kpa,aoltks->kltpos"
+    mid_real = contract(step, inner_cos, recv_real) - contract(step, inner_sin, recv_imag)
+    mid_imag = contract(step, inner_sin, recv_real) + contract(step, inner_cos, recv_imag)
+    mid_shape = (holo_count, slot_rows, inner_cos.shape[1], radix)
+    field_real, field_imag = finish(mid_real.reshape(mid_shape), mid_imag.reshape(mid_shape), table_p)
     magnitude = jnp.sqrt(field_real * field_real + field_imag * field_imag)
     local_peak = jnp.max(magnitude, axis=(1, 2))
     every = jnp.broadcast_to(local_peak[None, :], (devices, holo_count))

time: 385 us -> 506 us (1.31)
  matrix products: 101 us -> 165 us
  local copies, waits for them, and re-layouts: 119 us -> 170 us
  waiting for transfers between devices: 64.4 us -> 47.6 us
  other arithmetic: 55.2 us -> 71.5 us
    dot_general x30, matrix products: 101 us -> 165 us  [contract(): jnp.einsum(form, left, right, precision=lax.Precision.HIGH, preferred_ele...]
    unnamed x41 -> x45, local copies, waits for them, and re-layouts: 12.6 us -> 33.5 us
    add x0 -> x1, local copies, waits for them, and re-layouts: none -> 20.3 us  [body(): contract(step, inner_sin, recv_real) + contract(step, inner_cos, recv_imag)]
    sub x0 -> x1, local copies, waits for them, and re-layouts: none -> 19.9 us  [body(): contract(step, inner_cos, recv_real) - contract(step, inner_sin, recv_imag)]
    reshape x2 -> x3, local copies, waits for them, and re-layouts: 4.93 us -> 22.8 us  [body(): mid_real.reshape(mid_shape)]
    all_to_all x2, waiting for transfers between devices: 35.6 us -> 18.5 us  [the longest x1 18.4 us: body(): lax.all_to_all(pack(lift_imag), ('row', 'col'), 0, 0, tiled=True)]
    reshape x2 -> x3, local copies, waits for them, and re-layouts: 7.88 us -> 23.4 us  [body(): mid_imag.reshape(mid_shape)]
    reshape x4 -> x0, local copies, waits for them, and re-layouts: 13.8 us -> none  [the longest x2 9.36 us: pack(): picked.reshape(holo_count, share, strips, slot_rows)]
  transfers between devices with their start and end apart: 6 -> 6, of which waited for: 4 -> 3; matrix products, arithmetic and copies ran while one was open for 25% -> 23% of each run, Pallas kernels for 0% -> 0%
where the time goes in v8:
time: 506 us; the launch traced here: 499 us
  local copies, waits for them, and re-layouts  170 us (34%)
  matrix products  165 us (33%)
  other arithmetic  71.5 us (14%)
  waiting for transfers between devices  47.6 us (9%)
  starting transfers between devices  44.1 us (9%)
    dot_general x30, matrix products, contract(): jnp.einsum(form, left, right, precision=lax.Precision.HIGH, preferred_ele...  165 us
    unnamed x45, local copies, waits for them, and re-layouts  33.5 us
    sin x2, other arithmetic, make_tables(): jnp.sin(outer_angle).reshape(shape_four)  29.6 us
    reshape x3, local copies, waits for them, and re-layouts, body(): mid_imag.reshape(mid_shape)  23.4 us
    reshape x3, local copies, waits for them, and re-layouts, body(): mid_real.reshape(mid_shape)  22.8 us
    add x1, local copies, waits for them, and re-layouts, body(): contract(step, inner_sin, recv_real) + contract(step, inner_cos, recv_imag)  20.3 us
    sub x1, local copies, waits for them, and re-layouts, body(): contract(step, inner_cos, recv_real) - contract(step, inner_sin, recv_imag)  19.9 us
    all_to_all x1, waiting for transfers between devices, body(): lax.all_to_all(blocks, 'col', split_axis=1, concat_axis=1, tiled=True)  18.9 us
  transfers between devices with their start and end apart: 6, of which 3 were waited for; matrix products, arithmetic and copies ran while one was open for 23% of the time, Pallas kernels for 0%

profile of v8, /device:TPU:0, one launch (start us, length us, event | category | flops | bytes accessed | tf_op | source)
XLA Modules:
  0.0 499.1 jit_solution(17851327602457560940)
XLA Ops:
  10.3 18.6 %fusion.84 = (f32[2,32,64,128]{3,1,2,0:T(8,128)}, f32[2,32,64,128]{3,1,2,0:T(8,128)}, f32[2,32,64,128]{3,1,2,0:T(8,128)}, f32[2,32,64,128]{3,1,2,0:T(8,128)S(1)}) fusion(s32[128]{0:T(128)S(1)} %and_select_fusion.3, s32[2,32,64]{1,2,0:T(8,128)S(1)} %get-tuple-element.38, s32[2,32,64]{1,2,0:T(8,128)S(1)} %get-tuple-element.39), kind=kLoop, calls=%fused_computation.105 | loop fusion | flops 14680064 | bytes 8421888 | tf_op jit(solution)/shard_map/sin | solution.py:42
  29.2 11.0 %fusion.51 = (f32[2,128,32,128]{3,1,2,0:T(8,128)}, f32[2,128,32,128]{3,1,2,0:T(8,128)}) fusion(s32[128]{0:T(128)S(1)} %and_select_fusion, s32[128,32]{0,1:T(8,128)S(1)} %multiply_add_fusion.1), kind=kLoop, calls=%fused_computation.80 | loop fusion | flops 14680064 | bytes 8405504 | tf_op jit(solution)/shard_map/sin | solution.py:42
  40.2 18.9 %all-to-all-done = f32[2,8,64,1024]{3,2,0,1:T(8,128)} async-done(((f32[2,8,64,1024]{3,2,0,1:T(8,128)}), f32[2,8,64,1024]{3,2,0,1:T(8,128)}, u32[]{:S(2)}, u32[]{:S(2)}) %all-to-all-start) | async-done | bytes 4194336 | tf_op jit(solution)/shard_map/all_to_all | solution.py:106
  66.5 6.4 %fusion.31 = f32[64,2,64,32]{2,3,1,0:T(8,128)S(1)} fusion(f32[2,64,64,128]{3,2,1,0:T(8,128)S(1)} %fusion.40, f32[2,32,64,128]{3,1,2,0:T(8,128)S(1)} %get-tuple-element.21), kind=kOutput, calls=%fused_computation.48 | convolution fusion | flops 201326592 | bytes 7340032 | tf_op jit(solution)/shard_map/kqpb,krpb->qpkr/dot_general | solution.py:22
  73.0 6.9 %subtract_bitcast_fusion.3 = f32[32,64,2,64]{3,0,2,1:T(8,128)S(1)} fusion(f32[64,2,64,32]{2,3,1,0:T(8,128)S(1)} %fusion.31, f32[2,32,64,128]{3,1,2,0:T(8,128)S(1)} %copy-done.12, f32[2,64,64,128]{3,2,1,0:T(8,128)S(1)} %fusion.37), kind=kOutput, calls=%fused_computation.85 | convolution fusion | flops 201588736 | bytes 8388608 | tf_op jit(solution)/shard_map/kqpb,krpb->qpkr/dot_general | solution.py:22
  86.2 9.5 %all-to-all-start.1 = ((f32[128,1,2048]{2,1,0:T(1,128)}), f32[128,1,2048]{2,1,0:T(1,128)S(1)}, u32[]{:S(2)}, u32[]{:S(2)}) async-start(f32[128,1,2048]{2,1,0:T(1,128)} %reshape.422), calls=%async_computation.1 | async-start | bytes 2097152 | tf_op jit(solution)/shard_map/all_to_all | solution.py:121
  95.8 9.3 %fusion.29 = f32[64,2,64,32]{2,3,1,0:T(8,128)S(1)} fusion(f32[2,64,64,128]{3,2,1,0:T(8,128)} %copy-done.8, f32[2,32,64,128]{3,1,2,0:T(8,128)} %get-tuple-element.19), kind=kOutput, calls=%fused_computation.46 | convolution fusion | flops 201326592 | bytes 7340032 | tf_op jit(solution)/shard_map/kqpb,krpb->qpkr/dot_general | solution.py:22
  105.0 6.4 %add_bitcast_fusion.3 = f32[32,64,2,64]{3,0,2,1:T(8,128)S(1)} fusion(f32[64,2,64,32]{2,3,1,0:T(8,128)S(1)} %fusion.29, f32[2,32,64,128]{3,1,2,0:T(8,128)S(1)} %get-tuple-element.21, f32[2,64,64,128]{3,2,1,0:T(8,128)S(1)} %copy-done.7), kind=kOutput, calls=%fused_computation.84 | convolution fusion | flops 201588736 | bytes 8388608 | tf_op jit(solution)/shard_map/kqpb,krpb->qpkr/dot_general | solution.py:22
  115.2 10.7 %all-to-all-start.2 = ((f32[128,1,2048]{2,1,0:T(1,128)}), f32[128,1,2048]{2,1,0:T(1,128)}, u32[]{:S(2)}, u32[]{:S(2)}) async-start(f32[128,1,2048]{2,1,0:T(1,128)} %reshape.424), calls=%async_computation.2 | async-start | bytes 2097152 | tf_op jit(solution)/shard_map/all_to_all | solution.py:122
  134.4 10.3 %all-to-all-done.2 = f32[128,1,2048]{2,1,0:T(1,128)} async-done(((f32[128,1,2048]{2,1,0:T(1,128)}), f32[128,1,2048]{2,1,0:T(1,128)}, u32[]{:S(2)}, u32[]{:S(2)}) %all-to-all-start.2) | async-done | bytes 1048608 | tf_op jit(solution)/shard_map/all_to_all | solution.py:122
  209.3 6.3 %fusion.81 = f32[128,32,2,16]{0,3,2,1:T(8,128)} fusion(f32[32,2,16,128]{3,2,1,0:T(8,128)S(1)} %fusion.23, f32[2,128,32,128]{3,1,2,0:T(8,128)} %get-tuple-element.28, f32[2,16,32,128]{3,2,1,0:T(8,128)S(1)} %fusion.77), kind=kOutput, calls=%fused_computation.104 | convolution fusion | flops 100794368 | bytes 5767168 | tf_op jit(solution)/shard_map/kqpb,krpb->qpkr/dot_general | solution.py:22
  223.4 5.3 %gather_fusion = f32[384,32,2,16]{1,3,2,0:T(8,128)} fusion(f32[128,32,2,16]{1,3,2,0:T(8,128)} %copy.277, s32[1024]{0:T(1024)S(1)} %pad_clamp_fusion), kind=kCustom, calls=%fused_computation.clone | custom fusion | bytes 3147264 | tf_op jit(solution)/shard_map/jit(_take)/gather | solution.py:160
  228.6 8.6 %select_multiply_fusion.1 = (f32[384,32,2,16]{1,3,2,0:T(8,128)}, f32[384,32,2,16]{1,3,2,0:T(8,128)}) fusion(f32[384,32,2,16]{1,3,2,0:T(8,128)} %gather_fusion, f32[384]{0:T(512)S(1)} %convert_element_type.45, pred[384]{0:T(512)(128)(4,1)S(1)} %compare_and_fusion, f32[384,32,2,16]{1,3,2,0:T(8,128)} %gather_fusion.1), kind=kLoop, calls=%fused_computation.9 | loop fusion | flops 1572864 | bytes 6293376 | tf_op jit(solution)/shard_map/mul | solution.py:160
  237.2 6.0 %reshape.426 = f32[128,1,3072]{2,1,0:T(1,128)} reshape(f32[128,3,2,16,32]{4,3,2,1,0:T(8,128)} %bitcast.189) | data formatting | bytes 3145728
  248.1 6.0 %reshape.428 = f32[128,1,3072]{2,1,0:T(1,128)} reshape(f32[128,3,2,16,32]{4,3,2,1,0:T(8,128)} %bitcast.188) | data formatting | bytes 3145728
  254.2 18.4 %all-to-all-done.4 = f32[128,1,3072]{2,1,0:T(1,128)S(1)} async-done(((f32[128,1,3072]{2,1,0:T(1,128)}), f32[128,1,3072]{2,1,0:T(1,128)S(1)}, u32[]{:S(2)}, u32[]{:S(2)}) %all-to-all-start.4) | async-done | bytes 1572896 | tf_op jit(solution)/shard_map/all_to_all | solution.py:164
  277.3 5.9 %reduce.8 = f32[128,3072]{1,0:T(8,128)} reduce(f32[128,1,3072]{2,1,0:T(1,128)S(1)} %all-to-all-done.4, f32[]{:T(128)} %broadcast.527), dimensions={1}, to_apply=%all_to_all.23.reduce_sub_computation | reduce | bytes 3145732 | tf_op jit(solution)/shard_map/all_to_all | solution.py:164
  288.3 16.1 %fusion = f32[2,8,3,32,16,32]{5,3,4,2,1,0:T(8,128)} fusion(f32[16,8,3,32,2,16]{3,5,4,2,1,0:T(8,128)} %bitcast.182, f32[2,32,16]{1,2,0:T(8,128)S(1)} %get-tuple-element.26), kind=kOutput, calls=%fused_computation.12 | convolution fusion | flops 75497472 | bytes 4722688 | tf_op jit(solution)/shard_map/kpa,aoltks->kltpos/dot_general | solution.py:22
  304.4 13.4 %fusion.2 = f32[2,8,3,32,16,32]{5,3,4,2,1,0:T(8,128)} fusion(f32[16,8,3,32,2,16]{3,5,4,2,1,0:T(8,128)S(1)} %bitcast.183, f32[2,32,16]{1,2,0:T(8,128)S(1)} %get-tuple-element.27), kind=kOutput, calls=%fused_computation.14 | convolution fusion | flops 75497472 | bytes 4722688 | tf_op jit(solution)/shard_map/kpa,aoltks->kltpos/dot_general | solution.py:22
  325.9 17.1 %add_bitcast_fusion = f32[2,3,32,32,8,16]{3,2,5,1,4,0:T(8,128)} fusion(f32[2,8,3,32,16,32]{5,3,4,2,1,0:T(8,128)} %fusion, f32[16,8,3,32,2,16]{3,5,4,2,1,0:T(8,128)} %bitcast.184, f32[2,32,16]{1,2,0:T(8,128)S(1)} %get-tuple-element.27), kind=kOutput, calls=%fused_computation.2 | convolution fusion | flops 76283904 | bytes 7868416 | tf_op jit(solution)/shard_map/kpa,aoltks->kltpos/dot_general | solution.py:22
  343.0 20.3 %copy.289 = f32[2,3,32,32,8,16]{2,1,5,4,3,0:T(4,128)} copy(f32[2,3,32,32,8,16]{3,2,5,1,4,0:T(8,128)} %add_bitcast_fusion) | data formatting | bytes 6291456 | tf_op jit(solution)/shard_map/add | solution.py:171
  363.3 16.6 %reshape.380 = f32[2,96,32,128]{1,3,2,0:T(8,128)} reshape(f32[2,3,32,32,8,16]{2,1,5,4,3,0:T(4,128)} %copy.289) | data formatting | bytes 6291456 | tf_op jit(solution)/shard_map/reshape | solution.py:173
  379.8 8.5 %fusion.145 = f32[2,32,96,128]{3,2,1,0:T(8,128)} fusion(f32[2,96,32,128]{1,3,2,0:T(8,128)} %reshape.380, f32[2,128,32,128]{3,1,2,0:T(8,128)} %get-tuple-element.28), kind=kOutput, calls=%fused_computation.230 | convolution fusion | flops 603979776 | bytes 10485760 | tf_op jit(solution)/shard_map/kqpb,krpb->krqp/dot_general | solution.py:22
  388.4 17.1 %subtract_bitcast_fusion = f32[2,3,32,32,8,16]{3,2,5,1,4,0:T(8,128)} fusion(f32[2,8,3,32,16,32]{5,3,4,2,1,0:T(8,128)} %fusion.2, f32[16,8,3,32,2,16]{3,5,4,2,1,0:T(8,128)} %bitcast.185, f32[2,32,16]{1,2,0:T(8,128)S(1)} %get-tuple-element.26), kind=kOutput, calls=%fused_computation.3 | convolution fusion | flops 76283904 | bytes 7868416 | tf_op jit(solution)/shard_map/kpa,aoltks->kltpos/dot_general | solution.py:22
  405.4 19.9 %copy.285 = f32[2,3,32,32,8,16]{2,1,5,4,3,0:T(4,128)} copy(f32[2,3,32,32,8,16]{3,2,5,1,4,0:T(8,128)} %subtract_bitcast_fusion) | data formatting | bytes 6291456 | tf_op jit(solution)/shard_map/sub | solution.py:170
  425.3 16.7 %reshape.379 = f32[2,96,32,128]{1,3,2,0:T(8,128)} reshape(f32[2,3,32,32,8,16]{2,1,5,4,3,0:T(4,128)} %copy.285) | data formatting | bytes 6291456 | tf_op jit(solution)/shard_map/reshape | solution.py:173
  442.1 7.2 %fusion.144 = f32[2,32,96,128]{3,2,1,0:T(8,128)S(1)} fusion(f32[2,96,32,128]{1,3,2,0:T(8,128)} %reshape.379, f32[2,128,32,128]{3,1,2,0:T(8,128)} %get-tuple-element.28), kind=kOutput, calls=%fused_computation.229 | convolution fusion | flops 603979776 | bytes 10485760 | tf_op jit(solution)/shard_map/kqpb,krpb->krqp/dot_general | solution.py:22
  452.8 5.7 %sqrt_reduce_fusion = (f32[2]{0:T(128)S(1)}, f32[2,96,128,32]{2,1,3,0:T(8,128)}) fusion(f32[2,96,128,32]{2,1,3,0:T(8,128)S(1)} %subtract_bitcast_fusion.1, f32[2,32,96,128]{3,2,1,0:T(8,128)S(1)} %copy-done.13, f32[2,96,32,128]{1,3,2,0:T(8,128)S(1)} %copy-done.5, f32[2,128,32,128]{3,1,2,0:T(8,128)S(1)} %copy-done.2), kind=kOutput, calls=%fused_computation.60 | convolution fusion | flops 607911936 | bytes 16777224 | tf_op jit(solution)/shard_map/kqpb,krpb->krqp/dot_general | solution.py:22
  459.1 10.0 %all-to-all-start.5 = ((f32[128,1,2]{2,1,0:T(1,128)}), f32[128,1,2]{2,1,0:T(1,128)S(1)}, u32[]{:S(2)}, u32[]{:S(2)}) async-start(f32[128,1,2]{2,1,0:T(1,128)} %broadcast_in_dim.49), calls=%async_computation.5 | async-start | bytes 131072 | tf_op jit(solution)/shard_map/all_to_all | solution.py:177
  474.5 5.1 %copy.295 = f32[2,96,128,32]{1,3,2,0:T(8,128)} copy(f32[2,96,128,32]{2,1,3,0:T(8,128)} %get-tuple-element.57) | data formatting | bytes 6291456 | tf_op jit(solution)/shard_map/add | solution.py:67
  479.8 7.0 %add_select_fusion.1 = (f32[2,1,96,4096]{2,3,0,1:T(8,128)S(1)}, f32[2,1,96,4096]{2,3,0,1:T(8,128)S(1)}) fusion(f32[2,96,128,32]{1,3,2,0:T(8,128)} %copy.295, f32[2]{0:T(128)S(1)} %multiply_add_fusion.2, f32[2,96,128,32]{1,3,2,0:T(8,128)} %copy.291, pred[96,4096]{0,1:T(8,128)(4,1)S(1)} %copy-done.15), kind=kLoop, calls=%fused_computation.30 | loop fusion | flops 14155776 | bytes 12976136 | tf_op jit(solution)/shard_map/jit(_where)/select_n | solution.py:187
  490.6 8.3 %copy.296 = f32[2,2,96,4096]{3,2,1,0:T(8,128)} copy(f32[2,2,96,4096]{2,3,0,1:T(8,128)} %pad_maximum_fusion) | data formatting | bytes 12582912 | tf_op jit(solution)/shard_map/stack | solution.py:189
  (122 shorter events, 144.8 us)
Async XLA Ops:
  4.8 4.7 copy-start.16
  4.8 54.3 %all-to-all-start = ((f32[2,8,64,1024]{3,2,0,1:T(8,128)}), f32[2,8,64,1024]{3,2,0,1:T(8,128)}, u32[]{:S(2)}, u32[]{:S(2)}) async-start(f32[2,8,64,1024]{3,2,0,1:T(8,128)} %copy.241), calls=%async_computation | async-start | bytes 8388608 | tf_op jit(solution)/shard_map/all_to_all | solution.py:106
  64.4 2.1 copy-start.8
  66.5 6.5 %copy-start.6 = (f32[2,64,64,128]{3,2,1,0:T(8,128)}, f32[2,64,64,128]{3,2,1,0:T(8,128)S(1)}, u32[]{:S(2)}) copy-start(f32[2,64,64,128]{3,2,1,0:T(8,128)S(1)} %fusion.37) | copy-start | bytes 12582916
  66.5 6.5 %copy-start.12 = (f32[2,32,64,128]{3,1,2,0:T(8,128)S(1)}, f32[2,32,64,128]{3,1,2,0:T(8,128)}, u32[]{:S(2)}) copy-start(f32[2,32,64,128]{3,1,2,0:T(8,128)} %get-tuple-element.19) | copy-start | bytes 6291460
  86.2 29.1 %all-to-all-start.1 = ((f32[128,1,2048]{2,1,0:T(1,128)}), f32[128,1,2048]{2,1,0:T(1,128)S(1)}, u32[]{:S(2)}, u32[]{:S(2)}) async-start(f32[128,1,2048]{2,1,0:T(1,128)} %reshape.422), calls=%async_computation.1 | async-start | bytes 2097152 | tf_op jit(solution)/shard_map/all_to_all | solution.py:121
  95.7 9.3 %copy-start.7 = (f32[2,64,64,128]{3,2,1,0:T(8,128)S(1)}, f32[2,64,64,128]{3,2,1,0:T(8,128)}, u32[]{:S(2)}) copy-start(f32[2,64,64,128]{3,2,1,0:T(8,128)} %copy-done.6) | copy-start | bytes 12582916
  112.7 13.3 %copy-start.17 = (s32[128]{0:T(128)S(1)}, s32[128]{0:T(128)}, u32[]{:S(2)}) copy-start(s32[128]{0:T(128)} %param.7) | copy-start | bytes 1540
  115.2 11.3 %copy-start.14 = (f32[128,1,2048]{2,1,0:T(1,128)}, f32[128,1,2048]{2,1,0:T(1,128)S(1)}, u32[]{:S(2)}) copy-start(f32[128,1,2048]{2,1,0:T(1,128)S(1)} %all-to-all-done.1) | copy-start | bytes 3145732
  115.2 29.4 %all-to-all-start.2 = ((f32[128,1,2048]{2,1,0:T(1,128)}), f32[128,1,2048]{2,1,0:T(1,128)}, u32[]{:S(2)}, u32[]{:S(2)}) async-start(f32[128,1,2048]{2,1,0:T(1,128)} %reshape.424), calls=%async_computation.2 | async-start | bytes 2097152 | tf_op jit(solution)/shard_map/all_to_all | solution.py:122
  153.5 2.7 copy-start.9
  177.7 3.8 copy-start.11
  177.7 6.6 %copy-start.10 = (f32[2,32,64,128]{3,1,2,0:T(8,128)S(1)}, f32[2,32,64,128]{3,1,2,0:T(8,128)}, u32[]{:S(2)}) copy-start(f32[2,32,64,128]{3,1,2,0:T(8,128)} %get-tuple-element.25) | copy-start | bytes 6291460
  192.6 2.2 copy-start.1
  194.8 7.3 %copy-start.3 = (f32[2,128,32,128]{3,1,2,0:T(8,128)S(1)}, f32[2,128,32,128]{3,1,2,0:T(8,128)}, u32[]{:S(2)}) copy-start(f32[2,128,32,128]{3,1,2,0:T(8,128)} %get-tuple-element.28) | copy-start | bytes 12582916
  243.2 29.4 %all-to-all-start.4 = ((f32[128,1,3072]{2,1,0:T(1,128)}), f32[128,1,3072]{2,1,0:T(1,128)S(1)}, u32[]{:S(2)}, u32[]{:S(2)}) async-start(f32[128,1,3072]{2,1,0:T(1,128)} %reshape.426), calls=%async_computation.4 | async-start | bytes 3145728 | tf_op jit(solution)/shard_map/all_to_all | solution.py:164
  272.6 45.2 %all-to-all-start.3 = ((f32[128,1,3072]{2,1,0:T(1,128)}), f32[128,1,3072]{2,1,0:T(1,128)S(1)}, u32[]{:S(2)}, u32[]{:S(2)}) async-start(f32[128,1,3072]{2,1,0:T(1,128)} %reshape.428), calls=%async_computation.3 | async-start | bytes 3145728 | tf_op jit(solution)/shard_map/all_to_all | solution.py:163
  288.3 16.1 %copy-start = (f32[128,3,2,16,32]{4,3,2,1,0:T(8,128)S(1)}, f32[128,3,2,16,32]{4,3,2,1,0:T(8,128)}, u32[]{:S(2)}) copy-start(f32[128,3,2,16,32]{4,3,2,1,0:T(8,128)} %reshape.427) | copy-start | bytes 4718596
  442.0 7.2 %copy-start.2 = (f32[2,128,32,128]{3,1,2,0:T(8,128)S(1)}, f32[2,128,32,128]{3,1,2,0:T(8,128)}, u32[]{:S(2)}) copy-start(f32[2,128,32,128]{3,1,2,0:T(8,128)} %get-tuple-element.29) | copy-start | bytes 12582916
  442.0 7.2 %copy-start.4 = (f32[2,96,32,128]{1,3,2,0:T(8,128)S(1)}, f32[2,96,32,128]{1,3,2,0:T(8,128)}, u32[]{:S(2)}) copy-start(f32[2,96,32,128]{1,3,2,0:T(8,128)} %reshape.380) | copy-start | bytes 9437188
  449.2 3.5 copy-start.5
  449.2 3.5 copy-start.13
  459.1 20.5 %all-to-all-start.5 = ((f32[128,1,2]{2,1,0:T(1,128)}), f32[128,1,2]{2,1,0:T(1,128)S(1)}, u32[]{:S(2)}, u32[]{:S(2)}) async-start(f32[128,1,2]{2,1,0:T(1,128)} %broadcast_in_dim.49), calls=%async_computation.5 | async-start | bytes 131072 | tf_op jit(solution)/shard_map/all_to_all | solution.py:177
  474.5 5.3 %copy-start.15 = (pred[96,4096]{0,1:T(8,128)(4,1)S(1)}, pred[96,4096]{0,1:T(8,128)(4,1)}, u32[]{:S(2)}) copy-start(pred[96,4096]{0,1:T(8,128)(4,1)} %fusion.44) | copy-start | bytes 1179652

commit v9 on v7

--- a/solution.py
+++ b/solution.py
@@ -131,9 +131,6 @@
     mid_imag = contract(step, inner_sin, recv_real) + contract(step, inner_cos, recv_imag)
     mid_shape = (holo_count, share, inner_cos.shape[1], radix)
     side_real, side_imag = finish(mid_real.reshape(mid_shape), mid_imag.reshape(mid_shape), table_u)
-    lift_real, lift_imag = transform(
-        side_real.reshape(holo_count, share, S), side_imag.reshape(holo_count, share, S), table_p
-    )
     strips = strip_owner.shape[0]
     strip_rows = P_SIZE // strips
     slot_rows = MOST * strip_rows
@@ -147,10 +144,22 @@
     source = jnp.sum(jnp.where(match, strip_ids[None, :], 0), axis=1)
     filled = jnp.any(match, axis=1).astype(jnp.float32)
 
+    inner_cos, inner_sin, outer_cos, outer_sin = table_p
+    side_shape = (holo_count, share, S // radix, radix)
+    side_real = side_real.reshape(side_shape)
+    side_imag = side_imag.reshape(side_shape)
+    step = "kpa,krab->krpb"
+    mid_real = contract(step, inner_cos, side_real) - contract(step, inner_sin, side_imag)
+    mid_imag = contract(step, inner_sin, side_real) + contract(step, inner_cos, side_imag)
+    form = "kqpb,krpb->qkrp"
+    lift_real = contract(form, outer_cos, mid_real) - contract(form, outer_sin, mid_imag)
+    lift_imag = contract(form, outer_cos, mid_imag) + contract(form, outer_sin, mid_real)
+
     def pack(part):
-        grouped = part.reshape(holo_count, share, strips, strip_rows)
-        picked = jnp.take(grouped, source, axis=2) * filled[None, None, :, None]
-        return jnp.transpose(picked.reshape(holo_count, share, strips, slot_rows), (2, 0, 1, 3))
+        grouped = part.reshape(strips, holo_count, share, strip_rows)
+        picked = jnp.take(grouped, source, axis=0) * filled[:, None, None, None]
+        picked = picked.reshape(devices, MOST, holo_count, share, strip_rows)
+        return jnp.transpose(picked, (0, 2, 3, 1, 4)).reshape(devices, holo_count, share, slot_rows)
 
     send_real = pack(lift_real)
     send_imag = pack(lift_imag)

time: 385 us -> 391 us (1.016)
  local copies, waits for them, and re-layouts: 119 us -> 104 us
  matrix products: 101 us -> 111 us
  other arithmetic: 55.2 us -> 61.5 us
  waiting for transfers between devices: 64.4 us -> 69.7 us
    gather x4 -> x2, local copies, waits for them, and re-layouts: 21.6 us -> 9.08 us  [pack(): picked = jnp.take(grouped, source, axis=0) * filled[:, None, None, None]]
    mul x2 -> x0, local copies, waits for them, and re-layouts: 10 us -> none  [pack(): picked = jnp.take(grouped, source, axis=2) * filled[None, None, :, None]]
    dot_general x30, matrix products: 101 us -> 111 us  [contract(): jnp.einsum(form, left, right, precision=lax.Precision.HIGH, preferred_ele...]
    mul x1, other arithmetic: 2.09 us -> 8.44 us  [pack(): picked = jnp.take(grouped, source, axis=0) * filled[:, None, None, None]]
    all_to_all x1, waiting for transfers between devices: 15.8 us -> 21 us  [body(): lax.all_to_all(send_real, ('row', 'col'), split_axis=0, concat_axis=2, ti...]
    transpose x2, local copies, waits for them, and re-layouts: 6.85 us -> 11.7 us  [pack(): jnp.transpose(picked, (0, 2, 3, 1, 4))]
    reshape x2, local copies, waits for them, and re-layouts: 9.36 us -> 5.21 us  [pack(): jnp.transpose(picked, (0, 2, 3, 1, 4))]
    unnamed x41 -> x39, local copies, waits for them, and re-layouts: 12.6 us -> 12.5 us
  transfers between devices with their start and end apart: 6 -> 6, of which waited for: 4 -> 4; matrix products, arithmetic and copies ran while one was open for 25% -> 23% of each run, Pallas kernels for 0% -> 0%
where the time goes in v9:
time: 391 us; the launch traced here: 386 us
  matrix products  111 us (28%)
  local copies, waits for them, and re-layouts  104 us (27%)
  waiting for transfers between devices  69.7 us (18%)
  other arithmetic  61.5 us (16%)
  starting transfers between devices  39.9 us (10%)
    dot_general x30, matrix products, contract(): jnp.einsum(form, left, right, precision=lax.Precision.HIGH, preferred_ele...  111 us
    sin x2, other arithmetic, make_tables(): jnp.sin(outer_angle).reshape(shape_four)  29.8 us
    all_to_all x1, waiting for transfers between devices, body(): lax.all_to_all(send_real, ('row', 'col'), split_axis=0, concat_axis=2, ti...  21 us
    all_to_all x1, waiting for transfers between devices, body(): lax.all_to_all(send_imag, ('row', 'col'), split_axis=0, concat_axis=2, ti...  19.9 us
    all_to_all x1, waiting for transfers between devices, body(): lax.all_to_all(blocks, 'col', split_axis=1, concat_axis=1, tiled=True)  18.7 us
    unnamed x39, local copies, waits for them, and re-layouts  12.5 us
    transpose x2, local copies, waits for them, and re-layouts, pack(): jnp.transpose(picked, (0, 2, 3, 1, 4))  11.7 us
    all_to_all x1, starting transfers between devices, body(): lax.all_to_all(spec_imag.reshape(send_shape), ('row', 'col'), 0, 0, tiled...  10.3 us
  transfers between devices with their start and end apart: 6, of which 4 were waited for; matrix products, arithmetic and copies ran while one was open for 23% of the time, Pallas kernels for 0%

profile of v9, /device:TPU:0, one launch (start us, length us, event | category | flops | bytes accessed | tf_op | source)
XLA Modules:
  0.0 386.4 jit_solution(6961661388830647791)
XLA Ops:
  0.0 4.8 %copy.231 = f32[2,8,64,1024]{3,2,0,1:T(8,128)} copy(f32[2,8,64,1024]{3,2,1,0:T(8,128)} %bitcast.207) | data formatting | bytes 8388608 | tf_op jit(solution)/shard_map/reshape | solution.py:105
  4.8 4.7 %all-to-all-start = ((f32[2,8,64,1024]{3,2,0,1:T(8,128)}), f32[2,8,64,1024]{3,2,0,1:T(8,128)}, u32[]{:S(2)}, u32[]{:S(2)}) async-start(f32[2,8,64,1024]{3,2,0,1:T(8,128)} %copy.231), calls=%async_computation | async-start | bytes 8388608 | tf_op jit(solution)/shard_map/all_to_all | solution.py:106
  10.3 18.6 %fusion.66 = (f32[2,32,64,128]{3,1,2,0:T(8,128)}, f32[2,32,64,128]{3,1,2,0:T(8,128)}, f32[2,32,64,128]{3,1,2,0:T(8,128)}, f32[2,32,64,128]{3,1,2,0:T(8,128)S(1)}) fusion(s32[128]{0:T(128)S(1)} %and_select_fusion.3, s32[2,32,64]{1,2,0:T(8,128)S(1)} %get-tuple-element.38, s32[2,32,64]{1,2,0:T(8,128)S(1)} %get-tuple-element.39), kind=kLoop, calls=%fused_computation.97 | loop fusion | flops 14680064 | bytes 8421888 | tf_op jit(solution)/shard_map/sin | solution.py:42
  29.2 11.2 %fusion.39 = (f32[2,128,32,128]{3,1,2,0:T(8,128)}, f32[2,128,32,128]{3,1,2,0:T(8,128)}) fusion(s32[128]{0:T(128)S(1)} %and_select_fusion, s32[128,32]{0,1:T(8,128)S(1)} %multiply_add_fusion.1), kind=kLoop, calls=%fused_computation.72 | loop fusion | flops 14680064 | bytes 8405504 | tf_op jit(solution)/shard_map/sin | solution.py:42
  40.5 18.7 %all-to-all-done = f32[2,8,64,1024]{3,2,0,1:T(8,128)} async-done(((f32[2,8,64,1024]{3,2,0,1:T(8,128)}), f32[2,8,64,1024]{3,2,0,1:T(8,128)}, u32[]{:S(2)}, u32[]{:S(2)}) %all-to-all-start) | async-done | bytes 4194336 | tf_op jit(solution)/shard_map/all_to_all | solution.py:106
  66.5 6.4 %fusion.11 = f32[64,2,64,32]{2,3,1,0:T(8,128)S(1)} fusion(f32[2,64,64,128]{3,2,1,0:T(8,128)S(1)} %fusion.28, f32[2,32,64,128]{3,1,2,0:T(8,128)S(1)} %get-tuple-element.21), kind=kOutput, calls=%fused_computation.30 | convolution fusion | flops 201326592 | bytes 7340032 | tf_op jit(solution)/shard_map/kqpb,krpb->qpkr/dot_general | solution.py:22
  73.0 6.5 %subtract_bitcast_fusion.3 = f32[32,64,2,64]{3,0,2,1:T(8,128)S(1)} fusion(f32[64,2,64,32]{2,3,1,0:T(8,128)S(1)} %fusion.11, f32[2,32,64,128]{3,1,2,0:T(8,128)S(1)} %copy-done.11, f32[2,64,64,128]{3,2,1,0:T(8,128)S(1)} %fusion.25), kind=kOutput, calls=%fused_computation.77 | convolution fusion | flops 201588736 | bytes 8388608 | tf_op jit(solution)/shard_map/kqpb,krpb->qpkr/dot_general | solution.py:22
  85.8 9.7 %all-to-all-start.1 = ((f32[128,1,2048]{2,1,0:T(1,128)}), f32[128,1,2048]{2,1,0:T(1,128)S(1)}, u32[]{:S(2)}, u32[]{:S(2)}) async-start(f32[128,1,2048]{2,1,0:T(1,128)} %reshape.422), calls=%async_computation.1 | async-start | bytes 2097152 | tf_op jit(solution)/shard_map/all_to_all | solution.py:121
  95.6 9.3 %fusion.9 = f32[64,2,64,32]{2,3,1,0:T(8,128)S(1)} fusion(f32[2,64,64,128]{3,2,1,0:T(8,128)} %copy-done.6, f32[2,32,64,128]{3,1,2,0:T(8,128)} %get-tuple-element.19), kind=kOutput, calls=%fused_computation.28 | convolution fusion | flops 201326592 | bytes 7340032 | tf_op jit(solution)/shard_map/kqpb,krpb->qpkr/dot_general | solution.py:22
  104.9 6.6 %add_bitcast_fusion.3 = f32[32,64,2,64]{3,0,2,1:T(8,128)S(1)} fusion(f32[64,2,64,32]{2,3,1,0:T(8,128)S(1)} %fusion.9, f32[2,32,64,128]{3,1,2,0:T(8,128)S(1)} %get-tuple-element.21, f32[2,64,64,128]{3,2,1,0:T(8,128)S(1)} %copy-done.5), kind=kOutput, calls=%fused_computation.76 | convolution fusion | flops 201588736 | bytes 8388608 | tf_op jit(solution)/shard_map/kqpb,krpb->qpkr/dot_general | solution.py:22
  115.2 10.3 %all-to-all-start.2 = ((f32[128,1,2048]{2,1,0:T(1,128)}), f32[128,1,2048]{2,1,0:T(1,128)}, u32[]{:S(2)}, u32[]{:S(2)}) async-start(f32[128,1,2048]{2,1,0:T(1,128)} %reshape.424), calls=%async_computation.2 | async-start | bytes 2097152 | tf_op jit(solution)/shard_map/all_to_all | solution.py:122
  126.6 4.3 %reduce.6 = f32[128,2048]{1,0:T(8,128)S(1)} reduce(f32[128,1,2048]{2,1,0:T(1,128)} %copy-done.13, f32[]{:T(128)} %broadcast.527), dimensions={1}, to_apply=%all_to_all.36.reduce_sub_computation | reduce | bytes 2097156 | tf_op jit(solution)/shard_map/all_to_all | solution.py:121
  134.0 10.2 %all-to-all-done.2 = f32[128,1,2048]{2,1,0:T(1,128)} async-done(((f32[128,1,2048]{2,1,0:T(1,128)}), f32[128,1,2048]{2,1,0:T(1,128)}, u32[]{:S(2)}, u32[]{:S(2)}) %all-to-all-start.2) | async-done | bytes 1048608 | tf_op jit(solution)/shard_map/all_to_all | solution.py:122
  144.2 4.3 %reduce.7 = f32[128,2048]{1,0:T(8,128)S(1)} reduce(f32[128,1,2048]{2,1,0:T(1,128)} %all-to-all-done.2, f32[]{:T(128)} %broadcast.527), dimensions={1}, to_apply=%all_to_all.37.reduce_sub_computation | reduce | bytes 2097156 | tf_op jit(solution)/shard_map/all_to_all | solution.py:122
  171.6 4.5 %copy.308 = f32[2,16,64,2,64]{4,3,1,2,0:T(2,128)} copy(f32[2,16,64,2,64]{2,4,1,3,0:T(8,128)} %subtract_bitcast_fusion.2) | data formatting | bytes 2097152 | tf_op jit(solution)/shard_map/reshape | solution.py:133
  210.1 6.3 %fusion.65 = f32[128,2,16,32]{0,2,3,1:T(8,128)} fusion(f32[2,32,16,128]{3,2,1,0:T(8,128)S(1)} %fusion.70, f32[2,128,32,128]{3,1,2,0:T(8,128)} %get-tuple-element.29, f32[2,16,32,128]{3,2,1,0:T(8,128)S(1)} %fusion.63), kind=kOutput, calls=%fused_computation.96 | convolution fusion | flops 100794368 | bytes 5767168 | tf_op jit(solution)/shard_map/kqpb,krpb->qkrp/dot_general | solution.py:22
  224.1 5.3 %gather_fusion.1 = f32[384,2,16,32]{3,2,1,0:T(8,128)} fusion(f32[128,2,16,32]{3,2,1,0:T(8,128)} %copy.272, s32[1024]{0:T(1024)S(1)} %pad_clamp_fusion), kind=kCustom, calls=%fused_computation.1.clone | custom fusion | bytes 3147264 | tf_op jit(solution)/shard_map/jit(_take)/gather | solution.py:160
  229.4 8.4 %select_multiply_fusion = (f32[384,2,16,32]{3,2,1,0:T(8,128)}, f32[384,2,16,32]{3,2,1,0:T(8,128)}) fusion(f32[384,2,16,32]{3,2,1,0:T(8,128)} %gather_fusion.1, f32[384]{0:T(512)S(1)} %convert_element_type.45, pred[384]{0:T(512)(128)(4,1)S(1)} %compare_and_fusion, f32[384,2,16,32]{3,2,1,0:T(8,128)} %gather_fusion), kind=kLoop, calls=%fused_computation.6 | loop fusion | flops 1572864 | bytes 6293376 | tf_op jit(solution)/shard_map/mul | solution.py:160
  237.8 5.3 %copy.266 = f32[128,2,16,3,32]{0,4,3,2,1:T(8,128)S(1)} copy(f32[128,2,16,3,32]{4,2,1,3,0:T(8,128)} %bitcast.195) | data formatting | bytes 3145728 | tf_op jit(solution)/shard_map/transpose | solution.py:162
  245.3 4.6 %all-to-all-start.3 = ((f32[128,2,16,96]{3,2,1,0:T(8,128)}), f32[128,2,16,96]{3,2,1,0:T(8,128)S(1)}, u32[]{:S(2)}, u32[]{:S(2)}) async-start(f32[128,2,16,96]{3,2,1,0:T(8,128)} %copy.267), calls=%async_computation.3 | async-start | bytes 4194304 | tf_op jit(solution)/shard_map/all_to_all | solution.py:166
  250.0 6.4 %copy.273 = f32[128,2,16,3,32]{0,4,3,2,1:T(8,128)} copy(f32[128,2,16,3,32]{4,2,1,3,0:T(8,128)} %bitcast.194) | data formatting | bytes 3145728 | tf_op jit(solution)/shard_map/transpose | solution.py:162
  259.4 21.0 %all-to-all-done.3 = f32[128,2,16,96]{3,2,1,0:T(8,128)S(1)} async-done(((f32[128,2,16,96]{3,2,1,0:T(8,128)}), f32[128,2,16,96]{3,2,1,0:T(8,128)S(1)}, u32[]{:S(2)}, u32[]{:S(2)}) %all-to-all-start.3) | async-done | bytes 1572896 | tf_op jit(solution)/shard_map/all_to_all | solution.py:166
  280.4 5.8 %all-to-all-start.4 = ((f32[128,2,16,96]{3,2,1,0:T(8,128)}), f32[128,2,16,96]{3,2,1,0:T(8,128)}, u32[]{:S(2)}, u32[]{:S(2)}) async-start(f32[128,2,16,96]{3,2,1,0:T(8,128)} %copy.274), calls=%async_computation.4 | async-start | bytes 4194304 | tf_op jit(solution)/shard_map/all_to_all | solution.py:167
  296.2 19.9 %all-to-all-done.4 = f32[128,2,16,96]{3,2,1,0:T(8,128)} async-done(((f32[128,2,16,96]{3,2,1,0:T(8,128)}), f32[128,2,16,96]{3,2,1,0:T(8,128)}, u32[]{:S(2)}, u32[]{:S(2)}) %all-to-all-start.4) | async-done | bytes 1572896 | tf_op jit(solution)/shard_map/all_to_all | solution.py:167
  325.3 5.4 %fusion.19 = f32[2,32,96,128]{3,2,1,0:T(8,128)S(1)} fusion(f32[2,128,32,128]{3,1,2,0:T(8,128)S(1)} %copy-done.1, f32[2,96,32,128]{3,2,1,0:T(8,128)S(1)} %add_bitcast_fusion.1), kind=kOutput, calls=%fused_computation.56 | convolution fusion | flops 603979776 | bytes 10485760 | tf_op jit(solution)/shard_map/kqpb,krpb->krqp/dot_general | solution.py:22
  330.8 5.4 %fusion.17 = f32[2,32,96,128]{3,2,1,0:T(8,128)S(1)} fusion(f32[2,128,32,128]{3,1,2,0:T(8,128)S(1)} %copy-done.3, f32[2,96,32,128]{3,2,1,0:T(8,128)S(1)} %add_bitcast_fusion.1), kind=kOutput, calls=%fused_computation.54 | convolution fusion | flops 603979776 | bytes 10485760 | tf_op jit(solution)/shard_map/kqpb,krpb->krqp/dot_general | solution.py:22
  338.0 5.5 %subtract_bitcast_fusion = f32[2,96,128,32]{2,1,3,0:T(8,128)S(1)} fusion(f32[2,32,96,128]{3,2,1,0:T(8,128)S(1)} %fusion.19, f32[2,128,32,128]{3,1,2,0:T(8,128)S(1)} %copy-done.3, f32[2,96,32,128]{3,2,1,0:T(8,128)S(1)} %subtract_bitcast_fusion.1), kind=kOutput, calls=%fused_computation.44 | convolution fusion | flops 604766208 | bytes 13631488 | tf_op jit(solution)/shard_map/kqpb,krpb->krqp/dot_general | solution.py:22
  343.5 7.5 %sqrt_reduce_fusion = (f32[2]{0:T(128)S(1)}, f32[2,96,128,32]{2,1,3,0:T(8,128)}) fusion(f32[2,96,128,32]{2,1,3,0:T(8,128)S(1)} %subtract_bitcast_fusion, f32[2,32,96,128]{3,2,1,0:T(8,128)S(1)} %fusion.17, f32[2,128,32,128]{3,1,2,0:T(8,128)S(1)} %copy-done.1, f32[2,96,32,128]{3,2,1,0:T(8,128)S(1)} %subtract_bitcast_fusion.1), kind=kOutput, calls=%fused_computation.42 | convolution fusion | flops 607911936 | bytes 16777224 | tf_op jit(solution)/shard_map/kqpb,krpb->krqp/dot_general | solution.py:22
  351.6 4.7 %all-to-all-start.5 = ((f32[128,1,2]{2,1,0:T(1,128)}), f32[128,1,2]{2,1,0:T(1,128)S(1)}, u32[]{:S(2)}, u32[]{:S(2)}) async-start(f32[128,1,2]{2,1,0:T(1,128)} %broadcast_in_dim.49), calls=%async_computation.5 | async-start | bytes 131072 | tf_op jit(solution)/shard_map/all_to_all | solution.py:179
  361.8 5.1 %copy.283 = f32[2,96,128,32]{1,3,2,0:T(8,128)} copy(f32[2,96,128,32]{2,1,3,0:T(8,128)} %get-tuple-element.57) | data formatting | bytes 6291456 | tf_op jit(solution)/shard_map/add | solution.py:67
  367.1 7.0 %add_select_fusion.1 = (f32[2,1,96,4096]{2,3,0,1:T(8,128)S(1)}, f32[2,1,96,4096]{2,3,0,1:T(8,128)S(1)}) fusion(f32[2,96,128,32]{1,3,2,0:T(8,128)} %copy.283, f32[2]{0:T(128)S(1)} %multiply_add_fusion.2, f32[2,96,128,32]{1,3,2,0:T(8,128)} %copy.279, pred[96,4096]{0,1:T(8,128)(4,1)S(1)} %copy-done.14), kind=kLoop, calls=%fused_computation.20 | loop fusion | flops 14155776 | bytes 12976136 | tf_op jit(solution)/shard_map/jit(_where)/select_n | solution.py:189
  377.9 8.3 %copy.284 = f32[2,2,96,4096]{3,2,1,0:T(8,128)} copy(f32[2,2,96,4096]{2,3,0,1:T(8,128)} %pad_maximum_fusion) | data formatting | bytes 12582912 | tf_op jit(solution)/shard_map/stack | solution.py:191
  (118 shorter events, 123.4 us)
Async XLA Ops:
  4.8 4.7 %copy-start.15 = (s32[2,2]{1,0:T(2,128)S(1)}, s32[2,2]{1,0:T(2,128)}, u32[]{:S(2)}) copy-start(s32[2,2]{1,0:T(2,128)} %param.6) | copy-start | bytes 52
  4.8 54.3 %all-to-all-start = ((f32[2,8,64,1024]{3,2,0,1:T(8,128)}), f32[2,8,64,1024]{3,2,0,1:T(8,128)}, u32[]{:S(2)}, u32[]{:S(2)}) async-start(f32[2,8,64,1024]{3,2,0,1:T(8,128)} %copy.231), calls=%async_computation | async-start | bytes 8388608 | tf_op jit(solution)/shard_map/all_to_all | solution.py:106
  64.4 2.1 copy-start.6
  66.5 6.5 %copy-start.4 = (f32[2,64,64,128]{3,2,1,0:T(8,128)}, f32[2,64,64,128]{3,2,1,0:T(8,128)S(1)}, u32[]{:S(2)}) copy-start(f32[2,64,64,128]{3,2,1,0:T(8,128)S(1)} %fusion.25) | copy-start | bytes 12582916
  66.5 6.5 %copy-start.11 = (f32[2,32,64,128]{3,1,2,0:T(8,128)S(1)}, f32[2,32,64,128]{3,1,2,0:T(8,128)}, u32[]{:S(2)}) copy-start(f32[2,32,64,128]{3,1,2,0:T(8,128)} %get-tuple-element.19) | copy-start | bytes 6291460
  85.8 29.5 %all-to-all-start.1 = ((f32[128,1,2048]{2,1,0:T(1,128)}), f32[128,1,2048]{2,1,0:T(1,128)S(1)}, u32[]{:S(2)}, u32[]{:S(2)}) async-start(f32[128,1,2048]{2,1,0:T(1,128)} %reshape.422), calls=%async_computation.1 | async-start | bytes 2097152 | tf_op jit(solution)/shard_map/all_to_all | solution.py:121
  95.6 9.3 %copy-start.5 = (f32[2,64,64,128]{3,2,1,0:T(8,128)S(1)}, f32[2,64,64,128]{3,2,1,0:T(8,128)}, u32[]{:S(2)}) copy-start(f32[2,64,64,128]{3,2,1,0:T(8,128)} %copy-done.4) | copy-start | bytes 12582916
  112.9 12.6 %copy-start.16 = (s32[128]{0:T(128)S(1)}, s32[128]{0:T(128)}, u32[]{:S(2)}) copy-start(s32[128]{0:T(128)} %param.7) | copy-start | bytes 1540
  115.2 10.9 %copy-start.13 = (f32[128,1,2048]{2,1,0:T(1,128)}, f32[128,1,2048]{2,1,0:T(1,128)S(1)}, u32[]{:S(2)}) copy-start(f32[128,1,2048]{2,1,0:T(1,128)S(1)} %all-to-all-done.1) | copy-start | bytes 3145732
  115.2 29.0 %all-to-all-start.2 = ((f32[128,1,2048]{2,1,0:T(1,128)}), f32[128,1,2048]{2,1,0:T(1,128)}, u32[]{:S(2)}, u32[]{:S(2)}) async-start(f32[128,1,2048]{2,1,0:T(1,128)} %reshape.424), calls=%async_computation.2 | async-start | bytes 2097152 | tf_op jit(solution)/shard_map/all_to_all | solution.py:122
  153.1 2.7 copy-start.7
  171.6 7.8 %copy-start.9 = (f32[2,32,64,128]{3,1,2,0:T(8,128)S(1)}, f32[2,32,64,128]{3,1,2,0:T(8,128)}, u32[]{:S(2)}) copy-start(f32[2,32,64,128]{3,1,2,0:T(8,128)} %get-tuple-element.24) | copy-start | bytes 6291460
  179.4 3.1 copy-start.10
  182.5 2.8 copy-start.8
  193.7 2.2 copy-start.2
  199.3 3.6 copy-start
  245.3 35.0 %all-to-all-start.3 = ((f32[128,2,16,96]{3,2,1,0:T(8,128)}), f32[128,2,16,96]{3,2,1,0:T(8,128)S(1)}, u32[]{:S(2)}, u32[]{:S(2)}) async-start(f32[128,2,16,96]{3,2,1,0:T(8,128)} %copy.267), calls=%async_computation.3 | async-start | bytes 4194304 | tf_op jit(solution)/shard_map/all_to_all | solution.py:166
  280.4 35.7 %all-to-all-start.4 = ((f32[128,2,16,96]{3,2,1,0:T(8,128)}), f32[128,2,16,96]{3,2,1,0:T(8,128)}, u32[]{:S(2)}, u32[]{:S(2)}) async-start(f32[128,2,16,96]{3,2,1,0:T(8,128)} %copy.274), calls=%async_computation.4 | async-start | bytes 4194304 | tf_op jit(solution)/shard_map/all_to_all | solution.py:167
  321.7 3.6 copy-start.1
  325.3 5.5 %copy-start.3 = (f32[2,128,32,128]{3,1,2,0:T(8,128)S(1)}, f32[2,128,32,128]{3,1,2,0:T(8,128)}, u32[]{:S(2)}) copy-start(f32[2,128,32,128]{3,1,2,0:T(8,128)} %get-tuple-element.28) | copy-start | bytes 12582916
  330.8 5.4 %copy-start.12 = (f32[2,96,128,32]{2,3,1,0:T(8,128)S(1)}, f32[2,96,128,32]{2,3,1,0:T(8,128)}, u32[]{:S(2)}) copy-start(f32[2,96,128,32]{2,3,1,0:T(8,128)} %fusion.108) | copy-start | bytes 9437188
  351.6 15.3 %all-to-all-start.5 = ((f32[128,1,2]{2,1,0:T(1,128)}), f32[128,1,2]{2,1,0:T(1,128)S(1)}, u32[]{:S(2)}, u32[]{:S(2)}) async-start(f32[128,1,2]{2,1,0:T(1,128)} %broadcast_in_dim.49), calls=%async_computation.5 | async-start | bytes 131072 | tf_op jit(solution)/shard_map/all_to_all | solution.py:179
  361.8 5.3 %copy-start.14 = (pred[96,4096]{0,1:T(8,128)(4,1)S(1)}, pred[96,4096]{0,1:T(8,128)(4,1)}, u32[]{:S(2)}) copy-start(pred[96,4096]{0,1:T(8,128)(4,1)} %fusion.32) | copy-start | bytes 1179652

commit v10 on v7

--- a/solution.py
+++ b/solution.py
@@ -3,6 +3,8 @@
 import jax
 import jax.numpy as jnp
 from jax import lax
+from jax.experimental import pallas as pl
+from jax.experimental.pallas import tpu as pltpu
 from jax.sharding import PartitionSpec as P
 
 H = 8192
@@ -168,18 +170,41 @@
     local_peak = jnp.max(magnitude, axis=(1, 2))
     every = jnp.broadcast_to(local_peak[None, :], (devices, holo_count))
     peak = jnp.max(lax.all_to_all(every, ("row", "col"), 0, 0, tiled=True), axis=0)
-    plus_real, plus_imag, minus_real, minus_imag = encode(
-        field_real, field_imag, peak[:, None, None]
-    )
     device_index = lax.axis_index("row") * col_devices + lax.axis_index("col")
     my_source = lax.dynamic_slice_in_dim(source, device_index * MOST, MOST)
     row_number = (
         my_source[:, None] * strip_rows + jnp.arange(strip_rows, dtype=jnp.int32)[None, :]
     ).reshape(slot_rows)
-    even = (row_number[:, None] + jnp.arange(P_SIZE, dtype=jnp.int32)[None, :]) % 2 == 0
-    out_real = jnp.where(even[None, :, :], plus_real, minus_real)
-    out_imag = jnp.where(even[None, :, :], plus_imag, minus_imag)
-    return jnp.stack([out_real, out_imag], axis=1)
+    parity = (row_number % 2)[:, None]
+    return encode_slots(peak, parity, field_real, field_imag)
+
+
+def encode_kernel(peak_ref, parity_ref, real_ref, imag_ref, out_ref):
+    peak = peak_ref[pl.program_id(0)]
+    plus_real, plus_imag, minus_real, minus_imag = encode(real_ref[0], imag_ref[0], peak)
+    column = lax.broadcasted_iota(jnp.int32, plus_real.shape, 1)
+    even = (parity_ref[...] + column) % 2 == 0
+    out_ref[0, 0] = jnp.where(even, plus_real, minus_real)
+    out_ref[0, 1] = jnp.where(even, plus_imag, minus_imag)
+
+
+def encode_slots(peak, parity, field_real, field_imag):
+    holo_count, rows, width = field_real.shape
+    split = 2 if rows % 16 == 0 else 1
+    block = rows // split
+    field_spec = pl.BlockSpec((1, block, width), lambda k, j: (k, j, 0))
+    return pl.pallas_call(
+        encode_kernel,
+        out_shape=jax.ShapeDtypeStruct((holo_count, 2, rows, width), jnp.float32),
+        grid=(holo_count, split),
+        in_specs=[
+            pl.BlockSpec(memory_space=pltpu.SMEM),
+            pl.BlockSpec((block, 1), lambda k, j: (j, 0)),
+            field_spec,
+            field_spec,
+        ],
+        out_specs=pl.BlockSpec((1, 2, block, width), lambda k, j: (k, 0, j, 0)),
+    )(peak, parity, field_real, field_imag)
 
 
 def solution(mesh):

time: 385 us -> 385 us (level)
  other arithmetic: 55.2 us -> 43.6 us
  Pallas kernels: 0 us -> 10.5 us
    pallas_call x0 -> x1, Pallas kernels: none -> 10.5 us  [encode_slots(): pl.pallas_call(encode_kernel, out_shape=jax.ShapeDtypeStruct((holo_count,...]
    select_n x1, other arithmetic: 7.03 us -> 0.64 us  [body(): parity = (row_number % 2)[:, None]]
    another operation x1 -> x2, local copies, waits for them, and re-layouts: 8.29 us -> 10.7 us  [the longest x1 5.43 us: body(): field_real = field_real.reshape(holo_count, slot_rows, P_SIZE)]
    unnamed x41 -> x43, local copies, waits for them, and re-layouts: 12.6 us -> 12.6 us
  transfers between devices with their start and end apart: 6 -> 6, of which waited for: 4 -> 4; matrix products, arithmetic and copies ran while one was open for 25% -> 27% of each run, Pallas kernels for 0% -> 0%
where the time goes in v10:
time: 385 us; the launch traced here: 380 us
  local copies, waits for them, and re-layouts  120 us (31%)
  matrix products  101 us (26%)
  waiting for transfers between devices  64.4 us (17%)
  other arithmetic  43.6 us (11%)
  starting transfers between devices  39.8 us (10%)
  Pallas kernels  10.5 us (3%)
    dot_general x30, matrix products, contract(): jnp.einsum(form, left, right, precision=lax.Precision.HIGH, preferred_ele...  101 us
    sin x2, other arithmetic, make_tables(): jnp.sin(outer_angle).reshape(shape_four)  29.8 us
    gather x4, local copies, waits for them, and re-layouts, pack(): picked = jnp.take(grouped, source, axis=2) * filled[None, None, :, None]  21.6 us
    all_to_all x1, waiting for transfers between devices, body(): lax.all_to_all(send_imag, ('row', 'col'), split_axis=0, concat_axis=2, ti...  19.8 us
    all_to_all x1, waiting for transfers between devices, body(): lax.all_to_all(blocks, 'col', split_axis=1, concat_axis=1, tiled=True)  18.3 us
    all_to_all x1, waiting for transfers between devices, body(): lax.all_to_all(send_real, ('row', 'col'), split_axis=0, concat_axis=2, ti...  15.8 us
    unnamed x43, local copies, waits for them, and re-layouts  12.6 us
    pallas_call x1, Pallas kernels, encode_slots(): pl.pallas_call(encode_kernel, out_shape=jax.ShapeDtypeStruct((holo_count,...  10.5 us
  transfers between devices with their start and end apart: 6, of which 4 were waited for; matrix products, arithmetic and copies ran while one was open for 27% of the time, Pallas kernels for 0%

profile of v10, /device:TPU:0, one launch (start us, length us, event | category | flops | bytes accessed | tf_op | source)
XLA Modules:
  0.0 380.3 jit_solution(1450950846703455186)
XLA Ops:
  0.0 4.8 %copy.310 = f32[2,8,64,1024]{3,2,0,1:T(8,128)} copy(f32[2,8,64,1024]{3,2,1,0:T(8,128)} %bitcast.189) | data formatting | bytes 8388608 | tf_op jit(solution)/shard_map/reshape | solution.py:107
  4.8 4.7 %all-to-all-start = ((f32[2,8,64,1024]{3,2,0,1:T(8,128)}), f32[2,8,64,1024]{3,2,0,1:T(8,128)}, u32[]{:S(2)}, u32[]{:S(2)}) async-start(f32[2,8,64,1024]{3,2,0,1:T(8,128)} %copy.310), calls=%async_computation | async-start | bytes 8388608 | tf_op jit(solution)/shard_map/all_to_all | solution.py:108
  10.4 18.6 %fusion.59 = (f32[2,32,64,128]{3,1,2,0:T(8,128)}, f32[2,32,64,128]{3,1,2,0:T(8,128)}, f32[2,32,64,128]{3,1,2,0:T(8,128)}, f32[2,32,64,128]{3,1,2,0:T(8,128)S(1)}) fusion(s32[128]{0:T(128)S(1)} %and_select_fusion.3, s32[2,32,64]{1,2,0:T(8,128)S(1)} %get-tuple-element.36, s32[2,32,64]{1,2,0:T(8,128)S(1)} %get-tuple-element.37), kind=kLoop, calls=%fused_computation.77 | loop fusion | flops 14680064 | bytes 8421888 | tf_op jit(solution)/shard_map/sin | solution.py:44
  29.6 11.2 %fusion.35 = (f32[2,128,32,128]{3,1,2,0:T(8,128)}, f32[2,128,32,128]{3,1,2,0:T(8,128)}) fusion(s32[128]{0:T(128)S(1)} %and_select_fusion, s32[128,32]{0,1:T(8,128)S(1)} %multiply_add_fusion), kind=kLoop, calls=%fused_computation.53 | loop fusion | flops 14680064 | bytes 8405504 | tf_op jit(solution)/shard_map/sin | solution.py:44
  40.9 18.3 %all-to-all-done = f32[2,8,64,1024]{3,2,0,1:T(8,128)} async-done(((f32[2,8,64,1024]{3,2,0,1:T(8,128)}), f32[2,8,64,1024]{3,2,0,1:T(8,128)}, u32[]{:S(2)}, u32[]{:S(2)}) %all-to-all-start) | async-done | bytes 4194336 | tf_op jit(solution)/shard_map/all_to_all | solution.py:108
  66.5 6.5 %fusion.9 = f32[64,2,64,32]{2,3,1,0:T(8,128)S(1)} fusion(f32[2,64,64,128]{3,2,1,0:T(8,128)S(1)} %fusion.26, f32[2,32,64,128]{3,1,2,0:T(8,128)S(1)} %get-tuple-element.21), kind=kOutput, calls=%fused_computation.16 | convolution fusion | flops 201326592 | bytes 7340032 | tf_op jit(solution)/shard_map/kqpb,krpb->qpkr/dot_general | solution.py:24
  73.0 6.5 %subtract_bitcast_fusion.3 = f32[32,64,2,64]{3,0,2,1:T(8,128)S(1)} fusion(f32[64,2,64,32]{2,3,1,0:T(8,128)S(1)} %fusion.9, f32[2,32,64,128]{3,1,2,0:T(8,128)S(1)} %copy-done.10, f32[2,64,64,128]{3,2,1,0:T(8,128)S(1)} %fusion.23), kind=kOutput, calls=%fused_computation.58 | convolution fusion | flops 201588736 | bytes 8388608 | tf_op jit(solution)/shard_map/kqpb,krpb->qpkr/dot_general | solution.py:24
  85.8 9.5 %all-to-all-start.1 = ((f32[128,1,2048]{2,1,0:T(1,128)}), f32[128,1,2048]{2,1,0:T(1,128)S(1)}, u32[]{:S(2)}, u32[]{:S(2)}) async-start(f32[128,1,2048]{2,1,0:T(1,128)} %reshape.323), calls=%async_computation.1 | async-start | bytes 2097152 | tf_op jit(solution)/shard_map/all_to_all | solution.py:123
  95.4 9.3 %fusion.7 = f32[64,2,64,32]{2,3,1,0:T(8,128)S(1)} fusion(f32[2,64,64,128]{3,2,1,0:T(8,128)} %copy-done.6, f32[2,32,64,128]{3,1,2,0:T(8,128)} %get-tuple-element.19), kind=kOutput, calls=%fused_computation.14 | convolution fusion | flops 201326592 | bytes 7340032 | tf_op jit(solution)/shard_map/kqpb,krpb->qpkr/dot_general | solution.py:24
  104.7 6.8 %add_bitcast_fusion.3 = f32[32,64,2,64]{3,0,2,1:T(8,128)S(1)} fusion(f32[64,2,64,32]{2,3,1,0:T(8,128)S(1)} %fusion.7, f32[2,32,64,128]{3,1,2,0:T(8,128)S(1)} %get-tuple-element.21, f32[2,64,64,128]{3,2,1,0:T(8,128)S(1)} %copy-done.5), kind=kOutput, calls=%fused_computation.57 | convolution fusion | flops 201588736 | bytes 8388608 | tf_op jit(solution)/shard_map/kqpb,krpb->qpkr/dot_general | solution.py:24
  115.3 10.3 %all-to-all-start.2 = ((f32[128,1,2048]{2,1,0:T(1,128)}), f32[128,1,2048]{2,1,0:T(1,128)}, u32[]{:S(2)}, u32[]{:S(2)}) async-start(f32[128,1,2048]{2,1,0:T(1,128)} %reshape.325), calls=%async_computation.2 | async-start | bytes 2097152 | tf_op jit(solution)/shard_map/all_to_all | solution.py:124
  126.5 4.3 %reduce.6 = f32[128,2048]{1,0:T(8,128)S(1)} reduce(f32[128,1,2048]{2,1,0:T(1,128)} %copy-done.16, f32[]{:T(128)} %broadcast.451), dimensions={1}, to_apply=%all_to_all.36.reduce_sub_computation | reduce | bytes 2097156 | tf_op jit(solution)/shard_map/all_to_all | solution.py:123
  133.9 10.4 %all-to-all-done.2 = f32[128,1,2048]{2,1,0:T(1,128)} async-done(((f32[128,1,2048]{2,1,0:T(1,128)}), f32[128,1,2048]{2,1,0:T(1,128)}, u32[]{:S(2)}, u32[]{:S(2)}) %all-to-all-start.2) | async-done | bytes 1048608 | tf_op jit(solution)/shard_map/all_to_all | solution.py:124
  144.3 4.3 %reduce.7 = f32[128,2048]{1,0:T(8,128)S(1)} reduce(f32[128,1,2048]{2,1,0:T(1,128)} %all-to-all-done.2, f32[]{:T(128)} %broadcast.451), dimensions={1}, to_apply=%all_to_all.37.reduce_sub_computation | reduce | bytes 2097156 | tf_op jit(solution)/shard_map/all_to_all | solution.py:124
  204.1 5.3 %gather_fusion.1 = f32[384,2,16,32]{3,2,1,0:T(8,128)} fusion(f32[2,16,128,32]{3,1,2,0:T(8,128)} %copy.352, s32[1024]{0:T(1024)S(1)} %pad_clamp_fusion), kind=kCustom, calls=%fused_computation.1.clone | custom fusion | bytes 3147264 | tf_op jit(solution)/shard_map/jit(_take)/gather | solution.py:154
  209.4 6.4 %copy.353 = f32[384,2,16,32]{0,3,2,1:T(8,128)} copy(f32[384,2,16,32]{3,2,1,0:T(8,128)} %gather_fusion.1) | data formatting | bytes 3145728 | tf_op jit(solution)/shard_map/jit(_take)/gather | solution.py:154
  220.1 5.6 %copy.345 = f32[384,2,16,32]{0,3,2,1:T(8,128)S(1)} copy(f32[384,2,16,32]{3,2,1,0:T(8,128)} %gather_fusion) | data formatting | bytes 3145728 | tf_op jit(solution)/shard_map/jit(_take)/gather | solution.py:154
  227.8 5.0 %copy.346 = f32[2,16,384,32]{3,2,1,0:T(8,128)} copy(f32[2,16,384,32]{2,3,1,0:T(8,128)} %get-tuple-element.45) | data formatting | bytes 3145728 | tf_op jit(solution)/shard_map/mul | solution.py:154
  239.5 4.6 %all-to-all-start.3 = ((f32[128,2,16,96]{3,2,1,0:T(8,128)}), f32[128,2,16,96]{3,2,1,0:T(8,128)S(1)}, u32[]{:S(2)}, u32[]{:S(2)}) async-start(f32[128,2,16,96]{3,2,1,0:T(8,128)} %copy.347), calls=%async_computation.3 | async-start | bytes 4194304 | tf_op jit(solution)/shard_map/all_to_all | solution.py:159
  244.2 5.0 %copy.354 = f32[2,16,384,32]{3,2,1,0:T(8,128)} copy(f32[2,16,384,32]{2,3,1,0:T(8,128)} %get-tuple-element.44) | data formatting | bytes 3145728 | tf_op jit(solution)/shard_map/mul | solution.py:154
  249.2 5.3 %reshape.283 = f32[2,16,128,96]{3,2,1,0:T(8,128)} reshape(f32[2,16,384,32]{3,2,1,0:T(8,128)} %copy.354) | data formatting | bytes 3145728 | tf_op jit(solution)/shard_map/reshape | solution.py:155
  258.7 15.8 %all-to-all-done.3 = f32[128,2,16,96]{3,2,1,0:T(8,128)S(1)} async-done(((f32[128,2,16,96]{3,2,1,0:T(8,128)}), f32[128,2,16,96]{3,2,1,0:T(8,128)S(1)}, u32[]{:S(2)}, u32[]{:S(2)}) %all-to-all-start.3) | async-done | bytes 1572896 | tf_op jit(solution)/shard_map/all_to_all | solution.py:159
  274.5 5.8 %all-to-all-start.4 = ((f32[128,2,16,96]{3,2,1,0:T(8,128)}), f32[128,2,16,96]{3,2,1,0:T(8,128)}, u32[]{:S(2)}, u32[]{:S(2)}) async-start(f32[128,2,16,96]{3,2,1,0:T(8,128)} %copy.355), calls=%async_computation.4 | async-start | bytes 4194304 | tf_op jit(solution)/shard_map/all_to_all | solution.py:160
  290.5 19.8 %all-to-all-done.4 = f32[128,2,16,96]{3,2,1,0:T(8,128)} async-done(((f32[128,2,16,96]{3,2,1,0:T(8,128)}), f32[128,2,16,96]{3,2,1,0:T(8,128)}, u32[]{:S(2)}, u32[]{:S(2)}) %all-to-all-start.4) | async-done | bytes 1572896 | tf_op jit(solution)/shard_map/all_to_all | solution.py:160
  319.4 5.4 %fusion.15 = f32[2,32,96,128]{3,2,1,0:T(8,128)S(1)} fusion(f32[2,128,32,128]{3,1,2,0:T(8,128)S(1)} %copy-done.3, f32[2,96,32,128]{3,2,1,0:T(8,128)S(1)} %add_bitcast_fusion.1), kind=kOutput, calls=%fused_computation.37 | convolution fusion | flops 603979776 | bytes 10485760 | tf_op jit(solution)/shard_map/kqpb,krpb->krqp/dot_general | solution.py:24
  324.9 5.4 %fusion.17 = f32[2,32,96,128]{3,2,1,0:T(8,128)S(1)} fusion(f32[2,128,32,128]{3,1,2,0:T(8,128)S(1)} %copy-done.1, f32[2,96,32,128]{3,2,1,0:T(8,128)S(1)} %add_bitcast_fusion.1), kind=kOutput, calls=%fused_computation.39 | convolution fusion | flops 603979776 | bytes 10485760 | tf_op jit(solution)/shard_map/kqpb,krpb->krqp/dot_general | solution.py:24
  332.0 5.6 %subtract_bitcast_fusion = f32[2,96,128,32]{2,1,3,0:T(8,128)S(1)} fusion(f32[2,32,96,128]{3,2,1,0:T(8,128)S(1)} %fusion.17, f32[2,128,32,128]{3,1,2,0:T(8,128)S(1)} %copy-done.3, f32[2,96,32,128]{3,2,1,0:T(8,128)S(1)} %subtract_bitcast_fusion.1), kind=kOutput, calls=%fused_computation.30 | convolution fusion | flops 604766208 | bytes 13631488 | tf_op jit(solution)/shard_map/kqpb,krpb->krqp/dot_general | solution.py:24
  337.6 7.5 %sqrt_reduce_fusion = (f32[2]{0:T(128)S(1)}, f32[2,96,128,32]{2,1,3,0:T(8,128)}) fusion(f32[2,96,128,32]{2,1,3,0:T(8,128)S(1)} %subtract_bitcast_fusion, f32[2,32,96,128]{3,2,1,0:T(8,128)S(1)} %fusion.15, f32[2,128,32,128]{3,1,2,0:T(8,128)S(1)} %copy-done.1, f32[2,96,32,128]{3,2,1,0:T(8,128)S(1)} %subtract_bitcast_fusion.1), kind=kOutput, calls=%fused_computation.28 | convolution fusion | flops 607911936 | bytes 16777224 | tf_op jit(solution)/shard_map/kqpb,krpb->krqp/dot_general | solution.py:24
  345.8 4.8 %all-to-all-start.5 = ((f32[128,1,2]{2,1,0:T(1,128)}), f32[128,1,2]{2,1,0:T(1,128)S(1)}, u32[]{:S(2)}, u32[]{:S(2)}) async-start(f32[128,1,2]{2,1,0:T(1,128)} %broadcast_in_dim.40), calls=%async_computation.5 | async-start | bytes 131072 | tf_op jit(solution)/shard_map/all_to_all | solution.py:172
  354.6 5.4 %copy.368.real_ref = f32[2,96,4096]{2,1,0:T(8,128)} copy(f32[2,96,4096]{1,2,0:T(8,128)} %bitcast.176) | data formatting | bytes 6291456 | tf_op jit(solution)/shard_map/reshape;reshape;reshape | solution.py:167
  363.3 5.3 %copy.369.imag_ref = f32[2,96,4096]{2,1,0:T(8,128)} copy(f32[2,96,4096]{1,2,0:T(8,128)} %bitcast.177) | data formatting | bytes 6291456 | tf_op jit(solution)/shard_map/reshape;reshape;reshape | solution.py:168
  369.3 10.5 %shard_map.37 = f32[2,2,96,4096]{3,2,1,0:T(8,128)} custom-call(f32[2]{0:T(128)} %reduce_max.19.peak_ref, s32[96,1]{1,0:T(8,128)} %add_select_fusion.9.parity_ref, f32[2,96,4096]{2,1,0:T(8,128)} %copy.368.real_ref, f32[2,96,4096]{2,1,0:T(8,128)} %copy.369.imag_ref), custom_call_target="tpu_custom_call" | custom-call | tf_op jit(solution)/shard_map/pallas_call | solution.py:196
  (125 shorter events, 124.9 us)
Async XLA Ops:
  4.8 4.8 %copy-start.17 = (s32[2,2]{1,0:T(2,128)S(1)}, s32[2,2]{1,0:T(2,128)}, u32[]{:S(2)}) copy-start(s32[2,2]{1,0:T(2,128)} %param.6) | copy-start | bytes 52
  4.8 54.4 %all-to-all-start = ((f32[2,8,64,1024]{3,2,0,1:T(8,128)}), f32[2,8,64,1024]{3,2,0,1:T(8,128)}, u32[]{:S(2)}, u32[]{:S(2)}) async-start(f32[2,8,64,1024]{3,2,0,1:T(8,128)} %copy.310), calls=%async_computation | async-start | bytes 8388608 | tf_op jit(solution)/shard_map/all_to_all | solution.py:108
  10.4 18.6 %copy-start.18 = (s32[128]{0:T(128)S(1)}, s32[128]{0:T(128)}, u32[]{:S(2)}) copy-start(s32[128]{0:T(128)} %param.7) | copy-start | bytes 1540
  64.4 8.6 %copy-start.4 = (f32[2,64,64,128]{3,2,1,0:T(8,128)}, f32[2,64,64,128]{3,2,1,0:T(8,128)S(1)}, u32[]{:S(2)}) copy-start(f32[2,64,64,128]{3,2,1,0:T(8,128)S(1)} %fusion.23) | copy-start | bytes 12582916
  66.5 6.5 %copy-start.6 = (f32[2,64,64,128]{3,2,1,0:T(8,128)}, f32[2,64,64,128]{3,2,1,0:T(8,128)S(1)}, u32[]{:S(2)}) copy-start(f32[2,64,64,128]{3,2,1,0:T(8,128)S(1)} %fusion.26) | copy-start | bytes 12582916
  66.5 6.5 %copy-start.10 = (f32[2,32,64,128]{3,1,2,0:T(8,128)S(1)}, f32[2,32,64,128]{3,1,2,0:T(8,128)}, u32[]{:S(2)}) copy-start(f32[2,32,64,128]{3,1,2,0:T(8,128)} %get-tuple-element.19) | copy-start | bytes 6291460
  85.8 29.5 %all-to-all-start.1 = ((f32[128,1,2048]{2,1,0:T(1,128)}), f32[128,1,2048]{2,1,0:T(1,128)S(1)}, u32[]{:S(2)}, u32[]{:S(2)}) async-start(f32[128,1,2048]{2,1,0:T(1,128)} %reshape.323), calls=%async_computation.1 | async-start | bytes 2097152 | tf_op jit(solution)/shard_map/all_to_all | solution.py:123
  95.4 9.3 %copy-start.5 = (f32[2,64,64,128]{3,2,1,0:T(8,128)S(1)}, f32[2,64,64,128]{3,2,1,0:T(8,128)}, u32[]{:S(2)}) copy-start(f32[2,64,64,128]{3,2,1,0:T(8,128)} %copy-done.4) | copy-start | bytes 12582916
  115.3 10.6 %copy-start.16 = (f32[128,1,2048]{2,1,0:T(1,128)}, f32[128,1,2048]{2,1,0:T(1,128)S(1)}, u32[]{:S(2)}) copy-start(f32[128,1,2048]{2,1,0:T(1,128)S(1)} %all-to-all-done.1) | copy-start | bytes 3145732
  115.3 29.0 %all-to-all-start.2 = ((f32[128,1,2048]{2,1,0:T(1,128)}), f32[128,1,2048]{2,1,0:T(1,128)}, u32[]{:S(2)}, u32[]{:S(2)}) async-start(f32[128,1,2048]{2,1,0:T(1,128)} %reshape.325), calls=%async_computation.2 | async-start | bytes 2097152 | tf_op jit(solution)/shard_map/all_to_all | solution.py:124
  153.4 2.7 copy-start.7
  166.1 2.7 copy-start.14
  171.3 3.7 copy-start.9
  178.0 1.8 copy-start.8
  179.8 1.8 copy-start.13
  184.5 2.2 copy-start.2
  190.1 3.8 %copy-start = (f32[2,128,32,128]{3,1,2,0:T(8,128)S(1)}, f32[2,128,32,128]{3,1,2,0:T(8,128)}, u32[]{:S(2)}) copy-start(f32[2,128,32,128]{3,1,2,0:T(8,128)} %get-tuple-element.29) | copy-start | bytes 12582916
  220.1 5.6 %copy-start.15 = (f32[384,2,16,32]{0,3,2,1:T(8,128)S(1)}, f32[384,2,16,32]{0,3,2,1:T(8,128)}, u32[]{:S(2)}) copy-start(f32[384,2,16,32]{0,3,2,1:T(8,128)} %copy.353) | copy-start | bytes 4718596
  239.5 35.0 %all-to-all-start.3 = ((f32[128,2,16,96]{3,2,1,0:T(8,128)}), f32[128,2,16,96]{3,2,1,0:T(8,128)S(1)}, u32[]{:S(2)}, u32[]{:S(2)}) async-start(f32[128,2,16,96]{3,2,1,0:T(8,128)} %copy.347), calls=%async_computation.3 | async-start | bytes 4194304 | tf_op jit(solution)/shard_map/all_to_all | solution.py:159
  274.5 35.7 %all-to-all-start.4 = ((f32[128,2,16,96]{3,2,1,0:T(8,128)}), f32[128,2,16,96]{3,2,1,0:T(8,128)}, u32[]{:S(2)}, u32[]{:S(2)}) async-start(f32[128,2,16,96]{3,2,1,0:T(8,128)} %copy.355), calls=%async_computation.4 | async-start | bytes 4194304 | tf_op jit(solution)/shard_map/all_to_all | solution.py:160
  315.8 3.6 copy-start.3
  319.4 5.5 %copy-start.1 = (f32[2,128,32,128]{3,1,2,0:T(8,128)S(1)}, f32[2,128,32,128]{3,1,2,0:T(8,128)}, u32[]{:S(2)}) copy-start(f32[2,128,32,128]{3,1,2,0:T(8,128)} %get-tuple-element.29) | copy-start | bytes 12582916
  324.9 5.5 %copy-start.12 = (f32[2,96,128,32]{2,3,1,0:T(8,128)S(1)}, f32[2,96,128,32]{2,3,1,0:T(8,128)}, u32[]{:S(2)}) copy-start(f32[2,96,128,32]{2,3,1,0:T(8,128)} %fusion.102) | copy-start | bytes 9437188
  345.8 22.9 %all-to-all-start.5 = ((f32[128,1,2]{2,1,0:T(1,128)}), f32[128,1,2]{2,1,0:T(1,128)S(1)}, u32[]{:S(2)}, u32[]{:S(2)}) async-start(f32[128,1,2]{2,1,0:T(1,128)} %broadcast_in_dim.40), calls=%async_computation.5 | async-start | bytes 131072 | tf_op jit(solution)/shard_map/all_to_all | solution.py:172
  354.6 5.4 %copy-start.11 = (f32[2,96,128,32]{2,1,3,0:T(8,128)S(1)}, f32[2,96,128,32]{2,1,3,0:T(8,128)}, u32[]{:S(2)}) copy-start(f32[2,96,128,32]{2,1,3,0:T(8,128)} %get-tuple-element.55) | copy-start | bytes 9437188

commit v11 on v10

--- a/solution.py
+++ b/solution.py
@@ -180,8 +180,18 @@
 
 
 def encode_kernel(peak_ref, parity_ref, real_ref, imag_ref, out_ref):
-    peak = peak_ref[pl.program_id(0)]
-    plus_real, plus_imag, minus_real, minus_imag = encode(real_ref[0], imag_ref[0], peak)
+    inverse = 1.0 / (headroom * peak_ref[pl.program_id(0)] + epsilon)
+    unit_real = real_ref[0] * inverse
+    unit_imag = imag_ref[0] * inverse
+    square = unit_real * unit_real + unit_imag * unit_imag
+    height = jnp.sqrt(1.0 - square)
+    shrink = lax.rsqrt(square + softness) * height
+    phase_real = unit_real * shrink
+    phase_imag = unit_imag * shrink
+    plus_real = unit_real - phase_imag
+    plus_imag = unit_imag + phase_real
+    minus_real = unit_real + phase_imag
+    minus_imag = unit_imag - phase_real
     column = lax.broadcasted_iota(jnp.int32, plus_real.shape, 1)
     even = (parity_ref[...] + column) % 2 == 0
     out_ref[0, 0] = jnp.where(even, plus_real, minus_real)

time: 385 us -> 384 us (level)
  no operation moved by 1% of the time
where the time goes in v11:
time: 384 us; the launch traced here: 379 us
  local copies, waits for them, and re-layouts  120 us (31%)
  matrix products  101 us (26%)
  waiting for transfers between devices  64.4 us (17%)
  other arithmetic  43.6 us (11%)
  starting transfers between devices  39.8 us (10%)
  Pallas kernels  9.16 us (2%)
    dot_general x30, matrix products, contract(): jnp.einsum(form, left, right, precision=lax.Precision.HIGH, preferred_ele...  101 us
    sin x2, other arithmetic, make_tables(): jnp.sin(outer_angle).reshape(shape_four)  29.8 us
    gather x4, local copies, waits for them, and re-layouts, pack(): picked = jnp.take(grouped, source, axis=2) * filled[None, None, :, None]  21.6 us
    all_to_all x1, waiting for transfers between devices, body(): lax.all_to_all(send_imag, ('row', 'col'), split_axis=0, concat_axis=2, ti...  19.8 us
    all_to_all x1, waiting for transfers between devices, body(): lax.all_to_all(blocks, 'col', split_axis=1, concat_axis=1, tiled=True)  18.3 us
    all_to_all x1, waiting for transfers between devices, body(): lax.all_to_all(send_real, ('row', 'col'), split_axis=0, concat_axis=2, ti...  15.8 us
    unnamed x43, local copies, waits for them, and re-layouts  12.6 us
    all_to_all x1, waiting for transfers between devices, body(): lax.all_to_all(spec_imag.reshape(send_shape), ('row', 'col'), 0, 0, tiled...  10.4 us
  transfers between devices with their start and end apart: 6, of which 4 were waited for; matrix products, arithmetic and copies ran while one was open for 27% of the time, Pallas kernels for 0%

profile of v11, /device:TPU:0, one launch (start us, length us, event | category | flops | bytes accessed | tf_op | source)
XLA Modules:
  0.0 378.9 jit_solution(2606180297450710068)
XLA Ops:
  0.0 4.8 %copy.310 = f32[2,8,64,1024]{3,2,0,1:T(8,128)} copy(f32[2,8,64,1024]{3,2,1,0:T(8,128)} %bitcast.189) | data formatting | bytes 8388608 | tf_op jit(solution)/shard_map/reshape | solution.py:107
  4.8 4.7 %all-to-all-start = ((f32[2,8,64,1024]{3,2,0,1:T(8,128)}), f32[2,8,64,1024]{3,2,0,1:T(8,128)}, u32[]{:S(2)}, u32[]{:S(2)}) async-start(f32[2,8,64,1024]{3,2,0,1:T(8,128)} %copy.310), calls=%async_computation | async-start | bytes 8388608 | tf_op jit(solution)/shard_map/all_to_all | solution.py:108
  10.4 18.6 %fusion.59 = (f32[2,32,64,128]{3,1,2,0:T(8,128)}, f32[2,32,64,128]{3,1,2,0:T(8,128)}, f32[2,32,64,128]{3,1,2,0:T(8,128)}, f32[2,32,64,128]{3,1,2,0:T(8,128)S(1)}) fusion(s32[128]{0:T(128)S(1)} %and_select_fusion.3, s32[2,32,64]{1,2,0:T(8,128)S(1)} %get-tuple-element.36, s32[2,32,64]{1,2,0:T(8,128)S(1)} %get-tuple-element.37), kind=kLoop, calls=%fused_computation.77 | loop fusion | flops 14680064 | bytes 8421888 | tf_op jit(solution)/shard_map/sin | solution.py:44
  29.6 11.2 %fusion.35 = (f32[2,128,32,128]{3,1,2,0:T(8,128)}, f32[2,128,32,128]{3,1,2,0:T(8,128)}) fusion(s32[128]{0:T(128)S(1)} %and_select_fusion, s32[128,32]{0,1:T(8,128)S(1)} %multiply_add_fusion), kind=kLoop, calls=%fused_computation.53 | loop fusion | flops 14680064 | bytes 8405504 | tf_op jit(solution)/shard_map/sin | solution.py:44
  40.9 18.3 %all-to-all-done = f32[2,8,64,1024]{3,2,0,1:T(8,128)} async-done(((f32[2,8,64,1024]{3,2,0,1:T(8,128)}), f32[2,8,64,1024]{3,2,0,1:T(8,128)}, u32[]{:S(2)}, u32[]{:S(2)}) %all-to-all-start) | async-done | bytes 4194336 | tf_op jit(solution)/shard_map/all_to_all | solution.py:108
  66.5 6.5 %fusion.9 = f32[64,2,64,32]{2,3,1,0:T(8,128)S(1)} fusion(f32[2,64,64,128]{3,2,1,0:T(8,128)S(1)} %fusion.26, f32[2,32,64,128]{3,1,2,0:T(8,128)S(1)} %get-tuple-element.21), kind=kOutput, calls=%fused_computation.16 | convolution fusion | flops 201326592 | bytes 7340032 | tf_op jit(solution)/shard_map/kqpb,krpb->qpkr/dot_general | solution.py:24
  73.0 6.5 %subtract_bitcast_fusion.3 = f32[32,64,2,64]{3,0,2,1:T(8,128)S(1)} fusion(f32[64,2,64,32]{2,3,1,0:T(8,128)S(1)} %fusion.9, f32[2,32,64,128]{3,1,2,0:T(8,128)S(1)} %copy-done.10, f32[2,64,64,128]{3,2,1,0:T(8,128)S(1)} %fusion.23), kind=kOutput, calls=%fused_computation.58 | convolution fusion | flops 201588736 | bytes 8388608 | tf_op jit(solution)/shard_map/kqpb,krpb->qpkr/dot_general | solution.py:24
  85.8 9.5 %all-to-all-start.1 = ((f32[128,1,2048]{2,1,0:T(1,128)}), f32[128,1,2048]{2,1,0:T(1,128)S(1)}, u32[]{:S(2)}, u32[]{:S(2)}) async-start(f32[128,1,2048]{2,1,0:T(1,128)} %reshape.323), calls=%async_computation.1 | async-start | bytes 2097152 | tf_op jit(solution)/shard_map/all_to_all | solution.py:123
  95.4 9.3 %fusion.7 = f32[64,2,64,32]{2,3,1,0:T(8,128)S(1)} fusion(f32[2,64,64,128]{3,2,1,0:T(8,128)} %copy-done.6, f32[2,32,64,128]{3,1,2,0:T(8,128)} %get-tuple-element.19), kind=kOutput, calls=%fused_computation.14 | convolution fusion | flops 201326592 | bytes 7340032 | tf_op jit(solution)/shard_map/kqpb,krpb->qpkr/dot_general | solution.py:24
  104.7 6.8 %add_bitcast_fusion.3 = f32[32,64,2,64]{3,0,2,1:T(8,128)S(1)} fusion(f32[64,2,64,32]{2,3,1,0:T(8,128)S(1)} %fusion.7, f32[2,32,64,128]{3,1,2,0:T(8,128)S(1)} %get-tuple-element.21, f32[2,64,64,128]{3,2,1,0:T(8,128)S(1)} %copy-done.5), kind=kOutput, calls=%fused_computation.57 | convolution fusion | flops 201588736 | bytes 8388608 | tf_op jit(solution)/shard_map/kqpb,krpb->qpkr/dot_general | solution.py:24
  115.3 10.3 %all-to-all-start.2 = ((f32[128,1,2048]{2,1,0:T(1,128)}), f32[128,1,2048]{2,1,0:T(1,128)}, u32[]{:S(2)}, u32[]{:S(2)}) async-start(f32[128,1,2048]{2,1,0:T(1,128)} %reshape.325), calls=%async_computation.2 | async-start | bytes 2097152 | tf_op jit(solution)/shard_map/all_to_all | solution.py:124
  126.5 4.3 %reduce.6 = f32[128,2048]{1,0:T(8,128)S(1)} reduce(f32[128,1,2048]{2,1,0:T(1,128)} %copy-done.16, f32[]{:T(128)} %broadcast.451), dimensions={1}, to_apply=%all_to_all.36.reduce_sub_computation | reduce | bytes 2097156 | tf_op jit(solution)/shard_map/all_to_all | solution.py:123
  133.9 10.4 %all-to-all-done.2 = f32[128,1,2048]{2,1,0:T(1,128)} async-done(((f32[128,1,2048]{2,1,0:T(1,128)}), f32[128,1,2048]{2,1,0:T(1,128)}, u32[]{:S(2)}, u32[]{:S(2)}) %all-to-all-start.2) | async-done | bytes 1048608 | tf_op jit(solution)/shard_map/all_to_all | solution.py:124
  144.3 4.3 %reduce.7 = f32[128,2048]{1,0:T(8,128)S(1)} reduce(f32[128,1,2048]{2,1,0:T(1,128)} %all-to-all-done.2, f32[]{:T(128)} %broadcast.451), dimensions={1}, to_apply=%all_to_all.37.reduce_sub_computation | reduce | bytes 2097156 | tf_op jit(solution)/shard_map/all_to_all | solution.py:124
  204.1 5.3 %gather_fusion.1 = f32[384,2,16,32]{3,2,1,0:T(8,128)} fusion(f32[2,16,128,32]{3,1,2,0:T(8,128)} %copy.352, s32[1024]{0:T(1024)S(1)} %pad_clamp_fusion), kind=kCustom, calls=%fused_computation.1.clone | custom fusion | bytes 3147264 | tf_op jit(solution)/shard_map/jit(_take)/gather | solution.py:154
  209.4 6.4 %copy.353 = f32[384,2,16,32]{0,3,2,1:T(8,128)} copy(f32[384,2,16,32]{3,2,1,0:T(8,128)} %gather_fusion.1) | data formatting | bytes 3145728 | tf_op jit(solution)/shard_map/jit(_take)/gather | solution.py:154
  220.1 5.6 %copy.345 = f32[384,2,16,32]{0,3,2,1:T(8,128)S(1)} copy(f32[384,2,16,32]{3,2,1,0:T(8,128)} %gather_fusion) | data formatting | bytes 3145728 | tf_op jit(solution)/shard_map/jit(_take)/gather | solution.py:154
  227.8 5.0 %copy.346 = f32[2,16,384,32]{3,2,1,0:T(8,128)} copy(f32[2,16,384,32]{2,3,1,0:T(8,128)} %get-tuple-element.45) | data formatting | bytes 3145728 | tf_op jit(solution)/shard_map/mul | solution.py:154
  239.5 4.6 %all-to-all-start.3 = ((f32[128,2,16,96]{3,2,1,0:T(8,128)}), f32[128,2,16,96]{3,2,1,0:T(8,128)S(1)}, u32[]{:S(2)}, u32[]{:S(2)}) async-start(f32[128,2,16,96]{3,2,1,0:T(8,128)} %copy.347), calls=%async_computation.3 | async-start | bytes 4194304 | tf_op jit(solution)/shard_map/all_to_all | solution.py:159
  244.2 5.0 %copy.354 = f32[2,16,384,32]{3,2,1,0:T(8,128)} copy(f32[2,16,384,32]{2,3,1,0:T(8,128)} %get-tuple-element.44) | data formatting | bytes 3145728 | tf_op jit(solution)/shard_map/mul | solution.py:154
  249.2 5.3 %reshape.283 = f32[2,16,128,96]{3,2,1,0:T(8,128)} reshape(f32[2,16,384,32]{3,2,1,0:T(8,128)} %copy.354) | data formatting | bytes 3145728 | tf_op jit(solution)/shard_map/reshape | solution.py:155
  258.7 15.8 %all-to-all-done.3 = f32[128,2,16,96]{3,2,1,0:T(8,128)S(1)} async-done(((f32[128,2,16,96]{3,2,1,0:T(8,128)}), f32[128,2,16,96]{3,2,1,0:T(8,128)S(1)}, u32[]{:S(2)}, u32[]{:S(2)}) %all-to-all-start.3) | async-done | bytes 1572896 | tf_op jit(solution)/shard_map/all_to_all | solution.py:159
  274.5 5.8 %all-to-all-start.4 = ((f32[128,2,16,96]{3,2,1,0:T(8,128)}), f32[128,2,16,96]{3,2,1,0:T(8,128)}, u32[]{:S(2)}, u32[]{:S(2)}) async-start(f32[128,2,16,96]{3,2,1,0:T(8,128)} %copy.355), calls=%async_computation.4 | async-start | bytes 4194304 | tf_op jit(solution)/shard_map/all_to_all | solution.py:160
  290.5 19.8 %all-to-all-done.4 = f32[128,2,16,96]{3,2,1,0:T(8,128)} async-done(((f32[128,2,16,96]{3,2,1,0:T(8,128)}), f32[128,2,16,96]{3,2,1,0:T(8,128)}, u32[]{:S(2)}, u32[]{:S(2)}) %all-to-all-start.4) | async-done | bytes 1572896 | tf_op jit(solution)/shard_map/all_to_all | solution.py:160
  319.4 5.4 %fusion.15 = f32[2,32,96,128]{3,2,1,0:T(8,128)S(1)} fusion(f32[2,128,32,128]{3,1,2,0:T(8,128)S(1)} %copy-done.3, f32[2,96,32,128]{3,2,1,0:T(8,128)S(1)} %add_bitcast_fusion.1), kind=kOutput, calls=%fused_computation.37 | convolution fusion | flops 603979776 | bytes 10485760 | tf_op jit(solution)/shard_map/kqpb,krpb->krqp/dot_general | solution.py:24
  324.9 5.4 %fusion.17 = f32[2,32,96,128]{3,2,1,0:T(8,128)S(1)} fusion(f32[2,128,32,128]{3,1,2,0:T(8,128)S(1)} %copy-done.1, f32[2,96,32,128]{3,2,1,0:T(8,128)S(1)} %add_bitcast_fusion.1), kind=kOutput, calls=%fused_computation.39 | convolution fusion | flops 603979776 | bytes 10485760 | tf_op jit(solution)/shard_map/kqpb,krpb->krqp/dot_general | solution.py:24
  332.0 5.6 %subtract_bitcast_fusion = f32[2,96,128,32]{2,1,3,0:T(8,128)S(1)} fusion(f32[2,32,96,128]{3,2,1,0:T(8,128)S(1)} %fusion.17, f32[2,128,32,128]{3,1,2,0:T(8,128)S(1)} %copy-done.3, f32[2,96,32,128]{3,2,1,0:T(8,128)S(1)} %subtract_bitcast_fusion.1), kind=kOutput, calls=%fused_computation.30 | convolution fusion | flops 604766208 | bytes 13631488 | tf_op jit(solution)/shard_map/kqpb,krpb->krqp/dot_general | solution.py:24
  337.6 7.5 %sqrt_reduce_fusion = (f32[2]{0:T(128)S(1)}, f32[2,96,128,32]{2,1,3,0:T(8,128)}) fusion(f32[2,96,128,32]{2,1,3,0:T(8,128)S(1)} %subtract_bitcast_fusion, f32[2,32,96,128]{3,2,1,0:T(8,128)S(1)} %fusion.15, f32[2,128,32,128]{3,1,2,0:T(8,128)S(1)} %copy-done.1, f32[2,96,32,128]{3,2,1,0:T(8,128)S(1)} %subtract_bitcast_fusion.1), kind=kOutput, calls=%fused_computation.28 | convolution fusion | flops 607911936 | bytes 16777224 | tf_op jit(solution)/shard_map/kqpb,krpb->krqp/dot_general | solution.py:24
  345.8 4.8 %all-to-all-start.5 = ((f32[128,1,2]{2,1,0:T(1,128)}), f32[128,1,2]{2,1,0:T(1,128)S(1)}, u32[]{:S(2)}, u32[]{:S(2)}) async-start(f32[128,1,2]{2,1,0:T(1,128)} %broadcast_in_dim.40), calls=%async_computation.5 | async-start | bytes 131072 | tf_op jit(solution)/shard_map/all_to_all | solution.py:172
  354.6 5.4 %copy.368.real_ref = f32[2,96,4096]{2,1,0:T(8,128)} copy(f32[2,96,4096]{1,2,0:T(8,128)} %bitcast.176) | data formatting | bytes 6291456 | tf_op jit(solution)/shard_map/reshape;reshape;reshape | solution.py:167
  363.3 5.3 %copy.369.imag_ref = f32[2,96,4096]{2,1,0:T(8,128)} copy(f32[2,96,4096]{1,2,0:T(8,128)} %bitcast.177) | data formatting | bytes 6291456 | tf_op jit(solution)/shard_map/reshape;reshape;reshape | solution.py:168
  369.3 9.2 %shard_map.37 = f32[2,2,96,4096]{3,2,1,0:T(8,128)} custom-call(f32[2]{0:T(128)} %reduce_max.19.peak_ref, s32[96,1]{1,0:T(8,128)} %add_select_fusion.9.parity_ref, f32[2,96,4096]{2,1,0:T(8,128)} %copy.368.real_ref, f32[2,96,4096]{2,1,0:T(8,128)} %copy.369.imag_ref), custom_call_target="tpu_custom_call" | custom-call | tf_op jit(solution)/shard_map/pallas_call | solution.py:206
  (125 shorter events, 124.9 us)
Async XLA Ops:
  4.8 4.8 %copy-start.17 = (s32[2,2]{1,0:T(2,128)S(1)}, s32[2,2]{1,0:T(2,128)}, u32[]{:S(2)}) copy-start(s32[2,2]{1,0:T(2,128)} %param.6) | copy-start | bytes 52
  4.8 54.4 %all-to-all-start = ((f32[2,8,64,1024]{3,2,0,1:T(8,128)}), f32[2,8,64,1024]{3,2,0,1:T(8,128)}, u32[]{:S(2)}, u32[]{:S(2)}) async-start(f32[2,8,64,1024]{3,2,0,1:T(8,128)} %copy.310), calls=%async_computation | async-start | bytes 8388608 | tf_op jit(solution)/shard_map/all_to_all | solution.py:108
  10.4 18.6 %copy-start.18 = (s32[128]{0:T(128)S(1)}, s32[128]{0:T(128)}, u32[]{:S(2)}) copy-start(s32[128]{0:T(128)} %param.7) | copy-start | bytes 1540
  64.4 8.6 %copy-start.4 = (f32[2,64,64,128]{3,2,1,0:T(8,128)}, f32[2,64,64,128]{3,2,1,0:T(8,128)S(1)}, u32[]{:S(2)}) copy-start(f32[2,64,64,128]{3,2,1,0:T(8,128)S(1)} %fusion.23) | copy-start | bytes 12582916
  66.5 6.5 %copy-start.6 = (f32[2,64,64,128]{3,2,1,0:T(8,128)}, f32[2,64,64,128]{3,2,1,0:T(8,128)S(1)}, u32[]{:S(2)}) copy-start(f32[2,64,64,128]{3,2,1,0:T(8,128)S(1)} %fusion.26) | copy-start | bytes 12582916
  66.5 6.5 %copy-start.10 = (f32[2,32,64,128]{3,1,2,0:T(8,128)S(1)}, f32[2,32,64,128]{3,1,2,0:T(8,128)}, u32[]{:S(2)}) copy-start(f32[2,32,64,128]{3,1,2,0:T(8,128)} %get-tuple-element.19) | copy-start | bytes 6291460
  85.8 29.5 %all-to-all-start.1 = ((f32[128,1,2048]{2,1,0:T(1,128)}), f32[128,1,2048]{2,1,0:T(1,128)S(1)}, u32[]{:S(2)}, u32[]{:S(2)}) async-start(f32[128,1,2048]{2,1,0:T(1,128)} %reshape.323), calls=%async_computation.1 | async-start | bytes 2097152 | tf_op jit(solution)/shard_map/all_to_all | solution.py:123
  95.4 9.3 %copy-start.5 = (f32[2,64,64,128]{3,2,1,0:T(8,128)S(1)}, f32[2,64,64,128]{3,2,1,0:T(8,128)}, u32[]{:S(2)}) copy-start(f32[2,64,64,128]{3,2,1,0:T(8,128)} %copy-done.4) | copy-start | bytes 12582916
  115.3 10.6 %copy-start.16 = (f32[128,1,2048]{2,1,0:T(1,128)}, f32[128,1,2048]{2,1,0:T(1,128)S(1)}, u32[]{:S(2)}) copy-start(f32[128,1,2048]{2,1,0:T(1,128)S(1)} %all-to-all-done.1) | copy-start | bytes 3145732
  115.3 29.0 %all-to-all-start.2 = ((f32[128,1,2048]{2,1,0:T(1,128)}), f32[128,1,2048]{2,1,0:T(1,128)}, u32[]{:S(2)}, u32[]{:S(2)}) async-start(f32[128,1,2048]{2,1,0:T(1,128)} %reshape.325), calls=%async_computation.2 | async-start | bytes 2097152 | tf_op jit(solution)/shard_map/all_to_all | solution.py:124
  153.4 2.7 copy-start.7
  166.1 2.7 copy-start.14
  171.3 3.7 copy-start.9
  178.0 1.8 copy-start.8
  179.8 1.8 copy-start.13
  184.5 2.2 copy-start.2
  190.1 3.8 %copy-start = (f32[2,128,32,128]{3,1,2,0:T(8,128)S(1)}, f32[2,128,32,128]{3,1,2,0:T(8,128)}, u32[]{:S(2)}) copy-start(f32[2,128,32,128]{3,1,2,0:T(8,128)} %get-tuple-element.29) | copy-start | bytes 12582916
  220.1 5.6 %copy-start.15 = (f32[384,2,16,32]{0,3,2,1:T(8,128)S(1)}, f32[384,2,16,32]{0,3,2,1:T(8,128)}, u32[]{:S(2)}) copy-start(f32[384,2,16,32]{0,3,2,1:T(8,128)} %copy.353) | copy-start | bytes 4718596
  239.5 35.0 %all-to-all-start.3 = ((f32[128,2,16,96]{3,2,1,0:T(8,128)}), f32[128,2,16,96]{3,2,1,0:T(8,128)S(1)}, u32[]{:S(2)}, u32[]{:S(2)}) async-start(f32[128,2,16,96]{3,2,1,0:T(8,128)} %copy.347), calls=%async_computation.3 | async-start | bytes 4194304 | tf_op jit(solution)/shard_map/all_to_all | solution.py:159
  274.5 35.7 %all-to-all-start.4 = ((f32[128,2,16,96]{3,2,1,0:T(8,128)}), f32[128,2,16,96]{3,2,1,0:T(8,128)}, u32[]{:S(2)}, u32[]{:S(2)}) async-start(f32[128,2,16,96]{3,2,1,0:T(8,128)} %copy.355), calls=%async_computation.4 | async-start | bytes 4194304 | tf_op jit(solution)/shard_map/all_to_all | solution.py:160
  315.8 3.6 copy-start.3
  319.4 5.5 %copy-start.1 = (f32[2,128,32,128]{3,1,2,0:T(8,128)S(1)}, f32[2,128,32,128]{3,1,2,0:T(8,128)}, u32[]{:S(2)}) copy-start(f32[2,128,32,128]{3,1,2,0:T(8,128)} %get-tuple-element.29) | copy-start | bytes 12582916
  324.9 5.4 %copy-start.12 = (f32[2,96,128,32]{2,3,1,0:T(8,128)S(1)}, f32[2,96,128,32]{2,3,1,0:T(8,128)}, u32[]{:S(2)}) copy-start(f32[2,96,128,32]{2,3,1,0:T(8,128)} %fusion.102) | copy-start | bytes 9437188
  345.8 22.9 %all-to-all-start.5 = ((f32[128,1,2]{2,1,0:T(1,128)}), f32[128,1,2]{2,1,0:T(1,128)S(1)}, u32[]{:S(2)}, u32[]{:S(2)}) async-start(f32[128,1,2]{2,1,0:T(1,128)} %broadcast_in_dim.40), calls=%async_computation.5 | async-start | bytes 131072 | tf_op jit(solution)/shard_map/all_to_all | solution.py:172
  354.6 5.4 %copy-start.11 = (f32[2,96,128,32]{2,1,3,0:T(8,128)S(1)}, f32[2,96,128,32]{2,1,3,0:T(8,128)}, u32[]{:S(2)}) copy-start(f32[2,96,128,32]{2,1,3,0:T(8,128)} %get-tuple-element.55) | copy-start | bytes 9437188

commit v12 on v11

--- a/solution.py
+++ b/solution.py
@@ -181,8 +181,9 @@
 
 def encode_kernel(peak_ref, parity_ref, real_ref, imag_ref, out_ref):
     inverse = 1.0 / (headroom * peak_ref[pl.program_id(0)] + epsilon)
-    unit_real = real_ref[0] * inverse
-    unit_imag = imag_ref[0] * inverse
+    _, coarse, fine, rows = real_ref.shape
+    unit_real = real_ref[0].reshape(coarse * fine, rows).T * inverse
+    unit_imag = imag_ref[0].reshape(coarse * fine, rows).T * inverse
     square = unit_real * unit_real + unit_imag * unit_imag
     height = jnp.sqrt(1.0 - square)
     shrink = lax.rsqrt(square + softness) * height
@@ -200,21 +201,27 @@
 
 def encode_slots(peak, parity, field_real, field_imag):
     holo_count, rows, width = field_real.shape
-    split = 2 if rows % 16 == 0 else 1
-    block = rows // split
-    field_spec = pl.BlockSpec((1, block, width), lambda k, j: (k, j, 0))
+    fine = P_SIZE // radix
+    coarse = width // fine
+    part = 16
+    split = coarse // part
+    field_spec = pl.BlockSpec((1, part, fine, rows), lambda k, j: (k, j, 0, 0))
+
+    def coarse_major(field):
+        return jnp.transpose(field.reshape(holo_count, rows, coarse, fine), (0, 2, 3, 1))
+
     return pl.pallas_call(
         encode_kernel,
         out_shape=jax.ShapeDtypeStruct((holo_count, 2, rows, width), jnp.float32),
         grid=(holo_count, split),
         in_specs=[
             pl.BlockSpec(memory_space=pltpu.SMEM),
-            pl.BlockSpec((block, 1), lambda k, j: (j, 0)),
+            pl.BlockSpec((rows, 1), lambda k, j: (0, 0)),
             field_spec,
             field_spec,
         ],
-        out_specs=pl.BlockSpec((1, 2, block, width), lambda k, j: (k, 0, j, 0)),
-    )(peak, parity, field_real, field_imag)
+        out_specs=pl.BlockSpec((1, 2, rows, part * fine), lambda k, j: (k, 0, 0, j)),
+    )(peak, parity, coarse_major(field_real), coarse_major(field_imag))
 
 
 def solution(mesh):

time: 384 us -> 405 us (1.055)
  waiting for transfers between devices: 64.4 us -> 73 us
  other arithmetic: 43.6 us -> 52 us
  Pallas kernels: 9.16 us -> 14 us
    another operation x2 -> x0, local copies, waits for them, and re-layouts: 10.7 us -> none  [the longest x1 5.43 us: body(): field_real = field_real.reshape(holo_count, slot_rows, P_SIZE)]
    all_to_all x1, waiting for transfers between devices: 0.01 us -> 8.61 us  [body(): lax.all_to_all(every, ('row', 'col'), 0, 0, tiled=True)]
    dot_general x0 -> x2, local copies, waits for them, and re-layouts: none -> 8.56 us  [contract(): jnp.einsum(form, left, right, precision=lax.Precision.HIGH, preferred_ele...]
    add x0 -> x1, other arithmetic: none -> 8.39 us  [finish(): contract('kqpb,krpb->krqp', outer_cos, mid_imag)]
    pallas_call x1, Pallas kernels: 9.16 us -> 14 us  [encode_slots(): pl.pallas_call(encode_kernel, out_shape=jax.ShapeDtypeStruct((holo_count,...]
  transfers between devices with their start and end apart: 6 -> 6, of which waited for: 4 -> 5; matrix products, arithmetic and copies ran while one was open for 27% -> 21% of each run, Pallas kernels for 0% -> 0%
where the time goes in v12:
time: 405 us; the launch traced here: 400 us
  local copies, waits for them, and re-layouts  116 us (29%)
  matrix products  104 us (26%)
  waiting for transfers between devices  73 us (18%)
  other arithmetic  52 us (13%)
  starting transfers between devices  39.6 us (10%)
  Pallas kernels  14 us (3%)
    dot_general x30, matrix products, contract(): jnp.einsum(form, left, right, precision=lax.Precision.HIGH, preferred_ele...  104 us
    sin x2, other arithmetic, make_tables(): jnp.sin(outer_angle).reshape(shape_four)  29.8 us
    gather x4, local copies, waits for them, and re-layouts, pack(): picked = jnp.take(grouped, source, axis=2) * filled[None, None, :, None]  21.6 us
    all_to_all x1, waiting for transfers between devices, body(): lax.all_to_all(send_imag, ('row', 'col'), split_axis=0, concat_axis=2, ti...  19.8 us
    all_to_all x1, waiting for transfers between devices, body(): lax.all_to_all(blocks, 'col', split_axis=1, concat_axis=1, tiled=True)  18.4 us
    all_to_all x1, waiting for transfers between devices, body(): lax.all_to_all(send_real, ('row', 'col'), split_axis=0, concat_axis=2, ti...  15.8 us
    pallas_call x1, Pallas kernels, encode_slots(): pl.pallas_call(encode_kernel, out_shape=jax.ShapeDtypeStruct((holo_count,...  14 us
    unnamed x43, local copies, waits for them, and re-layouts  12.6 us
  transfers between devices with their start and end apart: 6, of which 5 were waited for; matrix products, arithmetic and copies ran while one was open for 21% of the time, Pallas kernels for 0%

profile of v12, /device:TPU:0, one launch (start us, length us, event | category | flops | bytes accessed | tf_op | source)
XLA Modules:
  0.0 399.8 jit_solution(5171079941972036231)
XLA Ops:
  0.0 4.8 %copy.312 = f32[2,8,64,1024]{3,2,0,1:T(8,128)} copy(f32[2,8,64,1024]{3,2,1,0:T(8,128)} %bitcast.185) | data formatting | bytes 8388608 | tf_op jit(solution)/shard_map/reshape | solution.py:107
  4.8 4.7 %all-to-all-start = ((f32[2,8,64,1024]{3,2,0,1:T(8,128)}), f32[2,8,64,1024]{3,2,0,1:T(8,128)}, u32[]{:S(2)}, u32[]{:S(2)}) async-start(f32[2,8,64,1024]{3,2,0,1:T(8,128)} %copy.312), calls=%async_computation | async-start | bytes 8388608 | tf_op jit(solution)/shard_map/all_to_all | solution.py:108
  10.4 18.6 %fusion.58 = (f32[2,32,64,128]{3,1,2,0:T(8,128)}, f32[2,32,64,128]{3,1,2,0:T(8,128)}, f32[2,32,64,128]{3,1,2,0:T(8,128)}, f32[2,32,64,128]{3,1,2,0:T(8,128)S(1)}) fusion(s32[128]{0:T(128)S(1)} %and_select_fusion.3, s32[2,32,64]{1,2,0:T(8,128)S(1)} %get-tuple-element.38, s32[2,32,64]{1,2,0:T(8,128)S(1)} %get-tuple-element.39), kind=kLoop, calls=%fused_computation.77 | loop fusion | flops 14680064 | bytes 8421888 | tf_op jit(solution)/shard_map/sin | solution.py:44
  29.6 11.2 %fusion.35 = (f32[2,128,32,128]{3,1,2,0:T(8,128)}, f32[2,128,32,128]{3,1,2,0:T(8,128)}) fusion(s32[128]{0:T(128)S(1)} %and_select_fusion, s32[128,32]{0,1:T(8,128)S(1)} %multiply_add_fusion), kind=kLoop, calls=%fused_computation.51 | loop fusion | flops 14680064 | bytes 8405504 | tf_op jit(solution)/shard_map/sin | solution.py:44
  40.8 18.4 %all-to-all-done = f32[2,8,64,1024]{3,2,0,1:T(8,128)} async-done(((f32[2,8,64,1024]{3,2,0,1:T(8,128)}), f32[2,8,64,1024]{3,2,0,1:T(8,128)}, u32[]{:S(2)}, u32[]{:S(2)}) %all-to-all-start) | async-done | bytes 4194336 | tf_op jit(solution)/shard_map/all_to_all | solution.py:108
  66.5 6.5 %fusion.9 = f32[64,2,64,32]{2,3,1,0:T(8,128)S(1)} fusion(f32[2,64,64,128]{3,2,1,0:T(8,128)S(1)} %fusion.26, f32[2,32,64,128]{3,1,2,0:T(8,128)S(1)} %get-tuple-element.21), kind=kOutput, calls=%fused_computation.17 | convolution fusion | flops 201326592 | bytes 7340032 | tf_op jit(solution)/shard_map/kqpb,krpb->qpkr/dot_general | solution.py:24
  73.0 6.5 %subtract_bitcast_fusion.2 = f32[32,64,2,64]{3,0,2,1:T(8,128)S(1)} fusion(f32[64,2,64,32]{2,3,1,0:T(8,128)S(1)} %fusion.9, f32[2,32,64,128]{3,1,2,0:T(8,128)S(1)} %copy-done.10, f32[2,64,64,128]{3,2,1,0:T(8,128)S(1)} %fusion.23), kind=kOutput, calls=%fused_computation.56 | convolution fusion | flops 201588736 | bytes 8388608 | tf_op jit(solution)/shard_map/kqpb,krpb->qpkr/dot_general | solution.py:24
  85.8 9.5 %all-to-all-start.1 = ((f32[128,1,2048]{2,1,0:T(1,128)}), f32[128,1,2048]{2,1,0:T(1,128)S(1)}, u32[]{:S(2)}, u32[]{:S(2)}) async-start(f32[128,1,2048]{2,1,0:T(1,128)} %reshape.323), calls=%async_computation.1 | async-start | bytes 2097152 | tf_op jit(solution)/shard_map/all_to_all | solution.py:123
  95.4 9.3 %fusion.7 = f32[64,2,64,32]{2,3,1,0:T(8,128)S(1)} fusion(f32[2,64,64,128]{3,2,1,0:T(8,128)} %copy-done.6, f32[2,32,64,128]{3,1,2,0:T(8,128)} %get-tuple-element.19), kind=kOutput, calls=%fused_computation.15 | convolution fusion | flops 201326592 | bytes 7340032 | tf_op jit(solution)/shard_map/kqpb,krpb->qpkr/dot_general | solution.py:24
  104.7 6.8 %add_bitcast_fusion.2 = f32[32,64,2,64]{3,0,2,1:T(8,128)S(1)} fusion(f32[64,2,64,32]{2,3,1,0:T(8,128)S(1)} %fusion.7, f32[2,32,64,128]{3,1,2,0:T(8,128)S(1)} %get-tuple-element.21, f32[2,64,64,128]{3,2,1,0:T(8,128)S(1)} %copy-done.5), kind=kOutput, calls=%fused_computation.55 | convolution fusion | flops 201588736 | bytes 8388608 | tf_op jit(solution)/shard_map/kqpb,krpb->qpkr/dot_general | solution.py:24
  115.3 10.3 %all-to-all-start.2 = ((f32[128,1,2048]{2,1,0:T(1,128)}), f32[128,1,2048]{2,1,0:T(1,128)}, u32[]{:S(2)}, u32[]{:S(2)}) async-start(f32[128,1,2048]{2,1,0:T(1,128)} %reshape.325), calls=%async_computation.2 | async-start | bytes 2097152 | tf_op jit(solution)/shard_map/all_to_all | solution.py:124
  133.9 10.4 %all-to-all-done.2 = f32[128,1,2048]{2,1,0:T(1,128)} async-done(((f32[128,1,2048]{2,1,0:T(1,128)}), f32[128,1,2048]{2,1,0:T(1,128)}, u32[]{:S(2)}, u32[]{:S(2)}) %all-to-all-start.2) | async-done | bytes 1048608 | tf_op jit(solution)/shard_map/all_to_all | solution.py:124
  204.1 5.3 %gather_fusion.1 = f32[384,2,16,32]{3,2,1,0:T(8,128)} fusion(f32[2,16,128,32]{3,1,2,0:T(8,128)} %copy.354, s32[1024]{0:T(1024)S(1)} %pad_clamp_fusion), kind=kCustom, calls=%fused_computation.1.clone | custom fusion | bytes 3147264 | tf_op jit(solution)/shard_map/jit(_take)/gather | solution.py:154
  209.4 6.4 %copy.355 = f32[384,2,16,32]{0,3,2,1:T(8,128)} copy(f32[384,2,16,32]{3,2,1,0:T(8,128)} %gather_fusion.1) | data formatting | bytes 3145728 | tf_op jit(solution)/shard_map/jit(_take)/gather | solution.py:154
  220.1 5.6 %copy.347 = f32[384,2,16,32]{0,3,2,1:T(8,128)S(1)} copy(f32[384,2,16,32]{3,2,1,0:T(8,128)} %gather_fusion) | data formatting | bytes 3145728 | tf_op jit(solution)/shard_map/jit(_take)/gather | solution.py:154
  227.8 5.0 %copy.348 = f32[2,16,384,32]{3,2,1,0:T(8,128)} copy(f32[2,16,384,32]{2,3,1,0:T(8,128)} %get-tuple-element.47) | data formatting | bytes 3145728 | tf_op jit(solution)/shard_map/mul | solution.py:154
  239.5 4.6 %all-to-all-start.3 = ((f32[128,2,16,96]{3,2,1,0:T(8,128)}), f32[128,2,16,96]{3,2,1,0:T(8,128)S(1)}, u32[]{:S(2)}, u32[]{:S(2)}) async-start(f32[128,2,16,96]{3,2,1,0:T(8,128)} %copy.349), calls=%async_computation.3 | async-start | bytes 4194304 | tf_op jit(solution)/shard_map/all_to_all | solution.py:159
  244.2 5.0 %copy.356 = f32[2,16,384,32]{3,2,1,0:T(8,128)} copy(f32[2,16,384,32]{2,3,1,0:T(8,128)} %get-tuple-element.46) | data formatting | bytes 3145728 | tf_op jit(solution)/shard_map/mul | solution.py:154
  249.2 5.3 %reshape.283 = f32[2,16,128,96]{3,2,1,0:T(8,128)} reshape(f32[2,16,384,32]{3,2,1,0:T(8,128)} %copy.356) | data formatting | bytes 3145728 | tf_op jit(solution)/shard_map/reshape | solution.py:155
  258.7 15.8 %all-to-all-done.3 = f32[128,2,16,96]{3,2,1,0:T(8,128)S(1)} async-done(((f32[128,2,16,96]{3,2,1,0:T(8,128)}), f32[128,2,16,96]{3,2,1,0:T(8,128)S(1)}, u32[]{:S(2)}, u32[]{:S(2)}) %all-to-all-start.3) | async-done | bytes 1572896 | tf_op jit(solution)/shard_map/all_to_all | solution.py:159
  274.5 5.8 %all-to-all-start.4 = ((f32[128,2,16,96]{3,2,1,0:T(8,128)}), f32[128,2,16,96]{3,2,1,0:T(8,128)}, u32[]{:S(2)}, u32[]{:S(2)}) async-start(f32[128,2,16,96]{3,2,1,0:T(8,128)} %copy.357), calls=%async_computation.4 | async-start | bytes 4194304 | tf_op jit(solution)/shard_map/all_to_all | solution.py:160
  290.5 19.8 %all-to-all-done.4 = f32[128,2,16,96]{3,2,1,0:T(8,128)} async-done(((f32[128,2,16,96]{3,2,1,0:T(8,128)}), f32[128,2,16,96]{3,2,1,0:T(8,128)}, u32[]{:S(2)}, u32[]{:S(2)}) %all-to-all-start.4) | async-done | bytes 1572896 | tf_op jit(solution)/shard_map/all_to_all | solution.py:160
  319.4 5.4 %fusion.17 = f32[2,32,96,128]{3,2,1,0:T(8,128)S(1)} fusion(f32[2,128,32,128]{3,1,2,0:T(8,128)S(1)} %copy-done.3, f32[2,96,32,128]{3,2,1,0:T(8,128)S(1)} %add_bitcast_fusion), kind=kOutput, calls=%fused_computation.37 | convolution fusion | flops 603979776 | bytes 10485760 | tf_op jit(solution)/shard_map/kqpb,krpb->krqp/dot_general | solution.py:24
  324.9 7.1 %fusion.15 = f32[2,32,96,128]{3,2,1,0:T(8,128)} fusion(f32[2,128,32,128]{3,1,2,0:T(8,128)S(1)} %copy-done.1, f32[2,96,32,128]{3,2,1,0:T(8,128)S(1)} %add_bitcast_fusion), kind=kOutput, calls=%fused_computation.35 | convolution fusion | flops 603979776 | bytes 10485760 | tf_op jit(solution)/shard_map/kqpb,krpb->krqp/dot_general | solution.py:24
  333.5 7.3 %fusion.19 = f32[2,32,96,128]{3,2,1,0:T(8,128)} fusion(f32[2,128,32,128]{3,1,2,0:T(8,128)S(1)} %copy-done.3, f32[2,96,32,128]{3,2,1,0:T(8,128)S(1)} %subtract_bitcast_fusion), kind=kOutput, calls=%fused_computation.39 | convolution fusion | flops 603979776 | bytes 10485760 | tf_op jit(solution)/shard_map/kqpb,krpb->krqp/dot_general | solution.py:24
  340.7 7.1 %fusion.41 = f32[2,32,96,128]{3,2,1,0:T(8,128)} fusion(f32[2,32,96,128]{3,2,1,0:T(8,128)S(1)} %fusion.17, f32[2,128,32,128]{3,1,2,0:T(8,128)S(1)} %copy-done.1, f32[2,96,32,128]{3,2,1,0:T(8,128)S(1)} %subtract_bitcast_fusion), kind=kOutput, calls=%fused_computation.61 | convolution fusion | flops 604766208 | bytes 13631488 | tf_op jit(solution)/shard_map/kqpb,krpb->krqp/dot_general | solution.py:24
  347.8 5.4 %copy.362 = f32[2,32,96,128]{2,1,3,0:T(8,128)} copy(f32[2,32,96,128]{3,2,1,0:T(8,128)} %fusion.41) | data formatting | bytes 6291456 | tf_op jit(solution)/shard_map/sub | solution.py:66
  356.5 5.2 %copy.367 = f32[2,32,96,128]{2,1,3,0:T(8,128)} copy(f32[2,32,96,128]{3,2,1,0:T(8,128)} %fusion.19) | data formatting | bytes 6291456 | tf_op jit(solution)/shard_map/kqpb,krpb->krqp/dot_general | solution.py:24
  361.7 8.4 %add_bitcast_fusion.3 = (f32[2,128,32,96]{3,2,1,0:T(8,128)}, f32[2]{0:T(128)S(1)}) fusion(f32[2,32,96,128]{2,1,3,0:T(8,128)} %copy.366, f32[2,32,96,128]{2,1,3,0:T(8,128)} %copy.367, f32[2,32,96,128]{2,1,3,0:T(8,128)} %copy.362), kind=kLoop, calls=%fused_computation.62 | loop fusion | flops 3932158 | bytes 12582920 | tf_op jit(solution)/shard_map/add | solution.py:69
  370.8 4.6 %all-to-all-start.5 = ((f32[128,1,2]{2,1,0:T(1,128)}), f32[128,1,2]{2,1,0:T(1,128)S(1)}, u32[]{:S(2)}, u32[]{:S(2)}) async-start(f32[128,1,2]{2,1,0:T(1,128)} %broadcast_in_dim.40), calls=%async_computation.5 | async-start | bytes 131072 | tf_op jit(solution)/shard_map/all_to_all | solution.py:172
  376.0 8.6 %all-to-all-done.5 = f32[128,1,2]{2,1,0:T(1,128)S(1)} async-done(((f32[128,1,2]{2,1,0:T(1,128)}), f32[128,1,2]{2,1,0:T(1,128)S(1)}, u32[]{:S(2)}, u32[]{:S(2)}) %all-to-all-start.5) | async-done | bytes 1056 | tf_op jit(solution)/shard_map/all_to_all | solution.py:172
  385.3 14.0 %shard_map.37 = f32[2,2,96,4096]{3,2,1,0:T(8,128)} custom-call(f32[2]{0:T(128)} %reduce_max.19.peak_ref, s32[96,1]{1,0:T(8,128)} %add_select_fusion.9.parity_ref, f32[2,128,32,96]{3,2,1,0:T(8,128)} %bitcast.171, f32[2,128,32,96]{3,2,1,0:T(8,128)} %get-tuple-element.32.imag_ref), custom_call_target="tpu_custom_call" | custom-call | tf_op jit(solution)/shard_map/pallas_call | solution.py:213
  (125 shorter events, 130.1 us)
Async XLA Ops:
  4.8 4.8 %copy-start.17 = (s32[2,2]{1,0:T(2,128)S(1)}, s32[2,2]{1,0:T(2,128)}, u32[]{:S(2)}) copy-start(s32[2,2]{1,0:T(2,128)} %param.6) | copy-start | bytes 52
  4.8 54.4 %all-to-all-start = ((f32[2,8,64,1024]{3,2,0,1:T(8,128)}), f32[2,8,64,1024]{3,2,0,1:T(8,128)}, u32[]{:S(2)}, u32[]{:S(2)}) async-start(f32[2,8,64,1024]{3,2,0,1:T(8,128)} %copy.312), calls=%async_computation | async-start | bytes 8388608 | tf_op jit(solution)/shard_map/all_to_all | solution.py:108
  10.4 18.6 %copy-start.18 = (s32[128]{0:T(128)S(1)}, s32[128]{0:T(128)}, u32[]{:S(2)}) copy-start(s32[128]{0:T(128)} %param.7) | copy-start | bytes 1540
  64.4 8.6 %copy-start.4 = (f32[2,64,64,128]{3,2,1,0:T(8,128)}, f32[2,64,64,128]{3,2,1,0:T(8,128)S(1)}, u32[]{:S(2)}) copy-start(f32[2,64,64,128]{3,2,1,0:T(8,128)S(1)} %fusion.23) | copy-start | bytes 12582916
  66.5 6.5 %copy-start.6 = (f32[2,64,64,128]{3,2,1,0:T(8,128)}, f32[2,64,64,128]{3,2,1,0:T(8,128)S(1)}, u32[]{:S(2)}) copy-start(f32[2,64,64,128]{3,2,1,0:T(8,128)S(1)} %fusion.26) | copy-start | bytes 12582916
  66.5 6.5 %copy-start.10 = (f32[2,32,64,128]{3,1,2,0:T(8,128)S(1)}, f32[2,32,64,128]{3,1,2,0:T(8,128)}, u32[]{:S(2)}) copy-start(f32[2,32,64,128]{3,1,2,0:T(8,128)} %get-tuple-element.19) | copy-start | bytes 6291460
  85.8 29.5 %all-to-all-start.1 = ((f32[128,1,2048]{2,1,0:T(1,128)}), f32[128,1,2048]{2,1,0:T(1,128)S(1)}, u32[]{:S(2)}, u32[]{:S(2)}) async-start(f32[128,1,2048]{2,1,0:T(1,128)} %reshape.323), calls=%async_computation.1 | async-start | bytes 2097152 | tf_op jit(solution)/shard_map/all_to_all | solution.py:123
  95.4 9.3 %copy-start.5 = (f32[2,64,64,128]{3,2,1,0:T(8,128)S(1)}, f32[2,64,64,128]{3,2,1,0:T(8,128)}, u32[]{:S(2)}) copy-start(f32[2,64,64,128]{3,2,1,0:T(8,128)} %copy-done.4) | copy-start | bytes 12582916
  115.3 10.6 %copy-start.16 = (f32[128,1,2048]{2,1,0:T(1,128)}, f32[128,1,2048]{2,1,0:T(1,128)S(1)}, u32[]{:S(2)}) copy-start(f32[128,1,2048]{2,1,0:T(1,128)S(1)} %all-to-all-done.1) | copy-start | bytes 3145732
  115.3 29.0 %all-to-all-start.2 = ((f32[128,1,2048]{2,1,0:T(1,128)}), f32[128,1,2048]{2,1,0:T(1,128)}, u32[]{:S(2)}, u32[]{:S(2)}) async-start(f32[128,1,2048]{2,1,0:T(1,128)} %reshape.325), calls=%async_computation.2 | async-start | bytes 2097152 | tf_op jit(solution)/shard_map/all_to_all | solution.py:124
  153.5 2.7 copy-start.7
  166.1 2.7 copy-start.14
  171.3 3.7 copy-start.9
  178.0 1.8 copy-start.8
  179.8 1.8 copy-start.13
  184.5 2.2 copy-start
  190.1 3.8 copy-start.2
  220.1 5.6 %copy-start.15 = (f32[384,2,16,32]{0,3,2,1:T(8,128)S(1)}, f32[384,2,16,32]{0,3,2,1:T(8,128)}, u32[]{:S(2)}) copy-start(f32[384,2,16,32]{0,3,2,1:T(8,128)} %copy.355) | copy-start | bytes 4718596
  239.5 35.0 %all-to-all-start.3 = ((f32[128,2,16,96]{3,2,1,0:T(8,128)}), f32[128,2,16,96]{3,2,1,0:T(8,128)S(1)}, u32[]{:S(2)}, u32[]{:S(2)}) async-start(f32[128,2,16,96]{3,2,1,0:T(8,128)} %copy.349), calls=%async_computation.3 | async-start | bytes 4194304 | tf_op jit(solution)/shard_map/all_to_all | solution.py:159
  274.5 35.7 %all-to-all-start.4 = ((f32[128,2,16,96]{3,2,1,0:T(8,128)}), f32[128,2,16,96]{3,2,1,0:T(8,128)}, u32[]{:S(2)}, u32[]{:S(2)}) async-start(f32[128,2,16,96]{3,2,1,0:T(8,128)} %copy.357), calls=%async_computation.4 | async-start | bytes 4194304 | tf_op jit(solution)/shard_map/all_to_all | solution.py:160
  315.8 3.6 copy-start.3
  319.4 5.5 %copy-start.1 = (f32[2,128,32,128]{3,1,2,0:T(8,128)S(1)}, f32[2,128,32,128]{3,1,2,0:T(8,128)}, u32[]{:S(2)}) copy-start(f32[2,128,32,128]{3,1,2,0:T(8,128)} %get-tuple-element.28) | copy-start | bytes 12582916
  324.9 7.1 %copy-start.12 = (f32[2,96,128,32]{2,3,1,0:T(8,128)S(1)}, f32[2,96,128,32]{2,3,1,0:T(8,128)}, u32[]{:S(2)}) copy-start(f32[2,96,128,32]{2,3,1,0:T(8,128)} %fusion.101) | copy-start | bytes 9437188
  347.8 5.4 %copy-start.11 = (f32[2,32,96,128]{3,2,1,0:T(8,128)S(1)}, f32[2,32,96,128]{3,2,1,0:T(8,128)}, u32[]{:S(2)}) copy-start(f32[2,32,96,128]{3,2,1,0:T(8,128)} %fusion.15) | copy-start | bytes 9437188
  370.8 13.8 %all-to-all-start.5 = ((f32[128,1,2]{2,1,0:T(1,128)}), f32[128,1,2]{2,1,0:T(1,128)S(1)}, u32[]{:S(2)}, u32[]{:S(2)}) async-start(f32[128,1,2]{2,1,0:T(1,128)} %broadcast_in_dim.40), calls=%async_computation.5 | async-start | bytes 131072 | tf_op jit(solution)/shard_map/all_to_all | solution.py:172

commit v13 on v11

--- a/solution.py
+++ b/solution.py
@@ -156,16 +156,19 @@
 
     send_real = pack(lift_real)
     send_imag = pack(lift_imag)
-    piece_real = lax.all_to_all(send_real, ("row", "col"), split_axis=0, concat_axis=2, tiled=True)
-    piece_imag = lax.all_to_all(send_imag, ("row", "col"), split_axis=0, concat_axis=2, tiled=True)
-    single, lead, width, count = piece_real.shape
-    rows_real = jnp.swapaxes(piece_real.reshape(lead, width, count), 1, 2)
-    rows_imag = jnp.swapaxes(piece_imag.reshape(lead, width, count), 1, 2)
+    dense = (devices, 1, holo_count * share * slot_rows)
+    piece_real = lax.all_to_all(send_real.reshape(dense), ("row", "col"), 0, 0, tiled=True)
+    piece_imag = lax.all_to_all(send_imag.reshape(dense), ("row", "col"), 0, 0, tiled=True)
+
+    def unpack(piece):
+        piece = piece.reshape(devices, holo_count, share, slot_rows)
+        return jnp.transpose(piece, (1, 3, 0, 2)).reshape(holo_count, slot_rows, devices * share)
+
+    rows_real = unpack(piece_real)
+    rows_imag = unpack(piece_imag)
     out_real, out_imag = transform(rows_real, rows_imag, table_p)
-    field_real = out_real.reshape(single, lead, count, P_SIZE)
-    field_imag = out_imag.reshape(single, lead, count, P_SIZE)
-    field_real = field_real.reshape(holo_count, slot_rows, P_SIZE)
-    field_imag = field_imag.reshape(holo_count, slot_rows, P_SIZE)
+    field_real = out_real.reshape(holo_count, slot_rows, P_SIZE)
+    field_imag = out_imag.reshape(holo_count, slot_rows, P_SIZE)
     magnitude = jnp.sqrt(field_real * field_real + field_imag * field_imag)
     local_peak = jnp.max(magnitude, axis=(1, 2))
     every = jnp.broadcast_to(local_peak[None, :], (devices, holo_count))

time: 384 us -> 377 us (0.982)
  waiting for transfers between devices: 64.4 us -> 49.4 us
  local copies, waits for them, and re-layouts: 120 us -> 128 us
    reshape x2 -> x4, local copies, waits for them, and re-layouts: 4.47 us -> 19.7 us  [the longest x1 5.44 us: finish(): out_real.reshape(batch, rows, count)]
    all_to_all x2, waiting for transfers between devices: 35.6 us -> 20.6 us  [the longest x1 10.5 us: body(): lax.all_to_all(send_imag.reshape(dense), ('row', 'col'), 0, 0, tiled=True)]
    another operation x2 -> x0, local copies, waits for them, and re-layouts: 10.7 us -> none  [the longest x1 5.43 us: body(): field_real = field_real.reshape(holo_count, slot_rows, P_SIZE)]
    transpose x0 -> x2, local copies, waits for them, and re-layouts: none -> 3.89 us  [unpack(): jnp.transpose(piece, (1, 3, 0, 2))]
    unnamed x43 -> x45, local copies, waits for them, and re-layouts: 12.6 us -> 12.6 us
  transfers between devices with their start and end apart: 6 -> 6, of which waited for: 4 -> 4; matrix products, arithmetic and copies ran while one was open for 27% -> 28% of each run, Pallas kernels for 0% -> 0%
where the time goes in v13:
time: 377 us; the launch traced here: 372 us
  local copies, waits for them, and re-layouts  128 us (34%)
  matrix products  101 us (27%)
  waiting for transfers between devices  49.4 us (13%)
  other arithmetic  43.6 us (12%)
  starting transfers between devices  39.8 us (11%)
  Pallas kernels  9.16 us (2%)
    dot_general x30, matrix products, contract(): jnp.einsum(form, left, right, precision=lax.Precision.HIGH, preferred_ele...  101 us
    sin x2, other arithmetic, make_tables(): jnp.sin(outer_angle).reshape(shape_four)  29.8 us
    gather x4, local copies, waits for them, and re-layouts, pack(): picked = jnp.take(grouped, source, axis=2) * filled[None, None, :, None]  21.6 us
    all_to_all x1, waiting for transfers between devices, body(): lax.all_to_all(blocks, 'col', split_axis=1, concat_axis=1, tiled=True)  18.3 us
    unnamed x45, local copies, waits for them, and re-layouts  12.6 us
    all_to_all x1, waiting for transfers between devices, body(): lax.all_to_all(send_imag.reshape(dense), ('row', 'col'), 0, 0, tiled=True)  10.5 us
    all_to_all x1, waiting for transfers between devices, body(): lax.all_to_all(spec_imag.reshape(send_shape), ('row', 'col'), 0, 0, tiled...  10.4 us
    all_to_all x1, starting transfers between devices, body(): lax.all_to_all(spec_imag.reshape(send_shape), ('row', 'col'), 0, 0, tiled...  10.3 us
  transfers between devices with their start and end apart: 6, of which 4 were waited for; matrix products, arithmetic and copies ran while one was open for 28% of the time, Pallas kernels for 0%

profile of v13, /device:TPU:0, one launch (start us, length us, event | category | flops | bytes accessed | tf_op | source)
XLA Modules:
  0.0 372.0 jit_solution(4041985286790039249)
XLA Ops:
  0.0 4.8 %copy.338 = f32[2,8,64,1024]{3,2,0,1:T(8,128)} copy(f32[2,8,64,1024]{3,2,1,0:T(8,128)} %bitcast.186) | data formatting | bytes 8388608 | tf_op jit(solution)/shard_map/reshape | solution.py:107
  4.8 4.7 %all-to-all-start = ((f32[2,8,64,1024]{3,2,0,1:T(8,128)}), f32[2,8,64,1024]{3,2,0,1:T(8,128)}, u32[]{:S(2)}, u32[]{:S(2)}) async-start(f32[2,8,64,1024]{3,2,0,1:T(8,128)} %copy.338), calls=%async_computation | async-start | bytes 8388608 | tf_op jit(solution)/shard_map/all_to_all | solution.py:108
  10.4 18.6 %fusion.59 = (f32[2,32,64,128]{3,1,2,0:T(8,128)}, f32[2,32,64,128]{3,1,2,0:T(8,128)}, f32[2,32,64,128]{3,1,2,0:T(8,128)}, f32[2,32,64,128]{3,1,2,0:T(8,128)S(1)}) fusion(s32[128]{0:T(128)S(1)} %and_select_fusion.3, s32[2,32,64]{1,2,0:T(8,128)S(1)} %get-tuple-element.36, s32[2,32,64]{1,2,0:T(8,128)S(1)} %get-tuple-element.37), kind=kLoop, calls=%fused_computation.77 | loop fusion | flops 14680064 | bytes 8421888 | tf_op jit(solution)/shard_map/sin | solution.py:44
  29.6 11.2 %fusion.35 = (f32[2,128,32,128]{3,1,2,0:T(8,128)}, f32[2,128,32,128]{3,1,2,0:T(8,128)}) fusion(s32[128]{0:T(128)S(1)} %and_select_fusion, s32[128,32]{0,1:T(8,128)S(1)} %multiply_add_fusion), kind=kLoop, calls=%fused_computation.53 | loop fusion | flops 14680064 | bytes 8405504 | tf_op jit(solution)/shard_map/sin | solution.py:44
  40.9 18.3 %all-to-all-done = f32[2,8,64,1024]{3,2,0,1:T(8,128)} async-done(((f32[2,8,64,1024]{3,2,0,1:T(8,128)}), f32[2,8,64,1024]{3,2,0,1:T(8,128)}, u32[]{:S(2)}, u32[]{:S(2)}) %all-to-all-start) | async-done | bytes 4194336 | tf_op jit(solution)/shard_map/all_to_all | solution.py:108
  66.5 6.5 %fusion.9 = f32[64,2,64,32]{2,3,1,0:T(8,128)S(1)} fusion(f32[2,64,64,128]{3,2,1,0:T(8,128)S(1)} %fusion.26, f32[2,32,64,128]{3,1,2,0:T(8,128)S(1)} %get-tuple-element.21), kind=kOutput, calls=%fused_computation.16 | convolution fusion | flops 201326592 | bytes 7340032 | tf_op jit(solution)/shard_map/kqpb,krpb->qpkr/dot_general | solution.py:24
  73.0 6.5 %subtract_bitcast_fusion.3 = f32[32,64,2,64]{3,0,2,1:T(8,128)S(1)} fusion(f32[64,2,64,32]{2,3,1,0:T(8,128)S(1)} %fusion.9, f32[2,32,64,128]{3,1,2,0:T(8,128)S(1)} %copy-done.10, f32[2,64,64,128]{3,2,1,0:T(8,128)S(1)} %fusion.23), kind=kOutput, calls=%fused_computation.58 | convolution fusion | flops 201588736 | bytes 8388608 | tf_op jit(solution)/shard_map/kqpb,krpb->qpkr/dot_general | solution.py:24
  85.8 9.5 %all-to-all-start.1 = ((f32[128,1,2048]{2,1,0:T(1,128)}), f32[128,1,2048]{2,1,0:T(1,128)S(1)}, u32[]{:S(2)}, u32[]{:S(2)}) async-start(f32[128,1,2048]{2,1,0:T(1,128)} %reshape.329), calls=%async_computation.1 | async-start | bytes 2097152 | tf_op jit(solution)/shard_map/all_to_all | solution.py:123
  95.4 9.3 %fusion.7 = f32[64,2,64,32]{2,3,1,0:T(8,128)S(1)} fusion(f32[2,64,64,128]{3,2,1,0:T(8,128)} %copy-done.6, f32[2,32,64,128]{3,1,2,0:T(8,128)} %get-tuple-element.19), kind=kOutput, calls=%fused_computation.14 | convolution fusion | flops 201326592 | bytes 7340032 | tf_op jit(solution)/shard_map/kqpb,krpb->qpkr/dot_general | solution.py:24
  104.7 6.8 %add_bitcast_fusion.3 = f32[32,64,2,64]{3,0,2,1:T(8,128)S(1)} fusion(f32[64,2,64,32]{2,3,1,0:T(8,128)S(1)} %fusion.7, f32[2,32,64,128]{3,1,2,0:T(8,128)S(1)} %get-tuple-element.21, f32[2,64,64,128]{3,2,1,0:T(8,128)S(1)} %copy-done.5), kind=kOutput, calls=%fused_computation.57 | convolution fusion | flops 201588736 | bytes 8388608 | tf_op jit(solution)/shard_map/kqpb,krpb->qpkr/dot_general | solution.py:24
  115.3 10.3 %all-to-all-start.2 = ((f32[128,1,2048]{2,1,0:T(1,128)}), f32[128,1,2048]{2,1,0:T(1,128)}, u32[]{:S(2)}, u32[]{:S(2)}) async-start(f32[128,1,2048]{2,1,0:T(1,128)} %reshape.331), calls=%async_computation.2 | async-start | bytes 2097152 | tf_op jit(solution)/shard_map/all_to_all | solution.py:124
  133.9 10.4 %all-to-all-done.2 = f32[128,1,2048]{2,1,0:T(1,128)} async-done(((f32[128,1,2048]{2,1,0:T(1,128)}), f32[128,1,2048]{2,1,0:T(1,128)}, u32[]{:S(2)}, u32[]{:S(2)}) %all-to-all-start.2) | async-done | bytes 1048608 | tf_op jit(solution)/shard_map/all_to_all | solution.py:124
  144.3 4.3 %reduce.7 = f32[128,2048]{1,0:T(8,128)S(1)} reduce(f32[128,1,2048]{2,1,0:T(1,128)} %all-to-all-done.2, f32[]{:T(128)} %broadcast.451), dimensions={1}, to_apply=%all_to_all.21.reduce_sub_computation | reduce | bytes 2097156 | tf_op jit(solution)/shard_map/all_to_all | solution.py:124
  204.1 5.3 %gather_fusion.1 = f32[384,2,16,32]{3,2,1,0:T(8,128)} fusion(f32[2,16,128,32]{3,1,2,0:T(8,128)} %copy.382, s32[1024]{0:T(1024)S(1)} %pad_clamp_fusion), kind=kCustom, calls=%fused_computation.1.clone | custom fusion | bytes 3147264 | tf_op jit(solution)/shard_map/jit(_take)/gather | solution.py:154
  209.4 6.4 %copy.383 = f32[384,2,16,32]{0,3,2,1:T(8,128)} copy(f32[384,2,16,32]{3,2,1,0:T(8,128)} %gather_fusion.1) | data formatting | bytes 3145728 | tf_op jit(solution)/shard_map/jit(_take)/gather | solution.py:154
  215.8 4.3 %gather_fusion = f32[384,2,16,32]{3,2,1,0:T(8,128)} fusion(f32[2,16,128,32]{3,1,2,0:T(8,128)S(1)} %copy.372, s32[1024]{0:T(1024)S(1)} %pad_clamp_fusion), kind=kCustom, calls=%fused_computation.clone | custom fusion | bytes 3147264 | tf_op jit(solution)/shard_map/jit(_take)/gather | solution.py:154
  220.1 5.6 %copy.373 = f32[384,2,16,32]{0,3,2,1:T(8,128)S(1)} copy(f32[384,2,16,32]{3,2,1,0:T(8,128)} %gather_fusion) | data formatting | bytes 3145728 | tf_op jit(solution)/shard_map/jit(_take)/gather | solution.py:154
  227.9 5.0 %copy.374 = f32[2,16,384,32]{3,2,1,0:T(8,128)} copy(f32[2,16,384,32]{2,3,1,0:T(8,128)} %get-tuple-element.45) | data formatting | bytes 3145728 | tf_op jit(solution)/shard_map/mul | solution.py:154
  238.7 4.5 %copy.376 = f32[128,1,3072]{2,1,0:T(1,128)} copy(f32[128,1,3072]{0,2,1:T(8,128)} %bitcast.182) | data formatting | bytes 3145728 | tf_op jit(solution)/shard_map/reshape | solution.py:160
  243.1 5.8 %all-to-all-start.3 = ((f32[128,1,3072]{2,1,0:T(1,128)}), f32[128,1,3072]{2,1,0:T(1,128)}, u32[]{:S(2)}, u32[]{:S(2)}) async-start(f32[128,1,3072]{2,1,0:T(1,128)} %copy.376), calls=%async_computation.3 | async-start | bytes 3145728 | tf_op jit(solution)/shard_map/all_to_all | solution.py:160
  258.7 4.5 %copy.386 = f32[128,1,3072]{2,1,0:T(1,128)} copy(f32[128,1,3072]{0,2,1:T(8,128)} %bitcast.183) | data formatting | bytes 3145728 | tf_op jit(solution)/shard_map/reshape | solution.py:161
  263.2 10.1 %all-to-all-done.3 = f32[128,1,3072]{2,1,0:T(1,128)} async-done(((f32[128,1,3072]{2,1,0:T(1,128)}), f32[128,1,3072]{2,1,0:T(1,128)}, u32[]{:S(2)}, u32[]{:S(2)}) %all-to-all-start.3) | async-done | bytes 1572896 | tf_op jit(solution)/shard_map/all_to_all | solution.py:160
  273.3 4.6 %all-to-all-start.4 = ((f32[128,1,3072]{2,1,0:T(1,128)}), f32[128,1,3072]{2,1,0:T(1,128)S(1)}, u32[]{:S(2)}, u32[]{:S(2)}) async-start(f32[128,1,3072]{2,1,0:T(1,128)} %copy.386), calls=%async_computation.4 | async-start | bytes 3145728 | tf_op jit(solution)/shard_map/all_to_all | solution.py:161
  292.2 10.5 %all-to-all-done.4 = f32[128,1,3072]{2,1,0:T(1,128)S(1)} async-done(((f32[128,1,3072]{2,1,0:T(1,128)}), f32[128,1,3072]{2,1,0:T(1,128)S(1)}, u32[]{:S(2)}, u32[]{:S(2)}) %all-to-all-start.4) | async-done | bytes 1572896 | tf_op jit(solution)/shard_map/all_to_all | solution.py:161
  312.4 5.4 %fusion.15 = f32[2,32,96,128]{3,2,1,0:T(8,128)S(1)} fusion(f32[2,128,32,128]{3,1,2,0:T(8,128)S(1)} %copy-done.3, f32[2,96,32,128]{3,2,1,0:T(8,128)S(1)} %add_bitcast_fusion.1), kind=kOutput, calls=%fused_computation.37 | convolution fusion | flops 603979776 | bytes 10485760 | tf_op jit(solution)/shard_map/kqpb,krpb->krqp/dot_general | solution.py:24
  317.9 5.4 %fusion.17 = f32[2,32,96,128]{3,2,1,0:T(8,128)S(1)} fusion(f32[2,128,32,128]{3,1,2,0:T(8,128)S(1)} %copy-done.1, f32[2,96,32,128]{3,2,1,0:T(8,128)S(1)} %add_bitcast_fusion.1), kind=kOutput, calls=%fused_computation.39 | convolution fusion | flops 603979776 | bytes 10485760 | tf_op jit(solution)/shard_map/kqpb,krpb->krqp/dot_general | solution.py:24
  325.0 5.6 %subtract_bitcast_fusion = f32[2,96,128,32]{2,1,3,0:T(8,128)S(1)} fusion(f32[2,32,96,128]{3,2,1,0:T(8,128)S(1)} %fusion.17, f32[2,128,32,128]{3,1,2,0:T(8,128)S(1)} %copy-done.3, f32[2,96,32,128]{3,2,1,0:T(8,128)S(1)} %subtract_bitcast_fusion.1), kind=kOutput, calls=%fused_computation.30 | convolution fusion | flops 604766208 | bytes 13631488 | tf_op jit(solution)/shard_map/kqpb,krpb->krqp/dot_general | solution.py:24
  330.6 7.5 %sqrt_reduce_fusion = (f32[2]{0:T(128)S(1)}, f32[2,96,128,32]{2,1,3,0:T(8,128)}) fusion(f32[2,96,128,32]{2,1,3,0:T(8,128)S(1)} %subtract_bitcast_fusion, f32[2,32,96,128]{3,2,1,0:T(8,128)S(1)} %fusion.15, f32[2,128,32,128]{3,1,2,0:T(8,128)S(1)} %copy-done.1, f32[2,96,32,128]{3,2,1,0:T(8,128)S(1)} %subtract_bitcast_fusion.1), kind=kOutput, calls=%fused_computation.28 | convolution fusion | flops 607911936 | bytes 16777224 | tf_op jit(solution)/shard_map/kqpb,krpb->krqp/dot_general | solution.py:24
  338.7 4.8 %all-to-all-start.5 = ((f32[128,1,2]{2,1,0:T(1,128)}), f32[128,1,2]{2,1,0:T(1,128)S(1)}, u32[]{:S(2)}, u32[]{:S(2)}) async-start(f32[128,1,2]{2,1,0:T(1,128)} %broadcast_in_dim.40), calls=%async_computation.5 | async-start | bytes 131072 | tf_op jit(solution)/shard_map/all_to_all | solution.py:175
  347.6 5.4 %copy.402.real_ref = f32[2,96,4096]{2,1,0:T(8,128)} copy(f32[2,96,4096]{1,2,0:T(8,128)} %bitcast.170) | data formatting | bytes 6291456 | tf_op jit(solution)/shard_map/reshape | solution.py:73
  356.3 5.3 %copy.403.imag_ref = f32[2,96,4096]{2,1,0:T(8,128)} copy(f32[2,96,4096]{1,2,0:T(8,128)} %bitcast.171) | data formatting | bytes 6291456 | tf_op jit(solution)/shard_map/reshape | solution.py:73
  362.3 9.2 %shard_map.37 = f32[2,2,96,4096]{3,2,1,0:T(8,128)} custom-call(f32[2]{0:T(128)} %reduce_max.19.peak_ref, s32[96,1]{1,0:T(8,128)} %add_select_fusion.9.parity_ref, f32[2,96,4096]{2,1,0:T(8,128)} %copy.402.real_ref, f32[2,96,4096]{2,1,0:T(8,128)} %copy.403.imag_ref), custom_call_target="tpu_custom_call" | custom-call | tf_op jit(solution)/shard_map/pallas_call | solution.py:209
  (131 shorter events, 134.2 us)
Async XLA Ops:
  4.8 4.8 %copy-start.18 = (s32[2,2]{1,0:T(2,128)S(1)}, s32[2,2]{1,0:T(2,128)}, u32[]{:S(2)}) copy-start(s32[2,2]{1,0:T(2,128)} %param.6) | copy-start | bytes 52
  4.8 54.4 %all-to-all-start = ((f32[2,8,64,1024]{3,2,0,1:T(8,128)}), f32[2,8,64,1024]{3,2,0,1:T(8,128)}, u32[]{:S(2)}, u32[]{:S(2)}) async-start(f32[2,8,64,1024]{3,2,0,1:T(8,128)} %copy.338), calls=%async_computation | async-start | bytes 8388608 | tf_op jit(solution)/shard_map/all_to_all | solution.py:108
  10.4 18.6 %copy-start.19 = (s32[128]{0:T(128)S(1)}, s32[128]{0:T(128)}, u32[]{:S(2)}) copy-start(s32[128]{0:T(128)} %param.7) | copy-start | bytes 1540
  64.4 8.6 %copy-start.4 = (f32[2,64,64,128]{3,2,1,0:T(8,128)}, f32[2,64,64,128]{3,2,1,0:T(8,128)S(1)}, u32[]{:S(2)}) copy-start(f32[2,64,64,128]{3,2,1,0:T(8,128)S(1)} %fusion.23) | copy-start | bytes 12582916
  66.5 6.5 %copy-start.6 = (f32[2,64,64,128]{3,2,1,0:T(8,128)}, f32[2,64,64,128]{3,2,1,0:T(8,128)S(1)}, u32[]{:S(2)}) copy-start(f32[2,64,64,128]{3,2,1,0:T(8,128)S(1)} %fusion.26) | copy-start | bytes 12582916
  66.5 6.5 %copy-start.10 = (f32[2,32,64,128]{3,1,2,0:T(8,128)S(1)}, f32[2,32,64,128]{3,1,2,0:T(8,128)}, u32[]{:S(2)}) copy-start(f32[2,32,64,128]{3,1,2,0:T(8,128)} %get-tuple-element.19) | copy-start | bytes 6291460
  85.8 29.5 %all-to-all-start.1 = ((f32[128,1,2048]{2,1,0:T(1,128)}), f32[128,1,2048]{2,1,0:T(1,128)S(1)}, u32[]{:S(2)}, u32[]{:S(2)}) async-start(f32[128,1,2048]{2,1,0:T(1,128)} %reshape.329), calls=%async_computation.1 | async-start | bytes 2097152 | tf_op jit(solution)/shard_map/all_to_all | solution.py:123
  95.4 9.3 %copy-start.5 = (f32[2,64,64,128]{3,2,1,0:T(8,128)S(1)}, f32[2,64,64,128]{3,2,1,0:T(8,128)}, u32[]{:S(2)}) copy-start(f32[2,64,64,128]{3,2,1,0:T(8,128)} %copy-done.4) | copy-start | bytes 12582916
  115.3 10.6 %copy-start.17 = (f32[128,1,2048]{2,1,0:T(1,128)}, f32[128,1,2048]{2,1,0:T(1,128)S(1)}, u32[]{:S(2)}) copy-start(f32[128,1,2048]{2,1,0:T(1,128)S(1)} %all-to-all-done.1) | copy-start | bytes 3145732
  115.3 29.0 %all-to-all-start.2 = ((f32[128,1,2048]{2,1,0:T(1,128)}), f32[128,1,2048]{2,1,0:T(1,128)}, u32[]{:S(2)}, u32[]{:S(2)}) async-start(f32[128,1,2048]{2,1,0:T(1,128)} %reshape.331), calls=%async_computation.2 | async-start | bytes 2097152 | tf_op jit(solution)/shard_map/all_to_all | solution.py:124
  153.4 2.7 copy-start.7
  166.1 2.7 copy-start.14
  171.3 3.7 copy-start.9
  178.0 1.8 copy-start.8
  179.8 1.8 copy-start.13
  184.5 2.2 copy-start.2
  190.1 3.8 %copy-start = (f32[2,128,32,128]{3,1,2,0:T(8,128)S(1)}, f32[2,128,32,128]{3,1,2,0:T(8,128)}, u32[]{:S(2)}) copy-start(f32[2,128,32,128]{3,1,2,0:T(8,128)} %get-tuple-element.29) | copy-start | bytes 12582916
  220.1 5.6 %copy-start.16 = (f32[384,2,16,32]{0,3,2,1:T(8,128)S(1)}, f32[384,2,16,32]{0,3,2,1:T(8,128)}, u32[]{:S(2)}) copy-start(f32[384,2,16,32]{0,3,2,1:T(8,128)} %copy.383) | copy-start | bytes 4718596
  243.1 5.8 %copy-start.15 = (f32[2,16,384,32]{2,3,1,0:T(8,128)S(1)}, f32[2,16,384,32]{2,3,1,0:T(8,128)}, u32[]{:S(2)}) copy-start(f32[2,16,384,32]{2,3,1,0:T(8,128)} %get-tuple-element.44) | copy-start | bytes 4718596
  243.1 30.2 %all-to-all-start.3 = ((f32[128,1,3072]{2,1,0:T(1,128)}), f32[128,1,3072]{2,1,0:T(1,128)}, u32[]{:S(2)}, u32[]{:S(2)}) async-start(f32[128,1,3072]{2,1,0:T(1,128)} %copy.376), calls=%async_computation.3 | async-start | bytes 3145728 | tf_op jit(solution)/shard_map/all_to_all | solution.py:160
  273.3 29.4 %all-to-all-start.4 = ((f32[128,1,3072]{2,1,0:T(1,128)}), f32[128,1,3072]{2,1,0:T(1,128)S(1)}, u32[]{:S(2)}, u32[]{:S(2)}) async-start(f32[128,1,3072]{2,1,0:T(1,128)} %copy.386), calls=%async_computation.4 | async-start | bytes 3145728 | tf_op jit(solution)/shard_map/all_to_all | solution.py:161
  308.8 3.6 copy-start.3
  312.4 5.5 %copy-start.1 = (f32[2,128,32,128]{3,1,2,0:T(8,128)S(1)}, f32[2,128,32,128]{3,1,2,0:T(8,128)}, u32[]{:S(2)}) copy-start(f32[2,128,32,128]{3,1,2,0:T(8,128)} %get-tuple-element.29) | copy-start | bytes 12582916
  317.9 5.4 %copy-start.12 = (f32[2,96,128,32]{2,3,1,0:T(8,128)S(1)}, f32[2,96,128,32]{2,3,1,0:T(8,128)}, u32[]{:S(2)}) copy-start(f32[2,96,128,32]{2,3,1,0:T(8,128)} %fusion.102) | copy-start | bytes 9437188
  338.7 22.9 %all-to-all-start.5 = ((f32[128,1,2]{2,1,0:T(1,128)}), f32[128,1,2]{2,1,0:T(1,128)S(1)}, u32[]{:S(2)}, u32[]{:S(2)}) async-start(f32[128,1,2]{2,1,0:T(1,128)} %broadcast_in_dim.40), calls=%async_computation.5 | async-start | bytes 131072 | tf_op jit(solution)/shard_map/all_to_all | solution.py:175
  347.5 5.4 %copy-start.11 = (f32[2,96,128,32]{2,1,3,0:T(8,128)S(1)}, f32[2,96,128,32]{2,1,3,0:T(8,128)}, u32[]{:S(2)}) copy-start(f32[2,96,128,32]{2,1,3,0:T(8,128)} %get-tuple-element.55) | copy-start | bytes 9437188

commit v14 on v13

--- a/solution.py
+++ b/solution.py
@@ -105,20 +105,27 @@
     local_rows = holograms.shape[1]
     local_cols = holograms.shape[2]
     blocks = holograms.reshape(holo_count, col_devices, local_rows // col_devices, local_cols)
-    piece = lax.all_to_all(blocks, "col", split_axis=1, concat_axis=1, tiled=True)
-    lead, senders, count, width = piece.shape
-    single = 1
-    sender_blocks = width // radix
-    piece_five = piece.reshape(lead, senders, count, sender_blocks, radix)
-    inner_cos, inner_sin = table_v[0], table_v[1]
-    per_sender = inner_cos.shape[:2] + (senders, sender_blocks)
-    mid_real = contract("kpjc,kjrcb->krpb", inner_cos.reshape(per_sender), piece_five)
-    mid_imag = contract("kpjc,kjrcb->krpb", inner_sin.reshape(per_sender), piece_five)
     share = S // devices
-    outer_cos, outer_sin = table_v[2], table_v[3]
+    inner_cos, inner_sin, outer_cos, outer_sin = table_v
     form = "kqpb,krpb->qpkr"
-    spec_real = contract(form, outer_cos, mid_real) - contract(form, outer_sin, mid_imag)
-    spec_imag = contract(form, outer_cos, mid_imag) + contract(form, outer_sin, mid_real)
+    halves = 2
+    half_rows = blocks.shape[2] // halves
+    spec_parts = []
+    for h in range(halves):
+        part = blocks[:, :, h * half_rows : (h + 1) * half_rows]
+        piece = lax.all_to_all(part, "col", split_axis=1, concat_axis=1, tiled=True)
+        lead, senders, rows_here, width = piece.shape
+        sender_blocks = width // radix
+        piece_five = piece.reshape(lead, senders, rows_here, sender_blocks, radix)
+        per_sender = inner_cos.shape[:2] + (senders, sender_blocks)
+        mid_real = contract("kpjc,kjrcb->krpb", inner_cos.reshape(per_sender), piece_five)
+        mid_imag = contract("kpjc,kjrcb->krpb", inner_sin.reshape(per_sender), piece_five)
+        part_real = contract(form, outer_cos, mid_real) - contract(form, outer_sin, mid_imag)
+        part_imag = contract(form, outer_cos, mid_imag) + contract(form, outer_sin, mid_real)
+        spec_parts.append((part_real, part_imag))
+    spec_real = jnp.concatenate([part[0] for part in spec_parts], axis=3)
+    spec_imag = jnp.concatenate([part[1] for part in spec_parts], axis=3)
+    count = spec_real.shape[3]
     send_shape = (devices, share, holo_count, count)
     piece_real = lax.all_to_all(spec_real.reshape(send_shape), ("row", "col"), 0, 0, tiled=True)
     piece_imag = lax.all_to_all(spec_imag.reshape(send_shape), ("row", "col"), 0, 0, tiled=True)

time: 377 us -> 397 us (1.053)
  local copies, waits for them, and re-layouts: 128 us -> 137 us
  waiting for transfers between devices: 49.4 us -> 55.9 us
  starting transfers between devices: 39.8 us -> 43.9 us
    all_to_all x1, waiting for transfers between devices: 0.01 us -> 10.2 us  [body(): lax.all_to_all(spec_real.reshape(send_shape), ('row', 'col'), 0, 0, tiled...]
    slice x0 -> x3, local copies, waits for them, and re-layouts: none -> 8.62 us  [body(): part = blocks[:, :, h * half_rows:(h + 1) * half_rows]]
    all_to_all x1, waiting for transfers between devices: 10.4 us -> 2.18 us  [body(): lax.all_to_all(spec_imag.reshape(send_shape), ('row', 'col'), 0, 0, tiled...]
    reshape x1 -> x0, local copies, waits for them, and re-layouts: 4.79 us -> none  [body(): holograms.reshape(holo_count, col_devices, local_rows // col_devices, loc...]
    all_to_all x1 -> x2, waiting for transfers between devices: 18.3 us -> 22.8 us  [body(): piece = lax.all_to_all(part, 'col', split_axis=1, concat_axis=1, tiled=True)]
    all_to_all x1 -> x2, starting transfers between devices: 4.73 us -> 8.9 us  [body(): piece = lax.all_to_all(part, 'col', split_axis=1, concat_axis=1, tiled=True)]
    unnamed x45 -> x56, local copies, waits for them, and re-layouts: 12.6 us -> 16.8 us
    dot_general x30 -> x36, matrix products: 101 us -> 101 us  [contract(): jnp.einsum(form, left, right, precision=lax.Precision.HIGH, preferred_ele...]
  transfers between devices with their start and end apart: 6 -> 7, of which waited for: 4 -> 5; matrix products, arithmetic and copies ran while one was open for 28% -> 27% of each run, Pallas kernels for 0% -> 0%
where the time goes in v14:
time: 397 us; the launch traced here: 392 us
  local copies, waits for them, and re-layouts  137 us (35%)
  matrix products  101 us (25%)
  waiting for transfers between devices  55.9 us (14%)
  starting transfers between devices  43.9 us (11%)
  other arithmetic  43.3 us (11%)
  Pallas kernels  9.16 us (2%)
    dot_general x36, matrix products, contract(): jnp.einsum(form, left, right, precision=lax.Precision.HIGH, preferred_ele...  101 us
    sin x2, other arithmetic, make_tables(): jnp.sin(outer_angle).reshape(shape_four)  29.5 us
    all_to_all x2, waiting for transfers between devices, body(): piece = lax.all_to_all(part, 'col', split_axis=1, concat_axis=1, tiled=True)  22.8 us
    gather x4, local copies, waits for them, and re-layouts, pack(): picked = jnp.take(grouped, source, axis=2) * filled[None, None, :, None]  21.8 us
    unnamed x56, local copies, waits for them, and re-layouts  16.8 us
    all_to_all x1, starting transfers between devices, body(): lax.all_to_all(spec_imag.reshape(send_shape), ('row', 'col'), 0, 0, tiled...  11.6 us
    all_to_all x1, waiting for transfers between devices, body(): lax.all_to_all(send_imag.reshape(dense), ('row', 'col'), 0, 0, tiled=True)  10.5 us
    all_to_all x1, waiting for transfers between devices, body(): lax.all_to_all(spec_real.reshape(send_shape), ('row', 'col'), 0, 0, tiled...  10.2 us
  transfers between devices with their start and end apart: 7, of which 5 were waited for; matrix products, arithmetic and copies ran while one was open for 27% of the time, Pallas kernels for 0%

profile of v14, /device:TPU:0, one launch (start us, length us, event | category | flops | bytes accessed | tf_op | source)
XLA Modules:
  0.0 391.7 jit_solution(6257778886691665213)
XLA Ops:
  5.5 4.5 %all-to-all-start = ((f32[2,8,32,1024]{3,2,0,1:T(8,128)}), f32[2,8,32,1024]{3,2,0,1:T(8,128)S(1)}, u32[]{:S(2)}, u32[]{:S(2)}) async-start(f32[2,8,32,1024]{3,2,0,1:T(8,128)} %copy.407), calls=%async_computation | async-start | bytes 4194304 | tf_op jit(solution)/shard_map/all_to_all | solution.py:116
  14.3 22.8 %all-to-all-done = f32[2,8,32,1024]{3,2,0,1:T(8,128)S(1)} async-done(((f32[2,8,32,1024]{3,2,0,1:T(8,128)}), f32[2,8,32,1024]{3,2,0,1:T(8,128)S(1)}, u32[]{:S(2)}, u32[]{:S(2)}) %all-to-all-start) | async-done | bytes 2097184 | tf_op jit(solution)/shard_map/all_to_all | solution.py:116
  37.2 4.4 %all-to-all-start.1 = ((f32[2,8,32,1024]{3,2,0,1:T(8,128)}), f32[2,8,32,1024]{3,2,0,1:T(8,128)}, u32[]{:S(2)}, u32[]{:S(2)}) async-start(f32[2,8,32,1024]{3,2,0,1:T(8,128)} %copy.415), calls=%async_computation.1 | async-start | bytes 4194304 | tf_op jit(solution)/shard_map/all_to_all | solution.py:116
  41.6 18.6 %fusion.89 = (f32[2,32,64,128]{3,1,2,0:T(8,128)}, f32[2,32,64,128]{3,1,2,0:T(8,128)}, f32[2,32,64,128]{3,1,2,0:T(8,128)S(1)}, f32[2,32,64,128]{3,1,2,0:T(8,128)}) fusion(s32[128]{0:T(128)S(1)} %and_select_fusion.3, s32[2,32,64]{1,2,0:T(8,128)S(1)} %get-tuple-element.38, s32[2,32,64]{1,2,0:T(8,128)S(1)} %get-tuple-element.39), kind=kLoop, calls=%fused_computation.99 | loop fusion | flops 14680064 | bytes 8421888 | tf_op jit(solution)/shard_map/sin | solution.py:44
  60.5 10.9 %fusion.17 = (f32[2,128,32,128]{3,1,2,0:T(8,128)}, f32[2,128,32,128]{3,1,2,0:T(8,128)}) fusion(s32[128]{0:T(128)S(1)} %and_select_fusion, s32[128,32]{0,1:T(8,128)S(1)} %multiply_add_fusion), kind=kLoop, calls=%fused_computation.41 | loop fusion | flops 14680064 | bytes 8405504 | tf_op jit(solution)/shard_map/sin | solution.py:44
  84.8 4.5 %fusion.37 = f32[64,2,32,32]{2,3,1,0:T(8,128)} fusion(f32[2,32,64,128]{3,2,1,0:T(8,128)S(1)} %fusion.74, f32[2,32,64,128]{3,1,2,0:T(8,128)S(1)} %copy-done.4), kind=kOutput, calls=%fused_computation.67 | convolution fusion | flops 100663296 | bytes 4718592 | tf_op jit(solution)/shard_map/kqpb,krpb->qpkr/dot_general | solution.py:24
  106.2 11.6 %all-to-all-start.3 = ((f32[128,1,2048]{2,1,0:T(1,128)}), f32[128,1,2048]{2,1,0:T(1,128)S(1)}, u32[]{:S(2)}, u32[]{:S(2)}) async-start(f32[128,1,2048]{2,1,0:T(1,128)} %reshape.340), calls=%async_computation.3 | async-start | bytes 2097152 | tf_op jit(solution)/shard_map/all_to_all | solution.py:131
  117.8 5.4 %fusion.29 = f32[64,2,32,32]{2,3,1,0:T(8,128)S(1)} fusion(f32[2,32,64,128]{3,2,1,0:T(8,128)} %copy-done.5, f32[2,32,64,128]{3,1,2,0:T(8,128)} %get-tuple-element.21), kind=kOutput, calls=%fused_computation.59 | convolution fusion | flops 100663296 | bytes 4718592 | tf_op jit(solution)/shard_map/kqpb,krpb->qpkr/dot_general | solution.py:24
  136.7 8.1 %all-to-all-start.2 = ((f32[128,1,2048]{2,1,0:T(1,128)}), f32[128,1,2048]{2,1,0:T(1,128)}, u32[]{:S(2)}, u32[]{:S(2)}) async-start(f32[128,1,2048]{2,1,0:T(1,128)} %reshape.338), calls=%async_computation.2 | async-start | bytes 2097152 | tf_op jit(solution)/shard_map/all_to_all | solution.py:130
  153.3 10.2 %all-to-all-done.2 = f32[128,1,2048]{2,1,0:T(1,128)} async-done(((f32[128,1,2048]{2,1,0:T(1,128)}), f32[128,1,2048]{2,1,0:T(1,128)}, u32[]{:S(2)}, u32[]{:S(2)}) %all-to-all-start.2) | async-done | bytes 1048608 | tf_op jit(solution)/shard_map/all_to_all | solution.py:130
  163.5 4.4 %reduce.6 = f32[128,2048]{1,0:T(8,128)S(1)} reduce(f32[128,1,2048]{2,1,0:T(1,128)} %all-to-all-done.2, f32[]{:T(128)} %broadcast.451), dimensions={1}, to_apply=%all_to_all.24.reduce_sub_computation | reduce | bytes 2097156 | tf_op jit(solution)/shard_map/all_to_all | solution.py:130
  181.7 4.3 %copy.511 = f32[2,16,64,2,64]{4,3,1,2,0:T(2,128)} copy(f32[2,16,64,2,64]{2,4,1,3,0:T(8,128)} %subtract_bitcast_fusion.2) | data formatting | bytes 2097152 | tf_op jit(solution)/shard_map/reshape | solution.py:142
  223.8 5.3 %gather_fusion.1 = f32[384,2,16,32]{3,2,1,0:T(8,128)} fusion(f32[2,16,128,32]{3,1,2,0:T(8,128)} %copy.463, s32[1024]{0:T(1024)S(1)} %pad_clamp_fusion), kind=kCustom, calls=%fused_computation.1.clone | custom fusion | bytes 3147264 | tf_op jit(solution)/shard_map/jit(_take)/gather | solution.py:161
  229.1 6.4 %copy.464 = f32[384,2,16,32]{0,3,2,1:T(8,128)} copy(f32[384,2,16,32]{3,2,1,0:T(8,128)} %gather_fusion.1) | data formatting | bytes 3145728 | tf_op jit(solution)/shard_map/jit(_take)/gather | solution.py:161
  235.4 4.3 %gather_fusion = f32[384,2,16,32]{3,2,1,0:T(8,128)} fusion(f32[2,16,128,32]{3,1,2,0:T(8,128)S(1)} %copy.453, s32[1024]{0:T(1024)S(1)} %pad_clamp_fusion), kind=kCustom, calls=%fused_computation.clone | custom fusion | bytes 3147264 | tf_op jit(solution)/shard_map/jit(_take)/gather | solution.py:161
  239.8 5.8 %copy.454 = f32[384,2,16,32]{0,3,2,1:T(8,128)S(1)} copy(f32[384,2,16,32]{3,2,1,0:T(8,128)} %gather_fusion) | data formatting | bytes 3145728 | tf_op jit(solution)/shard_map/jit(_take)/gather | solution.py:161
  247.7 5.0 %copy.455 = f32[2,16,384,32]{3,2,1,0:T(8,128)} copy(f32[2,16,384,32]{2,3,1,0:T(8,128)} %get-tuple-element.47) | data formatting | bytes 3145728 | tf_op jit(solution)/shard_map/mul | solution.py:161
  252.7 4.1 %reshape.290 = f32[2,16,128,96]{3,2,1,0:T(8,128)S(1)} reshape(f32[2,16,384,32]{3,2,1,0:T(8,128)} %copy.455) | data formatting | bytes 3145728 | tf_op jit(solution)/shard_map/reshape | solution.py:162
  258.5 4.5 %copy.457 = f32[128,1,3072]{2,1,0:T(1,128)} copy(f32[128,1,3072]{0,2,1:T(8,128)} %bitcast.210) | data formatting | bytes 3145728 | tf_op jit(solution)/shard_map/reshape | solution.py:167
  263.0 5.8 %all-to-all-start.4 = ((f32[128,1,3072]{2,1,0:T(1,128)}), f32[128,1,3072]{2,1,0:T(1,128)}, u32[]{:S(2)}, u32[]{:S(2)}) async-start(f32[128,1,3072]{2,1,0:T(1,128)} %copy.457), calls=%async_computation.4 | async-start | bytes 3145728 | tf_op jit(solution)/shard_map/all_to_all | solution.py:167
  278.6 4.5 %copy.467 = f32[128,1,3072]{2,1,0:T(1,128)} copy(f32[128,1,3072]{0,2,1:T(8,128)} %bitcast.211) | data formatting | bytes 3145728 | tf_op jit(solution)/shard_map/reshape | solution.py:168
  283.1 10.1 %all-to-all-done.4 = f32[128,1,3072]{2,1,0:T(1,128)} async-done(((f32[128,1,3072]{2,1,0:T(1,128)}), f32[128,1,3072]{2,1,0:T(1,128)}, u32[]{:S(2)}, u32[]{:S(2)}) %all-to-all-start.4) | async-done | bytes 1572896 | tf_op jit(solution)/shard_map/all_to_all | solution.py:167
  293.3 4.6 %all-to-all-start.5 = ((f32[128,1,3072]{2,1,0:T(1,128)}), f32[128,1,3072]{2,1,0:T(1,128)S(1)}, u32[]{:S(2)}, u32[]{:S(2)}) async-start(f32[128,1,3072]{2,1,0:T(1,128)} %copy.467), calls=%async_computation.5 | async-start | bytes 3145728 | tf_op jit(solution)/shard_map/all_to_all | solution.py:168
  312.1 10.5 %all-to-all-done.5 = f32[128,1,3072]{2,1,0:T(1,128)S(1)} async-done(((f32[128,1,3072]{2,1,0:T(1,128)}), f32[128,1,3072]{2,1,0:T(1,128)S(1)}, u32[]{:S(2)}, u32[]{:S(2)}) %all-to-all-start.5) | async-done | bytes 1572896 | tf_op jit(solution)/shard_map/all_to_all | solution.py:168
  332.3 5.4 %fusion.3 = f32[2,32,96,128]{3,2,1,0:T(8,128)S(1)} fusion(f32[2,128,32,128]{3,1,2,0:T(8,128)S(1)} %copy-done.3, f32[2,96,32,128]{3,2,1,0:T(8,128)S(1)} %add_bitcast_fusion.1), kind=kOutput, calls=%fused_computation.25 | convolution fusion | flops 603979776 | bytes 10485760 | tf_op jit(solution)/shard_map/kqpb,krpb->krqp/dot_general | solution.py:24
  337.7 5.4 %fusion.5 = f32[2,32,96,128]{3,2,1,0:T(8,128)S(1)} fusion(f32[2,128,32,128]{3,1,2,0:T(8,128)S(1)} %copy-done.1, f32[2,96,32,128]{3,2,1,0:T(8,128)S(1)} %add_bitcast_fusion.1), kind=kOutput, calls=%fused_computation.27 | convolution fusion | flops 603979776 | bytes 10485760 | tf_op jit(solution)/shard_map/kqpb,krpb->krqp/dot_general | solution.py:24
  344.9 5.6 %subtract_bitcast_fusion = f32[2,96,128,32]{2,1,3,0:T(8,128)S(1)} fusion(f32[2,32,96,128]{3,2,1,0:T(8,128)S(1)} %fusion.5, f32[2,128,32,128]{3,1,2,0:T(8,128)S(1)} %copy-done.3, f32[2,96,32,128]{3,2,1,0:T(8,128)S(1)} %subtract_bitcast_fusion.1), kind=kOutput, calls=%fused_computation.18 | convolution fusion | flops 604766208 | bytes 13631488 | tf_op jit(solution)/shard_map/kqpb,krpb->krqp/dot_general | solution.py:24
  350.5 7.4 %sqrt_reduce_fusion = (f32[2]{0:T(128)S(1)}, f32[2,96,128,32]{2,1,3,0:T(8,128)}) fusion(f32[2,96,128,32]{2,1,3,0:T(8,128)S(1)} %subtract_bitcast_fusion, f32[2,32,96,128]{3,2,1,0:T(8,128)S(1)} %fusion.3, f32[2,128,32,128]{3,1,2,0:T(8,128)S(1)} %copy-done.1, f32[2,96,32,128]{3,2,1,0:T(8,128)S(1)} %subtract_bitcast_fusion.1), kind=kOutput, calls=%fused_computation.16 | convolution fusion | flops 607911936 | bytes 16777224 | tf_op jit(solution)/shard_map/kqpb,krpb->krqp/dot_general | solution.py:24
  358.6 4.9 %all-to-all-start.6 = ((f32[128,1,2]{2,1,0:T(1,128)}), f32[128,1,2]{2,1,0:T(1,128)S(1)}, u32[]{:S(2)}, u32[]{:S(2)}) async-start(f32[128,1,2]{2,1,0:T(1,128)} %broadcast_in_dim.40), calls=%async_computation.6 | async-start | bytes 131072 | tf_op jit(solution)/shard_map/all_to_all | solution.py:182
  367.4 5.4 %copy.483.real_ref = f32[2,96,4096]{2,1,0:T(8,128)} copy(f32[2,96,4096]{1,2,0:T(8,128)} %bitcast.197) | data formatting | bytes 6291456 | tf_op jit(solution)/shard_map/reshape | solution.py:73
  376.2 5.3 %copy.484.imag_ref = f32[2,96,4096]{2,1,0:T(8,128)} copy(f32[2,96,4096]{1,2,0:T(8,128)} %bitcast.198) | data formatting | bytes 6291456 | tf_op jit(solution)/shard_map/reshape | solution.py:73
  382.2 9.2 %shard_map.37 = f32[2,2,96,4096]{3,2,1,0:T(8,128)} custom-call(f32[2]{0:T(128)} %reduce_max.19.peak_ref, s32[96,1]{1,0:T(8,128)} %add_select_fusion.9.parity_ref, f32[2,96,4096]{2,1,0:T(8,128)} %copy.483.real_ref, f32[2,96,4096]{2,1,0:T(8,128)} %copy.484.imag_ref), custom_call_target="tpu_custom_call" | custom-call | tf_op jit(solution)/shard_map/pallas_call | solution.py:216
  (154 shorter events, 161.2 us)
Async XLA Ops:
  5.5 4.6 %copy-start.24 = (s32[128]{0:T(128)S(1)}, s32[128]{0:T(128)}, u32[]{:S(2)}) copy-start(s32[128]{0:T(128)} %param.7) | copy-start | bytes 1540
  5.5 4.8 %copy-start.23 = (s32[2,2]{1,0:T(2,128)S(1)}, s32[2,2]{1,0:T(2,128)}, u32[]{:S(2)}) copy-start(s32[2,2]{1,0:T(2,128)} %param.6) | copy-start | bytes 52
  5.5 31.7 %all-to-all-start = ((f32[2,8,32,1024]{3,2,0,1:T(8,128)}), f32[2,8,32,1024]{3,2,0,1:T(8,128)S(1)}, u32[]{:S(2)}, u32[]{:S(2)}) async-start(f32[2,8,32,1024]{3,2,0,1:T(8,128)} %copy.407), calls=%async_computation | async-start | bytes 4194304 | tf_op jit(solution)/shard_map/all_to_all | solution.py:116
  37.2 4.4 %copy-start.18 = (f32[2,8,32,1024]{3,2,0,1:T(8,128)}, f32[2,8,32,1024]{3,2,0,1:T(8,128)S(1)}, u32[]{:S(2)}) copy-start(f32[2,8,32,1024]{3,2,0,1:T(8,128)S(1)} %all-to-all-done) | copy-start | bytes 6291460
  37.2 36.0 %all-to-all-start.1 = ((f32[2,8,32,1024]{3,2,0,1:T(8,128)}), f32[2,8,32,1024]{3,2,0,1:T(8,128)}, u32[]{:S(2)}, u32[]{:S(2)}) async-start(f32[2,8,32,1024]{3,2,0,1:T(8,128)} %copy.415), calls=%async_computation.1 | async-start | bytes 4194304 | tf_op jit(solution)/shard_map/all_to_all | solution.py:116
  60.5 10.9 %copy-start.19 = (f32[2,8,32,1024]{3,2,0,1:T(8,128)S(1)}, f32[2,8,32,1024]{3,2,0,1:T(8,128)}, u32[]{:S(2)}) copy-start(f32[2,8,32,1024]{3,2,0,1:T(8,128)} %copy-done.18) | copy-start | bytes 6291460
  76.3 19.7 %copy-start.10 = (f32[2,32,64,128]{3,2,1,0:T(8,128)}, f32[2,32,64,128]{3,2,1,0:T(8,128)S(1)}, u32[]{:S(2)}) copy-start(f32[2,32,64,128]{3,2,1,0:T(8,128)S(1)} %fusion.77) | copy-start | bytes 6291460
  76.4 3.0 copy-start.6
  77.5 11.8 %copy-start.5 = (f32[2,32,64,128]{3,2,1,0:T(8,128)}, f32[2,32,64,128]{3,2,1,0:T(8,128)S(1)}, u32[]{:S(2)}) copy-start(f32[2,32,64,128]{3,2,1,0:T(8,128)S(1)} %fusion.80) | copy-start | bytes 6291460
  81.5 11.3 %copy-start.12 = (f32[2,32,64,128]{3,2,1,0:T(8,128)}, f32[2,32,64,128]{3,2,1,0:T(8,128)S(1)}, u32[]{:S(2)}) copy-start(f32[2,32,64,128]{3,2,1,0:T(8,128)S(1)} %fusion.71) | copy-start | bytes 6291460
  81.5 3.2 copy-start.4
  106.2 30.5 %all-to-all-start.3 = ((f32[128,1,2048]{2,1,0:T(1,128)}), f32[128,1,2048]{2,1,0:T(1,128)S(1)}, u32[]{:S(2)}, u32[]{:S(2)}) async-start(f32[128,1,2048]{2,1,0:T(1,128)} %reshape.340), calls=%async_computation.3 | async-start | bytes 2097152 | tf_op jit(solution)/shard_map/all_to_all | solution.py:131
  117.8 5.4 %copy-start.13 = (f32[2,32,64,128]{3,2,1,0:T(8,128)S(1)}, f32[2,32,64,128]{3,2,1,0:T(8,128)}, u32[]{:S(2)}) copy-start(f32[2,32,64,128]{3,2,1,0:T(8,128)} %copy-done.12) | copy-start | bytes 6291460
  117.8 5.4 %copy-start.20 = (f32[64,2,32,32]{2,3,1,0:T(8,128)S(1)}, f32[64,2,32,32]{2,3,1,0:T(8,128)}, u32[]{:S(2)}) copy-start(f32[64,2,32,32]{2,3,1,0:T(8,128)} %fusion.37) | copy-start | bytes 1572868
  123.2 3.2 copy-start.11
  136.7 26.8 %all-to-all-start.2 = ((f32[128,1,2048]{2,1,0:T(1,128)}), f32[128,1,2048]{2,1,0:T(1,128)}, u32[]{:S(2)}, u32[]{:S(2)}) async-start(f32[128,1,2048]{2,1,0:T(1,128)} %reshape.338), calls=%async_computation.2 | async-start | bytes 2097152 | tf_op jit(solution)/shard_map/all_to_all | solution.py:130
  173.4 2.7 copy-start.7
  186.0 2.7 copy-start.17
  191.2 3.6 copy-start.9
  197.8 1.8 copy-start.8
  199.6 1.8 copy-start.16
  204.3 2.2 copy-start.2
  209.9 3.7 copy-start
  239.8 5.8 %copy-start.22 = (f32[384,2,16,32]{0,3,2,1:T(8,128)S(1)}, f32[384,2,16,32]{0,3,2,1:T(8,128)}, u32[]{:S(2)}) copy-start(f32[384,2,16,32]{0,3,2,1:T(8,128)} %copy.464) | copy-start | bytes 4718596
  263.0 5.8 %copy-start.21 = (f32[2,16,384,32]{2,3,1,0:T(8,128)S(1)}, f32[2,16,384,32]{2,3,1,0:T(8,128)}, u32[]{:S(2)}) copy-start(f32[2,16,384,32]{2,3,1,0:T(8,128)} %get-tuple-element.46) | copy-start | bytes 4718596
  263.0 30.2 %all-to-all-start.4 = ((f32[128,1,3072]{2,1,0:T(1,128)}), f32[128,1,3072]{2,1,0:T(1,128)}, u32[]{:S(2)}, u32[]{:S(2)}) async-start(f32[128,1,3072]{2,1,0:T(1,128)} %copy.457), calls=%async_computation.4 | async-start | bytes 3145728 | tf_op jit(solution)/shard_map/all_to_all | solution.py:167
  293.3 29.4 %all-to-all-start.5 = ((f32[128,1,3072]{2,1,0:T(1,128)}), f32[128,1,3072]{2,1,0:T(1,128)S(1)}, u32[]{:S(2)}, u32[]{:S(2)}) async-start(f32[128,1,3072]{2,1,0:T(1,128)} %copy.467), calls=%async_computation.5 | async-start | bytes 3145728 | tf_op jit(solution)/shard_map/all_to_all | solution.py:168
  328.7 3.6 copy-start.3
  332.3 5.4 %copy-start.1 = (f32[2,128,32,128]{3,1,2,0:T(8,128)S(1)}, f32[2,128,32,128]{3,1,2,0:T(8,128)}, u32[]{:S(2)}) copy-start(f32[2,128,32,128]{3,1,2,0:T(8,128)} %get-tuple-element.29) | copy-start | bytes 12582916
  337.7 5.4 %copy-start.15 = (f32[2,96,128,32]{2,3,1,0:T(8,128)S(1)}, f32[2,96,128,32]{2,3,1,0:T(8,128)}, u32[]{:S(2)}) copy-start(f32[2,96,128,32]{2,3,1,0:T(8,128)} %fusion.134) | copy-start | bytes 9437188
  358.6 22.9 %all-to-all-start.6 = ((f32[128,1,2]{2,1,0:T(1,128)}), f32[128,1,2]{2,1,0:T(1,128)S(1)}, u32[]{:S(2)}, u32[]{:S(2)}) async-start(f32[128,1,2]{2,1,0:T(1,128)} %broadcast_in_dim.40), calls=%async_computation.6 | async-start | bytes 131072 | tf_op jit(solution)/shard_map/all_to_all | solution.py:182
  367.4 5.4 %copy-start.14 = (f32[2,96,128,32]{2,1,3,0:T(8,128)S(1)}, f32[2,96,128,32]{2,1,3,0:T(8,128)}, u32[]{:S(2)}) copy-start(f32[2,96,128,32]{2,1,3,0:T(8,128)} %get-tuple-element.57) | copy-start | bytes 9437188

commit v15 on v13

--- a/solution.py
+++ b/solution.py
@@ -133,9 +133,6 @@
     mid_imag = contract(step, inner_sin, recv_real) + contract(step, inner_cos, recv_imag)
     mid_shape = (holo_count, share, inner_cos.shape[1], radix)
     side_real, side_imag = finish(mid_real.reshape(mid_shape), mid_imag.reshape(mid_shape), table_u)
-    lift_real, lift_imag = transform(
-        side_real.reshape(holo_count, share, S), side_imag.reshape(holo_count, share, S), table_p
-    )
     strips = strip_owner.shape[0]
     strip_rows = P_SIZE // strips
     slot_rows = MOST * strip_rows
@@ -149,20 +146,30 @@
     source = jnp.sum(jnp.where(match, strip_ids[None, :], 0), axis=1)
     filled = jnp.any(match, axis=1).astype(jnp.float32)
 
+    inner_cos, inner_sin, outer_cos, outer_sin = table_p
+    side_shape = (holo_count, share, S // radix, radix)
+    side_real = side_real.reshape(side_shape)
+    side_imag = side_imag.reshape(side_shape)
+    step = "kpa,krab->krpb"
+    mid_real = contract(step, inner_cos, side_real) - contract(step, inner_sin, side_imag)
+    mid_imag = contract(step, inner_sin, side_real) + contract(step, inner_cos, side_imag)
+    form = "kqpb,krpb->qkrp"
+    lift_real = contract(form, outer_cos, mid_real) - contract(form, outer_sin, mid_imag)
+    lift_imag = contract(form, outer_cos, mid_imag) + contract(form, outer_sin, mid_real)
+    dense = (devices, 1, MOST * holo_count * share * strip_rows)
+
     def pack(part):
-        grouped = part.reshape(holo_count, share, strips, strip_rows)
-        picked = jnp.take(grouped, source, axis=2) * filled[None, None, :, None]
-        return jnp.transpose(picked.reshape(holo_count, share, strips, slot_rows), (2, 0, 1, 3))
-
-    send_real = pack(lift_real)
-    send_imag = pack(lift_imag)
-    dense = (devices, 1, holo_count * share * slot_rows)
-    piece_real = lax.all_to_all(send_real.reshape(dense), ("row", "col"), 0, 0, tiled=True)
-    piece_imag = lax.all_to_all(send_imag.reshape(dense), ("row", "col"), 0, 0, tiled=True)
+        grouped = part.reshape(strips, holo_count * share * strip_rows)
+        picked = jnp.take(grouped, source, axis=0) * filled[:, None]
+        return picked.reshape(dense)
+
+    piece_real = lax.all_to_all(pack(lift_real), ("row", "col"), 0, 0, tiled=True)
+    piece_imag = lax.all_to_all(pack(lift_imag), ("row", "col"), 0, 0, tiled=True)
 
     def unpack(piece):
-        piece = piece.reshape(devices, holo_count, share, slot_rows)
-        return jnp.transpose(piece, (1, 3, 0, 2)).reshape(holo_count, slot_rows, devices * share)
+        piece = piece.reshape(devices, MOST, holo_count, share, strip_rows)
+        rows = jnp.transpose(piece, (2, 1, 4, 0, 3))
+        return rows.reshape(holo_count, slot_rows, devices * share)
 
     rows_real = unpack(piece_real)
     rows_imag = unpack(piece_imag)

time: 377 us -> 384 us (1.019)
  matrix products: 101 us -> 109 us
  local copies, waits for them, and re-layouts: 128 us -> 121 us
  starting transfers between devices: 39.8 us -> 44.1 us
    gather x4 -> x2, local copies, waits for them, and re-layouts: 21.6 us -> 5.01 us  [pack(): picked = jnp.take(grouped, source, axis=0) * filled[:, None]]
    reshape x4, local copies, waits for them, and re-layouts: 17.1 us -> 6.49 us  [the longest x2 6.1 us: pack(): return picked.reshape(dense)]
    another operation x2, local copies, waits for them, and re-layouts: 2.48 us -> 11.6 us  [transform(): imag_four = imag_part.reshape(batch, rows, blocks, radix)]
    mul x2 -> x0, local copies, waits for them, and re-layouts: 8.96 us -> none  [pack(): picked = jnp.take(grouped, source, axis=2) * filled[None, None, :, None]]
    another operation x2, local copies, waits for them, and re-layouts: 2.26 us -> 11.2 us  [transform(): real_four = real_part.reshape(batch, rows, blocks, radix)]
    dot_general x30, matrix products: 101 us -> 109 us  [contract(): jnp.einsum(form, left, right, precision=lax.Precision.HIGH, preferred_ele...]
    transpose x4 -> x2, local copies, waits for them, and re-layouts: 7.3 us -> 14.4 us  [unpack(): rows = jnp.transpose(piece, (2, 1, 4, 0, 3))]
    all_to_all x1, starting transfers between devices: 4.84 us -> 9.96 us  [body(): lax.all_to_all(every, ('row', 'col'), 0, 0, tiled=True)]
  transfers between devices with their start and end apart: 6 -> 6, of which waited for: 4 -> 3; matrix products, arithmetic and copies ran while one was open for 28% -> 29% of each run, Pallas kernels for 0% -> 0%
where the time goes in v15:
time: 384 us; the launch traced here: 379 us
  local copies, waits for them, and re-layouts  121 us (32%)
  matrix products  109 us (28%)
  waiting for transfers between devices  50.6 us (13%)
  starting transfers between devices  44.1 us (11%)
  other arithmetic  43.6 us (11%)
  Pallas kernels  9.16 us (2%)
    dot_general x30, matrix products, contract(): jnp.einsum(form, left, right, precision=lax.Precision.HIGH, preferred_ele...  109 us
    sin x2, other arithmetic, make_tables(): jnp.sin(outer_angle).reshape(shape_four)  29.8 us
    all_to_all x1, waiting for transfers between devices, body(): lax.all_to_all(pack(lift_real), ('row', 'col'), 0, 0, tiled=True)  21.7 us
    all_to_all x1, waiting for transfers between devices, body(): lax.all_to_all(blocks, 'col', split_axis=1, concat_axis=1, tiled=True)  18.7 us
    transpose x2, local copies, waits for them, and re-layouts, unpack(): rows = jnp.transpose(piece, (2, 1, 4, 0, 3))  14.4 us
    unnamed x39, local copies, waits for them, and re-layouts  12.4 us
    another operation x2, local copies, waits for them, and re-layouts, transform(): imag_four = imag_part.reshape(batch, rows, blocks, radix)  11.6 us
    another operation x2, local copies, waits for them, and re-layouts, transform(): real_four = real_part.reshape(batch, rows, blocks, radix)  11.2 us
  transfers between devices with their start and end apart: 6, of which 3 were waited for; matrix products, arithmetic and copies ran while one was open for 29% of the time, Pallas kernels for 0%

profile of v15, /device:TPU:0, one launch (start us, length us, event | category | flops | bytes accessed | tf_op | source)
XLA Modules:
  0.0 378.5 jit_solution(4686868821922131232)
XLA Ops:
  0.0 4.7 %copy.268 = f32[2,8,64,1024]{3,2,0,1:T(8,128)} copy(f32[2,8,64,1024]{3,2,1,0:T(8,128)} %bitcast.172) | data formatting | bytes 8388608 | tf_op jit(solution)/shard_map/reshape | solution.py:107
  4.7 4.7 %all-to-all-start = ((f32[2,8,64,1024]{3,2,0,1:T(8,128)}), f32[2,8,64,1024]{3,2,0,1:T(8,128)}, u32[]{:S(2)}, u32[]{:S(2)}) async-start(f32[2,8,64,1024]{3,2,0,1:T(8,128)} %copy.268), calls=%async_computation | async-start | bytes 8388608 | tf_op jit(solution)/shard_map/all_to_all | solution.py:108
  10.3 18.6 %fusion.59 = (f32[2,32,64,128]{3,1,2,0:T(8,128)}, f32[2,32,64,128]{3,1,2,0:T(8,128)}, f32[2,32,64,128]{3,1,2,0:T(8,128)}, f32[2,32,64,128]{3,1,2,0:T(8,128)S(1)}) fusion(s32[128]{0:T(128)S(1)} %and_select_fusion.3, s32[2,32,64]{1,2,0:T(8,128)S(1)} %get-tuple-element.36, s32[2,32,64]{1,2,0:T(8,128)S(1)} %get-tuple-element.37), kind=kLoop, calls=%fused_computation.77 | loop fusion | flops 14680064 | bytes 8421888 | tf_op jit(solution)/shard_map/sin | solution.py:44
  29.2 11.2 %fusion.35 = (f32[2,128,32,128]{3,1,2,0:T(8,128)}, f32[2,128,32,128]{3,1,2,0:T(8,128)}) fusion(s32[128]{0:T(128)S(1)} %and_select_fusion, s32[128,32]{0,1:T(8,128)S(1)} %multiply_add_fusion), kind=kLoop, calls=%fused_computation.53 | loop fusion | flops 14680064 | bytes 8405504 | tf_op jit(solution)/shard_map/sin | solution.py:44
  40.4 18.7 %all-to-all-done = f32[2,8,64,1024]{3,2,0,1:T(8,128)} async-done(((f32[2,8,64,1024]{3,2,0,1:T(8,128)}), f32[2,8,64,1024]{3,2,0,1:T(8,128)}, u32[]{:S(2)}, u32[]{:S(2)}) %all-to-all-start) | async-done | bytes 4194336 | tf_op jit(solution)/shard_map/all_to_all | solution.py:108
  66.4 6.4 %fusion.9 = f32[64,2,64,32]{2,3,1,0:T(8,128)S(1)} fusion(f32[2,64,64,128]{3,2,1,0:T(8,128)S(1)} %fusion.26, f32[2,32,64,128]{3,1,2,0:T(8,128)S(1)} %get-tuple-element.21), kind=kOutput, calls=%fused_computation.16 | convolution fusion | flops 201326592 | bytes 7340032 | tf_op jit(solution)/shard_map/kqpb,krpb->qpkr/dot_general | solution.py:24
  72.9 6.5 %subtract_bitcast_fusion.3 = f32[32,64,2,64]{3,0,2,1:T(8,128)S(1)} fusion(f32[64,2,64,32]{2,3,1,0:T(8,128)S(1)} %fusion.9, f32[2,32,64,128]{3,1,2,0:T(8,128)S(1)} %copy-done.11, f32[2,64,64,128]{3,2,1,0:T(8,128)S(1)} %fusion.23), kind=kOutput, calls=%fused_computation.58 | convolution fusion | flops 201588736 | bytes 8388608 | tf_op jit(solution)/shard_map/kqpb,krpb->qpkr/dot_general | solution.py:24
  85.7 9.7 %all-to-all-start.1 = ((f32[128,1,2048]{2,1,0:T(1,128)}), f32[128,1,2048]{2,1,0:T(1,128)S(1)}, u32[]{:S(2)}, u32[]{:S(2)}) async-start(f32[128,1,2048]{2,1,0:T(1,128)} %reshape.331), calls=%async_computation.1 | async-start | bytes 2097152 | tf_op jit(solution)/shard_map/all_to_all | solution.py:123
  95.5 9.3 %fusion.7 = f32[64,2,64,32]{2,3,1,0:T(8,128)S(1)} fusion(f32[2,64,64,128]{3,2,1,0:T(8,128)} %copy-done.6, f32[2,32,64,128]{3,1,2,0:T(8,128)} %get-tuple-element.19), kind=kOutput, calls=%fused_computation.14 | convolution fusion | flops 201326592 | bytes 7340032 | tf_op jit(solution)/shard_map/kqpb,krpb->qpkr/dot_general | solution.py:24
  104.8 6.6 %add_bitcast_fusion.3 = f32[32,64,2,64]{3,0,2,1:T(8,128)S(1)} fusion(f32[64,2,64,32]{2,3,1,0:T(8,128)S(1)} %fusion.7, f32[2,32,64,128]{3,1,2,0:T(8,128)S(1)} %get-tuple-element.21, f32[2,64,64,128]{3,2,1,0:T(8,128)S(1)} %copy-done.5), kind=kOutput, calls=%fused_computation.57 | convolution fusion | flops 201588736 | bytes 8388608 | tf_op jit(solution)/shard_map/kqpb,krpb->qpkr/dot_general | solution.py:24
  115.1 10.3 %all-to-all-start.2 = ((f32[128,1,2048]{2,1,0:T(1,128)}), f32[128,1,2048]{2,1,0:T(1,128)}, u32[]{:S(2)}, u32[]{:S(2)}) async-start(f32[128,1,2048]{2,1,0:T(1,128)} %reshape.333), calls=%async_computation.2 | async-start | bytes 2097152 | tf_op jit(solution)/shard_map/all_to_all | solution.py:124
  126.5 4.3 %reduce.6 = f32[128,2048]{1,0:T(8,128)S(1)} reduce(f32[128,1,2048]{2,1,0:T(1,128)} %copy-done.14, f32[]{:T(128)} %broadcast.437), dimensions={1}, to_apply=%all_to_all.20.reduce_sub_computation | reduce | bytes 2097156 | tf_op jit(solution)/shard_map/all_to_all | solution.py:123
  133.9 10.2 %all-to-all-done.2 = f32[128,1,2048]{2,1,0:T(1,128)} async-done(((f32[128,1,2048]{2,1,0:T(1,128)}), f32[128,1,2048]{2,1,0:T(1,128)}, u32[]{:S(2)}, u32[]{:S(2)}) %all-to-all-start.2) | async-done | bytes 1048608 | tf_op jit(solution)/shard_map/all_to_all | solution.py:124
  144.1 4.3 %reduce.7 = f32[128,2048]{1,0:T(8,128)S(1)} reduce(f32[128,1,2048]{2,1,0:T(1,128)} %all-to-all-done.2, f32[]{:T(128)} %broadcast.437), dimensions={1}, to_apply=%all_to_all.21.reduce_sub_computation | reduce | bytes 2097156 | tf_op jit(solution)/shard_map/all_to_all | solution.py:124
  160.3 4.3 %copy.352 = f32[2,16,64,2,64]{4,3,1,2,0:T(2,128)} copy(f32[2,16,64,2,64]{2,4,1,3,0:T(8,128)} %add_bitcast_fusion.2) | data formatting | bytes 2097152 | tf_op jit(solution)/shard_map/reshape | solution.py:135
  210.5 5.1 %fusion.58 = f32[128,2,16,32]{0,2,3,1:T(8,128)S(1)} fusion(f32[2,32,16,128]{3,2,1,0:T(8,128)S(1)} %fusion.63, f32[2,128,32,128]{3,1,2,0:T(8,128)} %get-tuple-element.29, f32[2,16,32,128]{3,2,1,0:T(8,128)S(1)} %fusion.56), kind=kOutput, calls=%fused_computation.76 | convolution fusion | flops 100794368 | bytes 5767168 | tf_op jit(solution)/shard_map/kqpb,krpb->qkrp/dot_general | solution.py:24
  226.2 4.9 %all-to-all-start.3 = ((f32[128,1,3072]{2,1,0:T(1,128)}), f32[128,1,3072]{2,1,0:T(1,128)S(1)}, u32[]{:S(2)}, u32[]{:S(2)}) async-start(f32[128,1,3072]{2,1,0:T(1,128)} %reshape.325), calls=%async_computation.3 | async-start | bytes 3145728 | tf_op jit(solution)/shard_map/all_to_all | solution.py:166
  234.1 21.7 %all-to-all-done.3 = f32[128,1,3072]{2,1,0:T(1,128)S(1)} async-done(((f32[128,1,3072]{2,1,0:T(1,128)}), f32[128,1,3072]{2,1,0:T(1,128)S(1)}, u32[]{:S(2)}, u32[]{:S(2)}) %all-to-all-start.3) | async-done | bytes 1572896 | tf_op jit(solution)/shard_map/all_to_all | solution.py:166
  255.8 4.6 %all-to-all-start.4 = ((f32[128,1,3072]{2,1,0:T(1,128)}), f32[128,1,3072]{2,1,0:T(1,128)S(1)}, u32[]{:S(2)}, u32[]{:S(2)}) async-start(f32[128,1,3072]{2,1,0:T(1,128)} %reshape.326), calls=%async_computation.4 | async-start | bytes 3145728 | tf_op jit(solution)/shard_map/all_to_all | solution.py:167
  263.7 8.1 %copy.306 = f32[2,3,32,128,16]{2,1,4,3,0:T(4,128)} copy(f32[2,3,32,128,16]{3,2,4,0,1:T(8,128)} %bitcast.170) | data formatting | bytes 3145728 | tf_op jit(solution)/shard_map/transpose | solution.py:171
  271.8 9.0 %reshape_reshape.14 = f32[2,96,16,128]{1,3,2,0:T(8,128)} reshape(f32[2,3,32,128,16]{2,1,4,3,0:T(4,128)} %copy.306) | data formatting | bytes 3145728 | tf_op jit(solution)/shard_map/reshape;reshape | solution.py:53
  290.9 6.2 %copy.314 = f32[2,3,32,128,16]{2,1,4,3,0:T(4,128)} copy(f32[2,3,32,128,16]{3,2,4,0,1:T(8,128)S(1)} %bitcast.171) | data formatting | bytes 3145728 | tf_op jit(solution)/shard_map/transpose | solution.py:171
  297.1 9.0 %reshape_reshape.15 = f32[2,96,16,128]{1,3,2,0:T(8,128)} reshape(f32[2,3,32,128,16]{2,1,4,3,0:T(4,128)} %copy.314) | data formatting | bytes 3145728 | tf_op jit(solution)/shard_map/reshape;reshape | solution.py:57
  312.3 5.4 %fusion.17 = f32[2,32,96,128]{3,2,1,0:T(8,128)S(1)} fusion(f32[2,128,32,128]{3,1,2,0:T(8,128)S(1)} %copy-done.1, f32[2,96,32,128]{3,2,1,0:T(8,128)S(1)} %add_bitcast_fusion.1), kind=kOutput, calls=%fused_computation.39 | convolution fusion | flops 603979776 | bytes 10485760 | tf_op jit(solution)/shard_map/kqpb,krpb->krqp/dot_general | solution.py:24
  317.8 5.4 %fusion.15 = f32[2,32,96,128]{3,2,1,0:T(8,128)S(1)} fusion(f32[2,128,32,128]{3,1,2,0:T(8,128)S(1)} %copy-done.3, f32[2,96,32,128]{3,2,1,0:T(8,128)S(1)} %add_bitcast_fusion.1), kind=kOutput, calls=%fused_computation.37 | convolution fusion | flops 603979776 | bytes 10485760 | tf_op jit(solution)/shard_map/kqpb,krpb->krqp/dot_general | solution.py:24
  324.9 5.5 %subtract_bitcast_fusion = f32[2,96,128,32]{2,1,3,0:T(8,128)S(1)} fusion(f32[2,32,96,128]{3,2,1,0:T(8,128)S(1)} %fusion.17, f32[2,128,32,128]{3,1,2,0:T(8,128)S(1)} %copy-done.3, f32[2,96,32,128]{3,2,1,0:T(8,128)S(1)} %subtract_bitcast_fusion.1), kind=kOutput, calls=%fused_computation.30 | convolution fusion | flops 604766208 | bytes 13631488 | tf_op jit(solution)/shard_map/kqpb,krpb->krqp/dot_general | solution.py:24
  330.5 7.5 %sqrt_reduce_fusion = (f32[2]{0:T(128)S(1)}, f32[2,96,128,32]{2,1,3,0:T(8,128)}) fusion(f32[2,96,128,32]{2,1,3,0:T(8,128)S(1)} %subtract_bitcast_fusion, f32[2,32,96,128]{3,2,1,0:T(8,128)S(1)} %fusion.15, f32[2,128,32,128]{3,1,2,0:T(8,128)S(1)} %copy-done.1, f32[2,96,32,128]{3,2,1,0:T(8,128)S(1)} %subtract_bitcast_fusion.1), kind=kOutput, calls=%fused_computation.28 | convolution fusion | flops 607911936 | bytes 16777224 | tf_op jit(solution)/shard_map/kqpb,krpb->krqp/dot_general | solution.py:24
  338.6 10.0 %all-to-all-start.5 = ((f32[128,1,2]{2,1,0:T(1,128)}), f32[128,1,2]{2,1,0:T(1,128)S(1)}, u32[]{:S(2)}, u32[]{:S(2)}) async-start(f32[128,1,2]{2,1,0:T(1,128)} %broadcast_in_dim.40), calls=%async_computation.5 | async-start | bytes 131072 | tf_op jit(solution)/shard_map/all_to_all | solution.py:182
  352.5 5.2 %copy.327 = f32[2,96,128,32]{1,3,2,0:T(8,128)} copy(f32[2,96,128,32]{2,1,3,0:T(8,128)} %get-tuple-element.55) | data formatting | bytes 6291456 | tf_op jit(solution)/shard_map/add | solution.py:69
  357.7 5.4 %copy.329.imag_ref = f32[2,96,4096]{2,1,0:T(8,128)} copy(f32[2,96,4096]{1,2,0:T(8,128)} %bitcast.163) | data formatting | bytes 6291456 | tf_op jit(solution)/shard_map/reshape | solution.py:73
  363.1 5.3 %copy.328.real_ref = f32[2,96,4096]{2,1,0:T(8,128)} copy(f32[2,96,4096]{1,2,0:T(8,128)} %bitcast.162) | data formatting | bytes 6291456 | tf_op jit(solution)/shard_map/reshape | solution.py:73
  369.1 9.2 %shard_map.37 = f32[2,2,96,4096]{3,2,1,0:T(8,128)} custom-call(f32[2]{0:T(128)} %reduce_max.19.peak_ref, s32[96,1]{1,0:T(8,128)} %add_select_fusion.9.parity_ref, f32[2,96,4096]{2,1,0:T(8,128)} %copy.328.real_ref, f32[2,96,4096]{2,1,0:T(8,128)} %copy.329.imag_ref), custom_call_target="tpu_custom_call" | custom-call | tf_op jit(solution)/shard_map/pallas_call | solution.py:216
  (121 shorter events, 120.3 us)
Async XLA Ops:
  4.7 4.7 %copy-start.15 = (s32[2,2]{1,0:T(2,128)S(1)}, s32[2,2]{1,0:T(2,128)}, u32[]{:S(2)}) copy-start(s32[2,2]{1,0:T(2,128)} %param.6) | copy-start | bytes 52
  4.7 54.3 %all-to-all-start = ((f32[2,8,64,1024]{3,2,0,1:T(8,128)}), f32[2,8,64,1024]{3,2,0,1:T(8,128)}, u32[]{:S(2)}, u32[]{:S(2)}) async-start(f32[2,8,64,1024]{3,2,0,1:T(8,128)} %copy.268), calls=%async_computation | async-start | bytes 8388608 | tf_op jit(solution)/shard_map/all_to_all | solution.py:108
  64.3 2.1 copy-start.6
  66.4 6.5 %copy-start.4 = (f32[2,64,64,128]{3,2,1,0:T(8,128)}, f32[2,64,64,128]{3,2,1,0:T(8,128)S(1)}, u32[]{:S(2)}) copy-start(f32[2,64,64,128]{3,2,1,0:T(8,128)S(1)} %fusion.23) | copy-start | bytes 12582916
  66.4 6.5 %copy-start.11 = (f32[2,32,64,128]{3,1,2,0:T(8,128)S(1)}, f32[2,32,64,128]{3,1,2,0:T(8,128)}, u32[]{:S(2)}) copy-start(f32[2,32,64,128]{3,1,2,0:T(8,128)} %get-tuple-element.19) | copy-start | bytes 6291460
  85.7 29.5 %all-to-all-start.1 = ((f32[128,1,2048]{2,1,0:T(1,128)}), f32[128,1,2048]{2,1,0:T(1,128)S(1)}, u32[]{:S(2)}, u32[]{:S(2)}) async-start(f32[128,1,2048]{2,1,0:T(1,128)} %reshape.331), calls=%async_computation.1 | async-start | bytes 2097152 | tf_op jit(solution)/shard_map/all_to_all | solution.py:123
  95.5 9.3 %copy-start.5 = (f32[2,64,64,128]{3,2,1,0:T(8,128)S(1)}, f32[2,64,64,128]{3,2,1,0:T(8,128)}, u32[]{:S(2)}) copy-start(f32[2,64,64,128]{3,2,1,0:T(8,128)} %copy-done.4) | copy-start | bytes 12582916
  112.9 12.6 %copy-start.16 = (s32[128]{0:T(128)S(1)}, s32[128]{0:T(128)}, u32[]{:S(2)}) copy-start(s32[128]{0:T(128)} %param.7) | copy-start | bytes 1540
  115.1 10.9 %copy-start.14 = (f32[128,1,2048]{2,1,0:T(1,128)}, f32[128,1,2048]{2,1,0:T(1,128)S(1)}, u32[]{:S(2)}) copy-start(f32[128,1,2048]{2,1,0:T(1,128)S(1)} %all-to-all-done.1) | copy-start | bytes 3145732
  115.1 29.0 %all-to-all-start.2 = ((f32[128,1,2048]{2,1,0:T(1,128)}), f32[128,1,2048]{2,1,0:T(1,128)}, u32[]{:S(2)}, u32[]{:S(2)}) async-start(f32[128,1,2048]{2,1,0:T(1,128)} %reshape.333), calls=%async_computation.2 | async-start | bytes 2097152 | tf_op jit(solution)/shard_map/all_to_all | solution.py:124
  153.0 2.7 copy-start.7
  175.8 3.5 copy-start.9
  179.3 3.1 copy-start.10
  182.4 2.8 copy-start.8
  188.0 3.7 copy-start.13
  197.4 2.2 copy-start.2
  203.0 3.6 copy-start
  226.2 29.6 %all-to-all-start.3 = ((f32[128,1,3072]{2,1,0:T(1,128)}), f32[128,1,3072]{2,1,0:T(1,128)S(1)}, u32[]{:S(2)}, u32[]{:S(2)}) async-start(f32[128,1,3072]{2,1,0:T(1,128)} %reshape.325), calls=%async_computation.3 | async-start | bytes 3145728 | tf_op jit(solution)/shard_map/all_to_all | solution.py:166
  255.8 33.3 %all-to-all-start.4 = ((f32[128,1,3072]{2,1,0:T(1,128)}), f32[128,1,3072]{2,1,0:T(1,128)S(1)}, u32[]{:S(2)}, u32[]{:S(2)}) async-start(f32[128,1,3072]{2,1,0:T(1,128)} %reshape.326), calls=%async_computation.4 | async-start | bytes 3145728 | tf_op jit(solution)/shard_map/all_to_all | solution.py:167
  308.7 3.6 copy-start.1
  312.3 5.4 %copy-start.3 = (f32[2,128,32,128]{3,1,2,0:T(8,128)S(1)}, f32[2,128,32,128]{3,1,2,0:T(8,128)}, u32[]{:S(2)}) copy-start(f32[2,128,32,128]{3,1,2,0:T(8,128)} %get-tuple-element.28) | copy-start | bytes 12582916
  317.8 5.4 %copy-start.12 = (f32[2,96,128,32]{2,3,1,0:T(8,128)S(1)}, f32[2,96,128,32]{2,3,1,0:T(8,128)}, u32[]{:S(2)}) copy-start(f32[2,96,128,32]{2,3,1,0:T(8,128)} %fusion.102) | copy-start | bytes 9437188
  338.6 29.8 %all-to-all-start.5 = ((f32[128,1,2]{2,1,0:T(1,128)}), f32[128,1,2]{2,1,0:T(1,128)S(1)}, u32[]{:S(2)}, u32[]{:S(2)}) async-start(f32[128,1,2]{2,1,0:T(1,128)} %broadcast_in_dim.40), calls=%async_computation.5 | async-start | bytes 131072 | tf_op jit(solution)/shard_map/all_to_all | solution.py:182

commit v16 on v13

--- a/solution.py
+++ b/solution.py
@@ -203,7 +203,7 @@
 
 def encode_slots(peak, parity, field_real, field_imag):
     holo_count, rows, width = field_real.shape
-    split = 2 if rows % 16 == 0 else 1
+    split = 4 if rows % 32 == 0 else 1
     block = rows // split
     field_spec = pl.BlockSpec((1, block, width), lambda k, j: (k, j, 0))
     return pl.pallas_call(

time: 377 us -> 378 us (level)
  no operation moved by 1% of the time
where the time goes in v16:
time: 378 us; the launch traced here: 373 us
  local copies, waits for them, and re-layouts  128 us (34%)
  matrix products  101 us (27%)
  waiting for transfers between devices  49.4 us (13%)
  other arithmetic  43.6 us (12%)
  starting transfers between devices  39.8 us (11%)
  Pallas kernels  10.2 us (3%)
    dot_general x30, matrix products, contract(): jnp.einsum(form, left, right, precision=lax.Precision.HIGH, preferred_ele...  101 us
    sin x2, other arithmetic, make_tables(): jnp.sin(outer_angle).reshape(shape_four)  29.8 us
    gather x4, local copies, waits for them, and re-layouts, pack(): picked = jnp.take(grouped, source, axis=2) * filled[None, None, :, None]  21.6 us
    all_to_all x1, waiting for transfers between devices, body(): lax.all_to_all(blocks, 'col', split_axis=1, concat_axis=1, tiled=True)  18.3 us
    unnamed x45, local copies, waits for them, and re-layouts  12.6 us
    all_to_all x1, waiting for transfers between devices, body(): lax.all_to_all(send_imag.reshape(dense), ('row', 'col'), 0, 0, tiled=True)  10.5 us
    all_to_all x1, waiting for transfers between devices, body(): lax.all_to_all(spec_imag.reshape(send_shape), ('row', 'col'), 0, 0, tiled...  10.4 us
    all_to_all x1, starting transfers between devices, body(): lax.all_to_all(spec_imag.reshape(send_shape), ('row', 'col'), 0, 0, tiled...  10.3 us
  transfers between devices with their start and end apart: 6, of which 4 were waited for; matrix products, arithmetic and copies ran while one was open for 28% of the time, Pallas kernels for 0%

profile of v16, /device:TPU:0, one launch (start us, length us, event | category | flops | bytes accessed | tf_op | source)
XLA Modules:
  0.0 373.0 jit_solution(3629623974455651293)
XLA Ops:
  0.0 4.8 %copy.338 = f32[2,8,64,1024]{3,2,0,1:T(8,128)} copy(f32[2,8,64,1024]{3,2,1,0:T(8,128)} %bitcast.186) | data formatting | bytes 8388608 | tf_op jit(solution)/shard_map/reshape | solution.py:107
  4.8 4.7 %all-to-all-start = ((f32[2,8,64,1024]{3,2,0,1:T(8,128)}), f32[2,8,64,1024]{3,2,0,1:T(8,128)}, u32[]{:S(2)}, u32[]{:S(2)}) async-start(f32[2,8,64,1024]{3,2,0,1:T(8,128)} %copy.338), calls=%async_computation | async-start | bytes 8388608 | tf_op jit(solution)/shard_map/all_to_all | solution.py:108
  10.4 18.6 %fusion.59 = (f32[2,32,64,128]{3,1,2,0:T(8,128)}, f32[2,32,64,128]{3,1,2,0:T(8,128)}, f32[2,32,64,128]{3,1,2,0:T(8,128)}, f32[2,32,64,128]{3,1,2,0:T(8,128)S(1)}) fusion(s32[128]{0:T(128)S(1)} %and_select_fusion.3, s32[2,32,64]{1,2,0:T(8,128)S(1)} %get-tuple-element.36, s32[2,32,64]{1,2,0:T(8,128)S(1)} %get-tuple-element.37), kind=kLoop, calls=%fused_computation.77 | loop fusion | flops 14680064 | bytes 8421888 | tf_op jit(solution)/shard_map/sin | solution.py:44
  29.6 11.2 %fusion.35 = (f32[2,128,32,128]{3,1,2,0:T(8,128)}, f32[2,128,32,128]{3,1,2,0:T(8,128)}) fusion(s32[128]{0:T(128)S(1)} %and_select_fusion, s32[128,32]{0,1:T(8,128)S(1)} %multiply_add_fusion), kind=kLoop, calls=%fused_computation.53 | loop fusion | flops 14680064 | bytes 8405504 | tf_op jit(solution)/shard_map/sin | solution.py:44
  40.9 18.3 %all-to-all-done = f32[2,8,64,1024]{3,2,0,1:T(8,128)} async-done(((f32[2,8,64,1024]{3,2,0,1:T(8,128)}), f32[2,8,64,1024]{3,2,0,1:T(8,128)}, u32[]{:S(2)}, u32[]{:S(2)}) %all-to-all-start) | async-done | bytes 4194336 | tf_op jit(solution)/shard_map/all_to_all | solution.py:108
  66.5 6.5 %fusion.9 = f32[64,2,64,32]{2,3,1,0:T(8,128)S(1)} fusion(f32[2,64,64,128]{3,2,1,0:T(8,128)S(1)} %fusion.26, f32[2,32,64,128]{3,1,2,0:T(8,128)S(1)} %get-tuple-element.21), kind=kOutput, calls=%fused_computation.16 | convolution fusion | flops 201326592 | bytes 7340032 | tf_op jit(solution)/shard_map/kqpb,krpb->qpkr/dot_general | solution.py:24
  73.0 6.5 %subtract_bitcast_fusion.3 = f32[32,64,2,64]{3,0,2,1:T(8,128)S(1)} fusion(f32[64,2,64,32]{2,3,1,0:T(8,128)S(1)} %fusion.9, f32[2,32,64,128]{3,1,2,0:T(8,128)S(1)} %copy-done.10, f32[2,64,64,128]{3,2,1,0:T(8,128)S(1)} %fusion.23), kind=kOutput, calls=%fused_computation.58 | convolution fusion | flops 201588736 | bytes 8388608 | tf_op jit(solution)/shard_map/kqpb,krpb->qpkr/dot_general | solution.py:24
  85.8 9.5 %all-to-all-start.1 = ((f32[128,1,2048]{2,1,0:T(1,128)}), f32[128,1,2048]{2,1,0:T(1,128)S(1)}, u32[]{:S(2)}, u32[]{:S(2)}) async-start(f32[128,1,2048]{2,1,0:T(1,128)} %reshape.329), calls=%async_computation.1 | async-start | bytes 2097152 | tf_op jit(solution)/shard_map/all_to_all | solution.py:123
  95.4 9.3 %fusion.7 = f32[64,2,64,32]{2,3,1,0:T(8,128)S(1)} fusion(f32[2,64,64,128]{3,2,1,0:T(8,128)} %copy-done.6, f32[2,32,64,128]{3,1,2,0:T(8,128)} %get-tuple-element.19), kind=kOutput, calls=%fused_computation.14 | convolution fusion | flops 201326592 | bytes 7340032 | tf_op jit(solution)/shard_map/kqpb,krpb->qpkr/dot_general | solution.py:24
  104.7 6.8 %add_bitcast_fusion.3 = f32[32,64,2,64]{3,0,2,1:T(8,128)S(1)} fusion(f32[64,2,64,32]{2,3,1,0:T(8,128)S(1)} %fusion.7, f32[2,32,64,128]{3,1,2,0:T(8,128)S(1)} %get-tuple-element.21, f32[2,64,64,128]{3,2,1,0:T(8,128)S(1)} %copy-done.5), kind=kOutput, calls=%fused_computation.57 | convolution fusion | flops 201588736 | bytes 8388608 | tf_op jit(solution)/shard_map/kqpb,krpb->qpkr/dot_general | solution.py:24
  115.3 10.3 %all-to-all-start.2 = ((f32[128,1,2048]{2,1,0:T(1,128)}), f32[128,1,2048]{2,1,0:T(1,128)}, u32[]{:S(2)}, u32[]{:S(2)}) async-start(f32[128,1,2048]{2,1,0:T(1,128)} %reshape.331), calls=%async_computation.2 | async-start | bytes 2097152 | tf_op jit(solution)/shard_map/all_to_all | solution.py:124
  126.5 4.3 %reduce.6 = f32[128,2048]{1,0:T(8,128)S(1)} reduce(f32[128,1,2048]{2,1,0:T(1,128)} %copy-done.17, f32[]{:T(128)} %broadcast.451), dimensions={1}, to_apply=%all_to_all.20.reduce_sub_computation | reduce | bytes 2097156 | tf_op jit(solution)/shard_map/all_to_all | solution.py:123
  133.9 10.4 %all-to-all-done.2 = f32[128,1,2048]{2,1,0:T(1,128)} async-done(((f32[128,1,2048]{2,1,0:T(1,128)}), f32[128,1,2048]{2,1,0:T(1,128)}, u32[]{:S(2)}, u32[]{:S(2)}) %all-to-all-start.2) | async-done | bytes 1048608 | tf_op jit(solution)/shard_map/all_to_all | solution.py:124
  144.3 4.3 %reduce.7 = f32[128,2048]{1,0:T(8,128)S(1)} reduce(f32[128,1,2048]{2,1,0:T(1,128)} %all-to-all-done.2, f32[]{:T(128)} %broadcast.451), dimensions={1}, to_apply=%all_to_all.21.reduce_sub_computation | reduce | bytes 2097156 | tf_op jit(solution)/shard_map/all_to_all | solution.py:124
  204.1 5.3 %gather_fusion.1 = f32[384,2,16,32]{3,2,1,0:T(8,128)} fusion(f32[2,16,128,32]{3,1,2,0:T(8,128)} %copy.382, s32[1024]{0:T(1024)S(1)} %pad_clamp_fusion), kind=kCustom, calls=%fused_computation.1.clone | custom fusion | bytes 3147264 | tf_op jit(solution)/shard_map/jit(_take)/gather | solution.py:154
  209.4 6.4 %copy.383 = f32[384,2,16,32]{0,3,2,1:T(8,128)} copy(f32[384,2,16,32]{3,2,1,0:T(8,128)} %gather_fusion.1) | data formatting | bytes 3145728 | tf_op jit(solution)/shard_map/jit(_take)/gather | solution.py:154
  220.1 5.6 %copy.373 = f32[384,2,16,32]{0,3,2,1:T(8,128)S(1)} copy(f32[384,2,16,32]{3,2,1,0:T(8,128)} %gather_fusion) | data formatting | bytes 3145728 | tf_op jit(solution)/shard_map/jit(_take)/gather | solution.py:154
  227.9 5.0 %copy.374 = f32[2,16,384,32]{3,2,1,0:T(8,128)} copy(f32[2,16,384,32]{2,3,1,0:T(8,128)} %get-tuple-element.45) | data formatting | bytes 3145728 | tf_op jit(solution)/shard_map/mul | solution.py:154
  238.7 4.5 %copy.376 = f32[128,1,3072]{2,1,0:T(1,128)} copy(f32[128,1,3072]{0,2,1:T(8,128)} %bitcast.182) | data formatting | bytes 3145728 | tf_op jit(solution)/shard_map/reshape | solution.py:160
  243.1 5.8 %all-to-all-start.3 = ((f32[128,1,3072]{2,1,0:T(1,128)}), f32[128,1,3072]{2,1,0:T(1,128)}, u32[]{:S(2)}, u32[]{:S(2)}) async-start(f32[128,1,3072]{2,1,0:T(1,128)} %copy.376), calls=%async_computation.3 | async-start | bytes 3145728 | tf_op jit(solution)/shard_map/all_to_all | solution.py:160
  258.7 4.5 %copy.386 = f32[128,1,3072]{2,1,0:T(1,128)} copy(f32[128,1,3072]{0,2,1:T(8,128)} %bitcast.183) | data formatting | bytes 3145728 | tf_op jit(solution)/shard_map/reshape | solution.py:161
  263.2 10.1 %all-to-all-done.3 = f32[128,1,3072]{2,1,0:T(1,128)} async-done(((f32[128,1,3072]{2,1,0:T(1,128)}), f32[128,1,3072]{2,1,0:T(1,128)}, u32[]{:S(2)}, u32[]{:S(2)}) %all-to-all-start.3) | async-done | bytes 1572896 | tf_op jit(solution)/shard_map/all_to_all | solution.py:160
  273.3 4.6 %all-to-all-start.4 = ((f32[128,1,3072]{2,1,0:T(1,128)}), f32[128,1,3072]{2,1,0:T(1,128)S(1)}, u32[]{:S(2)}, u32[]{:S(2)}) async-start(f32[128,1,3072]{2,1,0:T(1,128)} %copy.386), calls=%async_computation.4 | async-start | bytes 3145728 | tf_op jit(solution)/shard_map/all_to_all | solution.py:161
  292.2 10.5 %all-to-all-done.4 = f32[128,1,3072]{2,1,0:T(1,128)S(1)} async-done(((f32[128,1,3072]{2,1,0:T(1,128)}), f32[128,1,3072]{2,1,0:T(1,128)S(1)}, u32[]{:S(2)}, u32[]{:S(2)}) %all-to-all-start.4) | async-done | bytes 1572896 | tf_op jit(solution)/shard_map/all_to_all | solution.py:161
  312.4 5.4 %fusion.15 = f32[2,32,96,128]{3,2,1,0:T(8,128)S(1)} fusion(f32[2,128,32,128]{3,1,2,0:T(8,128)S(1)} %copy-done.3, f32[2,96,32,128]{3,2,1,0:T(8,128)S(1)} %add_bitcast_fusion.1), kind=kOutput, calls=%fused_computation.37 | convolution fusion | flops 603979776 | bytes 10485760 | tf_op jit(solution)/shard_map/kqpb,krpb->krqp/dot_general | solution.py:24
  317.9 5.4 %fusion.17 = f32[2,32,96,128]{3,2,1,0:T(8,128)S(1)} fusion(f32[2,128,32,128]{3,1,2,0:T(8,128)S(1)} %copy-done.1, f32[2,96,32,128]{3,2,1,0:T(8,128)S(1)} %add_bitcast_fusion.1), kind=kOutput, calls=%fused_computation.39 | convolution fusion | flops 603979776 | bytes 10485760 | tf_op jit(solution)/shard_map/kqpb,krpb->krqp/dot_general | solution.py:24
  325.0 5.6 %subtract_bitcast_fusion = f32[2,96,128,32]{2,1,3,0:T(8,128)S(1)} fusion(f32[2,32,96,128]{3,2,1,0:T(8,128)S(1)} %fusion.17, f32[2,128,32,128]{3,1,2,0:T(8,128)S(1)} %copy-done.3, f32[2,96,32,128]{3,2,1,0:T(8,128)S(1)} %subtract_bitcast_fusion.1), kind=kOutput, calls=%fused_computation.30 | convolution fusion | flops 604766208 | bytes 13631488 | tf_op jit(solution)/shard_map/kqpb,krpb->krqp/dot_general | solution.py:24
  330.6 7.5 %sqrt_reduce_fusion = (f32[2]{0:T(128)S(1)}, f32[2,96,128,32]{2,1,3,0:T(8,128)}) fusion(f32[2,96,128,32]{2,1,3,0:T(8,128)S(1)} %subtract_bitcast_fusion, f32[2,32,96,128]{3,2,1,0:T(8,128)S(1)} %fusion.15, f32[2,128,32,128]{3,1,2,0:T(8,128)S(1)} %copy-done.1, f32[2,96,32,128]{3,2,1,0:T(8,128)S(1)} %subtract_bitcast_fusion.1), kind=kOutput, calls=%fused_computation.28 | convolution fusion | flops 607911936 | bytes 16777224 | tf_op jit(solution)/shard_map/kqpb,krpb->krqp/dot_general | solution.py:24
  338.7 4.8 %all-to-all-start.5 = ((f32[128,1,2]{2,1,0:T(1,128)}), f32[128,1,2]{2,1,0:T(1,128)S(1)}, u32[]{:S(2)}, u32[]{:S(2)}) async-start(f32[128,1,2]{2,1,0:T(1,128)} %broadcast_in_dim.40), calls=%async_computation.5 | async-start | bytes 131072 | tf_op jit(solution)/shard_map/all_to_all | solution.py:175
  347.6 5.4 %copy.402.real_ref = f32[2,96,4096]{2,1,0:T(8,128)} copy(f32[2,96,4096]{1,2,0:T(8,128)} %bitcast.170) | data formatting | bytes 6291456 | tf_op jit(solution)/shard_map/reshape | solution.py:73
  356.3 5.3 %copy.403.imag_ref = f32[2,96,4096]{2,1,0:T(8,128)} copy(f32[2,96,4096]{1,2,0:T(8,128)} %bitcast.171) | data formatting | bytes 6291456 | tf_op jit(solution)/shard_map/reshape | solution.py:73
  362.3 10.2 %shard_map.37 = f32[2,2,96,4096]{3,2,1,0:T(8,128)} custom-call(f32[2]{0:T(128)} %reduce_max.19.peak_ref, s32[96,1]{1,0:T(8,128)} %add_select_fusion.9.parity_ref, f32[2,96,4096]{2,1,0:T(8,128)} %copy.402.real_ref, f32[2,96,4096]{2,1,0:T(8,128)} %copy.403.imag_ref), custom_call_target="tpu_custom_call" | custom-call | tf_op jit(solution)/shard_map/pallas_call | solution.py:209
  (131 shorter events, 134.2 us)
Async XLA Ops:
  4.8 4.8 %copy-start.18 = (s32[2,2]{1,0:T(2,128)S(1)}, s32[2,2]{1,0:T(2,128)}, u32[]{:S(2)}) copy-start(s32[2,2]{1,0:T(2,128)} %param.6) | copy-start | bytes 52
  4.8 54.4 %all-to-all-start = ((f32[2,8,64,1024]{3,2,0,1:T(8,128)}), f32[2,8,64,1024]{3,2,0,1:T(8,128)}, u32[]{:S(2)}, u32[]{:S(2)}) async-start(f32[2,8,64,1024]{3,2,0,1:T(8,128)} %copy.338), calls=%async_computation | async-start | bytes 8388608 | tf_op jit(solution)/shard_map/all_to_all | solution.py:108
  10.4 18.6 %copy-start.19 = (s32[128]{0:T(128)S(1)}, s32[128]{0:T(128)}, u32[]{:S(2)}) copy-start(s32[128]{0:T(128)} %param.7) | copy-start | bytes 1540
  64.4 8.6 %copy-start.4 = (f32[2,64,64,128]{3,2,1,0:T(8,128)}, f32[2,64,64,128]{3,2,1,0:T(8,128)S(1)}, u32[]{:S(2)}) copy-start(f32[2,64,64,128]{3,2,1,0:T(8,128)S(1)} %fusion.23) | copy-start | bytes 12582916
  66.5 6.5 %copy-start.6 = (f32[2,64,64,128]{3,2,1,0:T(8,128)}, f32[2,64,64,128]{3,2,1,0:T(8,128)S(1)}, u32[]{:S(2)}) copy-start(f32[2,64,64,128]{3,2,1,0:T(8,128)S(1)} %fusion.26) | copy-start | bytes 12582916
  66.5 6.5 %copy-start.10 = (f32[2,32,64,128]{3,1,2,0:T(8,128)S(1)}, f32[2,32,64,128]{3,1,2,0:T(8,128)}, u32[]{:S(2)}) copy-start(f32[2,32,64,128]{3,1,2,0:T(8,128)} %get-tuple-element.19) | copy-start | bytes 6291460
  85.8 29.5 %all-to-all-start.1 = ((f32[128,1,2048]{2,1,0:T(1,128)}), f32[128,1,2048]{2,1,0:T(1,128)S(1)}, u32[]{:S(2)}, u32[]{:S(2)}) async-start(f32[128,1,2048]{2,1,0:T(1,128)} %reshape.329), calls=%async_computation.1 | async-start | bytes 2097152 | tf_op jit(solution)/shard_map/all_to_all | solution.py:123
  95.4 9.3 %copy-start.5 = (f32[2,64,64,128]{3,2,1,0:T(8,128)S(1)}, f32[2,64,64,128]{3,2,1,0:T(8,128)}, u32[]{:S(2)}) copy-start(f32[2,64,64,128]{3,2,1,0:T(8,128)} %copy-done.4) | copy-start | bytes 12582916
  115.3 10.6 %copy-start.17 = (f32[128,1,2048]{2,1,0:T(1,128)}, f32[128,1,2048]{2,1,0:T(1,128)S(1)}, u32[]{:S(2)}) copy-start(f32[128,1,2048]{2,1,0:T(1,128)S(1)} %all-to-all-done.1) | copy-start | bytes 3145732
  115.3 29.0 %all-to-all-start.2 = ((f32[128,1,2048]{2,1,0:T(1,128)}), f32[128,1,2048]{2,1,0:T(1,128)}, u32[]{:S(2)}, u32[]{:S(2)}) async-start(f32[128,1,2048]{2,1,0:T(1,128)} %reshape.331), calls=%async_computation.2 | async-start | bytes 2097152 | tf_op jit(solution)/shard_map/all_to_all | solution.py:124
  153.4 2.7 copy-start.7
  166.1 2.7 copy-start.14
  171.3 3.7 copy-start.9
  178.0 1.8 copy-start.8
  179.8 1.8 copy-start.13
  184.5 2.2 copy-start.2
  190.1 3.8 %copy-start = (f32[2,128,32,128]{3,1,2,0:T(8,128)S(1)}, f32[2,128,32,128]{3,1,2,0:T(8,128)}, u32[]{:S(2)}) copy-start(f32[2,128,32,128]{3,1,2,0:T(8,128)} %get-tuple-element.29) | copy-start | bytes 12582916
  220.1 5.6 %copy-start.16 = (f32[384,2,16,32]{0,3,2,1:T(8,128)S(1)}, f32[384,2,16,32]{0,3,2,1:T(8,128)}, u32[]{:S(2)}) copy-start(f32[384,2,16,32]{0,3,2,1:T(8,128)} %copy.383) | copy-start | bytes 4718596
  243.1 5.8 %copy-start.15 = (f32[2,16,384,32]{2,3,1,0:T(8,128)S(1)}, f32[2,16,384,32]{2,3,1,0:T(8,128)}, u32[]{:S(2)}) copy-start(f32[2,16,384,32]{2,3,1,0:T(8,128)} %get-tuple-element.44) | copy-start | bytes 4718596
  243.1 30.2 %all-to-all-start.3 = ((f32[128,1,3072]{2,1,0:T(1,128)}), f32[128,1,3072]{2,1,0:T(1,128)}, u32[]{:S(2)}, u32[]{:S(2)}) async-start(f32[128,1,3072]{2,1,0:T(1,128)} %copy.376), calls=%async_computation.3 | async-start | bytes 3145728 | tf_op jit(solution)/shard_map/all_to_all | solution.py:160
  273.3 29.4 %all-to-all-start.4 = ((f32[128,1,3072]{2,1,0:T(1,128)}), f32[128,1,3072]{2,1,0:T(1,128)S(1)}, u32[]{:S(2)}, u32[]{:S(2)}) async-start(f32[128,1,3072]{2,1,0:T(1,128)} %copy.386), calls=%async_computation.4 | async-start | bytes 3145728 | tf_op jit(solution)/shard_map/all_to_all | solution.py:161
  308.8 3.6 copy-start.3
  312.4 5.5 %copy-start.1 = (f32[2,128,32,128]{3,1,2,0:T(8,128)S(1)}, f32[2,128,32,128]{3,1,2,0:T(8,128)}, u32[]{:S(2)}) copy-start(f32[2,128,32,128]{3,1,2,0:T(8,128)} %get-tuple-element.29) | copy-start | bytes 12582916
  317.8 5.4 %copy-start.12 = (f32[2,96,128,32]{2,3,1,0:T(8,128)S(1)}, f32[2,96,128,32]{2,3,1,0:T(8,128)}, u32[]{:S(2)}) copy-start(f32[2,96,128,32]{2,3,1,0:T(8,128)} %fusion.102) | copy-start | bytes 9437188
  338.7 22.9 %all-to-all-start.5 = ((f32[128,1,2]{2,1,0:T(1,128)}), f32[128,1,2]{2,1,0:T(1,128)S(1)}, u32[]{:S(2)}, u32[]{:S(2)}) async-start(f32[128,1,2]{2,1,0:T(1,128)} %broadcast_in_dim.40), calls=%async_computation.5 | async-start | bytes 131072 | tf_op jit(solution)/shard_map/all_to_all | solution.py:175
  347.5 5.4 %copy-start.11 = (f32[2,96,128,32]{2,1,3,0:T(8,128)S(1)}, f32[2,96,128,32]{2,1,3,0:T(8,128)}, u32[]{:S(2)}) copy-start(f32[2,96,128,32]{2,1,3,0:T(8,128)} %get-tuple-element.55) | copy-start | bytes 9437188
